TPU v7x, 256 devices: a whole 4x4x8 slice. The times are simulated.
256 devices in a mesh: seq: 64 (over z, x, core), tensor: 4 (over y).
Axes of the slice: x: 4, y: 4, z: 8, core: 2. Of those that a mesh axis runs over, the one named last changes fastest.
Arguments:
- residual: bfloat16 [16384, 2048], P('seq', 'tensor'), may hold values from -0.29882812 to 0.29882812
- query: bfloat16 [16384, 2048], P('seq', 'tensor'), may hold values from -13 to 13
- new_keys: bfloat16 [16384, 2048], P('seq', 'tensor'), may hold values from -6 to 6
- new_values: bfloat16 [16384, 2048], P('seq', 'tensor'), may hold values from -6 to 6
- leaf_kv: bfloat16 [2, 4096, 2048], P(None, 'seq', 'tensor'), may hold values from -6 to 6
- branch_kv: bfloat16 [2, 4096, 2048], P(None, 'seq', 'tensor'), may hold values from -6 to 6
- root_kv: bfloat16 [2, 2048, 2048], P(None, 'seq', 'tensor'), may hold values from -10 to 10
- out_weight: bfloat16 [2048, 2048], P('tensor'), may hold values from -0.125 to 0.125
- norm_gain: float32 [2048], replicated, may hold values from 0.25 to 1.75
- norm_bias: float32 [2048], replicated, may hold values from -1.8 to 1.8
- up_weight: bfloat16 [2048, 4096], P(None, 'tensor'), may hold values from -0.125 to 0.125
- up_bias: float32 [4096], P('tensor'), may hold values from -3 to 3
- down_weight: bfloat16 [4096, 2048], P('tensor'), may hold values from -0.09375 to 0.09375
- down_bias: float32 [2048], replicated, may hold values from -1.8 to 1.8
- segment: int32 [64], replicated, may hold values from 0 to 15, never falling along the last dimension, each value on 1 to 8 neighbouring positions
- new_len: int32 [64], replicated, may hold values from 1 to 256, 12288 in all
Outputs:
- layer_out: bfloat16 [16384, 2048], P('seq', 'tensor')
Inputs may be any that keep to these rules, and one draw needn't show every extreme that they name: `segment`: never falling along the requests, so the requests of one branch node have consecutive indices; every node 0 to 15 has 1 to 8 requests and one has exactly 8. `new_len`: the largest is exactly 256; they sum to 12288.
All inputs are finite; a program needn't handle non-finite values.
Results may differ from a plain program's by a relative error of at most 0.018.
Values may be sent and summed in bfloat16 or wider, within the bound.
No kernel may reach another device: no remote copies, remote signals or barrier semaphores. Data moves between devices by JAX's collectives and lax.ppermute only.
A program may use at most 128 MiB of HBM per device.

v0:
```python
import jax
import jax.numpy as jnp
from jax import lax
from jax.sharding import PartitionSpec as P

HD = 128


NEGATIVE_FILL = -1e30
NORM_EPSILON = 1e-05
BLOCK_KEYS = 512


def attend(running, query_heads, key_rows, value_rows, allowed):
    largest, totals, accumulated = running
    head_count = query_heads.shape[1]
    head_width = query_heads.shape[2]
    key_heads = key_rows.reshape(key_rows.shape[0], head_count, head_width)
    value_heads = value_rows.reshape(value_rows.shape[0], head_count, head_width)
    scores = jnp.einsum(
        "qhd,khd->hqk", query_heads, key_heads, preferred_element_type=jnp.float32
    ) * head_width ** (-0.5)
    scores = jnp.where(allowed, scores, NEGATIVE_FILL)
    new_largest = jnp.maximum(largest, jnp.max(scores, axis=2))
    weights = jnp.where(allowed, jnp.exp(scores - new_largest[:, :, None]), 0.0)
    factor = jnp.exp(largest - new_largest)
    accumulated = accumulated * factor[:, :, None] + jnp.einsum(
        "hqk,khd->hqd",
        weights.astype(jnp.bfloat16),
        value_heads,
        preferred_element_type=jnp.float32,
    )
    totals = totals * factor + jnp.sum(weights, axis=2)
    return (new_largest, totals, accumulated)


def attend_blocks(running, query_heads, key_rows, value_rows):
    for block_start in range(0, key_rows.shape[0], BLOCK_KEYS):
        running = attend(
            running,
            query_heads,
            key_rows[block_start : block_start + BLOCK_KEYS],
            value_rows[block_start : block_start + BLOCK_KEYS],
            True,
        )
    return running


def per_device(
    residual,
    query,
    new_keys,
    new_values,
    leaf_kv,
    branch_kv,
    root_kv,
    out_weight,
    norm_gain,
    norm_bias,
    up_weight,
    up_bias,
    down_weight,
    down_bias,
    segment,
    new_len,
):
    row_count = query.shape[0]
    head_count = query.shape[1] // HD
    query_heads = query.reshape(row_count, head_count, HD)
    device = lax.axis_index("seq")
    my_segment = segment[device]
    branch_count = lax.axis_size("seq") // 4
    running = (
        jnp.full((head_count, row_count), NEGATIVE_FILL, jnp.float32),
        jnp.zeros((head_count, row_count), jnp.float32),
        jnp.zeros((head_count, row_count, HD), jnp.float32),
    )
    running = attend_blocks(
        running,
        query_heads,
        lax.all_gather(root_kv[0], "seq", axis=0, tiled=True),
        lax.all_gather(root_kv[1], "seq", axis=0, tiled=True),
    )
    key_rows = lax.all_gather(branch_kv[0], "seq", axis=0, tiled=True)
    value_rows = lax.all_gather(branch_kv[1], "seq", axis=0, tiled=True)
    feature_width = key_rows.shape[1]
    keys_mine = lax.dynamic_index_in_dim(
        key_rows.reshape(-1, branch_count, feature_width), my_segment, 1, keepdims=False
    )
    values_mine = lax.dynamic_index_in_dim(
        value_rows.reshape(-1, branch_count, feature_width), my_segment, 1, keepdims=False
    )
    running = attend_blocks(running, query_heads, keys_mine, values_mine)
    running = attend(running, query_heads, leaf_kv[0], leaf_kv[1], True)
    query_pos = jnp.arange(row_count, dtype=jnp.int32)
    allowed_new = (query_pos[None, :] <= query_pos[:, None]) & (
        query_pos[None, :] < new_len[device]
    )
    running = attend(running, query_heads, new_keys, new_values, allowed_new[None])
    largest, totals, accumulated = running
    attention = (
        jnp.transpose(accumulated / totals[:, :, None], (1, 0, 2))
        .reshape(row_count, head_count * HD)
        .astype(jnp.bfloat16)
    )
    projected = jnp.dot(attention, out_weight, preferred_element_type=jnp.float32)
    share_width = residual.shape[1]
    column = lax.axis_index("tensor") * share_width
    projected = lax.psum(projected.astype(jnp.bfloat16), "tensor").astype(jnp.float32)
    full_residual = lax.all_gather(residual, "tensor", axis=1, tiled=True)
    mid_full = (full_residual.astype(jnp.float32) + projected).astype(jnp.bfloat16)
    wide_mid = mid_full.astype(jnp.float32)
    row_mean = jnp.mean(wide_mid, axis=1, keepdims=True)
    row_var = jnp.mean(wide_mid * wide_mid, axis=1, keepdims=True) - row_mean * row_mean
    normed = (
        (wide_mid - row_mean) * lax.rsqrt(row_var + NORM_EPSILON) * norm_gain + norm_bias
    ).astype(jnp.bfloat16)
    up_sum = jnp.dot(normed, up_weight, preferred_element_type=jnp.float32)
    mid_share = lax.dynamic_slice_in_dim(mid_full, column, share_width, 1)
    hidden = jax.nn.gelu(up_sum + up_bias, approximate=False).astype(jnp.bfloat16)
    partial_value = jnp.dot(hidden, down_weight, preferred_element_type=jnp.float32)
    summed = lax.psum_scatter(
        partial_value.astype(jnp.bfloat16), "tensor", scatter_dimension=1, tiled=True
    ).astype(jnp.float32)
    down_share = lax.dynamic_slice_in_dim(down_bias, column, share_width, 0)
    return (summed + down_share + mid_share.astype(jnp.float32)).astype(jnp.bfloat16)


def solution(mesh):
    return jax.shard_map(
        per_device,
        mesh=mesh,
        in_specs=(
            P("seq", "tensor"),
            P("seq", "tensor"),
            P("seq", "tensor"),
            P("seq", "tensor"),
            P(None, "seq", "tensor"),
            P(None, "seq", "tensor"),
            P(None, "seq", "tensor"),
            P("tensor", None),
            P(),
            P(),
            P(None, "tensor"),
            P("tensor"),
            P("tensor", None),
            P(),
            P(),
            P(),
        ),
        out_specs=P("seq", "tensor"),
        check_vma=False,
    )
```

profile of v0, /device:TPU:2, one launch (start us, length us, event | category | flops | bytes accessed | tf_op | source)
XLA Modules:
  0.0 453.0 jit_solution(13293988858656092174)
XLA Ops:
  6.5 1.5 fusion.182
  8.2 0.7 all-gather.12.cloned.1.call-update
  8.9 1.5 fusion.181
  11.7 1.2 dynamic_slice.22
  12.9 0.6 iota_compare_fusion.1
  13.6 1.3 dynamic_slice.19
  16.2 0.9 fusion.180
  17.1 1.8 copy.117
  19.5 1.9 fusion.184
  21.4 2.0 fusion.183
  23.4 66.1 %all-gather.14.cloned.1.call-done = bf16[1,2048,512]{2,1,0:T(8,128)(2,1)} async-done(((bf16[1,32,512]{2,1,0:T(8,128)(2,1)}), bf16[1,2048,512]{2,1,0:T(8,128)(2,1)}) %all-gather.14.cloned.1.call-update) | async-done | bytes 2097168 | tf_op jit(solution)/shard_map/all_gather | solution.py:82
  89.5 2.9 fusion.178
  92.4 2.1 copy.97
  94.4 72.8 %all-gather.12.cloned.1.call-done = bf16[1,2048,512]{2,1,0:T(8,128)(2,1)} async-done(((bf16[1,32,512]{2,1,0:T(8,128)(2,1)}), bf16[1,2048,512]{2,1,0:T(8,128)(2,1)}) %all-gather.12.cloned.1.call-update) | async-done | bytes 2097168 | tf_op jit(solution)/shard_map/all_gather | solution.py:81
  167.2 2.9 fusion.179
  170.1 2.1 copy.118
  172.2 2.0 copy.120
  174.2 2.1 copy.119
  176.3 2.1 copy.121
  178.3 2.0 copy.93
  180.4 2.1 copy.89
  182.4 2.1 copy.85
  184.5 2.9 multiply_reduce_fusion
  187.4 1.7 multiply_reduce_fusion.2
  189.1 1.8 multiply_reduce_fusion.1
  190.9 2.3 multiply_reduce_fusion.3
  193.2 53.1 %all-gather.18.cloned.1.call-done = bf16[1,4096,512]{2,1,0:T(8,128)(2,1)} async-done(((bf16[1,64,512]{2,1,0:T(8,128)(2,1)}), bf16[1,4096,512]{2,1,0:T(8,128)(2,1)}) %all-gather.18.cloned.1.call-update) | async-done | bytes 4194320 | tf_op jit(solution)/shard_map/all_gather | solution.py:85
  246.3 78.8 %all-gather.16.cloned.1.call-done = bf16[1,4096,512]{2,1,0:T(8,128)(2,1)} async-done(((bf16[1,64,512]{2,1,0:T(8,128)(2,1)}), bf16[1,4096,512]{2,1,0:T(8,128)(2,1)}) %all-gather.16.cloned.1.call-update) | async-done | bytes 4194320 | tf_op jit(solution)/shard_map/all_gather | solution.py:84
  325.1 4.3 constant_dynamic-slice_fusion
  329.4 1.9 copy.122
  331.2 1.9 copy.98
  333.1 1.4 fusion.185
  334.5 0.7 fusion.176
  336.8 0.6 fusion.11
  337.9 0.6 fusion.9
  338.6 0.6 fusion.7
  340.3 0.7 fusion.23
  341.5 0.7 fusion.21
  342.5 0.7 fusion.19
  343.3 0.7 fusion.25
  344.3 1.8 convolution_convert_fusion
  346.1 5.9 %all-gather.10.cloned.1.call-done = bf16[256,2048]{1,0:T(8,128)(2,1)} async-done(((bf16[256,512]{1,0:T(8,128)(2,1)}), bf16[256,2048]{1,0:T(8,128)(2,1)}) %all-gather.10.cloned.1.call-update) | async-done | bytes 1048592 | tf_op jit(solution)/shard_map/all_gather | solution.py:110
  352.0 53.8 %all-reduce.2.cloned.1.call-done = bf16[256,2048]{1,0:T(8,128)(2,1)} async-done(((bf16[256,2048]{1,0:T(8,128)(2,1)}), bf16[256,2048]{1,0:T(8,128)(2,1)}) %all-reduce.2.cloned.1.call-update) | async-done | bytes 1048592 | tf_op jit(solution)/shard_map/psum | solution.py:109
  405.8 2.1 convert_reduce_fusion
  407.9 9.1 %convolution_convert_fusion.1 = bf16[256,2048]{1,0:T(8,128)(2,1)} fusion(bf16[1024,2048]{1,0:T(8,128)(2,1)} %param.28, bf16[2048,1024]{1,0:T(8,128)(2,1)} %param.26, bf16[256,2048]{1,0:T(8,128)(2,1)S(1)} %get-tuple-element.7, f32[2048]{0:T(1024)S(1)} %copy-done.18, f32[2048]{0:T(1024)S(1)} %copy-done.19, f32[256]{0:T(256)S(1)} %get-tuple-element.38, ...), kind=kOutput, calls=%fused_computation.4 | convolution fusion | flops 2168455168 | bytes 10508288 | tf_op jit(solution)/shard_map/dot_general | solution.py:121
  417.0 0.8 dynamic_slice.23
  417.8 26.7 %reduce-scatter.2.cloned.1.call-done = bf16[256,512]{1,0:T(8,128)(2,1)} async-done(((bf16[256,2048]{1,0:T(8,128)(2,1)}), bf16[256,512]{1,0:T(8,128)(2,1)}) %reduce-scatter.2.cloned.1.call-update) | async-done | bytes 262160 | tf_op jit(solution)/shard_map/reduce_scatter | solution.py:122
  444.4 1.7 add_convert_fusion.1
  (67 shorter events, 6.0 us)
Async XLA Ops:
  6.5 337.7 %copy-start = (bf16[512,2048]{1,0:T(8,128)(2,1)S(1)}, bf16[512,2048]{1,0:T(8,128)(2,1)}, u32[]{:S(2)}) copy-start(bf16[512,2048]{1,0:T(8,128)(2,1)} %param.23) | copy-start | bytes 6291460
  6.5 14.9 %copy-start.5 = (bf16[256,512]{1,0:T(8,128)(2,1)S(1)}, bf16[256,512]{1,0:T(8,128)(2,1)}, u32[]{:S(2)}) copy-start(bf16[256,512]{1,0:T(8,128)(2,1)} %param.17) | copy-start | bytes 786436
  6.5 82.9 %all-gather.14.cloned.1.call-start = ((), (), s32[]{:S(2)}) async-start(), calls=%async_computation.5 | async-start | bytes 2129920 | tf_op jit(solution)/shard_map/all_gather | solution.py:82
  8.1 159.1 %all-gather.12.cloned.1.call-start = ((), (), s32[]{:S(2)}) async-start(), calls=%async_computation.4 | async-start | bytes 2129920 | tf_op jit(solution)/shard_map/all_gather | solution.py:81
  8.9 237.4 %all-gather.18.cloned.1.call-start = ((), (), s32[]{:S(2)}) async-start(), calls=%async_computation.7 | async-start | bytes 4259840 | tf_op jit(solution)/shard_map/all_gather | solution.py:85
  10.5 314.7 %all-gather.16.cloned.1.call-start = ((), (), s32[]{:S(2)}) async-start(), calls=%async_computation.6 | async-start | bytes 4259840 | tf_op jit(solution)/shard_map/all_gather | solution.py:84
  11.0 340.9 %all-gather.10.cloned.1.call-start = ((), (), s32[]{:S(2)}) async-start(), calls=%async_computation.1 | async-start | bytes 1310720 | tf_op jit(solution)/shard_map/all_gather | solution.py:110
  11.6 394.2 %all-reduce.2.cloned.1.call-start = ((), (), s32[]{:S(2)}) async-start(), calls=%async_computation.2 | async-start | bytes 2097152 | tf_op jit(solution)/shard_map/psum | solution.py:109
  184.5 2.9 copy-start.12
  187.4 1.7 copy-start.11
  189.1 1.8 copy-start.10
  333.1 2.5 copy-start.15
  333.1 3.0 copy-start.14
  335.2 1.6 copy-start.1
  336.0 1.8 copy-start.2
  336.8 1.8 copy-start.3
  337.9 1.8 copy-start.4
  338.6 1.7 copy-start.16
  338.6 1.7 copy-start.17
  338.6 1.7 copy-start.9
  340.2 1.0 copy-start.13
  340.3 1.2 copy-start.8
  341.5 1.0 copy-start.7
  342.2 1.1 copy-start.6
  346.0 61.8 %copy-start.18 = (f32[2048]{0:T(1024)S(1)}, f32[2048]{0:T(1024)}, u32[]{:S(2)}) copy-start(f32[2048]{0:T(1024)} %param.25) | copy-start | bytes 24580
  346.0 61.9 %copy-start.19 = (f32[2048]{0:T(1024)S(1)}, f32[2048]{0:T(1024)}, u32[]{:S(2)}) copy-start(f32[2048]{0:T(1024)} %param.24) | copy-start | bytes 24580
  346.0 61.9 %copy-start.20 = (f32[1024]{0:T(1024)S(1)}, f32[1024]{0:T(1024)}, u32[]{:S(2)}) copy-start(f32[1024]{0:T(1024)} %param.27) | copy-start | bytes 12292
  346.1 98.4 %reduce-scatter.2.cloned.1.call-start = ((), (), s32[]{:S(2)}) async-start(), calls=%async_computation.3 | async-start | bytes 1310720 | tf_op jit(solution)/shard_map/reduce_scatter | solution.py:122
Sparse Core Ops, SparseCore 0:
  10.1 79.3 all-gather.13
  92.2 74.9 all-gather.11
  170.0 76.2 all-gather.17
  248.9 76.1 all-gather.15
  326.8 25.1 all-gather.9
  354.2 51.5 all-reduce.1
  417.1 27.2 reduce-scatter.1
where the time goes:
time: 454 us; the launch traced here: 453 us
  waiting for transfers between devices  359 us (79%)
  local copies, waits for them, and re-layouts  41.5 us (9%)
  matrix products  28.4 us (6%)
  between operations  15.7 us (3%)
  other arithmetic  8.22 us (2%)
    all_gather x1, waiting for transfers between devices, per_device(): key_rows = lax.all_gather(branch_kv[0], 'seq', axis=0, tiled=True)  78.8 us
    all_gather x1, waiting for transfers between devices, per_device(): lax.all_gather(root_kv[0], 'seq', axis=0, tiled=True)  72.8 us
    all_gather x1, waiting for transfers between devices, per_device(): lax.all_gather(root_kv[1], 'seq', axis=0, tiled=True)  66.1 us
    psum x1, waiting for transfers between devices, per_device(): lax.psum(projected.astype(jnp.bfloat16), 'tensor').astype(jnp.float32)  53.8 us
    all_gather x1, waiting for transfers between devices, per_device(): value_rows = lax.all_gather(branch_kv[1], 'seq', axis=0, tiled=True)  53.1 us
    reduce_scatter x1, waiting for transfers between devices, per_device(): lax.psum_scatter(partial_value.astype(jnp.bfloat16), 'tensor', scatter_di...  26.7 us
    dot_general x7, matrix products, attend(): jnp.einsum('qhd,khd->hqk', query_heads, key_heads, preferred_element_type...  13.9 us
    unnamed x47, local copies, waits for them, and re-layouts  12.4 us
  transfers between devices with their start and end apart: 7, of which 7 were waited for; matrix products, arithmetic and copies ran while one was open for 14% of the time, Pallas kernels for 0%

commit v1 on v0

--- a/solution.py
+++ b/solution.py
@@ -68,35 +68,34 @@
     head_count = query.shape[1] // HD
     query_heads = query.reshape(row_count, head_count, HD)
     device = lax.axis_index("seq")
-    my_segment = segment[device]
-    branch_count = lax.axis_size("seq") // 4
+    seq_size = lax.axis_size("seq")
+    branch_count = seq_size // 4
+    feature_width = branch_kv.shape[2]
+
+    root_full = lax.all_gather(root_kv, "seq", axis=1, tiled=True)
+
+    local_rows = branch_kv.shape[1] // branch_count
+    branch_local = branch_kv.reshape(2, local_rows, branch_count, feature_width)
+    picked = jnp.take(branch_local, segment, axis=2)
+    picked = jnp.transpose(picked, (2, 0, 1, 3))
+    arrived = lax.all_to_all(picked, "seq", 0, 0, tiled=True)
+    branch_mine = jnp.transpose(arrived, (1, 0, 2, 3)).reshape(
+        2, seq_size * local_rows, feature_width
+    )
+
     running = (
         jnp.full((head_count, row_count), NEGATIVE_FILL, jnp.float32),
         jnp.zeros((head_count, row_count), jnp.float32),
         jnp.zeros((head_count, row_count, HD), jnp.float32),
     )
-    running = attend_blocks(
-        running,
-        query_heads,
-        lax.all_gather(root_kv[0], "seq", axis=0, tiled=True),
-        lax.all_gather(root_kv[1], "seq", axis=0, tiled=True),
-    )
-    key_rows = lax.all_gather(branch_kv[0], "seq", axis=0, tiled=True)
-    value_rows = lax.all_gather(branch_kv[1], "seq", axis=0, tiled=True)
-    feature_width = key_rows.shape[1]
-    keys_mine = lax.dynamic_index_in_dim(
-        key_rows.reshape(-1, branch_count, feature_width), my_segment, 1, keepdims=False
-    )
-    values_mine = lax.dynamic_index_in_dim(
-        value_rows.reshape(-1, branch_count, feature_width), my_segment, 1, keepdims=False
-    )
-    running = attend_blocks(running, query_heads, keys_mine, values_mine)
-    running = attend(running, query_heads, leaf_kv[0], leaf_kv[1], True)
     query_pos = jnp.arange(row_count, dtype=jnp.int32)
     allowed_new = (query_pos[None, :] <= query_pos[:, None]) & (
         query_pos[None, :] < new_len[device]
     )
     running = attend(running, query_heads, new_keys, new_values, allowed_new[None])
+    running = attend(running, query_heads, leaf_kv[0], leaf_kv[1], True)
+    running = attend_blocks(running, query_heads, branch_mine[0], branch_mine[1])
+    running = attend_blocks(running, query_heads, root_full[0], root_full[1])
     largest, totals, accumulated = running
     attention = (
         jnp.transpose(accumulated / totals[:, :, None], (1, 0, 2))
@@ -106,9 +105,10 @@
     projected = jnp.dot(attention, out_weight, preferred_element_type=jnp.float32)
     share_width = residual.shape[1]
     column = lax.axis_index("tensor") * share_width
-    projected = lax.psum(projected.astype(jnp.bfloat16), "tensor").astype(jnp.float32)
-    full_residual = lax.all_gather(residual, "tensor", axis=1, tiled=True)
-    mid_full = (full_residual.astype(jnp.float32) + projected).astype(jnp.bfloat16)
+    own_residual = lax.dynamic_update_slice_in_dim(
+        jnp.zeros(projected.shape, jnp.float32), residual.astype(jnp.float32), column, 1
+    )
+    mid_full = lax.psum((projected + own_residual).astype(jnp.bfloat16), "tensor")
     wide_mid = mid_full.astype(jnp.float32)
     row_mean = jnp.mean(wide_mid, axis=1, keepdims=True)
     row_var = jnp.mean(wide_mid * wide_mid, axis=1, keepdims=True) - row_mean * row_mean

time: 454 us -> 244 us (0.54)
  waiting for transfers between devices: 359 us -> 134 us
  starting transfers between devices: 0.24 us -> 12.3 us
  local copies, waits for them, and re-layouts: 41.5 us -> 49.7 us
  matrix products: 28.4 us -> 21.5 us
    all_gather x5 -> x1, waiting for transfers between devices: 277 us -> 44.6 us  [per_device(): root_full = lax.all_gather(root_kv, 'seq', axis=1, tiled=True)]
    slice x5, local copies, waits for them, and re-layouts: 11.1 us -> 26 us  [attend_blocks(): value_rows[block_start:block_start + BLOCK_KEYS]]
    all_to_all x0 -> x1, waiting for transfers between devices: none -> 13.4 us  [per_device(): arrived = lax.all_to_all(picked, 'seq', 0, 0, tiled=True)]
    all_to_all x0 -> x1, starting transfers between devices: none -> 12 us  [per_device(): arrived = lax.all_to_all(picked, 'seq', 0, 0, tiled=True)]
    dynamic_slice x3 -> x0, local copies, waits for them, and re-layouts: 7.37 us -> none  [the longest x1 4.25 us: per_device(): lax.dynamic_index_in_dim(value_rows.reshape(-1, branch_count, feature_wid...]
    dot_general x7, matrix products: 13.9 us -> 7.61 us  [attend(): jnp.einsum('qhd,khd->hqk', query_heads, key_heads, preferred_element_type...]
    slice x3 -> x1, local copies, waits for them, and re-layouts: 5.95 us -> 0.18 us  [per_device(): branch_mine[1]]
    unnamed x47 -> x45, local copies, waits for them, and re-layouts: 12.4 us -> 17.6 us
  transfers between devices with their start and end apart: 7 -> 4, of which waited for: 7 -> 4; matrix products, arithmetic and copies ran while one was open for 14% -> 6% of each run, Pallas kernels for 0% -> 0%
where the time goes in v1:
time: 244 us; the launch traced here: 242 us
  waiting for transfers between devices  134 us (55%)
  local copies, waits for them, and re-layouts  49.7 us (20%)
  matrix products  21.5 us (9%)
  between operations  13.4 us (5%)
  starting transfers between devices  12.3 us (5%)
  other arithmetic  11.3 us (5%)
    psum x1, waiting for transfers between devices, per_device(): lax.psum((projected + own_residual).astype(jnp.bfloat16), 'tensor')  49.5 us
    all_gather x1, waiting for transfers between devices, per_device(): root_full = lax.all_gather(root_kv, 'seq', axis=1, tiled=True)  44.6 us
    reduce_scatter x1, waiting for transfers between devices, per_device(): lax.psum_scatter(partial_value.astype(jnp.bfloat16), 'tensor', scatter_di...  26.6 us
    slice x5, local copies, waits for them, and re-layouts, attend_blocks(): value_rows[block_start:block_start + BLOCK_KEYS]  26 us
    unnamed x45, local copies, waits for them, and re-layouts  17.6 us
    all_to_all x1, waiting for transfers between devices, per_device(): arrived = lax.all_to_all(picked, 'seq', 0, 0, tiled=True)  13.4 us
    all_to_all x1, starting transfers between devices, per_device(): arrived = lax.all_to_all(picked, 'seq', 0, 0, tiled=True)  12 us
    dot_general x1, matrix products, per_device(): jnp.dot(hidden, down_weight, preferred_element_type=jnp.float32)  9.47 us
  transfers between devices with their start and end apart: 4, of which 4 were waited for; matrix products, arithmetic and copies ran while one was open for 6% of the time, Pallas kernels for 0%

profile of v1, /device:TPU:2, one launch (start us, length us, event | category | flops | bytes accessed | tf_op | source)
XLA Modules:
  0.0 242.5 jit_solution(9575016087254586354)
XLA Ops:
  6.5 1.7 copy.85
  8.2 1.0 copy.80
  9.3 0.7 compare_select_fusion
  9.9 1.0 gather_fusion
  11.0 0.7 compare_and_fusion
  11.6 1.1 broadcast_select_fusion
  12.8 12.0 %all-to-all-start = ((bf16[64,2,4,512]{3,2,1,0:T(4,128)(2,1)}), bf16[64,2,4,512]{3,2,1,0:T(4,128)(2,1)S(1)}, u32[]{:S(2)}, u32[]{:S(2)}) async-start(bf16[64,2,4,512]{3,2,1,0:T(4,128)(2,1)} %broadcast_select_fusion), calls=%async_computation | async-start | bytes 1048576 | tf_op jit(solution)/shard_map/all_to_all | solution.py:81
  24.9 0.8 copy.108
  25.8 0.6 dynamic_slice.9
  26.4 0.6 iota_compare_fusion.1
  27.1 0.9 fusion.184
  28.0 2.2 fusion.185
  30.3 13.4 %all-to-all-done = bf16[64,2,4,512]{3,2,1,0:T(4,128)(2,1)S(1)} async-done(((bf16[64,2,4,512]{3,2,1,0:T(4,128)(2,1)}), bf16[64,2,4,512]{3,2,1,0:T(4,128)(2,1)S(1)}, u32[]{:S(2)}, u32[]{:S(2)}) %all-to-all-start) | async-done | bytes 524320 | tf_op jit(solution)/shard_map/all_to_all | solution.py:81
  43.8 0.8 reshape_squeeze.15
  44.6 0.8 reshape_squeeze.14
  45.4 1.4 fusion.183
  46.8 44.6 %all-gather.2.cloned.1.call-done = bf16[2,2048,512]{2,0,1:T(2,128)(2,1)} async-done(((bf16[2,32,512]{2,0,1:T(2,128)(2,1)}), bf16[2,2048,512]{2,0,1:T(2,128)(2,1)}) %all-gather.2.cloned.1.call-update) | async-done | bytes 4194320 | tf_op jit(solution)/shard_map/all_gather | solution.py:75
  91.4 12.1 %fusion.180 = (bf16[1,512,512]{2,0,1:T(2,128)(2,1)}, bf16[1,512,512]{2,0,1:T(2,128)(2,1)}, bf16[1,512,512]{2,0,1:T(2,128)(2,1)}, bf16[1,512,512]{2,0,1:T(2,128)(...) fusion(bf16[2,2048,512]{2,0,1:T(2,128)(2,1)} %all-gather.2.clon, ...), kind=kLoop, calls=%fused_computation.232 | loop fusion | bytes 8388608 | tf_op jit(solution)/shard_map/slice | solution.py:43
  103.5 3.5 %copy.101 = bf16[1,512,512]{1,2,0:T(8,128)(2,1)} copy(bf16[1,512,512]{2,0,1:T(2,128)(2,1)} %get-tuple-element.19) | data formatting | bytes 1048576 | tf_op jit(solution)/shard_map/slice | solution.py:43
  107.0 3.5 %copy.111 = bf16[1,512,512]{1,2,0:T(8,128)(2,1)} copy(bf16[1,512,512]{2,0,1:T(2,128)(2,1)} %get-tuple-element.20) | data formatting | bytes 1048576
  110.5 3.5 %copy.110 = bf16[1,512,512]{1,2,0:T(8,128)(2,1)} copy(bf16[1,512,512]{2,0,1:T(2,128)(2,1)} %get-tuple-element.21) | data formatting | bytes 1048576
  113.9 3.5 %copy.109 = bf16[1,512,512]{1,2,0:T(8,128)(2,1)} copy(bf16[1,512,512]{2,0,1:T(2,128)(2,1)} %get-tuple-element.22) | data formatting | bytes 1048576
  117.4 3.5 %copy.97 = bf16[1,512,512]{1,2,0:T(8,128)(2,1)} copy(bf16[1,512,512]{2,0,1:T(2,128)(2,1)} %get-tuple-element.23) | data formatting | bytes 1048576 | tf_op jit(solution)/shard_map/slice | solution.py:43
  120.9 3.5 %copy.93 = bf16[1,512,512]{1,2,0:T(8,128)(2,1)} copy(bf16[1,512,512]{2,0,1:T(2,128)(2,1)} %get-tuple-element.24) | data formatting | bytes 1048576 | tf_op jit(solution)/shard_map/slice | solution.py:43
  124.4 3.5 %copy.89 = bf16[1,512,512]{1,2,0:T(8,128)(2,1)} copy(bf16[1,512,512]{2,0,1:T(2,128)(2,1)} %get-tuple-element.25) | data formatting | bytes 1048576 | tf_op jit(solution)/shard_map/slice | solution.py:43
  127.9 3.5 %copy.112 = bf16[1,512,512]{1,2,0:T(8,128)(2,1)} copy(bf16[1,512,512]{2,0,1:T(2,128)(2,1)} %get-tuple-element.26) | data formatting | bytes 1048576
  131.3 1.6 multiply_reduce_fusion
  132.9 0.5 multiply_reduce_fusion.3
  133.5 0.5 copy-done.8
  134.0 0.5 multiply_reduce_fusion.2
  134.5 0.5 multiply_reduce_fusion.1
  135.1 0.4 fusion.61
  135.5 0.4 convolution_bitcast_fusion.5
  136.6 1.3 fusion.9
  137.9 1.3 fusion.5
  139.9 0.3 copy-done.6
  140.2 0.7 fusion.22
  141.0 0.7 fusion.20
  142.0 0.7 fusion.18
  142.7 0.7 fusion.29
  143.4 0.7 fusion.186
  144.5 1.2 convert_element_type.64
  146.0 49.5 %all-reduce.2.cloned.1.call-done = bf16[256,2048]{1,0:T(8,128)(2,1)} async-done(((bf16[256,2048]{1,0:T(8,128)(2,1)}), bf16[256,2048]{1,0:T(8,128)(2,1)}) %all-reduce.2.cloned.1.call-update) | async-done | bytes 1048592 | tf_op jit(solution)/shard_map/psum | solution.py:111
  195.5 1.7 convert_reduce_fusion
  197.3 9.5 %convolution_convert_fusion = bf16[256,2048]{1,0:T(8,128)(2,1)} fusion(bf16[1024,2048]{1,0:T(8,128)(2,1)} %param.28, bf16[2048,1024]{1,0:T(8,128)(2,1)} %param.26, bf16[256,2048]{1,0:T(8,128)(2,1)} %all-reduce.2.cloned.1.call-done, f32[2048]{0:T(1024)S(1)} %copy-done.16, f32[2048]{0:T(1024)S(1)} %copy-done.17, f32[256]{0:T(256)S(1)} %get-tuple-element.35, ...), kind=kOutput, calls=%fused_computation.4 | convolution fusion | flops 2168455168 | bytes 10508288 | tf_op jit(solution)/shard_map/dot_general | solution.py:121
  206.8 0.8 dynamic_slice.10
  207.5 26.6 %reduce-scatter.2.cloned.1.call-done = bf16[256,512]{1,0:T(8,128)(2,1)} async-done(((bf16[256,2048]{1,0:T(8,128)(2,1)}), bf16[256,512]{1,0:T(8,128)(2,1)}) %reduce-scatter.2.cloned.1.call-update) | async-done | bytes 262160 | tf_op jit(solution)/shard_map/reduce_scatter | solution.py:122
  234.1 1.8 add_convert_fusion
  (58 shorter events, 2.9 us)
Async XLA Ops:
  6.5 136.9 %copy-start = (bf16[512,2048]{1,0:T(8,128)(2,1)S(1)}, bf16[512,2048]{1,0:T(8,128)(2,1)}, u32[]{:S(2)}) copy-start(bf16[512,2048]{1,0:T(8,128)(2,1)} %param.23) | copy-start | bytes 6291460
  6.5 18.3 %copy-start.15 = (bf16[2,64,512]{2,1,0:T(8,128)(2,1)S(1)}, bf16[2,64,512]{2,1,0:T(8,128)(2,1)}, u32[]{:S(2)}) copy-start(bf16[2,64,512]{2,1,0:T(8,128)(2,1)} %param.20) | copy-start | bytes 393220
  6.5 18.4 %copy-start.14 = (bf16[256,512]{1,0:T(8,128)(2,1)S(1)}, bf16[256,512]{1,0:T(8,128)(2,1)}, u32[]{:S(2)}) copy-start(bf16[256,512]{1,0:T(8,128)(2,1)} %param.19) | copy-start | bytes 786436
  6.5 84.9 %all-gather.2.cloned.1.call-start = ((), (), s32[]{:S(2)}) async-start(), calls=%async_computation.2 | async-start | bytes 4259840 | tf_op jit(solution)/shard_map/all_gather | solution.py:75
  9.9 15.9 %copy-start.19 = (s32[64]{0:T(128)S(1)}, s32[64]{0:T(128)}, u32[]{:S(2)}) copy-start(s32[64]{0:T(128)} %param.31) | copy-start | bytes 772
  9.9 17.2 %copy-start.1 = (bf16[256,512]{1,0:T(8,128)(2,1)S(1)}, bf16[256,512]{1,0:T(8,128)(2,1)}, u32[]{:S(2)}) copy-start(bf16[256,512]{1,0:T(8,128)(2,1)} %param.17) | copy-start | bytes 786436
  12.8 30.9 %all-to-all-start = ((bf16[64,2,4,512]{3,2,1,0:T(4,128)(2,1)}), bf16[64,2,4,512]{3,2,1,0:T(4,128)(2,1)S(1)}, u32[]{:S(2)}, u32[]{:S(2)}) async-start(bf16[64,2,4,512]{3,2,1,0:T(4,128)(2,1)} %broadcast_select_fusion), calls=%async_computation | async-start | bytes 1048576 | tf_op jit(solution)/shard_map/all_to_all | solution.py:81
  24.8 170.7 %all-reduce.2.cloned.1.call-start = ((), (), s32[]{:S(2)}) async-start(), calls=%async_computation.3 | async-start | bytes 2097152 | tf_op jit(solution)/shard_map/psum | solution.py:111
  131.3 1.6 copy-start.9
  132.9 1.0 copy-start.8
  133.5 1.1 copy-start.7
  134.5 1.0 copy-start.10
  135.0 1.0 copy-start.3
  135.0 1.3 copy-start.2
  137.9 1.4 copy-start.11
  139.2 1.0 copy-start.6
  139.9 1.1 copy-start.5
  140.9 1.1 copy-start.4
  141.6 1.1 copy-start.12
  143.4 1.0 copy-start.13
  144.5 52.8 %copy-start.16 = (f32[2048]{0:T(1024)S(1)}, f32[2048]{0:T(1024)}, u32[]{:S(2)}) copy-start(f32[2048]{0:T(1024)} %param.25) | copy-start | bytes 24580
  144.5 52.8 %copy-start.17 = (f32[2048]{0:T(1024)S(1)}, f32[2048]{0:T(1024)}, u32[]{:S(2)}) copy-start(f32[2048]{0:T(1024)} %param.24) | copy-start | bytes 24580
  144.5 52.8 %copy-start.18 = (f32[1024]{0:T(1024)S(1)}, f32[1024]{0:T(1024)}, u32[]{:S(2)}) copy-start(f32[1024]{0:T(1024)} %param.27) | copy-start | bytes 12292
  145.7 88.4 %reduce-scatter.2.cloned.1.call-start = ((), (), s32[]{:S(2)}) async-start(), calls=%async_computation.4 | async-start | bytes 1310720 | tf_op jit(solution)/shard_map/reduce_scatter | solution.py:122
Sparse Core Ops, SparseCore 0:
  10.1 81.2 all-gather.1
  145.8 49.6 all-reduce.1
  206.9 27.1 reduce-scatter.1

commit v2 on v1

v2 whole, which is shorter than its diff:
```python
import jax
import jax.numpy as jnp
from jax import lax
from jax.sharding import PartitionSpec as P

HD = 128


NEGATIVE_FILL = -1e30
NORM_EPSILON = 1e-05
BLOCK_KEYS = 512


def attend(running, query_heads, key_heads, value_heads, allowed):
    largest, totals, accumulated = running
    head_width = query_heads.shape[2]
    scores = jnp.einsum(
        "hqd,hkd->hqk", query_heads, key_heads, preferred_element_type=jnp.float32
    ) * head_width ** (-0.5)
    scores = jnp.where(allowed, scores, NEGATIVE_FILL)
    new_largest = jnp.maximum(largest, jnp.max(scores, axis=2))
    weights = jnp.where(allowed, jnp.exp(scores - new_largest[:, :, None]), 0.0)
    factor = jnp.exp(largest - new_largest)
    accumulated = accumulated * factor[:, :, None] + jnp.einsum(
        "hqk,hkd->hqd",
        weights.astype(jnp.bfloat16),
        value_heads,
        preferred_element_type=jnp.float32,
    )
    totals = totals * factor + jnp.sum(weights, axis=2)
    return (new_largest, totals, accumulated)


def attend_blocks(running, query_heads, key_heads, value_heads):
    for block_start in range(0, key_heads.shape[1], BLOCK_KEYS):
        running = attend(
            running,
            query_heads,
            key_heads[:, block_start : block_start + BLOCK_KEYS],
            value_heads[:, block_start : block_start + BLOCK_KEYS],
            True,
        )
    return running


def head_major(rows, head_count):
    lead = rows.shape[:-2]
    split = rows.reshape(lead + (rows.shape[-2], head_count, HD))
    order = tuple(range(len(lead))) + (len(lead) + 1, len(lead), len(lead) + 2)
    return jnp.transpose(split, order)


def tensor_sum_scatter(partial, parts):
    rows, width = partial.shape
    pieces = jnp.transpose(
        partial.astype(jnp.bfloat16).reshape(rows, parts, width // parts), (1, 0, 2)
    )
    arrived = lax.all_to_all(pieces, "tensor", 0, 0, tiled=True)
    return jnp.sum(arrived.astype(jnp.float32), axis=0)


def tensor_gather(share, parts):
    rows, width = share.shape
    copies = jnp.broadcast_to(share[None], (parts, rows, width))
    arrived = lax.all_to_all(copies, "tensor", 0, 0, tiled=True)
    return jnp.transpose(arrived, (1, 0, 2)).reshape(rows, parts * width)


def per_device(
    residual,
    query,
    new_keys,
    new_values,
    leaf_kv,
    branch_kv,
    root_kv,
    out_weight,
    norm_gain,
    norm_bias,
    up_weight,
    up_bias,
    down_weight,
    down_bias,
    segment,
    new_len,
):
    row_count = query.shape[0]
    head_count = query.shape[1] // HD
    query_heads = head_major(query, head_count)
    device = lax.axis_index("seq")
    seq_size = lax.axis_size("seq")
    parts = lax.axis_size("tensor")
    branch_count = seq_size // 4
    feature_width = branch_kv.shape[2]

    root_full = lax.all_gather(head_major(root_kv, head_count), "seq", axis=2, tiled=True)

    local_rows = branch_kv.shape[1] // branch_count
    branch_local = branch_kv.reshape(2, local_rows, branch_count, feature_width)
    picked = jnp.take(branch_local, segment, axis=2)
    picked = head_major(jnp.transpose(picked, (2, 0, 1, 3)), head_count)
    arrived = lax.all_to_all(picked, "seq", 0, 0, tiled=True)
    branch_mine = jnp.transpose(arrived, (1, 2, 0, 3, 4)).reshape(
        2, head_count, seq_size * local_rows, HD
    )

    running = (
        jnp.full((head_count, row_count), NEGATIVE_FILL, jnp.float32),
        jnp.zeros((head_count, row_count), jnp.float32),
        jnp.zeros((head_count, row_count, HD), jnp.float32),
    )
    query_pos = jnp.arange(row_count, dtype=jnp.int32)
    allowed_new = (query_pos[None, :] <= query_pos[:, None]) & (
        query_pos[None, :] < new_len[device]
    )
    running = attend(
        running,
        query_heads,
        head_major(new_keys, head_count),
        head_major(new_values, head_count),
        allowed_new[None],
    )
    leaf_heads = head_major(leaf_kv, head_count)
    running = attend(running, query_heads, leaf_heads[0], leaf_heads[1], True)
    running = attend_blocks(running, query_heads, branch_mine[0], branch_mine[1])
    running = attend_blocks(running, query_heads, root_full[0], root_full[1])
    largest, totals, accumulated = running
    attention = (
        jnp.transpose(accumulated / totals[:, :, None], (1, 0, 2))
        .reshape(row_count, head_count * HD)
        .astype(jnp.bfloat16)
    )
    projected = jnp.dot(attention, out_weight, preferred_element_type=jnp.float32)
    share_width = residual.shape[1]
    column = lax.axis_index("tensor") * share_width
    mid_share = (
        tensor_sum_scatter(projected, parts) + residual.astype(jnp.float32)
    ).astype(jnp.bfloat16)
    mid_full = tensor_gather(mid_share, parts)
    wide_mid = mid_full.astype(jnp.float32)
    row_mean = jnp.mean(wide_mid, axis=1, keepdims=True)
    row_var = jnp.mean(wide_mid * wide_mid, axis=1, keepdims=True) - row_mean * row_mean
    normed = (
        (wide_mid - row_mean) * lax.rsqrt(row_var + NORM_EPSILON) * norm_gain + norm_bias
    ).astype(jnp.bfloat16)
    up_sum = jnp.dot(normed, up_weight, preferred_element_type=jnp.float32)
    hidden = jax.nn.gelu(up_sum + up_bias, approximate=False).astype(jnp.bfloat16)
    partial_value = jnp.dot(hidden, down_weight, preferred_element_type=jnp.float32)
    summed = tensor_sum_scatter(partial_value, parts)
    down_share = lax.dynamic_slice_in_dim(down_bias, column, share_width, 0)
    return (summed + down_share + mid_share.astype(jnp.float32)).astype(jnp.bfloat16)


def solution(mesh):
    return jax.shard_map(
        per_device,
        mesh=mesh,
        in_specs=(
            P("seq", "tensor"),
            P("seq", "tensor"),
            P("seq", "tensor"),
            P("seq", "tensor"),
            P(None, "seq", "tensor"),
            P(None, "seq", "tensor"),
            P(None, "seq", "tensor"),
            P("tensor", None),
            P(),
            P(),
            P(None, "tensor"),
            P("tensor"),
            P("tensor", None),
            P(),
            P(),
            P(),
        ),
        out_specs=P("seq", "tensor"),
        check_vma=False,
    )
```

time: 244 us -> 180 us (0.74)
  waiting for transfers between devices: 134 us -> 70.2 us
  blocking collectives: 0 us -> 36.8 us
  local copies, waits for them, and re-layouts: 49.7 us -> 15.3 us
  other arithmetic: 11.3 us -> 7.94 us
  starting transfers between devices: 12.3 us -> 15.5 us
    psum x1 -> x0, waiting for transfers between devices: 49.5 us -> none  [per_device(): lax.psum((projected + own_residual).astype(jnp.bfloat16), 'tensor')]
    all_to_all x0 -> x2, blocking collectives: none -> 36.8 us  [the longest x1 19.7 us: tensor_sum_scatter(): arrived = lax.all_to_all(pieces, 'tensor', 0, 0, tiled=True)]
    reduce_scatter x1 -> x0, waiting for transfers between devices: 26.6 us -> none  [per_device(): lax.psum_scatter(partial_value.astype(jnp.bfloat16), 'tensor', scatter_di...]
    slice x6 -> x1, local copies, waits for them, and re-layouts: 26 us -> 0.1 us  [per_device(): branch_mine[0]]
    unnamed x45 -> x26, local copies, waits for them, and re-layouts: 17.6 us -> 0.44 us
    all_to_all x0 -> x1, waiting for transfers between devices: none -> 12.7 us  [tensor_sum_scatter(): arrived = lax.all_to_all(pieces, 'tensor', 0, 0, tiled=True)]
    reshape x1 -> x4, local copies, waits for them, and re-layouts: 0.83 us -> 5.25 us  [the longest x2 2.81 us: head_major(): split = rows.reshape(lead + (rows.shape[-2], head_count, HD))]
    all_to_all x0 -> x1, starting transfers between devices: none -> 3.51 us  [tensor_sum_scatter(): arrived = lax.all_to_all(pieces, 'tensor', 0, 0, tiled=True)]
  transfers between devices with their start and end apart: 4 -> 3, of which waited for: 4 -> 3; matrix products, arithmetic and copies ran while one was open for 6% -> 8% of each run, Pallas kernels for 0% -> 0%
where the time goes in v2:
time: 180 us; the launch traced here: 179 us
  waiting for transfers between devices  70.2 us (39%)
  blocking collectives  36.8 us (20%)
  matrix products  19.6 us (11%)
  starting transfers between devices  15.5 us (9%)
  local copies, waits for them, and re-layouts  15.3 us (8%)
  between operations  13.7 us (8%)
  other arithmetic  7.94 us (4%)
    all_gather x1, waiting for transfers between devices, per_device(): lax.all_gather(head_major(root_kv, head_count), 'seq', axis=2, tiled=True)  45.8 us
    all_to_all x1, blocking collectives, tensor_sum_scatter(): arrived = lax.all_to_all(pieces, 'tensor', 0, 0, tiled=True)  19.7 us
    all_to_all x1, blocking collectives, tensor_gather(): arrived = lax.all_to_all(copies, 'tensor', 0, 0, tiled=True)  17.1 us
    all_to_all x1, waiting for transfers between devices, tensor_sum_scatter(): arrived = lax.all_to_all(pieces, 'tensor', 0, 0, tiled=True)  12.7 us
    all_to_all x1, starting transfers between devices, per_device(): arrived = lax.all_to_all(picked, 'seq', 0, 0, tiled=True)  12 us
    all_to_all x1, waiting for transfers between devices, per_device(): arrived = lax.all_to_all(picked, 'seq', 0, 0, tiled=True)  11.6 us
    dot_general x1, matrix products, per_device(): jnp.dot(hidden, down_weight, preferred_element_type=jnp.float32)  9.08 us
    dot_general x7, matrix products, attend(): jnp.einsum('hqd,hkd->hqk', query_heads, key_heads, preferred_element_type...  5.67 us
  transfers between devices with their start and end apart: 3, of which 3 were waited for; matrix products, arithmetic and copies ran while one was open for 8% of the time, Pallas kernels for 0%

profile of v2, /device:TPU:2, one launch (start us, length us, event | category | flops | bytes accessed | tf_op | source)
XLA Modules:
  0.0 179.1 jit_solution(16332202082956338432)
XLA Ops:
  6.5 1.6 bitcast_bitcast_fusion.13
  8.2 1.0 copy.65
  9.2 0.7 compare_select_fusion
  9.9 1.0 gather_fusion
  10.9 0.7 compare_and_fusion
  11.6 0.3 broadcast_select_fusion
  12.0 1.0 reshape.291
  13.0 12.0 %all-to-all-start = ((bf16[64,2,4,4,128]{4,2,3,1,0:T(4,128)(2,1)}), bf16[64,2,4,4,128]{4,2,3,1,0:T(4,128)(2,1)S(1)}, u32[]{:S(2)}, u32[]{:S(2)}) async-start(bf16[64,2,4,4,128]{4,2,3,1,0:T(4,128)(2,1)} %bitcast.14), calls=%async_computation | async-start | bytes 1048576 | tf_op jit(solution)/shard_map/all_to_all | solution.py:102
  25.0 1.8 %copy.87 = bf16[256,512]{0,1:T(8,128)(2,1)} copy(bf16[256,512]{1,0:T(8,128)(2,1)} %param.19) | data formatting | bytes 524288 | tf_op jit(solution)/shard_map/reshape | solution.py:48
  26.8 0.6 dynamic_slice.6
  27.4 0.6 iota_compare_fusion.1
  28.1 0.9 bitcast_bitcast_fusion.12
  29.1 0.9 fusion.169
  30.0 2.2 %fusion.170 = (f32[4,256]{1,0:T(4,128)S(1)}, f32[4,256,256]{1,2,0:T(8,128)}) fusion(pred[256,256]{0,1:T(8,128)(4,1)S(1)} %fusion.106, bf16[256,512]{1,0:T(8,128)(2,1)} %param.18, bf16[256,512]{1,0:T(8,128)(2,1)S(1)} %copy-done.1), kind=kOutput, calls=%fused_computation.240 | convolution fusion | flops 67894272 | bytes 1642496 | tf_op jit(solution)/shard_map/hqd,hkd->hqk/dot_general | solution.py:17
  32.3 11.6 %all-to-all-done = bf16[64,2,4,4,128]{4,2,3,1,0:T(4,128)(2,1)S(1)} async-done(((bf16[64,2,4,4,128]{4,2,3,1,0:T(4,128)(2,1)}), bf16[64,2,4,4,128]{4,2,3,1,0:T(4,128)(2,1)S(1)}, u32[]{:S(2)}, u32[]{:S(2)}) %all-to-all-start) | async-done | bytes 524320 | tf_op jit(solution)/shard_map/all_to_all | solution.py:102
  43.9 0.9 fusion.167
  44.9 0.4 fusion.168
  45.3 45.8 %all-gather.2.cloned.1.call-done = bf16[2,4,2048,128]{3,2,1,0:T(8,128)(2,1)} async-done(((bf16[2,4,32,128]{3,2,1,0:T(8,128)(2,1)}), bf16[2,4,2048,128]{3,2,1,0:T(8,128)(2,1)}) %all-gather.2.cloned.1.call-update) | async-done | bytes 4194320 | tf_op jit(solution)/shard_map/all_gather | solution.py:96
  91.1 2.5 %slice_bitcast_fusion = (bf16[4,2048,128]{2,1,0:T(8,128)(2,1)S(1)}, bf16[4,2048,128]{2,1,0:T(8,128)(2,1)S(1)}) fusion(bf16[2,4,2048,128]{3,2,1,0:T(8,128)(2,1)} %all-gather.2.cloned.1.call-done), kind=kLoop, calls=%fused_computation.3 | loop fusion | bytes 8388608 | tf_op jit(solution)/shard_map/squeeze | solution.py:126
  93.7 0.5 multiply_reduce_fusion.1
  94.2 0.5 multiply_reduce_fusion.2
  94.7 0.5 multiply_reduce_fusion.3
  95.2 0.5 multiply_reduce_fusion.4
  95.8 0.4 fusion.51
  96.2 0.4 convolution_bitcast_fusion.5
  96.8 0.3 copy-done.2
  97.1 0.2 fusion.53
  97.3 1.3 fusion.8
  98.6 1.3 fusion.4
  100.0 0.3 fusion.27
  100.3 0.3 fusion.25
  100.6 0.8 fusion.21
  101.4 0.8 fusion.19
  102.2 0.8 fusion.17
  102.9 0.8 fusion.28
  103.7 0.7 convolution_convert_fusion
  104.6 19.7 %all_to_all.20 = bf16[4,256,512]{2,1,0:T(8,128)(2,1)S(1)} all-to-all(bf16[4,256,512]{2,1,0:T(8,128)(2,1)S(1)} %bitcast.312), channel_id=1, replica_groups=mesh['seq'=64,'tensor'=4] {'tensor'}, dimensions={0} | all-to-all | bytes 2097152 | tf_op jit(solution)/shard_map/all_to_all | solution.py:58
  124.3 0.1 convert_reduce_fusion.1
  124.8 17.1 %all_to_all.21 = bf16[4,256,512]{1,2,0:T(8,128)(2,1)S(1)} all-to-all(bf16[4,256,512]{1,2,0:T(8,128)(2,1)S(1)} %broadcast_in_dim.94), channel_id=1, replica_groups=mesh['seq'=64,'tensor'=4] {'tensor'}, dimensions={0} | all-to-all | bytes 2097152 | tf_op jit(solution)/shard_map/all_to_all | solution.py:65
  141.9 0.3 convert_reduce_fusion.2
  142.2 0.7 fusion.3
  142.9 9.1 %convolution_convert_fusion.1 = bf16[256,2048]{1,0:T(8,128)(2,1)} fusion(bf16[1024,2048]{1,0:T(8,128)(2,1)} %param.28, bf16[256,2048]{0,1:T(8,128)(2,1)S(1)} %fusion.3, bf16[2048,1024]{1,0:T(8,128)(2,1)} %param.26, f32[1024]{0:T(1024)S(1)} %copy-done.11), kind=kOutput, calls=%fused_computation.2 | convolution fusion | flops 2165309440 | bytes 10489856 | tf_op jit(solution)/shard_map/dot_general | solution.py:148
  152.0 2.4 %copy.153 = bf16[32,4,8,512]{3,2,0,1:T(8,128)(2,1)} copy(bf16[32,4,8,512]{3,2,1,0:T(8,128)(2,1)} %bitcast.314) | data formatting | bytes 2097152 | tf_op jit(solution)/shard_map/reshape | solution.py:56
  154.4 3.5 %all-to-all-start.3 = ((bf16[4,256,512]{2,1,0:T(8,128)(2,1)}), bf16[4,256,512]{2,1,0:T(8,128)(2,1)S(1)}, u32[]{:S(2)}, u32[]{:S(2)}) async-start(bf16[4,256,512]{2,1,0:T(8,128)(2,1)} %bitcast.310), calls=%async_computation.3 | async-start | bytes 2097152 | tf_op jit(solution)/shard_map/all_to_all | solution.py:58
  157.9 0.8 dynamic_slice.7
  158.7 12.7 %all-to-all-done.3 = bf16[4,256,512]{2,1,0:T(8,128)(2,1)S(1)} async-done(((bf16[4,256,512]{2,1,0:T(8,128)(2,1)}), bf16[4,256,512]{2,1,0:T(8,128)(2,1)S(1)}, u32[]{:S(2)}, u32[]{:S(2)}) %all-to-all-start.3) | async-done | bytes 1048608 | tf_op jit(solution)/shard_map/all_to_all | solution.py:58
  171.4 0.1 convert_reduce_fusion
  171.5 0.8 add_convert_fusion
  (38 shorter events, 0.9 us)
Async XLA Ops:
  6.5 97.2 %copy-start = (bf16[512,2048]{1,0:T(8,128)(2,1)S(1)}, bf16[512,2048]{1,0:T(8,128)(2,1)}, u32[]{:S(2)}) copy-start(bf16[512,2048]{1,0:T(8,128)(2,1)} %param.23) | copy-start | bytes 6291460
  6.5 84.6 %all-gather.2.cloned.1.call-start = ((), (), s32[]{:S(2)}) async-start(), calls=%async_computation.4 | async-start | bytes 4259840 | tf_op jit(solution)/shard_map/all_gather | solution.py:96
  10.9 15.9 %copy-start.12 = (s32[64]{0:T(128)S(1)}, s32[64]{0:T(128)}, u32[]{:S(2)}) copy-start(s32[64]{0:T(128)} %param.31) | copy-start | bytes 772
  10.9 18.2 %copy-start.1 = (bf16[256,512]{1,0:T(8,128)(2,1)S(1)}, bf16[256,512]{1,0:T(8,128)(2,1)}, u32[]{:S(2)}) copy-start(bf16[256,512]{1,0:T(8,128)(2,1)} %param.17) | copy-start | bytes 786436
  13.0 30.9 %all-to-all-start = ((bf16[64,2,4,4,128]{4,2,3,1,0:T(4,128)(2,1)}), bf16[64,2,4,4,128]{4,2,3,1,0:T(4,128)(2,1)S(1)}, u32[]{:S(2)}, u32[]{:S(2)}) async-start(bf16[64,2,4,4,128]{4,2,3,1,0:T(4,128)(2,1)} %bitcast.14), calls=%async_computation | async-start | bytes 1048576 | tf_op jit(solution)/shard_map/all_to_all | solution.py:102
  29.1 15.8 %copy-start.6 = (bf16[2,4,64,128]{3,2,1,0:T(8,128)(2,1)}, bf16[2,4,64,128]{3,2,1,0:T(8,128)(2,1)S(1)}, u32[]{:S(2)}) copy-start(bf16[2,4,64,128]{3,2,1,0:T(8,128)(2,1)S(1)} %bitcast_bitcast_fusion.12) | copy-start | bytes 393220
  95.2 1.0 copy-start.4
  95.8 1.0 copy-start.3
  95.8 1.3 copy-start.2
  98.6 1.4 copy-start.5
  98.6 1.7 copy-start.7
  104.6 19.9 %copy-start.8 = (bf16[256,512]{1,0:T(8,128)(2,1)S(1)}, bf16[256,512]{1,0:T(8,128)(2,1)}, u32[]{:S(2)}) copy-start(bf16[256,512]{1,0:T(8,128)(2,1)} %param.16) | copy-start | bytes 786436
  124.7 17.5 %copy-start.9 = (f32[2048]{0:T(1024)S(1)}, f32[2048]{0:T(1024)}, u32[]{:S(2)}) copy-start(f32[2048]{0:T(1024)} %param.25) | copy-start | bytes 24580
  124.7 17.5 %copy-start.10 = (f32[2048]{0:T(1024)S(1)}, f32[2048]{0:T(1024)}, u32[]{:S(2)}) copy-start(f32[2048]{0:T(1024)} %param.24) | copy-start | bytes 24580
  141.9 1.1 copy-start.11
  154.4 17.0 %all-to-all-start.3 = ((bf16[4,256,512]{2,1,0:T(8,128)(2,1)}), bf16[4,256,512]{2,1,0:T(8,128)(2,1)S(1)}, u32[]{:S(2)}, u32[]{:S(2)}) async-start(bf16[4,256,512]{2,1,0:T(8,128)(2,1)} %bitcast.310), calls=%async_computation.3 | async-start | bytes 2097152 | tf_op jit(solution)/shard_map/all_to_all | solution.py:58
Sparse Core Ops, SparseCore 0:
  10.0 81.1 all-gather.1

commit v3 on v2

--- a/solution.py
+++ b/solution.py
@@ -64,6 +64,44 @@
     copies = jnp.broadcast_to(share[None], (parts, rows, width))
     arrived = lax.all_to_all(copies, "tensor", 0, 0, tiled=True)
     return jnp.transpose(arrived, (1, 0, 2)).reshape(rows, parts * width)
+
+
+def shift_pairs(shape, axis, step):
+    pairs = []
+    for index in range(shape[0] * shape[1] * shape[2]):
+        place = [index // (shape[1] * shape[2]), (index // shape[2]) % shape[1], index % shape[2]]
+        place[axis] = (place[axis] + step) % shape[axis]
+        pairs.append((index, (place[0] * shape[1] + place[1]) * shape[2] + place[2]))
+    return pairs
+
+
+def ring_along(block, shape, axis):
+    size = shape[axis]
+    up = shift_pairs(shape, axis, 1)
+    down = shift_pairs(shape, axis, -1)
+    pieces = [block]
+    from_below = block
+    from_above = block
+    for _ in range((size - 1) // 2):
+        from_below = lax.ppermute(from_below, "seq", up)
+        from_above = lax.ppermute(from_above, "seq", down)
+        pieces += [from_below, from_above]
+    if size % 2 == 0:
+        half = block.shape[2] // 2
+        first = lax.ppermute(from_below[:, :, :half], "seq", up)
+        second = lax.ppermute(from_above[:, :, half:], "seq", down)
+        pieces += [first, second]
+    return jnp.concatenate(pieces, axis=2)
+
+
+def ring_gather_seq(block, seq_size):
+    cores = 2
+    lanes = 4
+    shape = (seq_size // (lanes * cores), lanes, cores)
+    gathered = ring_along(block, shape, 0)
+    gathered = ring_along(gathered, shape, 1)
+    partner = lax.ppermute(gathered, "seq", shift_pairs(shape, 2, 1))
+    return jnp.concatenate([gathered, partner], axis=2)
 
 
 def per_device(
@@ -93,7 +131,7 @@
     branch_count = seq_size // 4
     feature_width = branch_kv.shape[2]
 
-    root_full = lax.all_gather(head_major(root_kv, head_count), "seq", axis=2, tiled=True)
+    root_full = ring_gather_seq(head_major(root_kv, head_count), seq_size)
 
     local_rows = branch_kv.shape[1] // branch_count
     branch_local = branch_kv.reshape(2, local_rows, branch_count, feature_width)
@@ -144,7 +182,9 @@
         (wide_mid - row_mean) * lax.rsqrt(row_var + NORM_EPSILON) * norm_gain + norm_bias
     ).astype(jnp.bfloat16)
     up_sum = jnp.dot(normed, up_weight, preferred_element_type=jnp.float32)
-    hidden = jax.nn.gelu(up_sum + up_bias, approximate=False).astype(jnp.bfloat16)
+    hidden = lax.optimization_barrier(
+        jax.nn.gelu(up_sum + up_bias, approximate=False).astype(jnp.bfloat16)
+    )
     partial_value = jnp.dot(hidden, down_weight, preferred_element_type=jnp.float32)
     summed = tensor_sum_scatter(partial_value, parts)
     down_share = lax.dynamic_slice_in_dim(down_bias, column, share_width, 0)

time: 180 us -> 157 us (0.87)
  waiting for transfers between devices: 70.2 us -> 37.9 us
  starting transfers between devices: 15.5 us -> 34.2 us
  between operations: 13.7 us -> 0.47 us
  local copies, waits for them, and re-layouts: 15.3 us -> 28 us
  matrix products: 19.6 us -> 13.5 us
  other arithmetic: 7.94 us -> 5.4 us
    all_gather x1 -> x0, waiting for transfers between devices: 45.8 us -> none  [per_device(): lax.all_gather(head_major(root_kv, head_count), 'seq', axis=2, tiled=True)]
    ppermute x0 -> x13, starting transfers between devices: none -> 20.2 us  [the longest x4 11.2 us: ring_along(): from_above = lax.ppermute(from_above, 'seq', down)]
    ppermute x0 -> x13, waiting for transfers between devices: none -> 15 us  [the longest x4 12.1 us: ring_along(): from_below = lax.ppermute(from_below, 'seq', up)]
    unnamed x26 -> x42, local copies, waits for them, and re-layouts: 0.44 us -> 11.3 us
    dot_general x1, matrix products: 9.08 us -> 1.28 us  [per_device(): jnp.dot(hidden, down_weight, preferred_element_type=jnp.float32)]
    concatenate x0 -> x2, local copies, waits for them, and re-layouts: none -> 4.22 us  [the longest x1 3.29 us: ring_gather_seq(): return jnp.concatenate([gathered, partner], axis=2)]
    dot_general x0 -> x1, matrix products: none -> 3.7 us  [per_device(): up_sum = jnp.dot(normed, up_weight, preferred_element_type=jnp.float32)]
  transfers between devices with their start and end apart: 3 -> 15, of which waited for: 3 -> 9; matrix products, arithmetic and copies ran while one was open for 8% -> 13% of each run, Pallas kernels for 0% -> 0%
where the time goes in v3:
time: 157 us; the launch traced here: 156 us
  waiting for transfers between devices  37.9 us (24%)
  blocking collectives  36.5 us (23%)
  starting transfers between devices  34.2 us (22%)
  local copies, waits for them, and re-layouts  28 us (18%)
  matrix products  13.5 us (9%)
  other arithmetic  5.4 us (3%)
    all_to_all x1, blocking collectives, tensor_sum_scatter(): arrived = lax.all_to_all(pieces, 'tensor', 0, 0, tiled=True)  19.7 us
    all_to_all x1, blocking collectives, tensor_gather(): arrived = lax.all_to_all(copies, 'tensor', 0, 0, tiled=True)  16.8 us
    all_to_all x1, waiting for transfers between devices, tensor_sum_scatter(): arrived = lax.all_to_all(pieces, 'tensor', 0, 0, tiled=True)  12.5 us
    ppermute x4, waiting for transfers between devices, ring_along(): from_below = lax.ppermute(from_below, 'seq', up)  12.1 us
    unnamed x42, local copies, waits for them, and re-layouts  11.3 us
    ppermute x4, starting transfers between devices, ring_along(): from_above = lax.ppermute(from_above, 'seq', down)  11.2 us
    all_to_all x1, starting transfers between devices, per_device(): arrived = lax.all_to_all(picked, 'seq', 0, 0, tiled=True)  10.5 us
    all_to_all x1, waiting for transfers between devices, per_device(): arrived = lax.all_to_all(picked, 'seq', 0, 0, tiled=True)  10.5 us
  transfers between devices with their start and end apart: 15, of which 9 were waited for; matrix products, arithmetic and copies ran while one was open for 13% of the time, Pallas kernels for 0%

profile of v3, /device:TPU:2, one launch (start us, length us, event | category | flops | bytes accessed | tf_op | source)
XLA Modules:
  0.0 155.9 jit_solution(8929697936028554225)
XLA Ops:
  0.0 1.0 bitcast_bitcast_fusion.13
  1.0 2.0 %collective-permute-start = (bf16[2,4,32,128]{3,2,1,0:T(8,128)(2,1)S(1)}, bf16[2,4,32,128]{3,2,1,0:T(8,128)(2,1)S(1)}, u32[]{:S(2)}, u32[]{:S(2)}) collective-permute-start(bf16[2,4,32,128]{3,2,1,0:T(8,128)(2,1)S(1)} %bitcast_bitcast_fusion.13), channel_id=1, source_target_pairs={{0,32},{4,36},{8,40},{12,44},{16,48},{20,52},{24,56},{28,60},{32,6... | collective-permute-start | bytes 196616 | tf_op jit(solution)/shard_map/ppermute | solution.py:86
  3.0 4.0 %collective-permute-start.1 = (bf16[2,4,32,128]{3,2,1,0:T(8,128)(2,1)S(1)}, bf16[2,4,32,128]{3,2,1,0:T(8,128)(2,1)S(1)}, u32[]{:S(2)}, u32[]{:S(2)}) collective-permute-start(bf16[2,4,32,128]{3,2,1,0:T(8,128)(2,1)S(1)} %bitcast_bitcast_fusion.13), channel_id=1, source_target_pairs={{0,224},{4,228},{8,232},{12,236},{16,240},{20,244},{24,248},{28,25... | collective-permute-start | bytes 196616 | tf_op jit(solution)/shard_map/ppermute | solution.py:87
  7.0 1.5 constant_dynamic-update-slice_fusion.21
  9.2 3.3 %collective-permute-start.3 = (bf16[2,4,32,128]{3,2,1,0:T(8,128)(2,1)S(1)}, bf16[2,4,32,128]{3,2,1,0:T(8,128)(2,1)S(1)}, u32[]{:S(2)}, u32[]{:S(2)}) collective-permute-start(bf16[2,4,32,128]{3,2,1,0:T(8,128)(2,1)S(1)} %collective-permute-done.1), channel_id=1, source_target_pairs={{0,224},{4,228},{8,232},{12,236},{16,240},{20,244},{24,248},{28,25... | collective-permute-start | bytes 196616 | tf_op jit(solution)/shard_map/ppermute | solution.py:87
  12.5 0.7 constant_dynamic-update-slice_fusion.20
  13.2 0.7 constant_dynamic-update-slice_fusion.19
  13.9 0.8 collective-permute-done.2
  14.7 3.3 %collective-permute-start.5 = (bf16[2,4,32,128]{3,2,1,0:T(8,128)(2,1)S(1)}, bf16[2,4,32,128]{3,2,1,0:T(8,128)(2,1)S(1)}, u32[]{:S(2)}, u32[]{:S(2)}) collective-permute-start(bf16[2,4,32,128]{3,2,1,0:T(8,128)(2,1)S(1)} %collective-permute-done.3), channel_id=1, source_target_pairs={{0,224},{4,228},{8,232},{12,236},{16,240},{20,244},{24,248},{28,25... | collective-permute-start | bytes 196616 | tf_op jit(solution)/shard_map/ppermute | solution.py:87
  18.0 0.7 constant_dynamic-update-slice_fusion.18
  18.7 0.7 constant_dynamic-update-slice_fusion.17
  19.4 0.7 collective-permute-done.4
  20.2 3.3 %collective-permute-start.7 = (bf16[2,4,16,128]{3,2,1,0:T(8,128)(2,1)S(1)}, bf16[2,4,16,128]{3,2,1,0:T(8,128)(2,1)S(1)}, u32[]{:S(2)}, u32[]{:S(2)}) collective-permute-start(bf16[2,4,16,128]{3,2,1,0:T(8,128)(2,1)S(1)} %slice.81), channel_id=1, source_target_pairs={{0,224},{4,228},{8,232},{12,236},{16,240},{20,244},{24,248},{28,25... | collective-permute-start | bytes 98312 | tf_op jit(solution)/shard_map/ppermute | solution.py:92
  23.5 0.7 constant_dynamic-update-slice_fusion.16
  24.2 0.7 constant_dynamic-update-slice_fusion.15
  25.9 0.7 constant_dynamic-update-slice_fusion.13
  26.6 1.5 collective-permute-start.8
  28.6 10.0 %collective-permute-done.8 = bf16[2,4,256,128]{3,2,1,0:T(8,128)(2,1)S(1)} collective-permute-done((bf16[2,4,256,128]{3,2,1,0:T(8,128)(2,1)S(1)}, bf16[2,4,256,128]{3,2,1,0:T(8,128)(2,1)S(1)}, u32[]{:S(2)}, u32[]{:S(2)}) %collective-permute-start.8) | collective-permute-done | bytes 524320 | tf_op jit(solution)/shard_map/ppermute | solution.py:86
  38.6 1.6 %collective-permute-start.10 = (bf16[2,4,128,128]{3,2,1,0:T(8,128)(2,1)S(1)}, bf16[2,4,128,128]{3,2,1,0:T(8,128)(2,1)S(1)}, u32[]{:S(2)}, u32[]{:S(2)}) collective-permute-start(bf16[2,4,128,128]{3,2,1,0:T(8,128)(2,1)S(1)} %slice.82), channel_id=1, source_target_pairs={{0,8},{4,12},{8,16},{12,20},{16,24},{20,28},{24,0},{28,4},{32,40},... | collective-permute-start | bytes 786440 | tf_op jit(solution)/shard_map/ppermute | solution.py:91
  40.8 1.2 constant_dynamic-update-slice_fusion.12
  42.0 1.2 constant_dynamic-update-slice_fusion.11
  43.2 1.8 %collective-permute-done.10 = bf16[2,4,128,128]{3,2,1,0:T(8,128)(2,1)S(1)} collective-permute-done((bf16[2,4,128,128]{3,2,1,0:T(8,128)(2,1)S(1)}, bf16[2,4,128,128]{3,2,1,0:T(8,128)(2,1)S(1)}, u32[]{:S(2)}, u32[]{:S(2)}) %collective-permute-start.10) | collective-permute-done | bytes 262176 | tf_op jit(solution)/shard_map/ppermute | solution.py:91
  45.1 1.0 constant_dynamic-update-slice_fusion.10
  46.7 0.9 constant_dynamic-update-slice_fusion.9
  47.7 1.0 gather_fusion
  49.1 1.0 reshape.291
  50.2 10.5 %all-to-all-start = ((bf16[64,2,4,4,128]{4,2,3,1,0:T(4,128)(2,1)}), bf16[64,2,4,4,128]{4,2,3,1,0:T(4,128)(2,1)}, u32[]{:S(2)}, u32[]{:S(2)}) async-start(bf16[64,2,4,4,128]{4,2,3,1,0:T(4,128)(2,1)} %bitcast.14), calls=%async_computation | async-start | bytes 1048576 | tf_op jit(solution)/shard_map/all_to_all | solution.py:140
  60.7 1.8 %copy.107 = bf16[256,512]{0,1:T(8,128)(2,1)} copy(bf16[256,512]{1,0:T(8,128)(2,1)} %param.19) | data formatting | bytes 524288 | tf_op jit(solution)/shard_map/reshape | solution.py:48
  63.8 0.9 bitcast_bitcast_fusion.12
  65.4 0.9 fusion.112
  66.3 1.3 fusion.113
  67.6 10.5 %all-to-all-done = bf16[64,2,4,4,128]{4,2,3,1,0:T(4,128)(2,1)} async-done(((bf16[64,2,4,4,128]{4,2,3,1,0:T(4,128)(2,1)}), bf16[64,2,4,4,128]{4,2,3,1,0:T(4,128)(2,1)}, u32[]{:S(2)}, u32[]{:S(2)}) %all-to-all-start) | async-done | bytes 524320 | tf_op jit(solution)/shard_map/all_to_all | solution.py:140
  78.1 1.2 fusion.110
  79.9 3.3 %constant_dynamic-update-slice_fusion.22 = bf16[2,4,2048,128]{3,2,1,0:T(8,128)(2,1)} fusion(bf16[2,4,2048,128]{3,2,1,0:T(8,128)(2,1)} %get-tuple-element.28, bf16[2,4,1024,128]{3,2,1,0:T(8,128)(2,1)} %collective-permute-done.12), kind=kLoop, calls=%fused_computation.156 | loop fusion | bytes 4194304 | tf_op jit(solution)/shard_map/concatenate | solution.py:104
  83.2 2.5 %slice_bitcast_fusion = (bf16[4,2048,128]{2,1,0:T(8,128)(2,1)S(1)}, bf16[4,2048,128]{2,1,0:T(8,128)(2,1)S(1)}) fusion(bf16[2,4,2048,128]{3,2,1,0:T(8,128)(2,1)} %constant_dynamic-update-slice_fusion.22), kind=kLoop, calls=%fused_computation.3 | loop fusion | bytes 8388608 | tf_op jit(solution)/shard_map/squeeze | solution.py:164
  88.7 0.7 fusion.8
  89.4 0.7 fusion.12
  93.3 0.7 convolution_convert_fusion
  94.2 19.7 %all_to_all.20 = bf16[4,256,512]{2,1,0:T(8,128)(2,1)S(1)} all-to-all(bf16[4,256,512]{2,1,0:T(8,128)(2,1)S(1)} %bitcast.367), channel_id=1, replica_groups=mesh['seq'=64,'tensor'=4] {'tensor'}, dimensions={0} | all-to-all | bytes 2097152 | tf_op jit(solution)/shard_map/all_to_all | solution.py:58
  114.3 16.8 %all_to_all.21 = bf16[4,256,512]{1,2,0:T(8,128)(2,1)S(1)} all-to-all(bf16[4,256,512]{1,2,0:T(8,128)(2,1)S(1)} %broadcast_in_dim.94), channel_id=1, replica_groups=mesh['seq'=64,'tensor'=4] {'tensor'}, dimensions={0} | all-to-all | bytes 2097152 | tf_op jit(solution)/shard_map/all_to_all | solution.py:65
  131.5 0.7 fusion.3
  132.2 3.7 %fusion.35 = bf16[256,1024]{1,0:T(8,128)(2,1)S(1)} fusion(bf16[256,2048]{0,1:T(8,128)(2,1)S(1)} %fusion.3, bf16[2048,1024]{1,0:T(8,128)(2,1)S(1)} %copy-done.10, f32[1024]{0:T(1024)S(1)} %copy-done.12), kind=kOutput, calls=%fused_computation.64 | convolution fusion | flops 1091043328 | bytes 5771264 | tf_op jit(solution)/shard_map/dot_general | solution.py:184
  135.9 1.3 convolution_convert_fusion.1
  137.2 1.1 copy.179
  138.3 3.5 %all-to-all-start.3 = ((bf16[4,256,512]{2,1,0:T(8,128)(2,1)}), bf16[4,256,512]{2,1,0:T(8,128)(2,1)S(1)}, u32[]{:S(2)}, u32[]{:S(2)}) async-start(bf16[4,256,512]{2,1,0:T(8,128)(2,1)} %bitcast.365), calls=%async_computation.3 | async-start | bytes 2097152 | tf_op jit(solution)/shard_map/all_to_all | solution.py:58
  141.8 0.8 dynamic_slice.7
  142.6 12.5 %all-to-all-done.3 = bf16[4,256,512]{2,1,0:T(8,128)(2,1)S(1)} async-done(((bf16[4,256,512]{2,1,0:T(8,128)(2,1)}), bf16[4,256,512]{2,1,0:T(8,128)(2,1)S(1)}, u32[]{:S(2)}, u32[]{:S(2)}) %all-to-all-start.3) | async-done | bytes 1048608 | tf_op jit(solution)/shard_map/all_to_all | solution.py:58
  155.2 0.8 add_convert_fusion
  (84 shorter events, 13.6 us)
Async XLA Ops:
  0.0 93.3 %copy-start = (bf16[512,2048]{1,0:T(8,128)(2,1)S(1)}, bf16[512,2048]{1,0:T(8,128)(2,1)}, u32[]{:S(2)}) copy-start(bf16[512,2048]{1,0:T(8,128)(2,1)} %param.23) | copy-start | bytes 6291460
  0.0 28.6 %copy-start.13 = (s32[64]{0:T(128)S(1)}, s32[64]{0:T(128)}, u32[]{:S(2)}) copy-start(s32[64]{0:T(128)} %param.30) | copy-start | bytes 772
  1.0 8.2 %collective-permute-start = (bf16[2,4,32,128]{3,2,1,0:T(8,128)(2,1)S(1)}, bf16[2,4,32,128]{3,2,1,0:T(8,128)(2,1)S(1)}, u32[]{:S(2)}, u32[]{:S(2)}) collective-permute-start(bf16[2,4,32,128]{3,2,1,0:T(8,128)(2,1)S(1)} %bitcast_bitcast_fusion.13), channel_id=1, source_target_pairs={{0,32},{4,36},{8,40},{12,44},{16,48},{20,52},{24,56},{28,60},{32,6... | collective-permute-start | bytes 196616 | tf_op jit(solution)/shard_map/ppermute | solution.py:86
  3.0 6.2 %collective-permute-start.1 = (bf16[2,4,32,128]{3,2,1,0:T(8,128)(2,1)S(1)}, bf16[2,4,32,128]{3,2,1,0:T(8,128)(2,1)S(1)}, u32[]{:S(2)}, u32[]{:S(2)}) collective-permute-start(bf16[2,4,32,128]{3,2,1,0:T(8,128)(2,1)S(1)} %bitcast_bitcast_fusion.13), channel_id=1, source_target_pairs={{0,224},{4,228},{8,232},{12,236},{16,240},{20,244},{24,248},{28,25... | collective-permute-start | bytes 196616 | tf_op jit(solution)/shard_map/ppermute | solution.py:87
  9.2 5.5 %collective-permute-start.2 = (bf16[2,4,32,128]{3,2,1,0:T(8,128)(2,1)S(1)}, bf16[2,4,32,128]{3,2,1,0:T(8,128)(2,1)S(1)}, u32[]{:S(2)}, u32[]{:S(2)}) collective-permute-start(bf16[2,4,32,128]{3,2,1,0:T(8,128)(2,1)S(1)} %collective-permute-done), channel_id=1, source_target_pairs={{0,32},{4,36},{8,40},{12,44},{16,48},{20,52},{24,56},{28,60},{32,6... | collective-permute-start | bytes 196616 | tf_op jit(solution)/shard_map/ppermute | solution.py:86
  9.2 5.5 %collective-permute-start.3 = (bf16[2,4,32,128]{3,2,1,0:T(8,128)(2,1)S(1)}, bf16[2,4,32,128]{3,2,1,0:T(8,128)(2,1)S(1)}, u32[]{:S(2)}, u32[]{:S(2)}) collective-permute-start(bf16[2,4,32,128]{3,2,1,0:T(8,128)(2,1)S(1)} %collective-permute-done.1), channel_id=1, source_target_pairs={{0,224},{4,228},{8,232},{12,236},{16,240},{20,244},{24,248},{28,25... | collective-permute-start | bytes 196616 | tf_op jit(solution)/shard_map/ppermute | solution.py:87
  14.7 5.5 %collective-permute-start.4 = (bf16[2,4,32,128]{3,2,1,0:T(8,128)(2,1)S(1)}, bf16[2,4,32,128]{3,2,1,0:T(8,128)(2,1)S(1)}, u32[]{:S(2)}, u32[]{:S(2)}) collective-permute-start(bf16[2,4,32,128]{3,2,1,0:T(8,128)(2,1)S(1)} %collective-permute-done.2), channel_id=1, source_target_pairs={{0,32},{4,36},{8,40},{12,44},{16,48},{20,52},{24,56},{28,60},{32,6... | collective-permute-start | bytes 196616 | tf_op jit(solution)/shard_map/ppermute | solution.py:86
  14.7 5.5 %collective-permute-start.5 = (bf16[2,4,32,128]{3,2,1,0:T(8,128)(2,1)S(1)}, bf16[2,4,32,128]{3,2,1,0:T(8,128)(2,1)S(1)}, u32[]{:S(2)}, u32[]{:S(2)}) collective-permute-start(bf16[2,4,32,128]{3,2,1,0:T(8,128)(2,1)S(1)} %collective-permute-done.3), channel_id=1, source_target_pairs={{0,224},{4,228},{8,232},{12,236},{16,240},{20,244},{24,248},{28,25... | collective-permute-start | bytes 196616 | tf_op jit(solution)/shard_map/ppermute | solution.py:87
  20.2 5.1 %collective-permute-start.6 = (bf16[2,4,16,128]{3,2,1,0:T(8,128)(2,1)S(1)}, bf16[2,4,16,128]{3,2,1,0:T(8,128)(2,1)S(1)}, u32[]{:S(2)}, u32[]{:S(2)}) collective-permute-start(bf16[2,4,16,128]{3,2,1,0:T(8,128)(2,1)S(1)} %slice.80), channel_id=1, source_target_pairs={{0,32},{4,36},{8,40},{12,44},{16,48},{20,52},{24,56},{28,60},{32,6... | collective-permute-start | bytes 98312 | tf_op jit(solution)/shard_map/ppermute | solution.py:91
  20.2 5.8 %collective-permute-start.7 = (bf16[2,4,16,128]{3,2,1,0:T(8,128)(2,1)S(1)}, bf16[2,4,16,128]{3,2,1,0:T(8,128)(2,1)S(1)}, u32[]{:S(2)}, u32[]{:S(2)}) collective-permute-start(bf16[2,4,16,128]{3,2,1,0:T(8,128)(2,1)S(1)} %slice.81), channel_id=1, source_target_pairs={{0,224},{4,228},{8,232},{12,236},{16,240},{20,244},{24,248},{28,25... | collective-permute-start | bytes 98312 | tf_op jit(solution)/shard_map/ppermute | solution.py:92
  26.6 12.0 %collective-permute-start.8 = (bf16[2,4,256,128]{3,2,1,0:T(8,128)(2,1)S(1)}, bf16[2,4,256,128]{3,2,1,0:T(8,128)(2,1)S(1)}, u32[]{:S(2)}, u32[]{:S(2)}) collective-permute-start(bf16[2,4,256,128]{3,2,1,0:T(8,128)(2,1)S(1)} %get-tuple-element.54), channel_id=1, source_target_pairs={{0,8},{4,12},{8,16},{12,20},{16,24},{20,28},{24,0},{28,4},{32,40},... | collective-permute-start | bytes 1572872 | tf_op jit(solution)/shard_map/ppermute | solution.py:86
  28.1 12.1 %collective-permute-start.9 = (bf16[2,4,256,128]{3,2,1,0:T(8,128)(2,1)S(1)}, bf16[2,4,256,128]{3,2,1,0:T(8,128)(2,1)S(1)}, u32[]{:S(2)}, u32[]{:S(2)}) collective-permute-start(bf16[2,4,256,128]{3,2,1,0:T(8,128)(2,1)S(1)} %get-tuple-element.54), channel_id=1, source_target_pairs={{0,24},{4,28},{8,0},{12,4},{16,8},{20,12},{24,16},{28,20},{32,56},... | collective-permute-start | bytes 1572872 | tf_op jit(solution)/shard_map/ppermute | solution.py:87
  38.6 6.4 %collective-permute-start.10 = (bf16[2,4,128,128]{3,2,1,0:T(8,128)(2,1)S(1)}, bf16[2,4,128,128]{3,2,1,0:T(8,128)(2,1)S(1)}, u32[]{:S(2)}, u32[]{:S(2)}) collective-permute-start(bf16[2,4,128,128]{3,2,1,0:T(8,128)(2,1)S(1)} %slice.82), channel_id=1, source_target_pairs={{0,8},{4,12},{8,16},{12,20},{16,24},{20,28},{24,0},{28,4},{32,40},... | collective-permute-start | bytes 786440 | tf_op jit(solution)/shard_map/ppermute | solution.py:91
  40.2 6.4 %collective-permute-start.11 = (bf16[2,4,128,128]{3,2,1,0:T(8,128)(2,1)S(1)}, bf16[2,4,128,128]{3,2,1,0:T(8,128)(2,1)S(1)}, u32[]{:S(2)}, u32[]{:S(2)}) collective-permute-start(bf16[2,4,128,128]{3,2,1,0:T(8,128)(2,1)S(1)} %slice.83), channel_id=1, source_target_pairs={{0,24},{4,28},{8,0},{12,4},{16,8},{20,12},{24,16},{28,20},{32,56},... | collective-permute-start | bytes 786440 | tf_op jit(solution)/shard_map/ppermute | solution.py:92
  40.8 6.8 %copy-start.7 = (bf16[2,64,512]{2,1,0:T(8,128)(2,1)S(1)}, bf16[2,64,512]{2,1,0:T(8,128)(2,1)}, u32[]{:S(2)}) copy-start(bf16[2,64,512]{2,1,0:T(8,128)(2,1)} %param.21) | copy-start | bytes 393220
  47.6 32.3 %collective-permute-start.12 = (bf16[2,4,1024,128]{3,2,1,0:T(8,128)(2,1)}, bf16[2,4,1024,128]{3,2,1,0:T(8,128)(2,1)}, u32[]{:S(2)}, u32[]{:S(2)}) collective-permute-start(bf16[2,4,1024,128]{3,2,1,0:T(8,128)(2,1)} %get-tuple-element.27), channel_id=1, source_target_pairs={{0,4},{4,0},{8,12},{12,8},{16,20},{20,16},{24,28},{28,24},{32,36},... | collective-permute-start | bytes 6291464 | tf_op jit(solution)/shard_map/ppermute | solution.py:103
  48.7 13.7 %copy-start.14 = (s32[64]{0:T(128)S(1)}, s32[64]{0:T(128)}, u32[]{:S(2)}) copy-start(s32[64]{0:T(128)} %param.31) | copy-start | bytes 772
  48.8 16.7 %copy-start.1 = (bf16[256,512]{1,0:T(8,128)(2,1)S(1)}, bf16[256,512]{1,0:T(8,128)(2,1)}, u32[]{:S(2)}) copy-start(bf16[256,512]{1,0:T(8,128)(2,1)} %param.17) | copy-start | bytes 786436
  50.2 28.0 %all-to-all-start = ((bf16[64,2,4,4,128]{4,2,3,1,0:T(4,128)(2,1)}), bf16[64,2,4,4,128]{4,2,3,1,0:T(4,128)(2,1)}, u32[]{:S(2)}, u32[]{:S(2)}) async-start(bf16[64,2,4,4,128]{4,2,3,1,0:T(4,128)(2,1)} %bitcast.14), calls=%async_computation | async-start | bytes 1048576 | tf_op jit(solution)/shard_map/all_to_all | solution.py:140
  64.8 0.7 copy-start.4
  87.5 1.1 copy-start.2
  89.4 1.0 copy-start.3
  89.4 1.3 copy-start.5
  94.1 19.8 %copy-start.6 = (bf16[256,512]{1,0:T(8,128)(2,1)S(1)}, bf16[256,512]{1,0:T(8,128)(2,1)}, u32[]{:S(2)}) copy-start(bf16[256,512]{1,0:T(8,128)(2,1)} %param.16) | copy-start | bytes 786436
  114.2 17.2 %copy-start.8 = (f32[2048]{0:T(1024)S(1)}, f32[2048]{0:T(1024)}, u32[]{:S(2)}) copy-start(f32[2048]{0:T(1024)} %param.25) | copy-start | bytes 24580
  114.2 17.2 %copy-start.9 = (f32[2048]{0:T(1024)S(1)}, f32[2048]{0:T(1024)}, u32[]{:S(2)}) copy-start(f32[2048]{0:T(1024)} %param.24) | copy-start | bytes 24580
  114.3 17.9 %copy-start.10 = (bf16[2048,1024]{1,0:T(8,128)(2,1)S(1)}, bf16[2048,1024]{1,0:T(8,128)(2,1)}, u32[]{:S(2)}) copy-start(bf16[2048,1024]{1,0:T(8,128)(2,1)} %param.26) | copy-start | bytes 12582916
  131.1 1.1 copy-start.12
  132.2 3.7 %copy-start.11 = (bf16[1024,2048]{1,0:T(8,128)(2,1)S(1)}, bf16[1024,2048]{1,0:T(8,128)(2,1)}, u32[]{:S(2)}) copy-start(bf16[1024,2048]{1,0:T(8,128)(2,1)} %param.28) | copy-start | bytes 12582916
  138.3 16.7 %all-to-all-start.3 = ((bf16[4,256,512]{2,1,0:T(8,128)(2,1)}), bf16[4,256,512]{2,1,0:T(8,128)(2,1)S(1)}, u32[]{:S(2)}, u32[]{:S(2)}) async-start(bf16[4,256,512]{2,1,0:T(8,128)(2,1)} %bitcast.365), calls=%async_computation.3 | async-start | bytes 2097152 | tf_op jit(solution)/shard_map/all_to_all | solution.py:58

commit v4 on v3

--- a/solution.py
+++ b/solution.py
@@ -94,14 +94,15 @@
     return jnp.concatenate(pieces, axis=2)
 
 
-def ring_gather_seq(block, seq_size):
+def ring_gather_seq(block, seq_size, companion):
     cores = 2
     lanes = 4
     shape = (seq_size // (lanes * cores), lanes, cores)
     gathered = ring_along(block, shape, 0)
     gathered = ring_along(gathered, shape, 1)
+    gathered, companion = lax.optimization_barrier((gathered, companion))
     partner = lax.ppermute(gathered, "seq", shift_pairs(shape, 2, 1))
-    return jnp.concatenate([gathered, partner], axis=2)
+    return jnp.concatenate([gathered, partner], axis=2), companion
 
 
 def per_device(
@@ -131,13 +132,13 @@
     branch_count = seq_size // 4
     feature_width = branch_kv.shape[2]
 
-    root_full = ring_gather_seq(head_major(root_kv, head_count), seq_size)
-
     local_rows = branch_kv.shape[1] // branch_count
     branch_local = branch_kv.reshape(2, local_rows, branch_count, feature_width)
     picked = jnp.take(branch_local, segment, axis=2)
     picked = head_major(jnp.transpose(picked, (2, 0, 1, 3)), head_count)
     arrived = lax.all_to_all(picked, "seq", 0, 0, tiled=True)
+
+    root_full, arrived = ring_gather_seq(head_major(root_kv, head_count), seq_size, arrived)
     branch_mine = jnp.transpose(arrived, (1, 2, 0, 3, 4)).reshape(
         2, head_count, seq_size * local_rows, HD
     )

time: 157 us -> 150 us (0.955)
  local copies, waits for them, and re-layouts: 28 us -> 20.4 us
    all_to_all x1, waiting for transfers between devices: 10.5 us -> 0.01 us  [per_device(): arrived = lax.all_to_all(picked, 'seq', 0, 0, tiled=True)]
    ppermute x4, waiting for transfers between devices: 12.1 us -> 21.6 us  [ring_along(): from_below = lax.ppermute(from_below, 'seq', up)]
    squeeze x1, local copies, waits for them, and re-layouts: 2.52 us -> 0.27 us  [per_device(): running = attend_blocks(running, query_heads, root_full[0], root_full[1])]
    unnamed x42 -> x36, local copies, waits for them, and re-layouts: 11.3 us -> 9.63 us
    reshape x2, local copies, waits for them, and re-layouts: 2.81 us -> 1.13 us  [head_major(): split = rows.reshape(lead + (rows.shape[-2], head_count, HD))]
    ppermute x4, starting transfers between devices: 11.2 us -> 9.52 us  [ring_along(): from_above = lax.ppermute(from_above, 'seq', down)]
  transfers between devices with their start and end apart: 15 -> 15, of which waited for: 9 -> 7; matrix products, arithmetic and copies ran while one was open for 13% -> 13% of each run, Pallas kernels for 0% -> 0%
where the time goes in v4:
time: 150 us
  waiting for transfers between devices  38.8 us (26%)
  blocking collectives  37.7 us (25%)
  starting transfers between devices  32.8 us (22%)
  local copies, waits for them, and re-layouts  20.4 us (14%)
  matrix products  12.8 us (9%)
  other arithmetic  6.71 us (4%)
    ppermute x4, waiting for transfers between devices, ring_along(): from_below = lax.ppermute(from_below, 'seq', up)  21.6 us
    all_to_all x1, blocking collectives, tensor_sum_scatter(): arrived = lax.all_to_all(pieces, 'tensor', 0, 0, tiled=True)  20.2 us
    all_to_all x1, blocking collectives, tensor_gather(): arrived = lax.all_to_all(copies, 'tensor', 0, 0, tiled=True)  17.6 us
    all_to_all x1, waiting for transfers between devices, tensor_sum_scatter(): arrived = lax.all_to_all(pieces, 'tensor', 0, 0, tiled=True)  13.2 us
    unnamed x36, local copies, waits for them, and re-layouts  9.63 us
    ppermute x4, starting transfers between devices, ring_along(): from_above = lax.ppermute(from_above, 'seq', down)  9.52 us
    all_to_all x1, starting transfers between devices, per_device(): arrived = lax.all_to_all(picked, 'seq', 0, 0, tiled=True)  9.31 us
    ppermute x4, starting transfers between devices, ring_along(): from_below = lax.ppermute(from_below, 'seq', up)  5.01 us
  transfers between devices with their start and end apart: 15, of which 7 were waited for; matrix products, arithmetic and copies ran while one was open for 13% of the time, Pallas kernels for 0%

profile of v4, /device:TPU:2, one launch (start us, length us, event | category | flops | bytes accessed | tf_op | source)
XLA Modules:
  0.0 149.7 jit_solution(7907207245956213214)
XLA Ops:
  0.0 1.0 bitcast_bitcast_fusion.13
  1.0 2.0 %collective-permute-start = (bf16[2,4,32,128]{3,2,1,0:T(8,128)(2,1)S(1)}, bf16[2,4,32,128]{3,2,1,0:T(8,128)(2,1)S(1)}, u32[]{:S(2)}, u32[]{:S(2)}) collective-permute-start(bf16[2,4,32,128]{3,2,1,0:T(8,128)(2,1)S(1)} %bitcast_bitcast_fusion.13), channel_id=1, source_target_pairs={{0,32},{4,36},{8,40},{12,44},{16,48},{20,52},{24,56},{28,60},{32,6... | collective-permute-start | bytes 196616 | tf_op jit(solution)/shard_map/ppermute | solution.py:86
  3.0 4.0 %collective-permute-start.1 = (bf16[2,4,32,128]{3,2,1,0:T(8,128)(2,1)S(1)}, bf16[2,4,32,128]{3,2,1,0:T(8,128)(2,1)S(1)}, u32[]{:S(2)}, u32[]{:S(2)}) collective-permute-start(bf16[2,4,32,128]{3,2,1,0:T(8,128)(2,1)S(1)} %bitcast_bitcast_fusion.13), channel_id=1, source_target_pairs={{0,224},{4,228},{8,232},{12,236},{16,240},{20,244},{24,248},{28,25... | collective-permute-start | bytes 196616 | tf_op jit(solution)/shard_map/ppermute | solution.py:87
  7.0 0.7 compare_select_fusion
  7.7 0.7 compare_and_fusion
  8.3 1.0 copy.78
  9.4 1.0 gather_fusion
  10.8 1.0 reshape.291
  11.7 9.3 %all-to-all-start = ((bf16[64,2,4,4,128]{4,2,3,1,0:T(4,128)(2,1)}), bf16[64,2,4,4,128]{4,2,3,1,0:T(4,128)(2,1)S(1)}, u32[]{:S(2)}, u32[]{:S(2)}) async-start(bf16[64,2,4,4,128]{4,2,3,1,0:T(4,128)(2,1)} %bitcast.15), calls=%async_computation | async-start | bytes 1048576 | tf_op jit(solution)/shard_map/all_to_all | solution.py:139
  21.1 0.7 constant_dynamic-update-slice_fusion.8
  21.7 1.5 collective-permute-start.2
  23.2 1.8 %collective-permute-start.3 = (bf16[2,4,32,128]{3,2,1,0:T(8,128)(2,1)S(1)}, bf16[2,4,32,128]{3,2,1,0:T(8,128)(2,1)S(1)}, u32[]{:S(2)}, u32[]{:S(2)}) collective-permute-start(bf16[2,4,32,128]{3,2,1,0:T(8,128)(2,1)S(1)} %collective-permute-done.1), channel_id=1, source_target_pairs={{0,224},{4,228},{8,232},{12,236},{16,240},{20,244},{24,248},{28,25... | collective-permute-start | bytes 196616 | tf_op jit(solution)/shard_map/ppermute | solution.py:87
  25.0 0.7 constant_dynamic-update-slice_fusion.7
  25.6 0.7 constant_dynamic-update-slice_fusion.6
  26.3 10.8 %collective-permute-done.2 = bf16[2,4,32,128]{3,2,1,0:T(8,128)(2,1)S(1)} collective-permute-done((bf16[2,4,32,128]{3,2,1,0:T(8,128)(2,1)S(1)}, bf16[2,4,32,128]{3,2,1,0:T(8,128)(2,1)S(1)}, u32[]{:S(2)}, u32[]{:S(2)}) %collective-permute-start.2) | collective-permute-done | bytes 65568 | tf_op jit(solution)/shard_map/ppermute | solution.py:86
  37.1 3.2 %collective-permute-start.5 = (bf16[2,4,32,128]{3,2,1,0:T(8,128)(2,1)S(1)}, bf16[2,4,32,128]{3,2,1,0:T(8,128)(2,1)S(1)}, u32[]{:S(2)}, u32[]{:S(2)}) collective-permute-start(bf16[2,4,32,128]{3,2,1,0:T(8,128)(2,1)S(1)} %collective-permute-done.3), channel_id=1, source_target_pairs={{0,224},{4,228},{8,232},{12,236},{16,240},{20,244},{24,248},{28,25... | collective-permute-start | bytes 196616 | tf_op jit(solution)/shard_map/ppermute | solution.py:87
  40.4 0.7 constant_dynamic-update-slice_fusion.5
  41.0 0.7 constant_dynamic-update-slice_fusion.4
  41.7 0.9 collective-permute-done.4
  42.6 3.2 %collective-permute-start.7 = (bf16[2,4,16,128]{3,2,1,0:T(8,128)(2,1)S(1)}, bf16[2,4,16,128]{3,2,1,0:T(8,128)(2,1)S(1)}, u32[]{:S(2)}, u32[]{:S(2)}) collective-permute-start(bf16[2,4,16,128]{3,2,1,0:T(8,128)(2,1)S(1)} %slice.79), channel_id=1, source_target_pairs={{0,224},{4,228},{8,232},{12,236},{16,240},{20,244},{24,248},{28,25... | collective-permute-start | bytes 98312 | tf_op jit(solution)/shard_map/ppermute | solution.py:92
  45.9 0.7 constant_dynamic-update-slice_fusion.3
  46.5 0.7 constant_dynamic-update-slice_fusion.2
  48.4 0.6 constant_dynamic-update-slice_fusion
  49.0 1.5 %collective-permute-start.8 = (bf16[2,4,256,128]{3,2,1,0:T(8,128)(2,1)S(1)}, bf16[2,4,256,128]{3,2,1,0:T(8,128)(2,1)S(1)}, u32[]{:S(2)}, u32[]{:S(2)}) collective-permute-start(bf16[2,4,256,128]{3,2,1,0:T(8,128)(2,1)S(1)} %get-tuple-element.41), channel_id=1, source_target_pairs={{0,8},{4,12},{8,16},{12,20},{16,24},{20,28},{24,0},{28,4},{32,40},... | collective-permute-start | bytes 1572872 | tf_op jit(solution)/shard_map/ppermute | solution.py:86
  51.0 9.9 %collective-permute-done.8 = bf16[2,4,256,128]{3,2,1,0:T(8,128)(2,1)S(1)} collective-permute-done((bf16[2,4,256,128]{3,2,1,0:T(8,128)(2,1)S(1)}, bf16[2,4,256,128]{3,2,1,0:T(8,128)(2,1)S(1)}, u32[]{:S(2)}, u32[]{:S(2)}) %collective-permute-start.8) | collective-permute-done | bytes 524320 | tf_op jit(solution)/shard_map/ppermute | solution.py:86
  61.0 1.7 %collective-permute-start.10 = (bf16[2,4,128,128]{3,2,1,0:T(8,128)(2,1)S(1)}, bf16[2,4,128,128]{3,2,1,0:T(8,128)(2,1)S(1)}, u32[]{:S(2)}, u32[]{:S(2)}) collective-permute-start(bf16[2,4,128,128]{3,2,1,0:T(8,128)(2,1)S(1)} %slice.80), channel_id=1, source_target_pairs={{0,8},{4,12},{8,16},{12,20},{16,24},{20,28},{24,0},{28,4},{32,40},... | collective-permute-start | bytes 786440 | tf_op jit(solution)/shard_map/ppermute | solution.py:91
  63.2 0.9 constant_dynamic-update-slice_fusion.12
  64.1 0.9 constant_dynamic-update-slice_fusion.11
  65.0 2.4 %collective-permute-done.10 = bf16[2,4,128,128]{3,2,1,0:T(8,128)(2,1)S(1)} collective-permute-done((bf16[2,4,128,128]{3,2,1,0:T(8,128)(2,1)S(1)}, bf16[2,4,128,128]{3,2,1,0:T(8,128)(2,1)S(1)}, u32[]{:S(2)}, u32[]{:S(2)}) %collective-permute-start.10) | collective-permute-done | bytes 262176 | tf_op jit(solution)/shard_map/ppermute | solution.py:91
  67.4 0.7 constant_dynamic-update-slice_fusion.10
  68.2 0.9 collective-permute-done.11
  69.1 0.8 constant_dynamic-update-slice_fusion.9
  71.7 1.3 fusion.113
  73.3 1.7 %constant_dynamic-update-slice_fusion.23 = bf16[2,4,2048,128]{3,2,1,0:T(8,128)(2,1)S(1)} fusion(bf16[2,4,1024,128]{3,2,1,0:T(8,128)(2,1)} %constant_dynamic-update-slice_fusion.9), kind=kLoop, calls=%fused_computation.160 | loop fusion | bytes 4194304
  75.4 1.9 %constant_dynamic-update-slice_fusion.22 = bf16[2,4,2048,128]{3,2,1,0:T(8,128)(2,1)S(1)} fusion(bf16[2,4,2048,128]{3,2,1,0:T(8,128)(2,1)S(1)} %constant_dynamic-update-slice_fusion.23, bf16[2,4,1024,128]{3,2,1,0:T(8,128)(2,1)} %collective-permute-done.12), kind=kLoop, calls=%fused_computation.159 | loop fusion | bytes 4194304 | tf_op jit(solution)/shard_map/concatenate | solution.py:105
  80.6 0.7 fusion.12
  81.3 0.7 fusion.8
  85.0 0.7 convolution_convert_fusion
  85.8 20.2 %all_to_all.20 = bf16[4,256,512]{2,1,0:T(8,128)(2,1)S(1)} all-to-all(bf16[4,256,512]{2,1,0:T(8,128)(2,1)S(1)} %bitcast.363), channel_id=1, replica_groups=mesh['seq'=64,'tensor'=4] {'tensor'}, dimensions={0} | all-to-all | bytes 2097152 | tf_op jit(solution)/shard_map/all_to_all | solution.py:58
  106.5 17.6 %all_to_all.21 = bf16[4,256,512]{1,2,0:T(8,128)(2,1)S(1)} all-to-all(bf16[4,256,512]{1,2,0:T(8,128)(2,1)S(1)} %broadcast_in_dim.94), channel_id=1, replica_groups=mesh['seq'=64,'tensor'=4] {'tensor'}, dimensions={0} | all-to-all | bytes 2097152 | tf_op jit(solution)/shard_map/all_to_all | solution.py:65
  124.4 0.7 fusion.3
  125.2 3.7 %fusion.35 = bf16[256,1024]{1,0:T(8,128)(2,1)S(1)} fusion(bf16[256,2048]{0,1:T(8,128)(2,1)S(1)} %fusion.3, bf16[2048,1024]{1,0:T(8,128)(2,1)S(1)} %copy-done.8, f32[1024]{0:T(1024)S(1)} %copy-done.10), kind=kOutput, calls=%fused_computation.64 | convolution fusion | flops 1091043328 | bytes 5771264 | tf_op jit(solution)/shard_map/dot_general | solution.py:185
  128.9 1.3 convolution_convert_fusion.1
  130.2 1.1 copy.177
  131.2 3.5 %all-to-all-start.3 = ((bf16[4,256,512]{2,1,0:T(8,128)(2,1)}), bf16[4,256,512]{2,1,0:T(8,128)(2,1)S(1)}, u32[]{:S(2)}, u32[]{:S(2)}) async-start(bf16[4,256,512]{2,1,0:T(8,128)(2,1)} %bitcast.361), calls=%async_computation.3 | async-start | bytes 2097152 | tf_op jit(solution)/shard_map/all_to_all | solution.py:58
  134.8 0.8 dynamic_slice.7
  135.5 13.2 %all-to-all-done.3 = bf16[4,256,512]{2,1,0:T(8,128)(2,1)S(1)} async-done(((bf16[4,256,512]{2,1,0:T(8,128)(2,1)}), bf16[4,256,512]{2,1,0:T(8,128)(2,1)S(1)}, u32[]{:S(2)}, u32[]{:S(2)}) %all-to-all-start.3) | async-done | bytes 1048608 | tf_op jit(solution)/shard_map/all_to_all | solution.py:58
  148.9 0.8 add_convert_fusion
  (79 shorter events, 12.2 us)
Async XLA Ops:
  0.0 85.0 %copy-start = (bf16[512,2048]{1,0:T(8,128)(2,1)S(1)}, bf16[512,2048]{1,0:T(8,128)(2,1)}, u32[]{:S(2)}) copy-start(bf16[512,2048]{1,0:T(8,128)(2,1)} %param.23) | copy-start | bytes 6291460
  1.0 20.7 %collective-permute-start = (bf16[2,4,32,128]{3,2,1,0:T(8,128)(2,1)S(1)}, bf16[2,4,32,128]{3,2,1,0:T(8,128)(2,1)S(1)}, u32[]{:S(2)}, u32[]{:S(2)}) collective-permute-start(bf16[2,4,32,128]{3,2,1,0:T(8,128)(2,1)S(1)} %bitcast_bitcast_fusion.13), channel_id=1, source_target_pairs={{0,32},{4,36},{8,40},{12,44},{16,48},{20,52},{24,56},{28,60},{32,6... | collective-permute-start | bytes 196616 | tf_op jit(solution)/shard_map/ppermute | solution.py:86
  3.0 20.2 %collective-permute-start.1 = (bf16[2,4,32,128]{3,2,1,0:T(8,128)(2,1)S(1)}, bf16[2,4,32,128]{3,2,1,0:T(8,128)(2,1)S(1)}, u32[]{:S(2)}, u32[]{:S(2)}) collective-permute-start(bf16[2,4,32,128]{3,2,1,0:T(8,128)(2,1)S(1)} %bitcast_bitcast_fusion.13), channel_id=1, source_target_pairs={{0,224},{4,228},{8,232},{12,236},{16,240},{20,244},{24,248},{28,25... | collective-permute-start | bytes 196616 | tf_op jit(solution)/shard_map/ppermute | solution.py:87
  9.4 11.7 %copy-start.2 = (bf16[2,32,512]{2,1,0:T(8,128)(2,1)S(1)}, bf16[2,32,512]{2,1,0:T(8,128)(2,1)}, u32[]{:S(2)}) copy-start(bf16[2,32,512]{2,1,0:T(8,128)(2,1)} %param.22) | copy-start | bytes 196612
  11.7 58.1 %all-to-all-start = ((bf16[64,2,4,4,128]{4,2,3,1,0:T(4,128)(2,1)}), bf16[64,2,4,4,128]{4,2,3,1,0:T(4,128)(2,1)S(1)}, u32[]{:S(2)}, u32[]{:S(2)}) async-start(bf16[64,2,4,4,128]{4,2,3,1,0:T(4,128)(2,1)} %bitcast.15), calls=%async_computation | async-start | bytes 1048576 | tf_op jit(solution)/shard_map/all_to_all | solution.py:139
  21.7 15.4 %collective-permute-start.2 = (bf16[2,4,32,128]{3,2,1,0:T(8,128)(2,1)S(1)}, bf16[2,4,32,128]{3,2,1,0:T(8,128)(2,1)S(1)}, u32[]{:S(2)}, u32[]{:S(2)}) collective-permute-start(bf16[2,4,32,128]{3,2,1,0:T(8,128)(2,1)S(1)} %collective-permute-done), channel_id=1, source_target_pairs={{0,32},{4,36},{8,40},{12,44},{16,48},{20,52},{24,56},{28,60},{32,6... | collective-permute-start | bytes 196616 | tf_op jit(solution)/shard_map/ppermute | solution.py:86
  23.2 13.9 %collective-permute-start.3 = (bf16[2,4,32,128]{3,2,1,0:T(8,128)(2,1)S(1)}, bf16[2,4,32,128]{3,2,1,0:T(8,128)(2,1)S(1)}, u32[]{:S(2)}, u32[]{:S(2)}) collective-permute-start(bf16[2,4,32,128]{3,2,1,0:T(8,128)(2,1)S(1)} %collective-permute-done.1), channel_id=1, source_target_pairs={{0,224},{4,228},{8,232},{12,236},{16,240},{20,244},{24,248},{28,25... | collective-permute-start | bytes 196616 | tf_op jit(solution)/shard_map/ppermute | solution.py:87
  37.1 5.5 %collective-permute-start.4 = (bf16[2,4,32,128]{3,2,1,0:T(8,128)(2,1)S(1)}, bf16[2,4,32,128]{3,2,1,0:T(8,128)(2,1)S(1)}, u32[]{:S(2)}, u32[]{:S(2)}) collective-permute-start(bf16[2,4,32,128]{3,2,1,0:T(8,128)(2,1)S(1)} %collective-permute-done.2), channel_id=1, source_target_pairs={{0,32},{4,36},{8,40},{12,44},{16,48},{20,52},{24,56},{28,60},{32,6... | collective-permute-start | bytes 196616 | tf_op jit(solution)/shard_map/ppermute | solution.py:86
  37.1 5.5 %collective-permute-start.5 = (bf16[2,4,32,128]{3,2,1,0:T(8,128)(2,1)S(1)}, bf16[2,4,32,128]{3,2,1,0:T(8,128)(2,1)S(1)}, u32[]{:S(2)}, u32[]{:S(2)}) collective-permute-start(bf16[2,4,32,128]{3,2,1,0:T(8,128)(2,1)S(1)} %collective-permute-done.3), channel_id=1, source_target_pairs={{0,224},{4,228},{8,232},{12,236},{16,240},{20,244},{24,248},{28,25... | collective-permute-start | bytes 196616 | tf_op jit(solution)/shard_map/ppermute | solution.py:87
  42.6 5.1 %collective-permute-start.6 = (bf16[2,4,16,128]{3,2,1,0:T(8,128)(2,1)S(1)}, bf16[2,4,16,128]{3,2,1,0:T(8,128)(2,1)S(1)}, u32[]{:S(2)}, u32[]{:S(2)}) collective-permute-start(bf16[2,4,16,128]{3,2,1,0:T(8,128)(2,1)S(1)} %slice.78), channel_id=1, source_target_pairs={{0,32},{4,36},{8,40},{12,44},{16,48},{20,52},{24,56},{28,60},{32,6... | collective-permute-start | bytes 98312 | tf_op jit(solution)/shard_map/ppermute | solution.py:91
  42.6 5.7 %collective-permute-start.7 = (bf16[2,4,16,128]{3,2,1,0:T(8,128)(2,1)S(1)}, bf16[2,4,16,128]{3,2,1,0:T(8,128)(2,1)S(1)}, u32[]{:S(2)}, u32[]{:S(2)}) collective-permute-start(bf16[2,4,16,128]{3,2,1,0:T(8,128)(2,1)S(1)} %slice.79), channel_id=1, source_target_pairs={{0,224},{4,228},{8,232},{12,236},{16,240},{20,244},{24,248},{28,25... | collective-permute-start | bytes 98312 | tf_op jit(solution)/shard_map/ppermute | solution.py:92
  49.0 20.9 %copy-start.3 = (bf16[256,512]{1,0:T(8,128)(2,1)S(1)}, bf16[256,512]{1,0:T(8,128)(2,1)}, u32[]{:S(2)}) copy-start(bf16[256,512]{1,0:T(8,128)(2,1)} %param.19) | copy-start | bytes 786436
  49.0 11.9 %collective-permute-start.8 = (bf16[2,4,256,128]{3,2,1,0:T(8,128)(2,1)S(1)}, bf16[2,4,256,128]{3,2,1,0:T(8,128)(2,1)S(1)}, u32[]{:S(2)}, u32[]{:S(2)}) collective-permute-start(bf16[2,4,256,128]{3,2,1,0:T(8,128)(2,1)S(1)} %get-tuple-element.41), channel_id=1, source_target_pairs={{0,8},{4,12},{8,16},{12,20},{16,24},{20,28},{24,0},{28,4},{32,40},... | collective-permute-start | bytes 1572872 | tf_op jit(solution)/shard_map/ppermute | solution.py:86
  50.6 12.1 %collective-permute-start.9 = (bf16[2,4,256,128]{3,2,1,0:T(8,128)(2,1)S(1)}, bf16[2,4,256,128]{3,2,1,0:T(8,128)(2,1)S(1)}, u32[]{:S(2)}, u32[]{:S(2)}) collective-permute-start(bf16[2,4,256,128]{3,2,1,0:T(8,128)(2,1)S(1)} %get-tuple-element.41), channel_id=1, source_target_pairs={{0,24},{4,28},{8,0},{12,4},{16,8},{20,12},{24,16},{28,20},{32,56},... | collective-permute-start | bytes 1572872 | tf_op jit(solution)/shard_map/ppermute | solution.py:87
  61.0 9.1 %copy-start.11 = (s32[64]{0:T(128)S(1)}, s32[64]{0:T(128)}, u32[]{:S(2)}) copy-start(s32[64]{0:T(128)} %param.31) | copy-start | bytes 772
  61.0 10.4 %copy-start.5 = (bf16[2,64,512]{2,1,0:T(8,128)(2,1)S(1)}, bf16[2,64,512]{2,1,0:T(8,128)(2,1)}, u32[]{:S(2)}) copy-start(bf16[2,64,512]{2,1,0:T(8,128)(2,1)} %param.20) | copy-start | bytes 393220
  61.0 6.4 %collective-permute-start.10 = (bf16[2,4,128,128]{3,2,1,0:T(8,128)(2,1)S(1)}, bf16[2,4,128,128]{3,2,1,0:T(8,128)(2,1)S(1)}, u32[]{:S(2)}, u32[]{:S(2)}) collective-permute-start(bf16[2,4,128,128]{3,2,1,0:T(8,128)(2,1)S(1)} %slice.80), channel_id=1, source_target_pairs={{0,8},{4,12},{8,16},{12,20},{16,24},{20,28},{24,0},{28,4},{32,40},... | collective-permute-start | bytes 786440 | tf_op jit(solution)/shard_map/ppermute | solution.py:91
  62.7 8.8 %copy-start.1 = (bf16[256,512]{1,0:T(8,128)(2,1)S(1)}, bf16[256,512]{1,0:T(8,128)(2,1)}, u32[]{:S(2)}) copy-start(bf16[256,512]{1,0:T(8,128)(2,1)} %param.17) | copy-start | bytes 786436
  62.7 6.4 %collective-permute-start.11 = (bf16[2,4,128,128]{3,2,1,0:T(8,128)(2,1)S(1)}, bf16[2,4,128,128]{3,2,1,0:T(8,128)(2,1)S(1)}, u32[]{:S(2)}, u32[]{:S(2)}) collective-permute-start(bf16[2,4,128,128]{3,2,1,0:T(8,128)(2,1)S(1)} %slice.81), channel_id=1, source_target_pairs={{0,24},{4,28},{8,0},{12,4},{16,8},{20,12},{24,16},{28,20},{32,56},... | collective-permute-start | bytes 786440 | tf_op jit(solution)/shard_map/ppermute | solution.py:92
  69.9 5.5 %collective-permute-start.12 = (bf16[2,4,1024,128]{3,2,1,0:T(8,128)(2,1)}, bf16[2,4,1024,128]{3,2,1,0:T(8,128)(2,1)}, u32[]{:S(2)}, u32[]{:S(2)}) collective-permute-start(bf16[2,4,1024,128]{3,2,1,0:T(8,128)(2,1)} %constant_dynamic-update-slice_fusion.9), channel_id=1, source_target_pairs={{0,4},{4,0},{8,12},{12,8},{16,20},{20,16},{24,28},{28,24},{32,36},... | collective-permute-start | bytes 6291464 | tf_op jit(solution)/shard_map/ppermute | solution.py:104
  85.8 20.3 %copy-start.4 = (bf16[256,512]{1,0:T(8,128)(2,1)S(1)}, bf16[256,512]{1,0:T(8,128)(2,1)}, u32[]{:S(2)}) copy-start(bf16[256,512]{1,0:T(8,128)(2,1)} %param.16) | copy-start | bytes 786436
  106.4 18.0 %copy-start.6 = (f32[2048]{0:T(1024)S(1)}, f32[2048]{0:T(1024)}, u32[]{:S(2)}) copy-start(f32[2048]{0:T(1024)} %param.25) | copy-start | bytes 24580
  106.4 18.0 %copy-start.7 = (f32[2048]{0:T(1024)S(1)}, f32[2048]{0:T(1024)}, u32[]{:S(2)}) copy-start(f32[2048]{0:T(1024)} %param.24) | copy-start | bytes 24580
  106.5 18.7 %copy-start.8 = (bf16[2048,1024]{1,0:T(8,128)(2,1)S(1)}, bf16[2048,1024]{1,0:T(8,128)(2,1)}, u32[]{:S(2)}) copy-start(bf16[2048,1024]{1,0:T(8,128)(2,1)} %param.26) | copy-start | bytes 12582916
  124.1 1.1 copy-start.10
  125.2 3.7 %copy-start.9 = (bf16[1024,2048]{1,0:T(8,128)(2,1)S(1)}, bf16[1024,2048]{1,0:T(8,128)(2,1)}, u32[]{:S(2)}) copy-start(bf16[1024,2048]{1,0:T(8,128)(2,1)} %param.28) | copy-start | bytes 12582916
  131.2 17.5 %all-to-all-start.3 = ((bf16[4,256,512]{2,1,0:T(8,128)(2,1)}), bf16[4,256,512]{2,1,0:T(8,128)(2,1)S(1)}, u32[]{:S(2)}, u32[]{:S(2)}) async-start(bf16[4,256,512]{2,1,0:T(8,128)(2,1)} %bitcast.361), calls=%async_computation.3 | async-start | bytes 2097152 | tf_op jit(solution)/shard_map/all_to_all | solution.py:58

commit v5 on v3

--- a/solution.py
+++ b/solution.py
@@ -91,17 +91,7 @@
         first = lax.ppermute(from_below[:, :, :half], "seq", up)
         second = lax.ppermute(from_above[:, :, half:], "seq", down)
         pieces += [first, second]
-    return jnp.concatenate(pieces, axis=2)
-
-
-def ring_gather_seq(block, seq_size):
-    cores = 2
-    lanes = 4
-    shape = (seq_size // (lanes * cores), lanes, cores)
-    gathered = ring_along(block, shape, 0)
-    gathered = ring_along(gathered, shape, 1)
-    partner = lax.ppermute(gathered, "seq", shift_pairs(shape, 2, 1))
-    return jnp.concatenate([gathered, partner], axis=2)
+    return pieces
 
 
 def per_device(
@@ -131,13 +121,22 @@
     branch_count = seq_size // 4
     feature_width = branch_kv.shape[2]
 
-    root_full = ring_gather_seq(head_major(root_kv, head_count), seq_size)
+    cores = 2
+    lanes = 4
+    ring_shape = (seq_size // (lanes * cores), lanes, cores)
+    z_block = jnp.concatenate(ring_along(head_major(root_kv, head_count), ring_shape, 0), axis=2)
 
     local_rows = branch_kv.shape[1] // branch_count
     branch_local = branch_kv.reshape(2, local_rows, branch_count, feature_width)
     picked = jnp.take(branch_local, segment, axis=2)
     picked = head_major(jnp.transpose(picked, (2, 0, 1, 3)), head_count)
+    z_block, picked = lax.optimization_barrier((z_block, picked))
     arrived = lax.all_to_all(picked, "seq", 0, 0, tiled=True)
+
+    x_pieces = ring_along(z_block, ring_shape, 1)
+    x_block = jnp.concatenate(x_pieces, axis=2)
+    x_block, arrived = lax.optimization_barrier((x_block, arrived))
+    partner = lax.ppermute(x_block, "seq", shift_pairs(ring_shape, 2, 1))
     branch_mine = jnp.transpose(arrived, (1, 2, 0, 3, 4)).reshape(
         2, head_count, seq_size * local_rows, HD
     )
@@ -160,8 +159,10 @@
     )
     leaf_heads = head_major(leaf_kv, head_count)
     running = attend(running, query_heads, leaf_heads[0], leaf_heads[1], True)
+    for piece in x_pieces:
+        running = attend_blocks(running, query_heads, piece[0], piece[1])
     running = attend_blocks(running, query_heads, branch_mine[0], branch_mine[1])
-    running = attend_blocks(running, query_heads, root_full[0], root_full[1])
+    running = attend_blocks(running, query_heads, partner[0], partner[1])
     largest, totals, accumulated = running
     attention = (
         jnp.transpose(accumulated / totals[:, :, None], (1, 0, 2))

time: 157 us -> 153 us (0.975)
  waiting for transfers between devices: 37.9 us -> 20.2 us
  matrix products: 13.5 us -> 21.9 us
  local copies, waits for them, and re-layouts: 28 us -> 30.8 us
  other arithmetic: 5.4 us -> 7.08 us
    all_to_all x1, waiting for transfers between devices: 10.5 us -> 0.01 us  [per_device(): arrived = lax.all_to_all(picked, 'seq', 0, 0, tiled=True)]
    ppermute x4, waiting for transfers between devices: 12.1 us -> 1.87 us  [ring_along(): from_below = lax.ppermute(from_below, 'seq', up)]
    dot_general x7 -> x10, matrix products: 4.4 us -> 9.04 us  [attend(): jnp.einsum('hqd,hkd->hqk', query_heads, key_heads, preferred_element_type...]
    dot_general x7 -> x10, matrix products: 3.35 us -> 7.11 us  [attend(): jnp.einsum('hqk,hkd->hqd', weights.astype(jnp.bfloat16), value_heads, pre...]
    concatenate x2, local copies, waits for them, and re-layouts: 4.22 us -> 1.37 us  [the longest x1 0.74 us: per_device(): x_block = jnp.concatenate(x_pieces, axis=2)]
    unnamed x42 -> x46, local copies, waits for them, and re-layouts: 11.3 us -> 13.3 us
  transfers between devices with their start and end apart: 15 -> 15, of which waited for: 9 -> 6; matrix products, arithmetic and copies ran while one was open for 13% -> 23% of each run, Pallas kernels for 0% -> 0%
where the time goes in v5:
time: 153 us; the launch traced here: 152 us
  blocking collectives  37.8 us (25%)
  starting transfers between devices  34 us (22%)
  local copies, waits for them, and re-layouts  30.8 us (20%)
  matrix products  21.9 us (14%)
  waiting for transfers between devices  20.2 us (13%)
  other arithmetic  7.08 us (5%)
    all_to_all x1, blocking collectives, tensor_sum_scatter(): arrived = lax.all_to_all(pieces, 'tensor', 0, 0, tiled=True)  20.2 us
    all_to_all x1, blocking collectives, tensor_gather(): arrived = lax.all_to_all(copies, 'tensor', 0, 0, tiled=True)  17.6 us
    unnamed x46, local copies, waits for them, and re-layouts  13.3 us
    all_to_all x1, waiting for transfers between devices, tensor_sum_scatter(): arrived = lax.all_to_all(pieces, 'tensor', 0, 0, tiled=True)  13.2 us
    ppermute x4, starting transfers between devices, ring_along(): from_above = lax.ppermute(from_above, 'seq', down)  11 us
    all_to_all x1, starting transfers between devices, per_device(): arrived = lax.all_to_all(picked, 'seq', 0, 0, tiled=True)  10.1 us
    dot_general x10, matrix products, attend(): jnp.einsum('hqd,hkd->hqk', query_heads, key_heads, preferred_element_type...  9.04 us
    dot_general x10, matrix products, attend(): jnp.einsum('hqk,hkd->hqd', weights.astype(jnp.bfloat16), value_heads, pre...  7.11 us
  transfers between devices with their start and end apart: 15, of which 6 were waited for; matrix products, arithmetic and copies ran while one was open for 23% of the time, Pallas kernels for 0%

profile of v5, /device:TPU:2, one launch (start us, length us, event | category | flops | bytes accessed | tf_op | source)
XLA Modules:
  0.0 152.2 jit_solution(5794658092547725232)
XLA Ops:
  0.0 1.6 %bitcast_bitcast_fusion.16 = bf16[2,4,32,128]{3,2,1,0:T(8,128)(2,1)} fusion(bf16[2,32,512]{2,1,0:T(8,128)(2,1)} %param.22), kind=kLoop, calls=%fused_computation.159 | loop fusion | bytes 131072 | tf_op jit(solution)/shard_map/transpose | solution.py:50
  1.6 1.9 %collective-permute-start = (bf16[2,4,32,128]{3,2,1,0:T(8,128)(2,1)}, bf16[2,4,32,128]{3,2,1,0:T(8,128)(2,1)S(1)}, u32[]{:S(2)}, u32[]{:S(2)}) collective-permute-start(bf16[2,4,32,128]{3,2,1,0:T(8,128)(2,1)} %bitcast_bitcast_fusion.16), channel_id=1, source_target_pairs={{0,32},{4,36},{8,40},{12,44},{16,48},{20,52},{24,56},{28,60},{32,6... | collective-permute-start | bytes 196616 | tf_op jit(solution)/shard_map/ppermute | solution.py:86
  3.6 3.9 %collective-permute-start.1 = (bf16[2,4,32,128]{3,2,1,0:T(8,128)(2,1)}, bf16[2,4,32,128]{3,2,1,0:T(8,128)(2,1)S(1)}, u32[]{:S(2)}, u32[]{:S(2)}) collective-permute-start(bf16[2,4,32,128]{3,2,1,0:T(8,128)(2,1)} %bitcast_bitcast_fusion.16), channel_id=1, source_target_pairs={{0,224},{4,228},{8,232},{12,236},{16,240},{20,244},{24,248},{28,25... | collective-permute-start | bytes 196616 | tf_op jit(solution)/shard_map/ppermute | solution.py:87
  8.8 1.0 copy.96
  9.8 1.6 %bitcast_bitcast_fusion.15 = bf16[2,4,64,128]{3,2,1,0:T(8,128)(2,1)} fusion(bf16[2,64,512]{2,1,0:T(8,128)(2,1)} %param.20), kind=kLoop, calls=%fused_computation.153 | loop fusion | bytes 262144 | tf_op jit(solution)/shard_map/transpose | solution.py:50
  11.4 1.0 gather_fusion
  15.1 3.2 %collective-permute-start.3 = (bf16[2,4,32,128]{3,2,1,0:T(8,128)(2,1)S(1)}, bf16[2,4,32,128]{3,2,1,0:T(8,128)(2,1)S(1)}, u32[]{:S(2)}, u32[]{:S(2)}) collective-permute-start(bf16[2,4,32,128]{3,2,1,0:T(8,128)(2,1)S(1)} %collective-permute-done.1), channel_id=1, source_target_pairs={{0,224},{4,228},{8,232},{12,236},{16,240},{20,244},{24,248},{28,25... | collective-permute-start | bytes 196616 | tf_op jit(solution)/shard_map/ppermute | solution.py:87
  19.0 0.9 collective-permute-done.2
  20.6 3.2 %collective-permute-start.5 = (bf16[2,4,32,128]{3,2,1,0:T(8,128)(2,1)S(1)}, bf16[2,4,32,128]{3,2,1,0:T(8,128)(2,1)S(1)}, u32[]{:S(2)}, u32[]{:S(2)}) collective-permute-start(bf16[2,4,32,128]{3,2,1,0:T(8,128)(2,1)S(1)} %collective-permute-done.3), channel_id=1, source_target_pairs={{0,224},{4,228},{8,232},{12,236},{16,240},{20,244},{24,248},{28,25... | collective-permute-start | bytes 196616 | tf_op jit(solution)/shard_map/ppermute | solution.py:87
  24.5 0.9 collective-permute-done.4
  25.8 3.6 %collective-permute-start.7 = (bf16[2,4,16,128]{3,2,1,0:T(8,128)(2,1)S(1)}, bf16[2,4,16,128]{3,2,1,0:T(8,128)(2,1)S(1)}, u32[]{:S(2)}, u32[]{:S(2)}) collective-permute-start(bf16[2,4,16,128]{3,2,1,0:T(8,128)(2,1)S(1)} %slice.103), channel_id=1, source_target_pairs={{0,224},{4,228},{8,232},{12,236},{16,240},{20,244},{24,248},{28,25... | collective-permute-start | bytes 98312 | tf_op jit(solution)/shard_map/ppermute | solution.py:92
  31.9 1.5 collective-permute-start.8
  34.6 1.0 copy.108
  35.5 10.1 %all-to-all-start = ((bf16[64,2,4,4,128]{4,2,3,1,0:T(4,128)(2,1)}), bf16[64,2,4,4,128]{4,2,3,1,0:T(4,128)(2,1)}, u32[]{:S(2)}, u32[]{:S(2)}) async-start(bf16[64,2,4,4,128]{4,2,3,1,0:T(4,128)(2,1)} %copy.108), calls=%async_computation | async-start | bytes 1048576 | tf_op jit(solution)/shard_map/all_to_all | solution.py:134
  45.8 1.3 fusion.139
  47.1 1.0 slice.108
  48.0 1.5 %collective-permute-start.10 = (bf16[2,4,128,128]{3,2,1,0:T(8,128)(2,1)S(1)}, bf16[2,4,128,128]{3,2,1,0:T(8,128)(2,1)S(1)}, u32[]{:S(2)}, u32[]{:S(2)}) collective-permute-start(bf16[2,4,128,128]{3,2,1,0:T(8,128)(2,1)S(1)} %slice.108), channel_id=1, source_target_pairs={{0,8},{4,12},{8,16},{12,20},{16,24},{20,28},{24,0},{28,4},{32,40},... | collective-permute-start | bytes 786440 | tf_op jit(solution)/shard_map/ppermute | solution.py:91
  49.6 1.9 %constant_dynamic-update-slice_fusion.13 = bf16[2,4,1024,128]{3,2,1,0:T(8,128)(2,1)} fusion(bf16[2,4,256,128]{3,2,1,0:T(8,128)(2,1)} %constant_dynamic-update-slice_fusion), kind=kLoop, calls=%fused_computation.175 | loop fusion | bytes 1048576
  51.5 1.0 slice.111
  52.5 0.8 collective-permute-start.11
  53.3 1.9 %constant_dynamic-update-slice_fusion.12 = bf16[2,4,1024,128]{3,2,1,0:T(8,128)(2,1)} fusion(bf16[2,4,1024,128]{3,2,1,0:T(8,128)(2,1)} %constant_dynamic-update-slice_fusion.13, bf16[2,4,256,128]{3,2,1,0:T(8,128)(2,1)} %collective-permute-done.8), kind=kLoop, calls=%fused_computation.174 | loop fusion | bytes 1048576
  55.3 1.9 %constant_dynamic-update-slice_fusion.11 = bf16[2,4,1024,128]{3,2,1,0:T(8,128)(2,1)} fusion(bf16[2,4,1024,128]{3,2,1,0:T(8,128)(2,1)} %constant_dynamic-update-slice_fusion.12, bf16[2,4,256,128]{3,2,1,0:T(8,128)(2,1)} %collective-permute-done.9), kind=kLoop, calls=%fused_computation.173 | loop fusion | bytes 1048576
  57.2 2.9 %collective-permute-done.10 = bf16[2,4,128,128]{3,2,1,0:T(8,128)(2,1)S(1)} collective-permute-done((bf16[2,4,128,128]{3,2,1,0:T(8,128)(2,1)S(1)}, bf16[2,4,128,128]{3,2,1,0:T(8,128)(2,1)S(1)}, u32[]{:S(2)}, u32[]{:S(2)}) %collective-permute-start.10) | collective-permute-done | bytes 262176 | tf_op jit(solution)/shard_map/ppermute | solution.py:91
  60.8 0.8 constant_dynamic-update-slice_fusion.10
  61.5 1.9 %collective-permute-done.11 = bf16[2,4,128,128]{3,2,1,0:T(8,128)(2,1)S(1)} collective-permute-done((bf16[2,4,128,128]{3,2,1,0:T(8,128)(2,1)S(1)}, bf16[2,4,128,128]{3,2,1,0:T(8,128)(2,1)S(1)}, u32[]{:S(2)}, u32[]{:S(2)}) %collective-permute-start.11) | collective-permute-done | bytes 262176 | tf_op jit(solution)/shard_map/ppermute | solution.py:92
  64.1 0.7 constant_dynamic-update-slice_fusion.9
  64.9 1.8 %fusion.138 = (f32[4,256]{1,0:T(4,128)S(1)}, f32[4,256,64]{1,2,0:T(8,128)}) fusion(bf16[2,4,64,128]{3,2,1,0:T(8,128)(2,1)} %bitcast_bitcast_fusion.15, bf16[256,512]{1,0:T(8,128)(2,1)S(1)} %copy-done.1), kind=kOutput, calls=%fused_computation.246 | convolution fusion | flops 16907264 | bytes 593920 | tf_op jit(solution)/shard_map/hqd,hkd->hqk/dot_general | solution.py:17
  66.6 1.8 %copy.137 = bf16[256,512]{0,1:T(8,128)(2,1)} copy(bf16[256,512]{1,0:T(8,128)(2,1)} %param.19) | data formatting | bytes 524288 | tf_op jit(solution)/shard_map/reshape | solution.py:48
  68.4 1.4 fusion.137
  69.8 1.4 fusion.136
  71.3 1.4 fusion.135
  73.2 1.2 fusion.131
  74.9 1.7 %slice_bitcast_fusion = (bf16[4,1024,128]{2,1,0:T(8,128)(2,1)S(1)}, bf16[4,1024,128]{2,1,0:T(8,128)(2,1)S(1)}) fusion(bf16[2,4,1024,128]{3,2,1,0:T(8,128)(2,1)} %collective-permute-done.12), kind=kLoop, calls=%fused_computation.74 | loop fusion | bytes 4194304 | tf_op jit(solution)/shard_map/squeeze | solution.py:165
  77.6 1.4 convolution_bitcast_fusion.8
  81.6 0.7 fusion.6
  82.8 1.4 convolution_bitcast_fusion.6
  84.7 1.5 %fusion.34 = f32[256,4,128]{0,2,1:T(8,128)S(1)} fusion(f32[256,4,128]{0,2,1:T(8,128)S(1)} %convolution_bitcast_fusion.3, f32[256,4,128]{0,2,1:T(8,128)S(1)} %convolution_bitcast_fusion.4, f32[256,4,128]{0,2,1:T(8,128)S(1)} %convolution_bitcast_fusion.5, f32[256,4,128]{0,2,1:T(8,128)S(1)} %convolution_bitcast_fusion.6, f32[256,4,128]{0,2,1:T(8,128)S(1)} %fusion.24, ...), kind=kOutput, calls=%fused_computation.64 | convolution fusion | flops 68943872 | bytes 4481024 | tf_op jit(solution)/shard_map/hqk,hkd->hqd/dot_general | solution.py:24
  87.5 0.7 convolution_convert_fusion
  88.3 20.2 %all_to_all.20 = bf16[4,256,512]{2,1,0:T(8,128)(2,1)S(1)} all-to-all(bf16[4,256,512]{2,1,0:T(8,128)(2,1)S(1)} %bitcast.464), channel_id=1, replica_groups=mesh['seq'=64,'tensor'=4] {'tensor'}, dimensions={0} | all-to-all | bytes 2097152 | tf_op jit(solution)/shard_map/all_to_all | solution.py:58
  109.0 17.6 %all_to_all.21 = bf16[4,256,512]{1,2,0:T(8,128)(2,1)S(1)} all-to-all(bf16[4,256,512]{1,2,0:T(8,128)(2,1)S(1)} %broadcast_in_dim.107), channel_id=1, replica_groups=mesh['seq'=64,'tensor'=4] {'tensor'}, dimensions={0} | all-to-all | bytes 2097152 | tf_op jit(solution)/shard_map/all_to_all | solution.py:65
  126.9 0.7 fusion.3
  127.7 3.7 %fusion.40 = bf16[256,1024]{1,0:T(8,128)(2,1)S(1)} fusion(bf16[256,2048]{0,1:T(8,128)(2,1)S(1)} %fusion.3, bf16[2048,1024]{1,0:T(8,128)(2,1)S(1)} %copy-done.13, f32[1024]{0:T(1024)S(1)} %copy-done.15), kind=kOutput, calls=%fused_computation.71 | convolution fusion | flops 1091043328 | bytes 5771264 | tf_op jit(solution)/shard_map/dot_general | solution.py:185
  131.4 1.3 convolution_convert_fusion.1
  132.7 1.1 copy.223
  133.7 3.5 %all-to-all-start.3 = ((bf16[4,256,512]{2,1,0:T(8,128)(2,1)}), bf16[4,256,512]{2,1,0:T(8,128)(2,1)S(1)}, u32[]{:S(2)}, u32[]{:S(2)}) async-start(bf16[4,256,512]{2,1,0:T(8,128)(2,1)} %bitcast.462), calls=%async_computation.3 | async-start | bytes 2097152 | tf_op jit(solution)/shard_map/all_to_all | solution.py:58
  137.3 0.8 dynamic_slice.7
  138.0 13.2 %all-to-all-done.3 = bf16[4,256,512]{2,1,0:T(8,128)(2,1)S(1)} async-done(((bf16[4,256,512]{2,1,0:T(8,128)(2,1)}), bf16[4,256,512]{2,1,0:T(8,128)(2,1)S(1)}, u32[]{:S(2)}, u32[]{:S(2)}) %all-to-all-start.3) | async-done | bytes 1048608 | tf_op jit(solution)/shard_map/all_to_all | solution.py:58
  151.4 0.8 add_convert_fusion
  (98 shorter events, 19.2 us)
Async XLA Ops:
  0.0 87.4 %copy-start = (bf16[512,2048]{1,0:T(8,128)(2,1)S(1)}, bf16[512,2048]{1,0:T(8,128)(2,1)}, u32[]{:S(2)}) copy-start(bf16[512,2048]{1,0:T(8,128)(2,1)} %param.23) | copy-start | bytes 6291460
  0.0 12.8 %copy-start.9 = (bf16[2,32,512]{2,1,0:T(8,128)(2,1)S(1)}, bf16[2,32,512]{2,1,0:T(8,128)(2,1)}, u32[]{:S(2)}) copy-start(bf16[2,32,512]{2,1,0:T(8,128)(2,1)} %param.22) | copy-start | bytes 196612
  1.6 12.8 %collective-permute-start = (bf16[2,4,32,128]{3,2,1,0:T(8,128)(2,1)}, bf16[2,4,32,128]{3,2,1,0:T(8,128)(2,1)S(1)}, u32[]{:S(2)}, u32[]{:S(2)}) collective-permute-start(bf16[2,4,32,128]{3,2,1,0:T(8,128)(2,1)} %bitcast_bitcast_fusion.16), channel_id=1, source_target_pairs={{0,32},{4,36},{8,40},{12,44},{16,48},{20,52},{24,56},{28,60},{32,6... | collective-permute-start | bytes 196616 | tf_op jit(solution)/shard_map/ppermute | solution.py:86
  3.6 11.6 %collective-permute-start.1 = (bf16[2,4,32,128]{3,2,1,0:T(8,128)(2,1)}, bf16[2,4,32,128]{3,2,1,0:T(8,128)(2,1)S(1)}, u32[]{:S(2)}, u32[]{:S(2)}) collective-permute-start(bf16[2,4,32,128]{3,2,1,0:T(8,128)(2,1)} %bitcast_bitcast_fusion.16), channel_id=1, source_target_pairs={{0,224},{4,228},{8,232},{12,236},{16,240},{20,244},{24,248},{28,25... | collective-permute-start | bytes 196616 | tf_op jit(solution)/shard_map/ppermute | solution.py:87
  11.4 2.5 %copy-start.16 = (s32[64]{0:T(128)S(1)}, s32[64]{0:T(128)}, u32[]{:S(2)}) copy-start(s32[64]{0:T(128)} %param.31) | copy-start | bytes 772
  13.7 32.1 %copy-start.1 = (bf16[256,512]{1,0:T(8,128)(2,1)S(1)}, bf16[256,512]{1,0:T(8,128)(2,1)}, u32[]{:S(2)}) copy-start(bf16[256,512]{1,0:T(8,128)(2,1)} %param.17) | copy-start | bytes 786436
  14.5 5.5 %collective-permute-start.2 = (bf16[2,4,32,128]{3,2,1,0:T(8,128)(2,1)S(1)}, bf16[2,4,32,128]{3,2,1,0:T(8,128)(2,1)S(1)}, u32[]{:S(2)}, u32[]{:S(2)}) collective-permute-start(bf16[2,4,32,128]{3,2,1,0:T(8,128)(2,1)S(1)} %collective-permute-done), channel_id=1, source_target_pairs={{0,32},{4,36},{8,40},{12,44},{16,48},{20,52},{24,56},{28,60},{32,6... | collective-permute-start | bytes 196616 | tf_op jit(solution)/shard_map/ppermute | solution.py:86
  15.1 5.5 %collective-permute-start.3 = (bf16[2,4,32,128]{3,2,1,0:T(8,128)(2,1)S(1)}, bf16[2,4,32,128]{3,2,1,0:T(8,128)(2,1)S(1)}, u32[]{:S(2)}, u32[]{:S(2)}) collective-permute-start(bf16[2,4,32,128]{3,2,1,0:T(8,128)(2,1)S(1)} %collective-permute-done.1), channel_id=1, source_target_pairs={{0,224},{4,228},{8,232},{12,236},{16,240},{20,244},{24,248},{28,25... | collective-permute-start | bytes 196616 | tf_op jit(solution)/shard_map/ppermute | solution.py:87
  19.9 5.5 %collective-permute-start.4 = (bf16[2,4,32,128]{3,2,1,0:T(8,128)(2,1)S(1)}, bf16[2,4,32,128]{3,2,1,0:T(8,128)(2,1)S(1)}, u32[]{:S(2)}, u32[]{:S(2)}) collective-permute-start(bf16[2,4,32,128]{3,2,1,0:T(8,128)(2,1)S(1)} %collective-permute-done.2), channel_id=1, source_target_pairs={{0,32},{4,36},{8,40},{12,44},{16,48},{20,52},{24,56},{28,60},{32,6... | collective-permute-start | bytes 196616 | tf_op jit(solution)/shard_map/ppermute | solution.py:86
  20.6 5.1 %collective-permute-start.5 = (bf16[2,4,32,128]{3,2,1,0:T(8,128)(2,1)S(1)}, bf16[2,4,32,128]{3,2,1,0:T(8,128)(2,1)S(1)}, u32[]{:S(2)}, u32[]{:S(2)}) collective-permute-start(bf16[2,4,32,128]{3,2,1,0:T(8,128)(2,1)S(1)} %collective-permute-done.3), channel_id=1, source_target_pairs={{0,224},{4,228},{8,232},{12,236},{16,240},{20,244},{24,248},{28,25... | collective-permute-start | bytes 196616 | tf_op jit(solution)/shard_map/ppermute | solution.py:87
  25.4 5.2 %collective-permute-start.6 = (bf16[2,4,16,128]{3,2,1,0:T(8,128)(2,1)S(1)}, bf16[2,4,16,128]{3,2,1,0:T(8,128)(2,1)S(1)}, u32[]{:S(2)}, u32[]{:S(2)}) collective-permute-start(bf16[2,4,16,128]{3,2,1,0:T(8,128)(2,1)S(1)} %slice.102), channel_id=1, source_target_pairs={{0,32},{4,36},{8,40},{12,44},{16,48},{20,52},{24,56},{28,60},{32,6... | collective-permute-start | bytes 98312 | tf_op jit(solution)/shard_map/ppermute | solution.py:91
  25.8 5.5 %collective-permute-start.7 = (bf16[2,4,16,128]{3,2,1,0:T(8,128)(2,1)S(1)}, bf16[2,4,16,128]{3,2,1,0:T(8,128)(2,1)S(1)}, u32[]{:S(2)}, u32[]{:S(2)}) collective-permute-start(bf16[2,4,16,128]{3,2,1,0:T(8,128)(2,1)S(1)} %slice.103), channel_id=1, source_target_pairs={{0,224},{4,228},{8,232},{12,236},{16,240},{20,244},{24,248},{28,25... | collective-permute-start | bytes 98312 | tf_op jit(solution)/shard_map/ppermute | solution.py:92
  31.9 15.2 %collective-permute-start.8 = (bf16[2,4,256,128]{3,2,1,0:T(8,128)(2,1)}, bf16[2,4,256,128]{3,2,1,0:T(8,128)(2,1)}, u32[]{:S(2)}, u32[]{:S(2)}) collective-permute-start(bf16[2,4,256,128]{3,2,1,0:T(8,128)(2,1)} %constant_dynamic-update-slice_fusion), channel_id=1, source_target_pairs={{0,8},{4,12},{8,16},{12,20},{16,24},{20,28},{24,0},{28,4},{32,40},... | collective-permute-start | bytes 1572872 | tf_op jit(solution)/shard_map/ppermute | solution.py:86
  33.9 17.6 %collective-permute-start.9 = (bf16[2,4,256,128]{3,2,1,0:T(8,128)(2,1)}, bf16[2,4,256,128]{3,2,1,0:T(8,128)(2,1)}, u32[]{:S(2)}, u32[]{:S(2)}) collective-permute-start(bf16[2,4,256,128]{3,2,1,0:T(8,128)(2,1)} %constant_dynamic-update-slice_fusion), channel_id=1, source_target_pairs={{0,24},{4,28},{8,0},{12,4},{16,8},{20,12},{24,16},{28,20},{32,56},... | collective-permute-start | bytes 1572872 | tf_op jit(solution)/shard_map/ppermute | solution.py:87
  35.5 29.3 %all-to-all-start = ((bf16[64,2,4,4,128]{4,2,3,1,0:T(4,128)(2,1)}), bf16[64,2,4,4,128]{4,2,3,1,0:T(4,128)(2,1)}, u32[]{:S(2)}, u32[]{:S(2)}) async-start(bf16[64,2,4,4,128]{4,2,3,1,0:T(4,128)(2,1)} %copy.108), calls=%async_computation | async-start | bytes 1048576 | tf_op jit(solution)/shard_map/all_to_all | solution.py:134
  48.0 12.0 %collective-permute-start.10 = (bf16[2,4,128,128]{3,2,1,0:T(8,128)(2,1)S(1)}, bf16[2,4,128,128]{3,2,1,0:T(8,128)(2,1)S(1)}, u32[]{:S(2)}, u32[]{:S(2)}) collective-permute-start(bf16[2,4,128,128]{3,2,1,0:T(8,128)(2,1)S(1)} %slice.108), channel_id=1, source_target_pairs={{0,8},{4,12},{8,16},{12,20},{16,24},{20,28},{24,0},{28,4},{32,40},... | collective-permute-start | bytes 786440 | tf_op jit(solution)/shard_map/ppermute | solution.py:91
  52.5 10.9 %collective-permute-start.11 = (bf16[2,4,128,128]{3,2,1,0:T(8,128)(2,1)S(1)}, bf16[2,4,128,128]{3,2,1,0:T(8,128)(2,1)S(1)}, u32[]{:S(2)}, u32[]{:S(2)}) collective-permute-start(bf16[2,4,128,128]{3,2,1,0:T(8,128)(2,1)S(1)} %slice.111), channel_id=1, source_target_pairs={{0,24},{4,28},{8,0},{12,4},{16,8},{20,12},{24,16},{28,20},{32,56},... | collective-permute-start | bytes 786440 | tf_op jit(solution)/shard_map/ppermute | solution.py:92
  60.1 0.7 copy-start.3
  63.4 0.7 copy-start.5
  64.9 10.1 %collective-permute-start.12 = (bf16[2,4,1024,128]{3,2,1,0:T(8,128)(2,1)}, bf16[2,4,1024,128]{3,2,1,0:T(8,128)(2,1)}, u32[]{:S(2)}, u32[]{:S(2)}) collective-permute-start(bf16[2,4,1024,128]{3,2,1,0:T(8,128)(2,1)} %constant_dynamic-update-slice_fusion.9), channel_id=1, source_target_pairs={{0,4},{4,0},{8,12},{12,8},{16,20},{20,16},{24,28},{28,24},{32,36},... | collective-permute-start | bytes 6291464 | tf_op jit(solution)/shard_map/ppermute | solution.py:139
  68.4 4.2 %copy-start.4 = (bf16[2,4,128,128]{3,2,1,0:T(8,128)(2,1)S(1)}, bf16[2,4,128,128]{3,2,1,0:T(8,128)(2,1)}, u32[]{:S(2)}) copy-start(bf16[2,4,128,128]{3,2,1,0:T(8,128)(2,1)} %copy-done.3) | copy-start | bytes 786436
  69.8 3.1 %copy-start.6 = (bf16[2,4,128,128]{3,2,1,0:T(8,128)(2,1)S(1)}, bf16[2,4,128,128]{3,2,1,0:T(8,128)(2,1)}, u32[]{:S(2)}) copy-start(bf16[2,4,128,128]{3,2,1,0:T(8,128)(2,1)} %copy-done.5) | copy-start | bytes 786436
  79.6 1.3 copy-start.2
  80.1 1.0 copy-start.7
  81.6 0.9 copy-start.8
  88.3 20.3 %copy-start.10 = (bf16[256,512]{1,0:T(8,128)(2,1)S(1)}, bf16[256,512]{1,0:T(8,128)(2,1)}, u32[]{:S(2)}) copy-start(bf16[256,512]{1,0:T(8,128)(2,1)} %param.16) | copy-start | bytes 786436
  108.8 18.0 %copy-start.11 = (f32[2048]{0:T(1024)S(1)}, f32[2048]{0:T(1024)}, u32[]{:S(2)}) copy-start(f32[2048]{0:T(1024)} %param.25) | copy-start | bytes 24580
  108.9 18.0 %copy-start.12 = (f32[2048]{0:T(1024)S(1)}, f32[2048]{0:T(1024)}, u32[]{:S(2)}) copy-start(f32[2048]{0:T(1024)} %param.24) | copy-start | bytes 24580
  108.9 18.7 %copy-start.13 = (bf16[2048,1024]{1,0:T(8,128)(2,1)S(1)}, bf16[2048,1024]{1,0:T(8,128)(2,1)}, u32[]{:S(2)}) copy-start(bf16[2048,1024]{1,0:T(8,128)(2,1)} %param.26) | copy-start | bytes 12582916
  126.5 1.1 copy-start.15
  127.6 3.7 %copy-start.14 = (bf16[1024,2048]{1,0:T(8,128)(2,1)S(1)}, bf16[1024,2048]{1,0:T(8,128)(2,1)}, u32[]{:S(2)}) copy-start(bf16[1024,2048]{1,0:T(8,128)(2,1)} %param.28) | copy-start | bytes 12582916
  133.7 17.5 %all-to-all-start.3 = ((bf16[4,256,512]{2,1,0:T(8,128)(2,1)}), bf16[4,256,512]{2,1,0:T(8,128)(2,1)S(1)}, u32[]{:S(2)}, u32[]{:S(2)}) async-start(bf16[4,256,512]{2,1,0:T(8,128)(2,1)} %bitcast.462), calls=%async_computation.3 | async-start | bytes 2097152 | tf_op jit(solution)/shard_map/all_to_all | solution.py:58

commit v6 on v4

--- a/solution.py
+++ b/solution.py
@@ -103,6 +103,10 @@
     gathered, companion = lax.optimization_barrier((gathered, companion))
     partner = lax.ppermute(gathered, "seq", shift_pairs(shape, 2, 1))
     return jnp.concatenate([gathered, partner], axis=2), companion
+
+
+def tensor_shift(parts, step):
+    return [(i, (i + step) % parts) for i in range(parts)]
 
 
 def per_device(
@@ -143,6 +147,24 @@
         2, head_count, seq_size * local_rows, HD
     )
 
+    core = device % 2
+    half_columns = out_weight.shape[1] // 2
+    weight_half = lax.dynamic_slice_in_dim(out_weight, core * half_columns, half_columns, 1)
+    weight_mine = jnp.concatenate(
+        [weight_half]
+        + [lax.ppermute(weight_half, "tensor", tensor_shift(parts, k)) for k in range(1, parts)],
+        axis=0,
+    )
+    weight_other = lax.ppermute(weight_mine, "seq", [(i, i ^ 1) for i in range(seq_size)])
+    residual_blocks = jnp.stack(
+        [residual]
+        + [lax.ppermute(residual, "tensor", tensor_shift(parts, k)) for k in range(1, parts)]
+    )
+    block_order = (lax.axis_index("tensor") - jnp.arange(parts)) % parts
+    residual_full = jnp.concatenate(
+        [residual_blocks[block_order[p]] for p in range(parts)], axis=1
+    )
+
     running = (
         jnp.full((head_count, row_count), NEGATIVE_FILL, jnp.float32),
         jnp.zeros((head_count, row_count), jnp.float32),
@@ -169,13 +191,20 @@
         .reshape(row_count, head_count * HD)
         .astype(jnp.bfloat16)
     )
-    projected = jnp.dot(attention, out_weight, preferred_element_type=jnp.float32)
     share_width = residual.shape[1]
     column = lax.axis_index("tensor") * share_width
-    mid_share = (
-        tensor_sum_scatter(projected, parts) + residual.astype(jnp.float32)
-    ).astype(jnp.bfloat16)
-    mid_full = tensor_gather(mid_share, parts)
+    attention_blocks = [attention] + [
+        lax.ppermute(attention, "tensor", tensor_shift(parts, k)) for k in range(1, parts)
+    ]
+    attention_all = jnp.concatenate(attention_blocks, axis=1)
+    mine = jnp.dot(attention_all, weight_mine, preferred_element_type=jnp.float32)
+    other = jnp.dot(attention_all, weight_other, preferred_element_type=jnp.float32)
+    first_core = core == 0
+    projected = jnp.concatenate(
+        [jnp.where(first_core, mine, other), jnp.where(first_core, other, mine)], axis=1
+    )
+    mid_full = (residual_full.astype(jnp.float32) + projected).astype(jnp.bfloat16)
+    mid_share = lax.dynamic_slice_in_dim(mid_full, column, share_width, 1)
     wide_mid = mid_full.astype(jnp.float32)
     row_mean = jnp.mean(wide_mid, axis=1, keepdims=True)
     row_var = jnp.mean(wide_mid * wide_mid, axis=1, keepdims=True) - row_mean * row_mean

time: 150 us -> 157 us (1.047); the launches traced: 150 us -> 154 us
  blocking collectives: 37.7 us -> 0 us
  starting transfers between devices: 32.8 us -> 56.7 us
  between operations: 0.49 us -> 7.97 us
  local copies, waits for them, and re-layouts: 20.4 us -> 27.7 us
  other arithmetic: 6.71 us -> 10.1 us
    all_to_all x2 -> x0, blocking collectives: 37.7 us -> none  [the longest x1 20.2 us: tensor_sum_scatter(): arrived = lax.all_to_all(pieces, 'tensor', 0, 0, tiled=True)]
    ppermute x0 -> x10, starting transfers between devices: none -> 23.3 us  [the longest x3 11.7 us: per_device(): lax.ppermute(residual, 'tensor', tensor_shift(parts, k))]
    ppermute x4, waiting for transfers between devices: 21.6 us -> 1.72 us  [ring_along(): from_below = lax.ppermute(from_below, 'seq', up)]
    ppermute x0 -> x10, waiting for transfers between devices: none -> 11.3 us  [the longest x3 9.5 us: per_device(): lax.ppermute(attention, 'tensor', tensor_shift(parts, k))]
    ppermute x4, waiting for transfers between devices: 0.01 us -> 9 us  [ring_along(): from_above = lax.ppermute(from_above, 'seq', down)]
    unnamed x36 -> x44, local copies, waits for them, and re-layouts: 9.63 us -> 13.2 us
    ppermute x2, waiting for transfers between devices: 2.98 us -> 0.52 us  [ring_along(): first = lax.ppermute(from_below[:, :, :half], 'seq', up)]
    concatenate x0 -> x1, other arithmetic: none -> 2.09 us  [per_device(): jnp.concatenate([weight_half] + [lax.ppermute(weight_half, 'tensor', tens...]
  transfers between devices with their start and end apart: 15 -> 25, of which waited for: 7 -> 10; matrix products, arithmetic and copies ran while one was open for 13% -> 24% of each run, Pallas kernels for 0% -> 0%
where the time goes in v6:
time: 157 us; the launch traced here: 154 us
  starting transfers between devices  56.7 us (36%)
  waiting for transfers between devices  37.9 us (24%)
  local copies, waits for them, and re-layouts  27.7 us (18%)
  matrix products  13.9 us (9%)
  other arithmetic  10.1 us (6%)
  between operations  7.97 us (5%)
    all_to_all x1, waiting for transfers between devices, tensor_sum_scatter(): arrived = lax.all_to_all(pieces, 'tensor', 0, 0, tiled=True)  14.4 us
    unnamed x44, local copies, waits for them, and re-layouts  13.2 us
    ppermute x3, starting transfers between devices, per_device(): lax.ppermute(residual, 'tensor', tensor_shift(parts, k))  11.7 us
    ppermute x4, starting transfers between devices, ring_along(): from_above = lax.ppermute(from_above, 'seq', down)  11.1 us
    ppermute x3, waiting for transfers between devices, per_device(): lax.ppermute(attention, 'tensor', tensor_shift(parts, k))  9.5 us
    all_to_all x1, starting transfers between devices, per_device(): arrived = lax.all_to_all(picked, 'seq', 0, 0, tiled=True)  9.2 us
    ppermute x4, waiting for transfers between devices, ring_along(): from_above = lax.ppermute(from_above, 'seq', down)  9 us
    ppermute x3, starting transfers between devices, per_device(): lax.ppermute(weight_half, 'tensor', tensor_shift(parts, k))  5.9 us
  transfers between devices with their start and end apart: 25, of which 10 were waited for; matrix products, arithmetic and copies ran while one was open for 24% of the time, Pallas kernels for 0%

profile of v6, /device:TPU:2, one launch (start us, length us, event | category | flops | bytes accessed | tf_op | source)
XLA Modules:
  0.0 154.3 jit_solution(6931884381484375772)
XLA Ops:
  0.0 1.0 bitcast_bitcast_fusion.12
  1.0 2.0 %collective-permute-start.3 = (bf16[2,4,32,128]{3,2,1,0:T(8,128)(2,1)S(1)}, bf16[2,4,32,128]{3,2,1,0:T(8,128)(2,1)S(1)}, u32[]{:S(2)}, u32[]{:S(2)}) collective-permute-start(bf16[2,4,32,128]{3,2,1,0:T(8,128)(2,1)S(1)} %bitcast_bitcast_fusion.12), channel_id=1, source_target_pairs={{0,32},{4,36},{8,40},{12,44},{16,48},{20,52},{24,56},{28,60},{32,6... | collective-permute-start | bytes 196616 | tf_op jit(solution)/shard_map/ppermute | solution.py:86
  3.0 4.0 %collective-permute-start.4 = (bf16[2,4,32,128]{3,2,1,0:T(8,128)(2,1)S(1)}, bf16[2,4,32,128]{3,2,1,0:T(8,128)(2,1)S(1)}, u32[]{:S(2)}, u32[]{:S(2)}) collective-permute-start(bf16[2,4,32,128]{3,2,1,0:T(8,128)(2,1)S(1)} %bitcast_bitcast_fusion.12), channel_id=1, source_target_pairs={{0,224},{4,228},{8,232},{12,236},{16,240},{20,244},{24,248},{28,25... | collective-permute-start | bytes 196616 | tf_op jit(solution)/shard_map/ppermute | solution.py:87
  7.0 1.5 constant_dynamic-update-slice_fusion.8
  9.9 1.0 copy.76
  10.9 1.0 gather_fusion
  12.0 3.2 %collective-permute-start.6 = (bf16[2,4,32,128]{3,2,1,0:T(8,128)(2,1)S(1)}, bf16[2,4,32,128]{3,2,1,0:T(8,128)(2,1)S(1)}, u32[]{:S(2)}, u32[]{:S(2)}) collective-permute-start(bf16[2,4,32,128]{3,2,1,0:T(8,128)(2,1)S(1)} %collective-permute-done.4), channel_id=1, source_target_pairs={{0,224},{4,228},{8,232},{12,236},{16,240},{20,244},{24,248},{28,25... | collective-permute-start | bytes 196616 | tf_op jit(solution)/shard_map/ppermute | solution.py:87
  16.6 0.9 collective-permute-done.5
  17.5 3.2 %collective-permute-start.8 = (bf16[2,4,32,128]{3,2,1,0:T(8,128)(2,1)S(1)}, bf16[2,4,32,128]{3,2,1,0:T(8,128)(2,1)S(1)}, u32[]{:S(2)}, u32[]{:S(2)}) collective-permute-start(bf16[2,4,32,128]{3,2,1,0:T(8,128)(2,1)S(1)} %collective-permute-done.6), channel_id=1, source_target_pairs={{0,224},{4,228},{8,232},{12,236},{16,240},{20,244},{24,248},{28,25... | collective-permute-start | bytes 196616 | tf_op jit(solution)/shard_map/ppermute | solution.py:87
  22.1 0.9 collective-permute-done.7
  23.0 3.2 %collective-permute-start.10 = (bf16[2,4,16,128]{3,2,1,0:T(8,128)(2,1)S(1)}, bf16[2,4,16,128]{3,2,1,0:T(8,128)(2,1)S(1)}, u32[]{:S(2)}, u32[]{:S(2)}) collective-permute-start(bf16[2,4,16,128]{3,2,1,0:T(8,128)(2,1)S(1)} %slice.95), channel_id=1, source_target_pairs={{0,224},{4,228},{8,232},{12,236},{16,240},{20,244},{24,248},{28,25... | collective-permute-start | bytes 98312 | tf_op jit(solution)/shard_map/ppermute | solution.py:92
  29.4 1.5 collective-permute-start.11
  31.2 1.0 reshape.282
  32.2 9.2 %all-to-all-start = ((bf16[64,2,4,4,128]{4,2,3,1,0:T(4,128)(2,1)}), bf16[64,2,4,4,128]{4,2,3,1,0:T(4,128)(2,1)}, u32[]{:S(2)}, u32[]{:S(2)}) async-start(bf16[64,2,4,4,128]{4,2,3,1,0:T(4,128)(2,1)} %bitcast.27), calls=%async_computation | async-start | bytes 1048576 | tf_op jit(solution)/shard_map/all_to_all | solution.py:143
  42.2 1.7 %collective-permute-start.19 = (bf16[512,1024]{1,0:T(8,128)(2,1)S(1)}, bf16[512,1024]{1,0:T(8,128)(2,1)}, u32[]{:S(2)}, u32[]{:S(2)}) collective-permute-start(bf16[512,1024]{1,0:T(8,128)(2,1)S(1)} %constant_dynamic-slice_fusion), channel_id=1, source_target_pairs={{0,1},{1,2},{2,3},{3,0},{4,5},{5,6},{6,7},{7,4},{8,9},{9,10},{10,1... | collective-permute-start | bytes 3145736 | tf_op jit(solution)/shard_map/ppermute | solution.py:155
  43.8 2.9 %collective-permute-start.20 = (bf16[512,1024]{1,0:T(8,128)(2,1)S(1)}, bf16[512,1024]{1,0:T(8,128)(2,1)}, u32[]{:S(2)}, u32[]{:S(2)}) collective-permute-start(bf16[512,1024]{1,0:T(8,128)(2,1)S(1)} %constant_dynamic-slice_fusion), channel_id=1, source_target_pairs={{0,2},{1,3},{2,0},{3,1},{4,6},{5,7},{6,4},{7,5},{8,10},{9,11},{10,... | collective-permute-start | bytes 3145736 | tf_op jit(solution)/shard_map/ppermute | solution.py:155
  46.7 1.3 collective-permute-start.21
  49.3 1.0 slice.96
  50.4 1.6 %collective-permute-start.13 = (bf16[2,4,128,128]{3,2,1,0:T(8,128)(2,1)S(1)}, bf16[2,4,128,128]{3,2,1,0:T(8,128)(2,1)S(1)}, u32[]{:S(2)}, u32[]{:S(2)}) collective-permute-start(bf16[2,4,128,128]{3,2,1,0:T(8,128)(2,1)S(1)} %slice.96), channel_id=1, source_target_pairs={{0,8},{4,12},{8,16},{12,20},{16,24},{20,28},{24,0},{28,4},{32,40},... | collective-permute-start | bytes 786440 | tf_op jit(solution)/shard_map/ppermute | solution.py:91
  51.9 9.0 %collective-permute-done.12 = bf16[2,4,256,128]{3,2,1,0:T(8,128)(2,1)} collective-permute-done((bf16[2,4,256,128]{3,2,1,0:T(8,128)(2,1)}, bf16[2,4,256,128]{3,2,1,0:T(8,128)(2,1)}, u32[]{:S(2)}, u32[]{:S(2)}) %collective-permute-start.12) | collective-permute-done | bytes 524320 | tf_op jit(solution)/shard_map/ppermute | solution.py:87
  60.9 1.0 slice.97
  62.4 2.0 %constant_dynamic-update-slice_fusion.12 = bf16[2,4,1024,128]{3,2,1,0:T(8,128)(2,1)} fusion(bf16[2,4,1024,128]{3,2,1,0:T(8,128)(2,1)} %get-tuple-element.49, bf16[2,4,256,128]{3,2,1,0:T(8,128)(2,1)} %collective-permute-done.11), kind=kLoop, calls=%fused_computation.163 | loop fusion | bytes 1048576
  64.4 1.9 %constant_dynamic-update-slice_fusion.11 = bf16[2,4,1024,128]{3,2,1,0:T(8,128)(2,1)} fusion(bf16[2,4,1024,128]{3,2,1,0:T(8,128)(2,1)} %constant_dynamic-update-slice_fusion.12, bf16[2,4,256,128]{3,2,1,0:T(8,128)(2,1)} %collective-permute-done.12), kind=kLoop, calls=%fused_computation.162 | loop fusion | bytes 1048576
  66.3 1.6 %collective-permute-start = (bf16[256,512]{1,0:T(8,128)(2,1)}, bf16[256,512]{1,0:T(8,128)(2,1)}, u32[]{:S(2)}, u32[]{:S(2)}) collective-permute-start(bf16[256,512]{1,0:T(8,128)(2,1)} %param.16), channel_id=1, source_target_pairs={{0,1},{1,2},{2,3},{3,0},{4,5},{5,6},{6,7},{7,4},{8,9},{9,10},{10,1... | collective-permute-start | bytes 786440 | tf_op jit(solution)/shard_map/ppermute | solution.py:161
  67.9 0.7 constant_dynamic-update-slice_fusion.10
  68.7 1.0 collective-permute-done.14
  69.7 0.8 constant_dynamic-update-slice_fusion.9
  79.4 1.4 fusion.125
  81.5 10.1 %collective-permute-start.1 = (bf16[256,512]{1,0:T(8,128)(2,1)}, bf16[256,512]{1,0:T(8,128)(2,1)S(1)}, u32[]{:S(2)}, u32[]{:S(2)}) collective-permute-start(bf16[256,512]{1,0:T(8,128)(2,1)} %param.16), channel_id=1, source_target_pairs={{0,2},{1,3},{2,0},{3,1},{4,6},{5,7},{6,4},{7,5},{8,10},{9,11},{10,... | collective-permute-start | bytes 786440 | tf_op jit(solution)/shard_map/ppermute | solution.py:161
  91.6 1.8 %collective-permute-done.20 = bf16[512,1024]{1,0:T(8,128)(2,1)} collective-permute-done((bf16[512,1024]{1,0:T(8,128)(2,1)S(1)}, bf16[512,1024]{1,0:T(8,128)(2,1)}, u32[]{:S(2)}, u32[]{:S(2)}) %collective-permute-start.20) | collective-permute-done | bytes 1048608 | tf_op jit(solution)/shard_map/ppermute | solution.py:155
  93.3 2.1 %pad_maximum_fusion = bf16[2048,1024]{1,0:T(8,128)(2,1)S(1)} fusion(bf16[512,1024]{1,0:T(8,128)(2,1)} %collective-permute-done.21, bf16[512,1024]{1,0:T(8,128)(2,1)} %collective-permute-done.20, bf16[512,1024]{1,0:T(8,128)(2,1)} %collective-permute-done.19, bf16[512,1024]{1,0:T(8,128)(2,1)S(1)} %constant_dynamic-slice_fusion), kind=kLoop, calls=%fused_computation.1 | loop fusion | flops 16777216 | bytes 8388608 | tf_op jit(solution)/shard_map/concatenate | solution.py:153
  95.8 1.9 %constant_dynamic-update-slice_fusion.22 = bf16[2,4,2048,128]{3,2,1,0:T(8,128)(2,1)S(1)} fusion(bf16[2,4,2048,128]{3,2,1,0:T(8,128)(2,1)S(1)} %constant_dynamic-update-slice_fusion.23, bf16[2,4,1024,128]{3,2,1,0:T(8,128)(2,1)} %collective-permute-done.15), kind=kLoop, calls=%fused_computation.173 | loop fusion | bytes 4194304 | tf_op jit(solution)/shard_map/concatenate | solution.py:105
  105.4 2.1 %collective-permute-start.16 = (bf16[256,512]{0,1:T(8,128)(2,1)S(1)}, bf16[256,512]{0,1:T(8,128)(2,1)S(1)}, u32[]{:S(2)}, u32[]{:S(2)}) collective-permute-start(bf16[256,512]{0,1:T(8,128)(2,1)S(1)} %bitcast.365), channel_id=1, source_target_pairs={{0,1},{1,2},{2,3},{3,0},{4,5},{5,6},{6,7},{7,4},{8,9},{9,10},{10,1... | collective-permute-start | bytes 786440 | tf_op jit(solution)/shard_map/ppermute | solution.py:197
  107.5 1.7 %collective-permute-start.17 = (bf16[256,512]{0,1:T(8,128)(2,1)S(1)}, bf16[256,512]{0,1:T(8,128)(2,1)S(1)}, u32[]{:S(2)}, u32[]{:S(2)}) collective-permute-start(bf16[256,512]{0,1:T(8,128)(2,1)S(1)} %bitcast.366), channel_id=1, source_target_pairs={{0,2},{1,3},{2,0},{3,1},{4,6},{5,7},{6,4},{7,5},{8,10},{9,11},{10,... | collective-permute-start | bytes 786440 | tf_op jit(solution)/shard_map/ppermute | solution.py:197
  109.3 1.6 %collective-permute-start.18 = (bf16[256,512]{0,1:T(8,128)(2,1)S(1)}, bf16[256,512]{0,1:T(8,128)(2,1)S(1)}, u32[]{:S(2)}, u32[]{:S(2)}) collective-permute-start(bf16[256,512]{0,1:T(8,128)(2,1)S(1)} %bitcast.367), channel_id=1, source_target_pairs={{0,3},{1,0},{2,1},{3,2},{4,7},{5,4},{6,5},{7,6},{8,11},{9,8},{10,9... | collective-permute-start | bytes 786440 | tf_op jit(solution)/shard_map/ppermute | solution.py:197
  110.8 1.2 pad_maximum_fusion.1
  112.1 3.3 %collective-permute-done.16 = bf16[256,512]{0,1:T(8,128)(2,1)S(1)} collective-permute-done((bf16[256,512]{0,1:T(8,128)(2,1)S(1)}, bf16[256,512]{0,1:T(8,128)(2,1)S(1)}, u32[]{:S(2)}, u32[]{:S(2)}) %collective-permute-start.16) | collective-permute-done | bytes 262176 | tf_op jit(solution)/shard_map/ppermute | solution.py:197
  115.4 6.2 %collective-permute-done.17 = bf16[256,512]{0,1:T(8,128)(2,1)S(1)} collective-permute-done((bf16[256,512]{0,1:T(8,128)(2,1)S(1)}, bf16[256,512]{0,1:T(8,128)(2,1)S(1)}, u32[]{:S(2)}, u32[]{:S(2)}) %collective-permute-start.17) | collective-permute-done | bytes 262176 | tf_op jit(solution)/shard_map/ppermute | solution.py:197
  121.6 1.3 fusion.91
  122.9 1.3 broadcast_select_fusion.2
  124.7 2.0 %copy-done.9 = bf16[2048,1024]{1,0:T(8,128)(2,1)S(1)} copy-done((bf16[2048,1024]{1,0:T(8,128)(2,1)S(1)}, bf16[2048,1024]{1,0:T(8,128)(2,1)}, u32[]{:S(2)}) %copy-start.9) | copy-done | bytes 4194328
  126.7 4.0 %fusion.37 = bf16[256,1024]{1,0:T(8,128)(2,1)S(1)} fusion(bf16[2048,1024]{1,0:T(8,128)(2,1)S(1)} %copy-done.9, bf16[256,2048]{1,0:T(8,128)(2,1)S(1)} %get-tuple-element.11, f32[2048]{0:T(1024)S(1)} %copy-done.12, f32[2048]{0:T(1024)S(1)} %copy-done.13, f32[256]{0:T(256)S(1)} %get-tuple-element.56, f32[256]{0:T(256)S(1)} %get-tuple-element.55, ...), kind=kOutput, calls=%fused_computation.67 | convolution fusion | flops 1094189056 | bytes 5789696 | tf_op jit(solution)/shard_map/dot_general | solution.py:214
  130.7 1.3 convolution_convert_fusion
  132.0 1.1 copy.171
  133.1 4.2 %all-to-all-start.1 = ((bf16[4,256,512]{2,1,0:T(8,128)(2,1)}), bf16[4,256,512]{2,1,0:T(8,128)(2,1)S(1)}, u32[]{:S(2)}, u32[]{:S(2)}) async-start(bf16[4,256,512]{2,1,0:T(8,128)(2,1)} %bitcast.357), calls=%async_computation.1 | async-start | bytes 2097152 | tf_op jit(solution)/shard_map/all_to_all | solution.py:58
  137.3 0.8 dynamic_slice.30
  138.0 14.4 %all-to-all-done.1 = bf16[4,256,512]{2,1,0:T(8,128)(2,1)S(1)} async-done(((bf16[4,256,512]{2,1,0:T(8,128)(2,1)}), bf16[4,256,512]{2,1,0:T(8,128)(2,1)S(1)}, u32[]{:S(2)}, u32[]{:S(2)}) %all-to-all-start.1) | async-done | bytes 1048608 | tf_op jit(solution)/shard_map/all_to_all | solution.py:58
  152.6 1.7 %add_convert_fusion = bf16[256,512]{1,0:T(8,128)(2,1)} fusion(f32[256,512]{1,0:T(8,128)S(1)} %convert_reduce_fusion.1, bf16[256,2048]{1,0:T(8,128)(2,1)} %copy-done.4, s32[]{:T(128)S(6)} %select_n.113, f32[512]{0:T(512)S(1)} %dynamic_slice.30), kind=kLoop, calls=%fused_computation.116 | loop fusion | flops 524288 | bytes 1050628 | tf_op jit(solution)/shard_map/convert_element_type | solution.py:221
  (106 shorter events, 21.0 us)
Async XLA Ops:
  0.0 42.1 %copy-start = (bf16[512,2048]{1,0:T(8,128)(2,1)S(1)}, bf16[512,2048]{1,0:T(8,128)(2,1)}, u32[]{:S(2)}) copy-start(bf16[512,2048]{1,0:T(8,128)(2,1)} %param.23) | copy-start | bytes 6291460
  1.0 10.9 %collective-permute-start.3 = (bf16[2,4,32,128]{3,2,1,0:T(8,128)(2,1)S(1)}, bf16[2,4,32,128]{3,2,1,0:T(8,128)(2,1)S(1)}, u32[]{:S(2)}, u32[]{:S(2)}) collective-permute-start(bf16[2,4,32,128]{3,2,1,0:T(8,128)(2,1)S(1)} %bitcast_bitcast_fusion.12), channel_id=1, source_target_pairs={{0,32},{4,36},{8,40},{12,44},{16,48},{20,52},{24,56},{28,60},{32,6... | collective-permute-start | bytes 196616 | tf_op jit(solution)/shard_map/ppermute | solution.py:86
  3.0 9.0 %collective-permute-start.4 = (bf16[2,4,32,128]{3,2,1,0:T(8,128)(2,1)S(1)}, bf16[2,4,32,128]{3,2,1,0:T(8,128)(2,1)S(1)}, u32[]{:S(2)}, u32[]{:S(2)}) collective-permute-start(bf16[2,4,32,128]{3,2,1,0:T(8,128)(2,1)S(1)} %bitcast_bitcast_fusion.12), channel_id=1, source_target_pairs={{0,224},{4,228},{8,232},{12,236},{16,240},{20,244},{24,248},{28,25... | collective-permute-start | bytes 196616 | tf_op jit(solution)/shard_map/ppermute | solution.py:87
  11.9 5.6 %collective-permute-start.5 = (bf16[2,4,32,128]{3,2,1,0:T(8,128)(2,1)S(1)}, bf16[2,4,32,128]{3,2,1,0:T(8,128)(2,1)S(1)}, u32[]{:S(2)}, u32[]{:S(2)}) collective-permute-start(bf16[2,4,32,128]{3,2,1,0:T(8,128)(2,1)S(1)} %collective-permute-done.3), channel_id=1, source_target_pairs={{0,32},{4,36},{8,40},{12,44},{16,48},{20,52},{24,56},{28,60},{32,6... | collective-permute-start | bytes 196616 | tf_op jit(solution)/shard_map/ppermute | solution.py:86
  12.0 5.5 %collective-permute-start.6 = (bf16[2,4,32,128]{3,2,1,0:T(8,128)(2,1)S(1)}, bf16[2,4,32,128]{3,2,1,0:T(8,128)(2,1)S(1)}, u32[]{:S(2)}, u32[]{:S(2)}) collective-permute-start(bf16[2,4,32,128]{3,2,1,0:T(8,128)(2,1)S(1)} %collective-permute-done.4), channel_id=1, source_target_pairs={{0,224},{4,228},{8,232},{12,236},{16,240},{20,244},{24,248},{28,25... | collective-permute-start | bytes 196616 | tf_op jit(solution)/shard_map/ppermute | solution.py:87
  17.5 5.5 %collective-permute-start.7 = (bf16[2,4,32,128]{3,2,1,0:T(8,128)(2,1)S(1)}, bf16[2,4,32,128]{3,2,1,0:T(8,128)(2,1)S(1)}, u32[]{:S(2)}, u32[]{:S(2)}) collective-permute-start(bf16[2,4,32,128]{3,2,1,0:T(8,128)(2,1)S(1)} %collective-permute-done.5), channel_id=1, source_target_pairs={{0,32},{4,36},{8,40},{12,44},{16,48},{20,52},{24,56},{28,60},{32,6... | collective-permute-start | bytes 196616 | tf_op jit(solution)/shard_map/ppermute | solution.py:86
  17.5 5.5 %collective-permute-start.8 = (bf16[2,4,32,128]{3,2,1,0:T(8,128)(2,1)S(1)}, bf16[2,4,32,128]{3,2,1,0:T(8,128)(2,1)S(1)}, u32[]{:S(2)}, u32[]{:S(2)}) collective-permute-start(bf16[2,4,32,128]{3,2,1,0:T(8,128)(2,1)S(1)} %collective-permute-done.6), channel_id=1, source_target_pairs={{0,224},{4,228},{8,232},{12,236},{16,240},{20,244},{24,248},{28,25... | collective-permute-start | bytes 196616 | tf_op jit(solution)/shard_map/ppermute | solution.py:87
  23.0 5.1 %collective-permute-start.9 = (bf16[2,4,16,128]{3,2,1,0:T(8,128)(2,1)S(1)}, bf16[2,4,16,128]{3,2,1,0:T(8,128)(2,1)S(1)}, u32[]{:S(2)}, u32[]{:S(2)}) collective-permute-start(bf16[2,4,16,128]{3,2,1,0:T(8,128)(2,1)S(1)} %slice.94), channel_id=1, source_target_pairs={{0,32},{4,36},{8,40},{12,44},{16,48},{20,52},{24,56},{28,60},{32,6... | collective-permute-start | bytes 98312 | tf_op jit(solution)/shard_map/ppermute | solution.py:91
  23.0 5.7 %collective-permute-start.10 = (bf16[2,4,16,128]{3,2,1,0:T(8,128)(2,1)S(1)}, bf16[2,4,16,128]{3,2,1,0:T(8,128)(2,1)S(1)}, u32[]{:S(2)}, u32[]{:S(2)}) collective-permute-start(bf16[2,4,16,128]{3,2,1,0:T(8,128)(2,1)S(1)} %slice.95), channel_id=1, source_target_pairs={{0,224},{4,228},{8,232},{12,236},{16,240},{20,244},{24,248},{28,25... | collective-permute-start | bytes 98312 | tf_op jit(solution)/shard_map/ppermute | solution.py:92
  29.4 19.9 %collective-permute-start.11 = (bf16[2,4,256,128]{3,2,1,0:T(8,128)(2,1)}, bf16[2,4,256,128]{3,2,1,0:T(8,128)(2,1)}, u32[]{:S(2)}, u32[]{:S(2)}) collective-permute-start(bf16[2,4,256,128]{3,2,1,0:T(8,128)(2,1)} %get-tuple-element.48), channel_id=1, source_target_pairs={{0,8},{4,12},{8,16},{12,20},{16,24},{20,28},{24,0},{28,4},{32,40},... | collective-permute-start | bytes 1572872 | tf_op jit(solution)/shard_map/ppermute | solution.py:86
  31.2 16.8 %copy-start.15 = (s32[64]{0:T(128)S(1)}, s32[64]{0:T(128)}, u32[]{:S(2)}) copy-start(s32[64]{0:T(128)} %param.31) | copy-start | bytes 772
  32.2 38.2 %all-to-all-start = ((bf16[64,2,4,4,128]{4,2,3,1,0:T(4,128)(2,1)}), bf16[64,2,4,4,128]{4,2,3,1,0:T(4,128)(2,1)}, u32[]{:S(2)}, u32[]{:S(2)}) async-start(bf16[64,2,4,4,128]{4,2,3,1,0:T(4,128)(2,1)} %bitcast.27), calls=%async_computation | async-start | bytes 1048576 | tf_op jit(solution)/shard_map/all_to_all | solution.py:143
  41.5 19.5 %collective-permute-start.12 = (bf16[2,4,256,128]{3,2,1,0:T(8,128)(2,1)}, bf16[2,4,256,128]{3,2,1,0:T(8,128)(2,1)}, u32[]{:S(2)}, u32[]{:S(2)}) collective-permute-start(bf16[2,4,256,128]{3,2,1,0:T(8,128)(2,1)} %get-tuple-element.48), channel_id=1, source_target_pairs={{0,24},{4,28},{8,0},{12,4},{16,8},{20,12},{24,16},{28,20},{32,56},... | collective-permute-start | bytes 1572872 | tf_op jit(solution)/shard_map/ppermute | solution.py:87
  42.2 39.4 %collective-permute-start.19 = (bf16[512,1024]{1,0:T(8,128)(2,1)S(1)}, bf16[512,1024]{1,0:T(8,128)(2,1)}, u32[]{:S(2)}, u32[]{:S(2)}) collective-permute-start(bf16[512,1024]{1,0:T(8,128)(2,1)S(1)} %constant_dynamic-slice_fusion), channel_id=1, source_target_pairs={{0,1},{1,2},{2,3},{3,0},{4,5},{5,6},{6,7},{7,4},{8,9},{9,10},{10,1... | collective-permute-start | bytes 3145736 | tf_op jit(solution)/shard_map/ppermute | solution.py:155
  43.8 49.5 %collective-permute-start.20 = (bf16[512,1024]{1,0:T(8,128)(2,1)S(1)}, bf16[512,1024]{1,0:T(8,128)(2,1)}, u32[]{:S(2)}, u32[]{:S(2)}) collective-permute-start(bf16[512,1024]{1,0:T(8,128)(2,1)S(1)} %constant_dynamic-slice_fusion), channel_id=1, source_target_pairs={{0,2},{1,3},{2,0},{3,1},{4,6},{5,7},{6,4},{7,5},{8,10},{9,11},{10,... | collective-permute-start | bytes 3145736 | tf_op jit(solution)/shard_map/ppermute | solution.py:155
  46.7 46.6 %collective-permute-start.21 = (bf16[512,1024]{1,0:T(8,128)(2,1)S(1)}, bf16[512,1024]{1,0:T(8,128)(2,1)}, u32[]{:S(2)}, u32[]{:S(2)}) collective-permute-start(bf16[512,1024]{1,0:T(8,128)(2,1)S(1)} %constant_dynamic-slice_fusion), channel_id=1, source_target_pairs={{0,3},{1,0},{2,1},{3,2},{4,7},{5,4},{6,5},{7,6},{8,11},{9,8},{10,9... | collective-permute-start | bytes 3145736 | tf_op jit(solution)/shard_map/ppermute | solution.py:155
  49.3 21.2 %copy-start.8 = (bf16[2,64,512]{2,1,0:T(8,128)(2,1)S(1)}, bf16[2,64,512]{2,1,0:T(8,128)(2,1)}, u32[]{:S(2)}) copy-start(bf16[2,64,512]{2,1,0:T(8,128)(2,1)} %param.20) | copy-start | bytes 393220
  50.3 20.2 %copy-start.2 = (bf16[256,512]{1,0:T(8,128)(2,1)S(1)}, bf16[256,512]{1,0:T(8,128)(2,1)}, u32[]{:S(2)}) copy-start(bf16[256,512]{1,0:T(8,128)(2,1)} %param.17) | copy-start | bytes 786436
  50.4 16.0 %collective-permute-start.13 = (bf16[2,4,128,128]{3,2,1,0:T(8,128)(2,1)S(1)}, bf16[2,4,128,128]{3,2,1,0:T(8,128)(2,1)S(1)}, u32[]{:S(2)}, u32[]{:S(2)}) collective-permute-start(bf16[2,4,128,128]{3,2,1,0:T(8,128)(2,1)S(1)} %slice.96), channel_id=1, source_target_pairs={{0,8},{4,12},{8,16},{12,20},{16,24},{20,28},{24,0},{28,4},{32,40},... | collective-permute-start | bytes 786440 | tf_op jit(solution)/shard_map/ppermute | solution.py:91
  61.9 14.6 %copy-start.7 = (bf16[256,512]{1,0:T(8,128)(2,1)S(1)}, bf16[256,512]{1,0:T(8,128)(2,1)}, u32[]{:S(2)}) copy-start(bf16[256,512]{1,0:T(8,128)(2,1)} %param.19) | copy-start | bytes 786436
  61.9 7.8 %collective-permute-start.14 = (bf16[2,4,128,128]{3,2,1,0:T(8,128)(2,1)S(1)}, bf16[2,4,128,128]{3,2,1,0:T(8,128)(2,1)S(1)}, u32[]{:S(2)}, u32[]{:S(2)}) collective-permute-start(bf16[2,4,128,128]{3,2,1,0:T(8,128)(2,1)S(1)} %slice.97), channel_id=1, source_target_pairs={{0,24},{4,28},{8,0},{12,4},{16,8},{20,12},{24,16},{28,20},{32,56},... | collective-permute-start | bytes 786440 | tf_op jit(solution)/shard_map/ppermute | solution.py:92
  62.4 16.7 %copy-start.11 = (bf16[256,512]{1,0:T(8,128)(2,1)S(1)}, bf16[256,512]{1,0:T(8,128)(2,1)}, u32[]{:S(2)}) copy-start(bf16[256,512]{1,0:T(8,128)(2,1)} %param.18) | copy-start | bytes 786436
  66.3 41.2 %collective-permute-start = (bf16[256,512]{1,0:T(8,128)(2,1)}, bf16[256,512]{1,0:T(8,128)(2,1)}, u32[]{:S(2)}, u32[]{:S(2)}) collective-permute-start(bf16[256,512]{1,0:T(8,128)(2,1)} %param.16), channel_id=1, source_target_pairs={{0,1},{1,2},{2,3},{3,0},{4,5},{5,6},{6,7},{7,4},{8,9},{9,10},{10,1... | collective-permute-start | bytes 786440 | tf_op jit(solution)/shard_map/ppermute | solution.py:161
  70.4 25.3 %collective-permute-start.15 = (bf16[2,4,1024,128]{3,2,1,0:T(8,128)(2,1)}, bf16[2,4,1024,128]{3,2,1,0:T(8,128)(2,1)}, u32[]{:S(2)}, u32[]{:S(2)}) collective-permute-start(bf16[2,4,1024,128]{3,2,1,0:T(8,128)(2,1)} %constant_dynamic-update-slice_fusion.9), channel_id=1, source_target_pairs={{0,4},{4,0},{8,12},{12,8},{16,20},{20,16},{24,28},{28,24},{32,36},... | collective-permute-start | bytes 6291464 | tf_op jit(solution)/shard_map/ppermute | solution.py:104
  70.6 5.2 %copy-start.5 = (bf16[2,4,64,128]{3,2,1,0:T(8,128)(2,1)}, bf16[2,4,64,128]{3,2,1,0:T(8,128)(2,1)S(1)}, u32[]{:S(2)}) copy-start(bf16[2,4,64,128]{3,2,1,0:T(8,128)(2,1)S(1)} %bitcast_bitcast_fusion.11) | copy-start | bytes 393220
  79.1 1.8 %copy-start.3 = (bf16[2,4,1024,128]{3,2,1,0:T(8,128)(2,1)S(1)}, bf16[2,4,1024,128]{3,2,1,0:T(8,128)(2,1)}, u32[]{:S(2)}) copy-start(bf16[2,4,1024,128]{3,2,1,0:T(8,128)(2,1)} %constant_dynamic-update-slice_fusion.9) | copy-start | bytes 6291460
  81.5 27.7 %collective-permute-start.1 = (bf16[256,512]{1,0:T(8,128)(2,1)}, bf16[256,512]{1,0:T(8,128)(2,1)S(1)}, u32[]{:S(2)}, u32[]{:S(2)}) collective-permute-start(bf16[256,512]{1,0:T(8,128)(2,1)} %param.16), channel_id=1, source_target_pairs={{0,2},{1,3},{2,0},{3,1},{4,6},{5,7},{6,4},{7,5},{8,10},{9,11},{10,... | collective-permute-start | bytes 786440 | tf_op jit(solution)/shard_map/ppermute | solution.py:161
  93.3 17.5 %collective-permute-start.2 = (bf16[256,512]{1,0:T(8,128)(2,1)}, bf16[256,512]{1,0:T(8,128)(2,1)S(1)}, u32[]{:S(2)}, u32[]{:S(2)}) collective-permute-start(bf16[256,512]{1,0:T(8,128)(2,1)} %param.16), channel_id=1, source_target_pairs={{0,3},{1,0},{2,1},{3,2},{4,7},{5,4},{6,5},{7,6},{8,11},{9,8},{10,9... | collective-permute-start | bytes 786440 | tf_op jit(solution)/shard_map/ppermute | solution.py:161
  95.4 26.2 %collective-permute-start.22 = (bf16[2048,1024]{1,0:T(8,128)(2,1)S(1)}, bf16[2048,1024]{1,0:T(8,128)(2,1)S(1)}, u32[]{:S(2)}, u32[]{:S(2)}) collective-permute-start(bf16[2048,1024]{1,0:T(8,128)(2,1)S(1)} %pad_maximum_fusion), channel_id=1, source_target_pairs={{0,4},{4,0},{8,12},{12,8},{16,20},{20,16},{24,28},{28,24},{32,36},... | collective-permute-start | bytes 12582920 | tf_op jit(solution)/shard_map/ppermute | solution.py:158
  101.9 0.9 copy-start.6
  105.4 10.0 %collective-permute-start.16 = (bf16[256,512]{0,1:T(8,128)(2,1)S(1)}, bf16[256,512]{0,1:T(8,128)(2,1)S(1)}, u32[]{:S(2)}, u32[]{:S(2)}) collective-permute-start(bf16[256,512]{0,1:T(8,128)(2,1)S(1)} %bitcast.365), channel_id=1, source_target_pairs={{0,1},{1,2},{2,3},{3,0},{4,5},{5,6},{6,7},{7,4},{8,9},{9,10},{10,1... | collective-permute-start | bytes 786440 | tf_op jit(solution)/shard_map/ppermute | solution.py:197
  107.5 14.0 %collective-permute-start.17 = (bf16[256,512]{0,1:T(8,128)(2,1)S(1)}, bf16[256,512]{0,1:T(8,128)(2,1)S(1)}, u32[]{:S(2)}, u32[]{:S(2)}) collective-permute-start(bf16[256,512]{0,1:T(8,128)(2,1)S(1)} %bitcast.366), channel_id=1, source_target_pairs={{0,2},{1,3},{2,0},{3,1},{4,6},{5,7},{6,4},{7,5},{8,10},{9,11},{10,... | collective-permute-start | bytes 786440 | tf_op jit(solution)/shard_map/ppermute | solution.py:197
  109.3 12.3 %collective-permute-start.18 = (bf16[256,512]{0,1:T(8,128)(2,1)S(1)}, bf16[256,512]{0,1:T(8,128)(2,1)S(1)}, u32[]{:S(2)}, u32[]{:S(2)}) collective-permute-start(bf16[256,512]{0,1:T(8,128)(2,1)S(1)} %bitcast.367), channel_id=1, source_target_pairs={{0,3},{1,0},{2,1},{3,2},{4,7},{5,4},{6,5},{7,6},{8,11},{9,8},{10,9... | collective-permute-start | bytes 786440 | tf_op jit(solution)/shard_map/ppermute | solution.py:197
  122.9 1.8 %copy-start.13 = (f32[2048]{0:T(1024)S(1)}, f32[2048]{0:T(1024)}, u32[]{:S(2)}) copy-start(f32[2048]{0:T(1024)} %param.24) | copy-start | bytes 24580
  124.2 2.6 %copy-start.9 = (bf16[2048,1024]{1,0:T(8,128)(2,1)S(1)}, bf16[2048,1024]{1,0:T(8,128)(2,1)}, u32[]{:S(2)}) copy-start(bf16[2048,1024]{1,0:T(8,128)(2,1)} %param.26) | copy-start | bytes 12582916
  124.2 2.6 %copy-start.12 = (f32[2048]{0:T(1024)S(1)}, f32[2048]{0:T(1024)}, u32[]{:S(2)}) copy-start(f32[2048]{0:T(1024)} %param.25) | copy-start | bytes 24580
  124.2 2.6 %copy-start.14 = (f32[1024]{0:T(1024)S(1)}, f32[1024]{0:T(1024)}, u32[]{:S(2)}) copy-start(f32[1024]{0:T(1024)} %param.27) | copy-start | bytes 12292
  124.7 6.0 %copy-start.4 = (bf16[256,2048]{1,0:T(8,128)(2,1)}, bf16[256,2048]{1,0:T(8,128)(2,1)S(1)}, u32[]{:S(2)}) copy-start(bf16[256,2048]{1,0:T(8,128)(2,1)S(1)} %get-tuple-element.11) | copy-start | bytes 3145732
  126.7 4.0 %copy-start.10 = (bf16[1024,2048]{1,0:T(8,128)(2,1)S(1)}, bf16[1024,2048]{1,0:T(8,128)(2,1)}, u32[]{:S(2)}) copy-start(bf16[1024,2048]{1,0:T(8,128)(2,1)} %param.28) | copy-start | bytes 12582916
  133.1 21.2 %copy-start.1 = (bf16[512,2048]{1,0:T(8,128)(2,1)S(1)}, bf16[512,2048]{1,0:T(8,128)(2,1)}, u32[]{:S(2)}) copy-start(bf16[512,2048]{1,0:T(8,128)(2,1)} %param.23) | copy-start | bytes 6291460
  133.1 19.3 %all-to-all-start.1 = ((bf16[4,256,512]{2,1,0:T(8,128)(2,1)}), bf16[4,256,512]{2,1,0:T(8,128)(2,1)S(1)}, u32[]{:S(2)}, u32[]{:S(2)}) async-start(bf16[4,256,512]{2,1,0:T(8,128)(2,1)} %bitcast.357), calls=%async_computation.1 | async-start | bytes 2097152 | tf_op jit(solution)/shard_map/all_to_all | solution.py:58

commit v7 on v4

--- a/solution.py
+++ b/solution.py
@@ -8,7 +8,7 @@
 
 NEGATIVE_FILL = -1e30
 NORM_EPSILON = 1e-05
-BLOCK_KEYS = 512
+BLOCK_KEYS = 2048
 
 
 def attend(running, query_heads, key_heads, value_heads, allowed):

time: 150 us -> 149 us (level)
    dot_general x7 -> x4, matrix products: 3.72 us -> 3.17 us  [attend(): jnp.einsum('hqd,hkd->hqk', query_heads, key_heads, preferred_element_type...]
    dot_general x7 -> x4, matrix products: 3.35 us -> 2.86 us  [attend(): jnp.einsum('hqk,hkd->hqd', weights.astype(jnp.bfloat16), value_heads, pre...]
  transfers between devices with their start and end apart: 15 -> 15, of which waited for: 7 -> 7; matrix products, arithmetic and copies ran while one was open for 13% -> 14% of each run, Pallas kernels for 0% -> 0%
where the time goes in v7:
time: 149 us; the launch traced here: 148 us
  waiting for transfers between devices  38.8 us (26%)
  blocking collectives  37.7 us (25%)
  starting transfers between devices  32.8 us (22%)
  local copies, waits for them, and re-layouts  20.1 us (13%)
  matrix products  11.7 us (8%)
  other arithmetic  6.66 us (4%)
    ppermute x4, waiting for transfers between devices, ring_along(): from_below = lax.ppermute(from_below, 'seq', up)  21.6 us
    all_to_all x1, blocking collectives, tensor_sum_scatter(): arrived = lax.all_to_all(pieces, 'tensor', 0, 0, tiled=True)  20.2 us
    all_to_all x1, blocking collectives, tensor_gather(): arrived = lax.all_to_all(copies, 'tensor', 0, 0, tiled=True)  17.6 us
    all_to_all x1, waiting for transfers between devices, tensor_sum_scatter(): arrived = lax.all_to_all(pieces, 'tensor', 0, 0, tiled=True)  13.2 us
    unnamed x36, local copies, waits for them, and re-layouts  9.68 us
    ppermute x4, starting transfers between devices, ring_along(): from_above = lax.ppermute(from_above, 'seq', down)  9.52 us
    all_to_all x1, starting transfers between devices, per_device(): arrived = lax.all_to_all(picked, 'seq', 0, 0, tiled=True)  9.31 us
    ppermute x4, starting transfers between devices, ring_along(): from_below = lax.ppermute(from_below, 'seq', up)  5.01 us
  transfers between devices with their start and end apart: 15, of which 7 were waited for; matrix products, arithmetic and copies ran while one was open for 14% of the time, Pallas kernels for 0%

profile of v7, /device:TPU:2, one launch (start us, length us, event | category | flops | bytes accessed | tf_op | source)
XLA Modules:
  0.0 148.2 jit_solution(8583104174836650539)
XLA Ops:
  0.0 1.0 bitcast_bitcast_fusion.10
  1.0 2.0 %collective-permute-start = (bf16[2,4,32,128]{3,2,1,0:T(8,128)(2,1)S(1)}, bf16[2,4,32,128]{3,2,1,0:T(8,128)(2,1)S(1)}, u32[]{:S(2)}, u32[]{:S(2)}) collective-permute-start(bf16[2,4,32,128]{3,2,1,0:T(8,128)(2,1)S(1)} %bitcast_bitcast_fusion.10), channel_id=1, source_target_pairs={{0,32},{4,36},{8,40},{12,44},{16,48},{20,52},{24,56},{28,60},{32,6... | collective-permute-start | bytes 196616 | tf_op jit(solution)/shard_map/ppermute | solution.py:86
  3.0 4.0 %collective-permute-start.1 = (bf16[2,4,32,128]{3,2,1,0:T(8,128)(2,1)S(1)}, bf16[2,4,32,128]{3,2,1,0:T(8,128)(2,1)S(1)}, u32[]{:S(2)}, u32[]{:S(2)}) collective-permute-start(bf16[2,4,32,128]{3,2,1,0:T(8,128)(2,1)S(1)} %bitcast_bitcast_fusion.10), channel_id=1, source_target_pairs={{0,224},{4,228},{8,232},{12,236},{16,240},{20,244},{24,248},{28,25... | collective-permute-start | bytes 196616 | tf_op jit(solution)/shard_map/ppermute | solution.py:87
  7.0 0.7 compare_select_fusion
  7.7 0.7 compare_and_fusion
  8.3 1.0 copy.60
  9.4 1.0 gather_fusion
  10.7 1.0 reshape.192
  11.7 9.3 %all-to-all-start = ((bf16[64,2,4,4,128]{4,2,3,1,0:T(4,128)(2,1)}), bf16[64,2,4,4,128]{4,2,3,1,0:T(4,128)(2,1)S(1)}, u32[]{:S(2)}, u32[]{:S(2)}) async-start(bf16[64,2,4,4,128]{4,2,3,1,0:T(4,128)(2,1)} %bitcast.15), calls=%async_computation | async-start | bytes 1048576 | tf_op jit(solution)/shard_map/all_to_all | solution.py:139
  21.1 0.7 constant_dynamic-update-slice_fusion.8
  21.7 1.5 collective-permute-start.2
  23.2 1.8 %collective-permute-start.3 = (bf16[2,4,32,128]{3,2,1,0:T(8,128)(2,1)S(1)}, bf16[2,4,32,128]{3,2,1,0:T(8,128)(2,1)S(1)}, u32[]{:S(2)}, u32[]{:S(2)}) collective-permute-start(bf16[2,4,32,128]{3,2,1,0:T(8,128)(2,1)S(1)} %collective-permute-done.1), channel_id=1, source_target_pairs={{0,224},{4,228},{8,232},{12,236},{16,240},{20,244},{24,248},{28,25... | collective-permute-start | bytes 196616 | tf_op jit(solution)/shard_map/ppermute | solution.py:87
  25.0 0.7 constant_dynamic-update-slice_fusion.7
  25.7 0.7 constant_dynamic-update-slice_fusion.6
  26.3 10.8 %collective-permute-done.2 = bf16[2,4,32,128]{3,2,1,0:T(8,128)(2,1)S(1)} collective-permute-done((bf16[2,4,32,128]{3,2,1,0:T(8,128)(2,1)S(1)}, bf16[2,4,32,128]{3,2,1,0:T(8,128)(2,1)S(1)}, u32[]{:S(2)}, u32[]{:S(2)}) %collective-permute-start.2) | collective-permute-done | bytes 65568 | tf_op jit(solution)/shard_map/ppermute | solution.py:86
  37.1 3.2 %collective-permute-start.5 = (bf16[2,4,32,128]{3,2,1,0:T(8,128)(2,1)S(1)}, bf16[2,4,32,128]{3,2,1,0:T(8,128)(2,1)S(1)}, u32[]{:S(2)}, u32[]{:S(2)}) collective-permute-start(bf16[2,4,32,128]{3,2,1,0:T(8,128)(2,1)S(1)} %collective-permute-done.3), channel_id=1, source_target_pairs={{0,224},{4,228},{8,232},{12,236},{16,240},{20,244},{24,248},{28,25... | collective-permute-start | bytes 196616 | tf_op jit(solution)/shard_map/ppermute | solution.py:87
  40.4 0.7 constant_dynamic-update-slice_fusion.5
  41.1 0.7 constant_dynamic-update-slice_fusion.4
  41.7 0.9 collective-permute-done.4
  42.6 3.2 %collective-permute-start.7 = (bf16[2,4,16,128]{3,2,1,0:T(8,128)(2,1)S(1)}, bf16[2,4,16,128]{3,2,1,0:T(8,128)(2,1)S(1)}, u32[]{:S(2)}, u32[]{:S(2)}) collective-permute-start(bf16[2,4,16,128]{3,2,1,0:T(8,128)(2,1)S(1)} %slice.47), channel_id=1, source_target_pairs={{0,224},{4,228},{8,232},{12,236},{16,240},{20,244},{24,248},{28,25... | collective-permute-start | bytes 98312 | tf_op jit(solution)/shard_map/ppermute | solution.py:92
  45.9 0.7 constant_dynamic-update-slice_fusion.3
  46.5 0.7 constant_dynamic-update-slice_fusion.2
  49.0 1.5 %collective-permute-start.8 = (bf16[2,4,256,128]{3,2,1,0:T(8,128)(2,1)S(1)}, bf16[2,4,256,128]{3,2,1,0:T(8,128)(2,1)S(1)}, u32[]{:S(2)}, u32[]{:S(2)}) collective-permute-start(bf16[2,4,256,128]{3,2,1,0:T(8,128)(2,1)S(1)} %get-tuple-element.33), channel_id=1, source_target_pairs={{0,8},{4,12},{8,16},{12,20},{16,24},{20,28},{24,0},{28,4},{32,40},... | collective-permute-start | bytes 1572872 | tf_op jit(solution)/shard_map/ppermute | solution.py:86
  51.0 9.9 %collective-permute-done.8 = bf16[2,4,256,128]{3,2,1,0:T(8,128)(2,1)S(1)} collective-permute-done((bf16[2,4,256,128]{3,2,1,0:T(8,128)(2,1)S(1)}, bf16[2,4,256,128]{3,2,1,0:T(8,128)(2,1)S(1)}, u32[]{:S(2)}, u32[]{:S(2)}) %collective-permute-start.8) | collective-permute-done | bytes 524320 | tf_op jit(solution)/shard_map/ppermute | solution.py:86
  61.0 1.7 %collective-permute-start.10 = (bf16[2,4,128,128]{3,2,1,0:T(8,128)(2,1)S(1)}, bf16[2,4,128,128]{3,2,1,0:T(8,128)(2,1)S(1)}, u32[]{:S(2)}, u32[]{:S(2)}) collective-permute-start(bf16[2,4,128,128]{3,2,1,0:T(8,128)(2,1)S(1)} %slice.48), channel_id=1, source_target_pairs={{0,8},{4,12},{8,16},{12,20},{16,24},{20,28},{24,0},{28,4},{32,40},... | collective-permute-start | bytes 786440 | tf_op jit(solution)/shard_map/ppermute | solution.py:91
  63.2 0.9 constant_dynamic-update-slice_fusion.12
  64.1 0.9 constant_dynamic-update-slice_fusion.11
  65.0 2.4 %collective-permute-done.10 = bf16[2,4,128,128]{3,2,1,0:T(8,128)(2,1)S(1)} collective-permute-done((bf16[2,4,128,128]{3,2,1,0:T(8,128)(2,1)S(1)}, bf16[2,4,128,128]{3,2,1,0:T(8,128)(2,1)S(1)}, u32[]{:S(2)}, u32[]{:S(2)}) %collective-permute-start.10) | collective-permute-done | bytes 262176 | tf_op jit(solution)/shard_map/ppermute | solution.py:91
  67.4 0.7 constant_dynamic-update-slice_fusion.10
  68.2 1.0 collective-permute-done.11
  69.1 0.8 constant_dynamic-update-slice_fusion.9
  71.7 1.3 fusion.79
  73.2 1.7 %constant_dynamic-update-slice_fusion.23 = bf16[2,4,2048,128]{3,2,1,0:T(8,128)(2,1)S(1)} fusion(bf16[2,4,1024,128]{3,2,1,0:T(8,128)(2,1)} %constant_dynamic-update-slice_fusion.9), kind=kLoop, calls=%fused_computation.117 | loop fusion | bytes 4194304
  75.4 1.9 %constant_dynamic-update-slice_fusion.22 = bf16[2,4,2048,128]{3,2,1,0:T(8,128)(2,1)S(1)} fusion(bf16[2,4,2048,128]{3,2,1,0:T(8,128)(2,1)S(1)} %constant_dynamic-update-slice_fusion.23, bf16[2,4,1024,128]{3,2,1,0:T(8,128)(2,1)} %collective-permute-done.12), kind=kLoop, calls=%fused_computation.116 | loop fusion | bytes 4194304 | tf_op jit(solution)/shard_map/concatenate | solution.py:105
  77.3 1.3 bitcast_reduce_fusion
  79.4 1.4 fusion.1
  81.7 1.8 %fusion.39 = bf16[256,4,128]{0,2,1:T(8,128)(2,1)S(1)} fusion(f32[256,4,128]{0,2,1:T(8,128)S(1)} %fusion.17, bf16[2,4,2048,128]{3,2,1,0:T(8,128)(2,1)S(1)} %constant_dynamic-update-slice_fusion.22, f32[4,2048,256]{2,1,0:T(8,128)S(1)} %get-tuple-element.43, f32[4,256]{1,0:T(4,128)S(1)} %get-tuple-element.14, f32[256,4]{0,1:T(4,128)S(1)} %get-tuple-element.11), kind=kOutput, calls=%fused_computation.64 | convolution fusion | flops 543555584 | bytes 11280384 | tf_op jit(solution)/shard_map/hqk,hkd->hqd/dot_general | solution.py:24
  83.5 0.7 convolution_convert_fusion
  84.4 20.2 %all_to_all.20 = bf16[4,256,512]{2,1,0:T(8,128)(2,1)S(1)} all-to-all(bf16[4,256,512]{2,1,0:T(8,128)(2,1)S(1)} %bitcast.261), channel_id=1, replica_groups=mesh['seq'=64,'tensor'=4] {'tensor'}, dimensions={0} | all-to-all | bytes 2097152 | tf_op jit(solution)/shard_map/all_to_all | solution.py:58
  105.0 17.6 %all_to_all.21 = bf16[4,256,512]{1,2,0:T(8,128)(2,1)S(1)} all-to-all(bf16[4,256,512]{1,2,0:T(8,128)(2,1)S(1)} %broadcast_in_dim.82), channel_id=1, replica_groups=mesh['seq'=64,'tensor'=4] {'tensor'}, dimensions={0} | all-to-all | bytes 2097152 | tf_op jit(solution)/shard_map/all_to_all | solution.py:65
  123.0 0.7 fusion.11
  123.7 3.7 %fusion.28 = bf16[256,1024]{1,0:T(8,128)(2,1)S(1)} fusion(bf16[256,2048]{0,1:T(8,128)(2,1)S(1)} %fusion.11, bf16[2048,1024]{1,0:T(8,128)(2,1)S(1)} %copy-done.8, f32[1024]{0:T(1024)S(1)} %copy-done.10), kind=kOutput, calls=%fused_computation.42 | convolution fusion | flops 1091043328 | bytes 5771264 | tf_op jit(solution)/shard_map/dot_general | solution.py:185
  127.4 1.3 convolution_convert_fusion.1
  128.7 1.1 copy.129
  129.8 3.5 %all-to-all-start.3 = ((bf16[4,256,512]{2,1,0:T(8,128)(2,1)}), bf16[4,256,512]{2,1,0:T(8,128)(2,1)S(1)}, u32[]{:S(2)}, u32[]{:S(2)}) async-start(bf16[4,256,512]{2,1,0:T(8,128)(2,1)} %bitcast.259), calls=%async_computation.3 | async-start | bytes 2097152 | tf_op jit(solution)/shard_map/all_to_all | solution.py:58
  133.3 0.8 dynamic_slice.7
  134.1 13.2 %all-to-all-done.3 = bf16[4,256,512]{2,1,0:T(8,128)(2,1)S(1)} async-done(((bf16[4,256,512]{2,1,0:T(8,128)(2,1)}), bf16[4,256,512]{2,1,0:T(8,128)(2,1)S(1)}, u32[]{:S(2)}, u32[]{:S(2)}) %all-to-all-start.3) | async-done | bytes 1048608 | tf_op jit(solution)/shard_map/all_to_all | solution.py:58
  147.4 0.8 add_convert_fusion
  (71 shorter events, 8.4 us)
Async XLA Ops:
  0.0 83.5 %copy-start = (bf16[512,2048]{1,0:T(8,128)(2,1)S(1)}, bf16[512,2048]{1,0:T(8,128)(2,1)}, u32[]{:S(2)}) copy-start(bf16[512,2048]{1,0:T(8,128)(2,1)} %param.23) | copy-start | bytes 6291460
  1.0 20.7 %collective-permute-start = (bf16[2,4,32,128]{3,2,1,0:T(8,128)(2,1)S(1)}, bf16[2,4,32,128]{3,2,1,0:T(8,128)(2,1)S(1)}, u32[]{:S(2)}, u32[]{:S(2)}) collective-permute-start(bf16[2,4,32,128]{3,2,1,0:T(8,128)(2,1)S(1)} %bitcast_bitcast_fusion.10), channel_id=1, source_target_pairs={{0,32},{4,36},{8,40},{12,44},{16,48},{20,52},{24,56},{28,60},{32,6... | collective-permute-start | bytes 196616 | tf_op jit(solution)/shard_map/ppermute | solution.py:86
  3.0 20.2 %collective-permute-start.1 = (bf16[2,4,32,128]{3,2,1,0:T(8,128)(2,1)S(1)}, bf16[2,4,32,128]{3,2,1,0:T(8,128)(2,1)S(1)}, u32[]{:S(2)}, u32[]{:S(2)}) collective-permute-start(bf16[2,4,32,128]{3,2,1,0:T(8,128)(2,1)S(1)} %bitcast_bitcast_fusion.10), channel_id=1, source_target_pairs={{0,224},{4,228},{8,232},{12,236},{16,240},{20,244},{24,248},{28,25... | collective-permute-start | bytes 196616 | tf_op jit(solution)/shard_map/ppermute | solution.py:87
  9.4 11.7 %copy-start.2 = (bf16[2,32,512]{2,1,0:T(8,128)(2,1)S(1)}, bf16[2,32,512]{2,1,0:T(8,128)(2,1)}, u32[]{:S(2)}) copy-start(bf16[2,32,512]{2,1,0:T(8,128)(2,1)} %param.22) | copy-start | bytes 196612
  11.7 58.1 %all-to-all-start = ((bf16[64,2,4,4,128]{4,2,3,1,0:T(4,128)(2,1)}), bf16[64,2,4,4,128]{4,2,3,1,0:T(4,128)(2,1)S(1)}, u32[]{:S(2)}, u32[]{:S(2)}) async-start(bf16[64,2,4,4,128]{4,2,3,1,0:T(4,128)(2,1)} %bitcast.15), calls=%async_computation | async-start | bytes 1048576 | tf_op jit(solution)/shard_map/all_to_all | solution.py:139
  21.7 15.4 %collective-permute-start.2 = (bf16[2,4,32,128]{3,2,1,0:T(8,128)(2,1)S(1)}, bf16[2,4,32,128]{3,2,1,0:T(8,128)(2,1)S(1)}, u32[]{:S(2)}, u32[]{:S(2)}) collective-permute-start(bf16[2,4,32,128]{3,2,1,0:T(8,128)(2,1)S(1)} %collective-permute-done), channel_id=1, source_target_pairs={{0,32},{4,36},{8,40},{12,44},{16,48},{20,52},{24,56},{28,60},{32,6... | collective-permute-start | bytes 196616 | tf_op jit(solution)/shard_map/ppermute | solution.py:86
  23.2 13.9 %collective-permute-start.3 = (bf16[2,4,32,128]{3,2,1,0:T(8,128)(2,1)S(1)}, bf16[2,4,32,128]{3,2,1,0:T(8,128)(2,1)S(1)}, u32[]{:S(2)}, u32[]{:S(2)}) collective-permute-start(bf16[2,4,32,128]{3,2,1,0:T(8,128)(2,1)S(1)} %collective-permute-done.1), channel_id=1, source_target_pairs={{0,224},{4,228},{8,232},{12,236},{16,240},{20,244},{24,248},{28,25... | collective-permute-start | bytes 196616 | tf_op jit(solution)/shard_map/ppermute | solution.py:87
  37.1 5.5 %collective-permute-start.4 = (bf16[2,4,32,128]{3,2,1,0:T(8,128)(2,1)S(1)}, bf16[2,4,32,128]{3,2,1,0:T(8,128)(2,1)S(1)}, u32[]{:S(2)}, u32[]{:S(2)}) collective-permute-start(bf16[2,4,32,128]{3,2,1,0:T(8,128)(2,1)S(1)} %collective-permute-done.2), channel_id=1, source_target_pairs={{0,32},{4,36},{8,40},{12,44},{16,48},{20,52},{24,56},{28,60},{32,6... | collective-permute-start | bytes 196616 | tf_op jit(solution)/shard_map/ppermute | solution.py:86
  37.1 5.5 %collective-permute-start.5 = (bf16[2,4,32,128]{3,2,1,0:T(8,128)(2,1)S(1)}, bf16[2,4,32,128]{3,2,1,0:T(8,128)(2,1)S(1)}, u32[]{:S(2)}, u32[]{:S(2)}) collective-permute-start(bf16[2,4,32,128]{3,2,1,0:T(8,128)(2,1)S(1)} %collective-permute-done.3), channel_id=1, source_target_pairs={{0,224},{4,228},{8,232},{12,236},{16,240},{20,244},{24,248},{28,25... | collective-permute-start | bytes 196616 | tf_op jit(solution)/shard_map/ppermute | solution.py:87
  42.6 5.1 %collective-permute-start.6 = (bf16[2,4,16,128]{3,2,1,0:T(8,128)(2,1)S(1)}, bf16[2,4,16,128]{3,2,1,0:T(8,128)(2,1)S(1)}, u32[]{:S(2)}, u32[]{:S(2)}) collective-permute-start(bf16[2,4,16,128]{3,2,1,0:T(8,128)(2,1)S(1)} %slice.46), channel_id=1, source_target_pairs={{0,32},{4,36},{8,40},{12,44},{16,48},{20,52},{24,56},{28,60},{32,6... | collective-permute-start | bytes 98312 | tf_op jit(solution)/shard_map/ppermute | solution.py:91
  42.6 5.7 %collective-permute-start.7 = (bf16[2,4,16,128]{3,2,1,0:T(8,128)(2,1)S(1)}, bf16[2,4,16,128]{3,2,1,0:T(8,128)(2,1)S(1)}, u32[]{:S(2)}, u32[]{:S(2)}) collective-permute-start(bf16[2,4,16,128]{3,2,1,0:T(8,128)(2,1)S(1)} %slice.47), channel_id=1, source_target_pairs={{0,224},{4,228},{8,232},{12,236},{16,240},{20,244},{24,248},{28,25... | collective-permute-start | bytes 98312 | tf_op jit(solution)/shard_map/ppermute | solution.py:92
  49.0 20.9 %copy-start.3 = (bf16[256,512]{1,0:T(8,128)(2,1)S(1)}, bf16[256,512]{1,0:T(8,128)(2,1)}, u32[]{:S(2)}) copy-start(bf16[256,512]{1,0:T(8,128)(2,1)} %param.19) | copy-start | bytes 786436
  49.0 11.9 %collective-permute-start.8 = (bf16[2,4,256,128]{3,2,1,0:T(8,128)(2,1)S(1)}, bf16[2,4,256,128]{3,2,1,0:T(8,128)(2,1)S(1)}, u32[]{:S(2)}, u32[]{:S(2)}) collective-permute-start(bf16[2,4,256,128]{3,2,1,0:T(8,128)(2,1)S(1)} %get-tuple-element.33), channel_id=1, source_target_pairs={{0,8},{4,12},{8,16},{12,20},{16,24},{20,28},{24,0},{28,4},{32,40},... | collective-permute-start | bytes 1572872 | tf_op jit(solution)/shard_map/ppermute | solution.py:86
  50.5 12.1 %collective-permute-start.9 = (bf16[2,4,256,128]{3,2,1,0:T(8,128)(2,1)S(1)}, bf16[2,4,256,128]{3,2,1,0:T(8,128)(2,1)S(1)}, u32[]{:S(2)}, u32[]{:S(2)}) collective-permute-start(bf16[2,4,256,128]{3,2,1,0:T(8,128)(2,1)S(1)} %get-tuple-element.33), channel_id=1, source_target_pairs={{0,24},{4,28},{8,0},{12,4},{16,8},{20,12},{24,16},{28,20},{32,56},... | collective-permute-start | bytes 1572872 | tf_op jit(solution)/shard_map/ppermute | solution.py:87
  60.9 9.1 %copy-start.11 = (s32[64]{0:T(128)S(1)}, s32[64]{0:T(128)}, u32[]{:S(2)}) copy-start(s32[64]{0:T(128)} %param.31) | copy-start | bytes 772
  61.0 10.4 %copy-start.5 = (bf16[2,64,512]{2,1,0:T(8,128)(2,1)S(1)}, bf16[2,64,512]{2,1,0:T(8,128)(2,1)}, u32[]{:S(2)}) copy-start(bf16[2,64,512]{2,1,0:T(8,128)(2,1)} %param.20) | copy-start | bytes 393220
  61.0 6.4 %collective-permute-start.10 = (bf16[2,4,128,128]{3,2,1,0:T(8,128)(2,1)S(1)}, bf16[2,4,128,128]{3,2,1,0:T(8,128)(2,1)S(1)}, u32[]{:S(2)}, u32[]{:S(2)}) collective-permute-start(bf16[2,4,128,128]{3,2,1,0:T(8,128)(2,1)S(1)} %slice.48), channel_id=1, source_target_pairs={{0,8},{4,12},{8,16},{12,20},{16,24},{20,28},{24,0},{28,4},{32,40},... | collective-permute-start | bytes 786440 | tf_op jit(solution)/shard_map/ppermute | solution.py:91
  62.6 8.8 %copy-start.1 = (bf16[256,512]{1,0:T(8,128)(2,1)S(1)}, bf16[256,512]{1,0:T(8,128)(2,1)}, u32[]{:S(2)}) copy-start(bf16[256,512]{1,0:T(8,128)(2,1)} %param.17) | copy-start | bytes 786436
  62.7 6.4 %collective-permute-start.11 = (bf16[2,4,128,128]{3,2,1,0:T(8,128)(2,1)S(1)}, bf16[2,4,128,128]{3,2,1,0:T(8,128)(2,1)S(1)}, u32[]{:S(2)}, u32[]{:S(2)}) collective-permute-start(bf16[2,4,128,128]{3,2,1,0:T(8,128)(2,1)S(1)} %slice.49), channel_id=1, source_target_pairs={{0,24},{4,28},{8,0},{12,4},{16,8},{20,12},{24,16},{28,20},{32,56},... | collective-permute-start | bytes 786440 | tf_op jit(solution)/shard_map/ppermute | solution.py:92
  69.9 5.5 %collective-permute-start.12 = (bf16[2,4,1024,128]{3,2,1,0:T(8,128)(2,1)}, bf16[2,4,1024,128]{3,2,1,0:T(8,128)(2,1)}, u32[]{:S(2)}, u32[]{:S(2)}) collective-permute-start(bf16[2,4,1024,128]{3,2,1,0:T(8,128)(2,1)} %constant_dynamic-update-slice_fusion.9), channel_id=1, source_target_pairs={{0,4},{4,0},{8,12},{12,8},{16,20},{20,16},{24,28},{28,24},{32,36},... | collective-permute-start | bytes 6291464 | tf_op jit(solution)/shard_map/ppermute | solution.py:104
  84.4 20.3 %copy-start.4 = (bf16[256,512]{1,0:T(8,128)(2,1)S(1)}, bf16[256,512]{1,0:T(8,128)(2,1)}, u32[]{:S(2)}) copy-start(bf16[256,512]{1,0:T(8,128)(2,1)} %param.16) | copy-start | bytes 786436
  104.9 18.0 %copy-start.6 = (f32[2048]{0:T(1024)S(1)}, f32[2048]{0:T(1024)}, u32[]{:S(2)}) copy-start(f32[2048]{0:T(1024)} %param.25) | copy-start | bytes 24580
  104.9 18.0 %copy-start.7 = (f32[2048]{0:T(1024)S(1)}, f32[2048]{0:T(1024)}, u32[]{:S(2)}) copy-start(f32[2048]{0:T(1024)} %param.24) | copy-start | bytes 24580
  105.0 18.7 %copy-start.8 = (bf16[2048,1024]{1,0:T(8,128)(2,1)S(1)}, bf16[2048,1024]{1,0:T(8,128)(2,1)}, u32[]{:S(2)}) copy-start(bf16[2048,1024]{1,0:T(8,128)(2,1)} %param.26) | copy-start | bytes 12582916
  122.6 1.1 copy-start.10
  123.7 3.7 %copy-start.9 = (bf16[1024,2048]{1,0:T(8,128)(2,1)S(1)}, bf16[1024,2048]{1,0:T(8,128)(2,1)}, u32[]{:S(2)}) copy-start(bf16[1024,2048]{1,0:T(8,128)(2,1)} %param.28) | copy-start | bytes 12582916
  129.8 17.5 %all-to-all-start.3 = ((bf16[4,256,512]{2,1,0:T(8,128)(2,1)}), bf16[4,256,512]{2,1,0:T(8,128)(2,1)S(1)}, u32[]{:S(2)}, u32[]{:S(2)}) async-start(bf16[4,256,512]{2,1,0:T(8,128)(2,1)} %bitcast.259), calls=%async_computation.3 | async-start | bytes 2097152 | tf_op jit(solution)/shard_map/all_to_all | solution.py:58

commit v8 on v7

--- a/solution.py
+++ b/solution.py
@@ -138,11 +138,6 @@
     picked = head_major(jnp.transpose(picked, (2, 0, 1, 3)), head_count)
     arrived = lax.all_to_all(picked, "seq", 0, 0, tiled=True)
 
-    root_full, arrived = ring_gather_seq(head_major(root_kv, head_count), seq_size, arrived)
-    branch_mine = jnp.transpose(arrived, (1, 2, 0, 3, 4)).reshape(
-        2, head_count, seq_size * local_rows, HD
-    )
-
     running = (
         jnp.full((head_count, row_count), NEGATIVE_FILL, jnp.float32),
         jnp.zeros((head_count, row_count), jnp.float32),
@@ -161,6 +156,13 @@
     )
     leaf_heads = head_major(leaf_kv, head_count)
     running = attend(running, query_heads, leaf_heads[0], leaf_heads[1], True)
+    root_full, (arrived, running) = ring_gather_seq(
+        head_major(root_kv, head_count), seq_size, (arrived, running)
+    )
+    branch_mine = jnp.transpose(arrived, (1, 2, 0, 3, 4)).reshape(
+        2, head_count, seq_size * local_rows, HD
+    )
+
     running = attend_blocks(running, query_heads, branch_mine[0], branch_mine[1])
     running = attend_blocks(running, query_heads, root_full[0], root_full[1])
     largest, totals, accumulated = running

time: 149 us -> 145 us (0.973)
  waiting for transfers between devices: 38.8 us -> 35 us
    ppermute x4, waiting for transfers between devices: 21.6 us -> 16.6 us  [ring_along(): from_below = lax.ppermute(from_below, 'seq', up)]
    ppermute x1, waiting for transfers between devices: 0.01 us -> 1.91 us  [ring_gather_seq(): partner = lax.ppermute(gathered, 'seq', shift_pairs(shape, 2, 1))]
    concatenate x1, local copies, waits for them, and re-layouts: 1.88 us -> 0.28 us  [ring_gather_seq(): return (jnp.concatenate([gathered, partner], axis=2), companion)]
    transpose x2, local copies, waits for them, and re-layouts: 1.02 us -> 2.56 us  [head_major(): return jnp.transpose(split, order)]
    unnamed x36 -> x38, local copies, waits for them, and re-layouts: 9.68 us -> 10.6 us
  transfers between devices with their start and end apart: 15 -> 15, of which waited for: 7 -> 8; matrix products, arithmetic and copies ran while one was open for 14% -> 15% of each run, Pallas kernels for 0% -> 0%
where the time goes in v8:
time: 145 us
  blocking collectives  36.7 us (25%)
  waiting for transfers between devices  35 us (24%)
  starting transfers between devices  33 us (23%)
  local copies, waits for them, and re-layouts  21.1 us (15%)
  matrix products  11.6 us (8%)
  other arithmetic  6.66 us (5%)
    all_to_all x1, blocking collectives, tensor_sum_scatter(): arrived = lax.all_to_all(pieces, 'tensor', 0, 0, tiled=True)  19.8 us
    all_to_all x1, blocking collectives, tensor_gather(): arrived = lax.all_to_all(copies, 'tensor', 0, 0, tiled=True)  16.9 us
    ppermute x4, waiting for transfers between devices, ring_along(): from_below = lax.ppermute(from_below, 'seq', up)  16.6 us
    all_to_all x1, waiting for transfers between devices, tensor_sum_scatter(): arrived = lax.all_to_all(pieces, 'tensor', 0, 0, tiled=True)  12.6 us
    unnamed x38, local copies, waits for them, and re-layouts  10.6 us
    ppermute x4, starting transfers between devices, ring_along(): from_above = lax.ppermute(from_above, 'seq', down)  9.52 us
    all_to_all x1, starting transfers between devices, per_device(): arrived = lax.all_to_all(picked, 'seq', 0, 0, tiled=True)  9.39 us
    ppermute x4, starting transfers between devices, ring_along(): from_below = lax.ppermute(from_below, 'seq', up)  5 us
  transfers between devices with their start and end apart: 15, of which 8 were waited for; matrix products, arithmetic and copies ran while one was open for 15% of the time, Pallas kernels for 0%

profile of v8, /device:TPU:2, one launch (start us, length us, event | category | flops | bytes accessed | tf_op | source)
XLA Modules:
  0.0 144.5 jit_solution(159829023952098649)
XLA Ops:
  0.0 1.6 %bitcast_bitcast_fusion.12 = bf16[2,4,32,128]{3,2,1,0:T(8,128)(2,1)} fusion(bf16[2,32,512]{2,1,0:T(8,128)(2,1)} %param.22), kind=kLoop, calls=%fused_computation.88 | loop fusion | bytes 131072 | tf_op jit(solution)/shard_map/transpose | solution.py:50
  1.6 1.9 %collective-permute-start = (bf16[2,4,32,128]{3,2,1,0:T(8,128)(2,1)}, bf16[2,4,32,128]{3,2,1,0:T(8,128)(2,1)}, u32[]{:S(2)}, u32[]{:S(2)}) collective-permute-start(bf16[2,4,32,128]{3,2,1,0:T(8,128)(2,1)} %bitcast_bitcast_fusion.12), channel_id=1, source_target_pairs={{0,32},{4,36},{8,40},{12,44},{16,48},{20,52},{24,56},{28,60},{32,6... | collective-permute-start | bytes 196616 | tf_op jit(solution)/shard_map/ppermute | solution.py:86
  3.5 3.9 %collective-permute-start.1 = (bf16[2,4,32,128]{3,2,1,0:T(8,128)(2,1)}, bf16[2,4,32,128]{3,2,1,0:T(8,128)(2,1)S(1)}, u32[]{:S(2)}, u32[]{:S(2)}) collective-permute-start(bf16[2,4,32,128]{3,2,1,0:T(8,128)(2,1)} %bitcast_bitcast_fusion.12), channel_id=1, source_target_pairs={{0,224},{4,228},{8,232},{12,236},{16,240},{20,244},{24,248},{28,25... | collective-permute-start | bytes 196616 | tf_op jit(solution)/shard_map/ppermute | solution.py:87
  7.5 0.7 compare_select_fusion
  8.2 0.7 compare_and_fusion
  8.8 1.0 copy.63
  9.9 1.0 gather_fusion
  11.3 1.0 reshape.139
  12.2 9.4 %all-to-all-start = ((bf16[64,2,4,4,128]{4,2,3,1,0:T(4,128)(2,1)}), bf16[64,2,4,4,128]{4,2,3,1,0:T(4,128)(2,1)S(1)}, u32[]{:S(2)}, u32[]{:S(2)}) async-start(bf16[64,2,4,4,128]{4,2,3,1,0:T(4,128)(2,1)} %bitcast.3), calls=%async_computation | async-start | bytes 1048576 | tf_op jit(solution)/shard_map/all_to_all | solution.py:139
  21.7 0.7 constant_dynamic-update-slice_fusion.8
  23.7 0.9 bitcast_bitcast_fusion.11
  25.5 1.5 %collective-permute-start.2 = (bf16[2,4,32,128]{3,2,1,0:T(8,128)(2,1)}, bf16[2,4,32,128]{3,2,1,0:T(8,128)(2,1)S(1)}, u32[]{:S(2)}, u32[]{:S(2)}) collective-permute-start(bf16[2,4,32,128]{3,2,1,0:T(8,128)(2,1)} %collective-permute-done), channel_id=1, source_target_pairs={{0,32},{4,36},{8,40},{12,44},{16,48},{20,52},{24,56},{28,60},{32,6... | collective-permute-start | bytes 196616 | tf_op jit(solution)/shard_map/ppermute | solution.py:86
  27.0 1.8 %collective-permute-start.3 = (bf16[2,4,32,128]{3,2,1,0:T(8,128)(2,1)S(1)}, bf16[2,4,32,128]{3,2,1,0:T(8,128)(2,1)S(1)}, u32[]{:S(2)}, u32[]{:S(2)}) collective-permute-start(bf16[2,4,32,128]{3,2,1,0:T(8,128)(2,1)S(1)} %collective-permute-done.1), channel_id=1, source_target_pairs={{0,224},{4,228},{8,232},{12,236},{16,240},{20,244},{24,248},{28,25... | collective-permute-start | bytes 196616 | tf_op jit(solution)/shard_map/ppermute | solution.py:87
  28.8 1.5 %constant_dynamic-update-slice_fusion.7 = (bf16[2,4,256,128]{3,2,1,0:T(8,128)(2,1)S(1)}, bf16[2,4,1024,128]{3,2,1,0:T(8,128)(2,1)}) fusion(bf16[2,4,256,128]{3,2,1,0:T(8,128)(2,1)S(1)} %copy-done.6, bf16[2,4,32,128]{3,2,1,0:T(8,128)(2,1)} %collective-permute-done, bf16[2,4,1024,128]{3,2,1,0:T(8,128)(2,1)} %get-tuple-element.39), kind=kLoop, calls=%fused_computation.98 | loop fusion | bytes 196608
  30.3 0.7 constant_dynamic-update-slice_fusion.6
  31.0 6.7 %collective-permute-done.2 = bf16[2,4,32,128]{3,2,1,0:T(8,128)(2,1)S(1)} collective-permute-done((bf16[2,4,32,128]{3,2,1,0:T(8,128)(2,1)}, bf16[2,4,32,128]{3,2,1,0:T(8,128)(2,1)S(1)}, u32[]{:S(2)}, u32[]{:S(2)}) %collective-permute-start.2) | collective-permute-done | bytes 65568 | tf_op jit(solution)/shard_map/ppermute | solution.py:86
  37.7 3.2 %collective-permute-start.5 = (bf16[2,4,32,128]{3,2,1,0:T(8,128)(2,1)S(1)}, bf16[2,4,32,128]{3,2,1,0:T(8,128)(2,1)S(1)}, u32[]{:S(2)}, u32[]{:S(2)}) collective-permute-start(bf16[2,4,32,128]{3,2,1,0:T(8,128)(2,1)S(1)} %collective-permute-done.3), channel_id=1, source_target_pairs={{0,224},{4,228},{8,232},{12,236},{16,240},{20,244},{24,248},{28,25... | collective-permute-start | bytes 196616 | tf_op jit(solution)/shard_map/ppermute | solution.py:87
  41.0 0.7 constant_dynamic-update-slice_fusion.5
  41.6 0.7 constant_dynamic-update-slice_fusion.4
  42.3 0.9 collective-permute-done.4
  43.2 3.2 %collective-permute-start.7 = (bf16[2,4,16,128]{3,2,1,0:T(8,128)(2,1)S(1)}, bf16[2,4,16,128]{3,2,1,0:T(8,128)(2,1)S(1)}, u32[]{:S(2)}, u32[]{:S(2)}) collective-permute-start(bf16[2,4,16,128]{3,2,1,0:T(8,128)(2,1)S(1)} %slice.45), channel_id=1, source_target_pairs={{0,224},{4,228},{8,232},{12,236},{16,240},{20,244},{24,248},{28,25... | collective-permute-start | bytes 98312 | tf_op jit(solution)/shard_map/ppermute | solution.py:92
  46.4 0.7 constant_dynamic-update-slice_fusion.3
  47.1 0.7 constant_dynamic-update-slice_fusion.2
  49.6 1.5 %collective-permute-start.8 = (bf16[2,4,256,128]{3,2,1,0:T(8,128)(2,1)S(1)}, bf16[2,4,256,128]{3,2,1,0:T(8,128)(2,1)S(1)}, u32[]{:S(2)}, u32[]{:S(2)}) collective-permute-start(bf16[2,4,256,128]{3,2,1,0:T(8,128)(2,1)S(1)} %get-tuple-element.40), channel_id=1, source_target_pairs={{0,8},{4,12},{8,16},{12,20},{16,24},{20,28},{24,0},{28,4},{32,40},... | collective-permute-start | bytes 1572872 | tf_op jit(solution)/shard_map/ppermute | solution.py:86
  52.4 9.0 %collective-permute-done.8 = bf16[2,4,256,128]{3,2,1,0:T(8,128)(2,1)S(1)} collective-permute-done((bf16[2,4,256,128]{3,2,1,0:T(8,128)(2,1)S(1)}, bf16[2,4,256,128]{3,2,1,0:T(8,128)(2,1)S(1)}, u32[]{:S(2)}, u32[]{:S(2)}) %collective-permute-start.8) | collective-permute-done | bytes 524320 | tf_op jit(solution)/shard_map/ppermute | solution.py:86
  61.4 1.8 %collective-permute-start.10 = (bf16[2,4,128,128]{3,2,1,0:T(8,128)(2,1)S(1)}, bf16[2,4,128,128]{3,2,1,0:T(8,128)(2,1)S(1)}, u32[]{:S(2)}, u32[]{:S(2)}) collective-permute-start(bf16[2,4,128,128]{3,2,1,0:T(8,128)(2,1)S(1)} %slice.46), channel_id=1, source_target_pairs={{0,8},{4,12},{8,16},{12,20},{16,24},{20,28},{24,0},{28,4},{32,40},... | collective-permute-start | bytes 786440 | tf_op jit(solution)/shard_map/ppermute | solution.py:91
  64.1 0.9 constant_dynamic-update-slice_fusion.12
  65.0 0.9 constant_dynamic-update-slice_fusion.11
  65.9 2.1 %collective-permute-done.10 = bf16[2,4,128,128]{3,2,1,0:T(8,128)(2,1)S(1)} collective-permute-done((bf16[2,4,128,128]{3,2,1,0:T(8,128)(2,1)S(1)}, bf16[2,4,128,128]{3,2,1,0:T(8,128)(2,1)S(1)}, u32[]{:S(2)}, u32[]{:S(2)}) %collective-permute-start.10) | collective-permute-done | bytes 262176 | tf_op jit(solution)/shard_map/ppermute | solution.py:91
  68.0 0.8 constant_dynamic-update-slice_fusion.10
  68.8 1.2 collective-permute-done.11
  70.0 0.8 constant_dynamic-update-slice_fusion.9
  71.1 1.7 %constant_dynamic-update-slice_fusion.23 = bf16[2,4,2048,128]{3,2,1,0:T(8,128)(2,1)S(1)} fusion(bf16[2,4,1024,128]{3,2,1,0:T(8,128)(2,1)} %constant_dynamic-update-slice_fusion.9), kind=kLoop, calls=%fused_computation.114 | loop fusion | bytes 4194304
  73.3 1.9 %collective-permute-done.12 = bf16[2,4,1024,128]{3,2,1,0:T(8,128)(2,1)S(1)} collective-permute-done((bf16[2,4,1024,128]{3,2,1,0:T(8,128)(2,1)}, bf16[2,4,1024,128]{3,2,1,0:T(8,128)(2,1)S(1)}, u32[]{:S(2)}, u32[]{:S(2)}) %collective-permute-start.12) | collective-permute-done | bytes 2097184 | tf_op jit(solution)/shard_map/ppermute | solution.py:104
  75.5 1.3 bitcast_reduce_fusion
  77.5 1.4 fusion.1
  78.9 2.4 %fusion.34 = bf16[256,4,128]{2,0,1:T(8,128)(2,1)S(1)} fusion(bf16[2,4,2048,128]{3,2,1,0:T(8,128)(2,1)S(1)} %constant_dynamic-update-slice_fusion.22, f32[4,2048,256]{2,1,0:T(8,128)S(1)} %get-tuple-element.54, f32[4,256]{1,0:T(4,128)S(1)} %get-tuple-element.20, f32[4,256,128]{2,1,0:T(8,128)S(1)} %fusion.42, f32[4,256,128]{2,1,0:T(8,128)S(1)} %convolution_add_fusion.1, ...), kind=kOutput, calls=%fused_computation.58 | convolution fusion | flops 543948800 | bytes 11812864 | tf_op jit(solution)/shard_map/hqk,hkd->hqd/dot_general | solution.py:24
  81.5 0.7 convolution_convert_fusion
  82.3 19.8 %all_to_all.20 = bf16[4,256,512]{2,1,0:T(8,128)(2,1)S(1)} all-to-all(bf16[4,256,512]{2,1,0:T(8,128)(2,1)S(1)} %bitcast.178), channel_id=1, replica_groups=mesh['seq'=64,'tensor'=4] {'tensor'}, dimensions={0} | all-to-all | bytes 2097152 | tf_op jit(solution)/shard_map/all_to_all | solution.py:58
  102.6 16.9 %all_to_all.21 = bf16[4,256,512]{1,2,0:T(8,128)(2,1)S(1)} all-to-all(bf16[4,256,512]{1,2,0:T(8,128)(2,1)S(1)} %broadcast_in_dim.79), channel_id=1, replica_groups=mesh['seq'=64,'tensor'=4] {'tensor'}, dimensions={0} | all-to-all | bytes 2097152 | tf_op jit(solution)/shard_map/all_to_all | solution.py:65
  119.9 0.7 fusion.11
  120.6 3.7 %fusion.20 = bf16[256,1024]{1,0:T(8,128)(2,1)S(1)} fusion(bf16[256,2048]{0,1:T(8,128)(2,1)S(1)} %fusion.11, bf16[2048,1024]{1,0:T(8,128)(2,1)S(1)} %copy-done.7, f32[1024]{0:T(1024)S(1)} %copy-done.11), kind=kOutput, calls=%fused_computation.35 | convolution fusion | flops 1091043328 | bytes 5771264 | tf_op jit(solution)/shard_map/dot_general | solution.py:187
  124.4 1.3 convolution_convert_fusion.1
  125.6 1.1 copy.146
  126.7 3.5 %all-to-all-start.3 = ((bf16[4,256,512]{2,1,0:T(8,128)(2,1)}), bf16[4,256,512]{2,1,0:T(8,128)(2,1)S(1)}, u32[]{:S(2)}, u32[]{:S(2)}) async-start(bf16[4,256,512]{2,1,0:T(8,128)(2,1)} %bitcast.176), calls=%async_computation.3 | async-start | bytes 2097152 | tf_op jit(solution)/shard_map/all_to_all | solution.py:58
  130.2 0.8 dynamic_slice.7
  131.0 12.6 %all-to-all-done.3 = bf16[4,256,512]{2,1,0:T(8,128)(2,1)S(1)} async-done(((bf16[4,256,512]{2,1,0:T(8,128)(2,1)}), bf16[4,256,512]{2,1,0:T(8,128)(2,1)S(1)}, u32[]{:S(2)}, u32[]{:S(2)}) %all-to-all-start.3) | async-done | bytes 1048608 | tf_op jit(solution)/shard_map/all_to_all | solution.py:58
  143.8 0.8 add_convert_fusion
  (75 shorter events, 9.4 us)
Async XLA Ops:
  0.0 81.4 %copy-start = (bf16[512,2048]{1,0:T(8,128)(2,1)S(1)}, bf16[512,2048]{1,0:T(8,128)(2,1)}, u32[]{:S(2)}) copy-start(bf16[512,2048]{1,0:T(8,128)(2,1)} %param.23) | copy-start | bytes 6291460
  1.6 23.9 %collective-permute-start = (bf16[2,4,32,128]{3,2,1,0:T(8,128)(2,1)}, bf16[2,4,32,128]{3,2,1,0:T(8,128)(2,1)}, u32[]{:S(2)}, u32[]{:S(2)}) collective-permute-start(bf16[2,4,32,128]{3,2,1,0:T(8,128)(2,1)} %bitcast_bitcast_fusion.12), channel_id=1, source_target_pairs={{0,32},{4,36},{8,40},{12,44},{16,48},{20,52},{24,56},{28,60},{32,6... | collective-permute-start | bytes 196616 | tf_op jit(solution)/shard_map/ppermute | solution.py:86
  3.5 23.5 %collective-permute-start.1 = (bf16[2,4,32,128]{3,2,1,0:T(8,128)(2,1)}, bf16[2,4,32,128]{3,2,1,0:T(8,128)(2,1)S(1)}, u32[]{:S(2)}, u32[]{:S(2)}) collective-permute-start(bf16[2,4,32,128]{3,2,1,0:T(8,128)(2,1)} %bitcast_bitcast_fusion.12), channel_id=1, source_target_pairs={{0,224},{4,228},{8,232},{12,236},{16,240},{20,244},{24,248},{28,25... | collective-permute-start | bytes 196616 | tf_op jit(solution)/shard_map/ppermute | solution.py:87
  9.8 11.8 %copy-start.2 = (bf16[2,32,512]{2,1,0:T(8,128)(2,1)S(1)}, bf16[2,32,512]{2,1,0:T(8,128)(2,1)}, u32[]{:S(2)}) copy-start(bf16[2,32,512]{2,1,0:T(8,128)(2,1)} %param.22) | copy-start | bytes 196612
  9.8 12.5 %copy-start.12 = (s32[64]{0:T(128)S(1)}, s32[64]{0:T(128)}, u32[]{:S(2)}) copy-start(s32[64]{0:T(128)} %param.31) | copy-start | bytes 772
  10.9 13.8 %copy-start.1 = (bf16[256,512]{1,0:T(8,128)(2,1)S(1)}, bf16[256,512]{1,0:T(8,128)(2,1)}, u32[]{:S(2)}) copy-start(bf16[256,512]{1,0:T(8,128)(2,1)} %param.17) | copy-start | bytes 786436
  11.2 13.7 %copy-start.9 = (bf16[256,512]{1,0:T(8,128)(2,1)S(1)}, bf16[256,512]{1,0:T(8,128)(2,1)}, u32[]{:S(2)}) copy-start(bf16[256,512]{1,0:T(8,128)(2,1)} %param.18) | copy-start | bytes 786436
  12.2 58.6 %all-to-all-start = ((bf16[64,2,4,4,128]{4,2,3,1,0:T(4,128)(2,1)}), bf16[64,2,4,4,128]{4,2,3,1,0:T(4,128)(2,1)S(1)}, u32[]{:S(2)}, u32[]{:S(2)}) async-start(bf16[64,2,4,4,128]{4,2,3,1,0:T(4,128)(2,1)} %bitcast.3), calls=%async_computation | async-start | bytes 1048576 | tf_op jit(solution)/shard_map/all_to_all | solution.py:139
  22.3 6.5 %copy-start.6 = (bf16[2,4,256,128]{3,2,1,0:T(8,128)(2,1)S(1)}, bf16[2,4,256,128]{3,2,1,0:T(8,128)(2,1)}, u32[]{:S(2)}) copy-start(bf16[2,4,256,128]{3,2,1,0:T(8,128)(2,1)} %get-tuple-element.38) | copy-start | bytes 1572868
  24.9 26.9 %copy-start.10 = (bf16[256,512]{1,0:T(8,128)(2,1)S(1)}, bf16[256,512]{1,0:T(8,128)(2,1)}, u32[]{:S(2)}) copy-start(bf16[256,512]{1,0:T(8,128)(2,1)} %param.19) | copy-start | bytes 786436
  25.5 12.2 %collective-permute-start.2 = (bf16[2,4,32,128]{3,2,1,0:T(8,128)(2,1)}, bf16[2,4,32,128]{3,2,1,0:T(8,128)(2,1)S(1)}, u32[]{:S(2)}, u32[]{:S(2)}) collective-permute-start(bf16[2,4,32,128]{3,2,1,0:T(8,128)(2,1)} %collective-permute-done), channel_id=1, source_target_pairs={{0,32},{4,36},{8,40},{12,44},{16,48},{20,52},{24,56},{28,60},{32,6... | collective-permute-start | bytes 196616 | tf_op jit(solution)/shard_map/ppermute | solution.py:86
  27.0 10.7 %collective-permute-start.3 = (bf16[2,4,32,128]{3,2,1,0:T(8,128)(2,1)S(1)}, bf16[2,4,32,128]{3,2,1,0:T(8,128)(2,1)S(1)}, u32[]{:S(2)}, u32[]{:S(2)}) collective-permute-start(bf16[2,4,32,128]{3,2,1,0:T(8,128)(2,1)S(1)} %collective-permute-done.1), channel_id=1, source_target_pairs={{0,224},{4,228},{8,232},{12,236},{16,240},{20,244},{24,248},{28,25... | collective-permute-start | bytes 196616 | tf_op jit(solution)/shard_map/ppermute | solution.py:87
  37.7 5.5 %collective-permute-start.4 = (bf16[2,4,32,128]{3,2,1,0:T(8,128)(2,1)S(1)}, bf16[2,4,32,128]{3,2,1,0:T(8,128)(2,1)S(1)}, u32[]{:S(2)}, u32[]{:S(2)}) collective-permute-start(bf16[2,4,32,128]{3,2,1,0:T(8,128)(2,1)S(1)} %collective-permute-done.2), channel_id=1, source_target_pairs={{0,32},{4,36},{8,40},{12,44},{16,48},{20,52},{24,56},{28,60},{32,6... | collective-permute-start | bytes 196616 | tf_op jit(solution)/shard_map/ppermute | solution.py:86
  37.7 5.5 %collective-permute-start.5 = (bf16[2,4,32,128]{3,2,1,0:T(8,128)(2,1)S(1)}, bf16[2,4,32,128]{3,2,1,0:T(8,128)(2,1)S(1)}, u32[]{:S(2)}, u32[]{:S(2)}) collective-permute-start(bf16[2,4,32,128]{3,2,1,0:T(8,128)(2,1)S(1)} %collective-permute-done.3), channel_id=1, source_target_pairs={{0,224},{4,228},{8,232},{12,236},{16,240},{20,244},{24,248},{28,25... | collective-permute-start | bytes 196616 | tf_op jit(solution)/shard_map/ppermute | solution.py:87
  43.2 5.1 %collective-permute-start.6 = (bf16[2,4,16,128]{3,2,1,0:T(8,128)(2,1)S(1)}, bf16[2,4,16,128]{3,2,1,0:T(8,128)(2,1)S(1)}, u32[]{:S(2)}, u32[]{:S(2)}) collective-permute-start(bf16[2,4,16,128]{3,2,1,0:T(8,128)(2,1)S(1)} %slice.44), channel_id=1, source_target_pairs={{0,32},{4,36},{8,40},{12,44},{16,48},{20,52},{24,56},{28,60},{32,6... | collective-permute-start | bytes 98312 | tf_op jit(solution)/shard_map/ppermute | solution.py:91
  43.2 5.7 %collective-permute-start.7 = (bf16[2,4,16,128]{3,2,1,0:T(8,128)(2,1)S(1)}, bf16[2,4,16,128]{3,2,1,0:T(8,128)(2,1)S(1)}, u32[]{:S(2)}, u32[]{:S(2)}) collective-permute-start(bf16[2,4,16,128]{3,2,1,0:T(8,128)(2,1)S(1)} %slice.45), channel_id=1, source_target_pairs={{0,224},{4,228},{8,232},{12,236},{16,240},{20,244},{24,248},{28,25... | collective-permute-start | bytes 98312 | tf_op jit(solution)/shard_map/ppermute | solution.py:92
  49.6 11.8 %collective-permute-start.8 = (bf16[2,4,256,128]{3,2,1,0:T(8,128)(2,1)S(1)}, bf16[2,4,256,128]{3,2,1,0:T(8,128)(2,1)S(1)}, u32[]{:S(2)}, u32[]{:S(2)}) collective-permute-start(bf16[2,4,256,128]{3,2,1,0:T(8,128)(2,1)S(1)} %get-tuple-element.40), channel_id=1, source_target_pairs={{0,8},{4,12},{8,16},{12,20},{16,24},{20,28},{24,0},{28,4},{32,40},... | collective-permute-start | bytes 1572872 | tf_op jit(solution)/shard_map/ppermute | solution.py:86
  51.2 12.3 %collective-permute-start.9 = (bf16[2,4,256,128]{3,2,1,0:T(8,128)(2,1)S(1)}, bf16[2,4,256,128]{3,2,1,0:T(8,128)(2,1)S(1)}, u32[]{:S(2)}, u32[]{:S(2)}) collective-permute-start(bf16[2,4,256,128]{3,2,1,0:T(8,128)(2,1)S(1)} %get-tuple-element.40), channel_id=1, source_target_pairs={{0,24},{4,28},{8,0},{12,4},{16,8},{20,12},{24,16},{28,20},{32,56},... | collective-permute-start | bytes 1572872 | tf_op jit(solution)/shard_map/ppermute | solution.py:87
  61.4 6.6 %collective-permute-start.10 = (bf16[2,4,128,128]{3,2,1,0:T(8,128)(2,1)S(1)}, bf16[2,4,128,128]{3,2,1,0:T(8,128)(2,1)S(1)}, u32[]{:S(2)}, u32[]{:S(2)}) collective-permute-start(bf16[2,4,128,128]{3,2,1,0:T(8,128)(2,1)S(1)} %slice.46), channel_id=1, source_target_pairs={{0,8},{4,12},{8,16},{12,20},{16,24},{20,28},{24,0},{28,4},{32,40},... | collective-permute-start | bytes 786440 | tf_op jit(solution)/shard_map/ppermute | solution.py:91
  63.6 6.4 %collective-permute-start.11 = (bf16[2,4,128,128]{3,2,1,0:T(8,128)(2,1)S(1)}, bf16[2,4,128,128]{3,2,1,0:T(8,128)(2,1)S(1)}, u32[]{:S(2)}, u32[]{:S(2)}) collective-permute-start(bf16[2,4,128,128]{3,2,1,0:T(8,128)(2,1)S(1)} %slice.47), channel_id=1, source_target_pairs={{0,24},{4,28},{8,0},{12,4},{16,8},{20,12},{24,16},{28,20},{32,56},... | collective-permute-start | bytes 786440 | tf_op jit(solution)/shard_map/ppermute | solution.py:92
  70.8 4.4 %collective-permute-start.12 = (bf16[2,4,1024,128]{3,2,1,0:T(8,128)(2,1)}, bf16[2,4,1024,128]{3,2,1,0:T(8,128)(2,1)S(1)}, u32[]{:S(2)}, u32[]{:S(2)}) collective-permute-start(bf16[2,4,1024,128]{3,2,1,0:T(8,128)(2,1)} %constant_dynamic-update-slice_fusion.9), channel_id=1, source_target_pairs={{0,4},{4,0},{8,12},{12,8},{16,20},{20,16},{24,28},{28,24},{32,36},... | collective-permute-start | bytes 6291464 | tf_op jit(solution)/shard_map/ppermute | solution.py:104
  82.3 20.0 %copy-start.3 = (bf16[256,512]{1,0:T(8,128)(2,1)S(1)}, bf16[256,512]{1,0:T(8,128)(2,1)}, u32[]{:S(2)}) copy-start(bf16[256,512]{1,0:T(8,128)(2,1)} %param.16) | copy-start | bytes 786436
  102.5 17.4 %copy-start.4 = (f32[2048]{0:T(1024)S(1)}, f32[2048]{0:T(1024)}, u32[]{:S(2)}) copy-start(f32[2048]{0:T(1024)} %param.25) | copy-start | bytes 24580
  102.5 17.4 %copy-start.5 = (f32[2048]{0:T(1024)S(1)}, f32[2048]{0:T(1024)}, u32[]{:S(2)}) copy-start(f32[2048]{0:T(1024)} %param.24) | copy-start | bytes 24580
  102.6 18.0 %copy-start.7 = (bf16[2048,1024]{1,0:T(8,128)(2,1)S(1)}, bf16[2048,1024]{1,0:T(8,128)(2,1)}, u32[]{:S(2)}) copy-start(bf16[2048,1024]{1,0:T(8,128)(2,1)} %param.26) | copy-start | bytes 12582916
  119.5 1.1 copy-start.11
  120.6 3.7 %copy-start.8 = (bf16[1024,2048]{1,0:T(8,128)(2,1)S(1)}, bf16[1024,2048]{1,0:T(8,128)(2,1)}, u32[]{:S(2)}) copy-start(bf16[1024,2048]{1,0:T(8,128)(2,1)} %param.28) | copy-start | bytes 12582916
  126.7 16.9 %all-to-all-start.3 = ((bf16[4,256,512]{2,1,0:T(8,128)(2,1)}), bf16[4,256,512]{2,1,0:T(8,128)(2,1)S(1)}, u32[]{:S(2)}, u32[]{:S(2)}) async-start(bf16[4,256,512]{2,1,0:T(8,128)(2,1)} %bitcast.176), calls=%async_computation.3 | async-start | bytes 2097152 | tf_op jit(solution)/shard_map/all_to_all | solution.py:58

commit v9 on v8

--- a/solution.py
+++ b/solution.py
@@ -102,7 +102,7 @@
     gathered = ring_along(gathered, shape, 1)
     gathered, companion = lax.optimization_barrier((gathered, companion))
     partner = lax.ppermute(gathered, "seq", shift_pairs(shape, 2, 1))
-    return jnp.concatenate([gathered, partner], axis=2), companion
+    return (gathered, partner), companion
 
 
 def per_device(
@@ -163,8 +163,10 @@
         2, head_count, seq_size * local_rows, HD
     )
 
+    root_own, root_partner = root_full
+    running = attend_blocks(running, query_heads, root_own[0], root_own[1])
     running = attend_blocks(running, query_heads, branch_mine[0], branch_mine[1])
-    running = attend_blocks(running, query_heads, root_full[0], root_full[1])
+    running = attend_blocks(running, query_heads, root_partner[0], root_partner[1])
     largest, totals, accumulated = running
     attention = (
         jnp.transpose(accumulated / totals[:, :, None], (1, 0, 2))

time: 145 us -> 146 us (level)
  matrix products: 11.6 us -> 14.7 us
  local copies, waits for them, and re-layouts: 21.1 us -> 19.1 us
    unnamed x38 -> x37, local copies, waits for them, and re-layouts: 10.6 us -> 8.86 us
    dot_general x4 -> x5, matrix products: 3.62 us -> 5.33 us  [attend(): jnp.einsum('hqk,hkd->hqd', weights.astype(jnp.bfloat16), value_heads, pre...]
    dot_general x4 -> x5, matrix products: 2.23 us -> 3.63 us  [attend(): jnp.einsum('hqd,hkd->hqk', query_heads, key_heads, preferred_element_type...]
where the time goes in v9:
time: 146 us; the launch traced here: 145 us
  blocking collectives  36.7 us (25%)
  waiting for transfers between devices  34.8 us (24%)
  starting transfers between devices  33 us (23%)
  local copies, waits for them, and re-layouts  19.1 us (13%)
  matrix products  14.7 us (10%)
  other arithmetic  6.65 us (5%)
    all_to_all x1, blocking collectives, tensor_sum_scatter(): arrived = lax.all_to_all(pieces, 'tensor', 0, 0, tiled=True)  19.8 us
    all_to_all x1, blocking collectives, tensor_gather(): arrived = lax.all_to_all(copies, 'tensor', 0, 0, tiled=True)  16.9 us
    ppermute x4, waiting for transfers between devices, ring_along(): from_below = lax.ppermute(from_below, 'seq', up)  16.6 us
    all_to_all x1, waiting for transfers between devices, tensor_sum_scatter(): arrived = lax.all_to_all(pieces, 'tensor', 0, 0, tiled=True)  12.6 us
    ppermute x4, starting transfers between devices, ring_along(): from_above = lax.ppermute(from_above, 'seq', down)  9.52 us
    all_to_all x1, starting transfers between devices, per_device(): arrived = lax.all_to_all(picked, 'seq', 0, 0, tiled=True)  9.39 us
    unnamed x37, local copies, waits for them, and re-layouts  8.86 us
    dot_general x5, matrix products, attend(): jnp.einsum('hqk,hkd->hqd', weights.astype(jnp.bfloat16), value_heads, pre...  5.33 us
  transfers between devices with their start and end apart: 15, of which 8 were waited for; matrix products, arithmetic and copies ran while one was open for 15% of the time, Pallas kernels for 0%

profile of v9, /device:TPU:2, one launch (start us, length us, event | category | flops | bytes accessed | tf_op | source)
XLA Modules:
  0.0 145.3 jit_solution(13525628429121798215)
XLA Ops:
  0.0 1.6 %bitcast_bitcast_fusion.13 = bf16[2,4,32,128]{3,2,1,0:T(8,128)(2,1)} fusion(bf16[2,32,512]{2,1,0:T(8,128)(2,1)} %param.22), kind=kLoop, calls=%fused_computation.103 | loop fusion | bytes 131072 | tf_op jit(solution)/shard_map/transpose | solution.py:50
  1.6 1.9 %collective-permute-start = (bf16[2,4,32,128]{3,2,1,0:T(8,128)(2,1)}, bf16[2,4,32,128]{3,2,1,0:T(8,128)(2,1)}, u32[]{:S(2)}, u32[]{:S(2)}) collective-permute-start(bf16[2,4,32,128]{3,2,1,0:T(8,128)(2,1)} %bitcast_bitcast_fusion.13), channel_id=1, source_target_pairs={{0,32},{4,36},{8,40},{12,44},{16,48},{20,52},{24,56},{28,60},{32,6... | collective-permute-start | bytes 196616 | tf_op jit(solution)/shard_map/ppermute | solution.py:86
  3.5 3.9 %collective-permute-start.1 = (bf16[2,4,32,128]{3,2,1,0:T(8,128)(2,1)}, bf16[2,4,32,128]{3,2,1,0:T(8,128)(2,1)S(1)}, u32[]{:S(2)}, u32[]{:S(2)}) collective-permute-start(bf16[2,4,32,128]{3,2,1,0:T(8,128)(2,1)} %bitcast_bitcast_fusion.13), channel_id=1, source_target_pairs={{0,224},{4,228},{8,232},{12,236},{16,240},{20,244},{24,248},{28,25... | collective-permute-start | bytes 196616 | tf_op jit(solution)/shard_map/ppermute | solution.py:87
  8.2 0.7 compare_and_fusion
  8.8 1.0 copy.72
  9.9 1.0 gather_fusion
  11.3 1.0 reshape.141
  12.3 9.4 %all-to-all-start = ((bf16[64,2,4,4,128]{4,2,3,1,0:T(4,128)(2,1)}), bf16[64,2,4,4,128]{4,2,3,1,0:T(4,128)(2,1)S(1)}, u32[]{:S(2)}, u32[]{:S(2)}) async-start(bf16[64,2,4,4,128]{4,2,3,1,0:T(4,128)(2,1)} %bitcast.3), calls=%async_computation | async-start | bytes 1048576 | tf_op jit(solution)/shard_map/all_to_all | solution.py:139
  21.7 0.7 constant_dynamic-update-slice_fusion.8
  23.7 0.9 bitcast_bitcast_fusion.12
  25.5 1.5 %collective-permute-start.2 = (bf16[2,4,32,128]{3,2,1,0:T(8,128)(2,1)}, bf16[2,4,32,128]{3,2,1,0:T(8,128)(2,1)S(1)}, u32[]{:S(2)}, u32[]{:S(2)}) collective-permute-start(bf16[2,4,32,128]{3,2,1,0:T(8,128)(2,1)} %collective-permute-done), channel_id=1, source_target_pairs={{0,32},{4,36},{8,40},{12,44},{16,48},{20,52},{24,56},{28,60},{32,6... | collective-permute-start | bytes 196616 | tf_op jit(solution)/shard_map/ppermute | solution.py:86
  27.0 1.8 %collective-permute-start.3 = (bf16[2,4,32,128]{3,2,1,0:T(8,128)(2,1)S(1)}, bf16[2,4,32,128]{3,2,1,0:T(8,128)(2,1)S(1)}, u32[]{:S(2)}, u32[]{:S(2)}) collective-permute-start(bf16[2,4,32,128]{3,2,1,0:T(8,128)(2,1)S(1)} %collective-permute-done.1), channel_id=1, source_target_pairs={{0,224},{4,228},{8,232},{12,236},{16,240},{20,244},{24,248},{28,25... | collective-permute-start | bytes 196616 | tf_op jit(solution)/shard_map/ppermute | solution.py:87
  28.8 1.5 %constant_dynamic-update-slice_fusion.7 = (bf16[2,4,256,128]{3,2,1,0:T(8,128)(2,1)S(1)}, bf16[2,4,1024,128]{3,2,1,0:T(8,128)(2,1)}) fusion(bf16[2,4,256,128]{3,2,1,0:T(8,128)(2,1)S(1)} %copy-done.6, bf16[2,4,32,128]{3,2,1,0:T(8,128)(2,1)} %collective-permute-done, bf16[2,4,1024,128]{3,2,1,0:T(8,128)(2,1)} %get-tuple-element.41), kind=kLoop, calls=%fused_computation.113 | loop fusion | bytes 196608
  30.4 0.7 constant_dynamic-update-slice_fusion.6
  31.0 6.7 %collective-permute-done.2 = bf16[2,4,32,128]{3,2,1,0:T(8,128)(2,1)S(1)} collective-permute-done((bf16[2,4,32,128]{3,2,1,0:T(8,128)(2,1)}, bf16[2,4,32,128]{3,2,1,0:T(8,128)(2,1)S(1)}, u32[]{:S(2)}, u32[]{:S(2)}) %collective-permute-start.2) | collective-permute-done | bytes 65568 | tf_op jit(solution)/shard_map/ppermute | solution.py:86
  37.7 3.2 %collective-permute-start.5 = (bf16[2,4,32,128]{3,2,1,0:T(8,128)(2,1)S(1)}, bf16[2,4,32,128]{3,2,1,0:T(8,128)(2,1)S(1)}, u32[]{:S(2)}, u32[]{:S(2)}) collective-permute-start(bf16[2,4,32,128]{3,2,1,0:T(8,128)(2,1)S(1)} %collective-permute-done.3), channel_id=1, source_target_pairs={{0,224},{4,228},{8,232},{12,236},{16,240},{20,244},{24,248},{28,25... | collective-permute-start | bytes 196616 | tf_op jit(solution)/shard_map/ppermute | solution.py:87
  41.0 0.7 constant_dynamic-update-slice_fusion.5
  42.3 0.9 collective-permute-done.4
  43.2 3.2 %collective-permute-start.7 = (bf16[2,4,16,128]{3,2,1,0:T(8,128)(2,1)S(1)}, bf16[2,4,16,128]{3,2,1,0:T(8,128)(2,1)S(1)}, u32[]{:S(2)}, u32[]{:S(2)}) collective-permute-start(bf16[2,4,16,128]{3,2,1,0:T(8,128)(2,1)S(1)} %slice.53), channel_id=1, source_target_pairs={{0,224},{4,228},{8,232},{12,236},{16,240},{20,244},{24,248},{28,25... | collective-permute-start | bytes 98312 | tf_op jit(solution)/shard_map/ppermute | solution.py:92
  46.5 0.7 constant_dynamic-update-slice_fusion.3
  47.2 0.7 constant_dynamic-update-slice_fusion.2
  49.6 1.5 %collective-permute-start.8 = (bf16[2,4,256,128]{3,2,1,0:T(8,128)(2,1)S(1)}, bf16[2,4,256,128]{3,2,1,0:T(8,128)(2,1)S(1)}, u32[]{:S(2)}, u32[]{:S(2)}) collective-permute-start(bf16[2,4,256,128]{3,2,1,0:T(8,128)(2,1)S(1)} %get-tuple-element.42), channel_id=1, source_target_pairs={{0,8},{4,12},{8,16},{12,20},{16,24},{20,28},{24,0},{28,4},{32,40},... | collective-permute-start | bytes 1572872 | tf_op jit(solution)/shard_map/ppermute | solution.py:86
  52.4 9.0 %collective-permute-done.8 = bf16[2,4,256,128]{3,2,1,0:T(8,128)(2,1)S(1)} collective-permute-done((bf16[2,4,256,128]{3,2,1,0:T(8,128)(2,1)S(1)}, bf16[2,4,256,128]{3,2,1,0:T(8,128)(2,1)S(1)}, u32[]{:S(2)}, u32[]{:S(2)}) %collective-permute-start.8) | collective-permute-done | bytes 524320 | tf_op jit(solution)/shard_map/ppermute | solution.py:86
  61.4 1.8 %collective-permute-start.10 = (bf16[2,4,128,128]{3,2,1,0:T(8,128)(2,1)S(1)}, bf16[2,4,128,128]{3,2,1,0:T(8,128)(2,1)S(1)}, u32[]{:S(2)}, u32[]{:S(2)}) collective-permute-start(bf16[2,4,128,128]{3,2,1,0:T(8,128)(2,1)S(1)} %slice.54), channel_id=1, source_target_pairs={{0,8},{4,12},{8,16},{12,20},{16,24},{20,28},{24,0},{28,4},{32,40},... | collective-permute-start | bytes 786440 | tf_op jit(solution)/shard_map/ppermute | solution.py:91
  64.1 0.9 constant_dynamic-update-slice_fusion.12
  65.0 0.9 constant_dynamic-update-slice_fusion.11
  65.9 2.1 %collective-permute-done.10 = bf16[2,4,128,128]{3,2,1,0:T(8,128)(2,1)S(1)} collective-permute-done((bf16[2,4,128,128]{3,2,1,0:T(8,128)(2,1)S(1)}, bf16[2,4,128,128]{3,2,1,0:T(8,128)(2,1)S(1)}, u32[]{:S(2)}, u32[]{:S(2)}) %collective-permute-start.10) | collective-permute-done | bytes 262176 | tf_op jit(solution)/shard_map/ppermute | solution.py:91
  68.0 0.8 constant_dynamic-update-slice_fusion.10
  68.8 1.2 collective-permute-done.11
  70.0 0.8 constant_dynamic-update-slice_fusion.9
  71.5 1.9 %bitcast_reduce_fusion.1 = (f32[4,256]{1,0:T(4,128)S(1)}, f32[4,1024,256]{2,1,0:T(8,128)S(1)}) fusion(bf16[2,4,1024,128]{3,2,1,0:T(8,128)(2,1)} %constant_dynamic-update-slice_fusion.9, bf16[256,512]{1,0:T(8,128)(2,1)S(1)} %copy-done.1), kind=kOutput, calls=%fused_computation.5 | convolution fusion | flops 270531584 | bytes 5509120 | tf_op jit(solution)/shard_map/hqd,hkd->hqk/dot_general | solution.py:17
  73.4 1.7 %collective-permute-done.12 = bf16[2,4,1024,128]{3,2,1,0:T(8,128)(2,1)S(1)} collective-permute-done((bf16[2,4,1024,128]{3,2,1,0:T(8,128)(2,1)}, bf16[2,4,1024,128]{3,2,1,0:T(8,128)(2,1)S(1)}, u32[]{:S(2)}, u32[]{:S(2)}) %collective-permute-start.12) | collective-permute-done | bytes 2097184 | tf_op jit(solution)/shard_map/ppermute | solution.py:104
  75.1 0.7 bitcast_reduce_fusion
  75.9 2.3 %fusion.8 = f32[4,256,128]{2,1,0:T(8,128)S(1)} fusion(f32[4,1024,256]{2,1,0:T(8,128)S(1)} %get-tuple-element.60, f32[4,256]{1,0:T(4,128)S(1)} %get-tuple-element.23, bf16[2,4,1024,128]{3,2,1,0:T(8,128)(2,1)} %constant_dynamic-update-slice_fusion.9), kind=kOutput, calls=%fused_computation.14 | convolution fusion | flops 271581184 | bytes 5771264 | tf_op jit(solution)/shard_map/hqk,hkd->hqd/dot_general | solution.py:24
  78.2 1.4 fusion.2
  80.0 1.0 fusion.23
  81.0 1.1 fusion.47
  82.3 0.7 convolution_convert_fusion
  83.2 19.8 %all_to_all.20 = bf16[4,256,512]{2,1,0:T(8,128)(2,1)S(1)} all-to-all(bf16[4,256,512]{2,1,0:T(8,128)(2,1)S(1)} %bitcast.203), channel_id=1, replica_groups=mesh['seq'=64,'tensor'=4] {'tensor'}, dimensions={0} | all-to-all | bytes 2097152 | tf_op jit(solution)/shard_map/all_to_all | solution.py:58
  103.4 16.9 %all_to_all.21 = bf16[4,256,512]{1,2,0:T(8,128)(2,1)S(1)} all-to-all(bf16[4,256,512]{1,2,0:T(8,128)(2,1)S(1)} %broadcast_in_dim.83), channel_id=1, replica_groups=mesh['seq'=64,'tensor'=4] {'tensor'}, dimensions={0} | all-to-all | bytes 2097152 | tf_op jit(solution)/shard_map/all_to_all | solution.py:65
  120.7 0.7 fusion.13
  121.5 3.7 %fusion.27 = bf16[256,1024]{1,0:T(8,128)(2,1)S(1)} fusion(bf16[256,2048]{0,1:T(8,128)(2,1)S(1)} %fusion.13, bf16[2048,1024]{1,0:T(8,128)(2,1)S(1)} %copy-done.7, f32[1024]{0:T(1024)S(1)} %copy-done.11), kind=kOutput, calls=%fused_computation.42 | convolution fusion | flops 1091043328 | bytes 5771264 | tf_op jit(solution)/shard_map/dot_general | solution.py:189
  125.2 1.3 convolution_convert_fusion.1
  126.5 1.1 copy.167
  127.5 3.5 %all-to-all-start.3 = ((bf16[4,256,512]{2,1,0:T(8,128)(2,1)}), bf16[4,256,512]{2,1,0:T(8,128)(2,1)S(1)}, u32[]{:S(2)}, u32[]{:S(2)}) async-start(bf16[4,256,512]{2,1,0:T(8,128)(2,1)} %bitcast.201), calls=%async_computation.3 | async-start | bytes 2097152 | tf_op jit(solution)/shard_map/all_to_all | solution.py:58
  131.1 0.8 dynamic_slice.7
  131.8 12.6 %all-to-all-done.3 = bf16[4,256,512]{2,1,0:T(8,128)(2,1)S(1)} async-done(((bf16[4,256,512]{2,1,0:T(8,128)(2,1)}), bf16[4,256,512]{2,1,0:T(8,128)(2,1)S(1)}, u32[]{:S(2)}, u32[]{:S(2)}) %all-to-all-start.3) | async-done | bytes 1048608 | tf_op jit(solution)/shard_map/all_to_all | solution.py:58
  144.6 0.8 add_convert_fusion
  (75 shorter events, 9.9 us)
Async XLA Ops:
  0.0 82.3 %copy-start = (bf16[512,2048]{1,0:T(8,128)(2,1)S(1)}, bf16[512,2048]{1,0:T(8,128)(2,1)}, u32[]{:S(2)}) copy-start(bf16[512,2048]{1,0:T(8,128)(2,1)} %param.23) | copy-start | bytes 6291460
  1.6 23.9 %collective-permute-start = (bf16[2,4,32,128]{3,2,1,0:T(8,128)(2,1)}, bf16[2,4,32,128]{3,2,1,0:T(8,128)(2,1)}, u32[]{:S(2)}, u32[]{:S(2)}) collective-permute-start(bf16[2,4,32,128]{3,2,1,0:T(8,128)(2,1)} %bitcast_bitcast_fusion.13), channel_id=1, source_target_pairs={{0,32},{4,36},{8,40},{12,44},{16,48},{20,52},{24,56},{28,60},{32,6... | collective-permute-start | bytes 196616 | tf_op jit(solution)/shard_map/ppermute | solution.py:86
  3.5 23.5 %collective-permute-start.1 = (bf16[2,4,32,128]{3,2,1,0:T(8,128)(2,1)}, bf16[2,4,32,128]{3,2,1,0:T(8,128)(2,1)S(1)}, u32[]{:S(2)}, u32[]{:S(2)}) collective-permute-start(bf16[2,4,32,128]{3,2,1,0:T(8,128)(2,1)} %bitcast_bitcast_fusion.13), channel_id=1, source_target_pairs={{0,224},{4,228},{8,232},{12,236},{16,240},{20,244},{24,248},{28,25... | collective-permute-start | bytes 196616 | tf_op jit(solution)/shard_map/ppermute | solution.py:87
  9.8 11.8 %copy-start.2 = (bf16[2,32,512]{2,1,0:T(8,128)(2,1)S(1)}, bf16[2,32,512]{2,1,0:T(8,128)(2,1)}, u32[]{:S(2)}) copy-start(bf16[2,32,512]{2,1,0:T(8,128)(2,1)} %param.22) | copy-start | bytes 196612
  9.8 12.5 %copy-start.12 = (s32[64]{0:T(128)S(1)}, s32[64]{0:T(128)}, u32[]{:S(2)}) copy-start(s32[64]{0:T(128)} %param.31) | copy-start | bytes 772
  10.9 13.8 %copy-start.1 = (bf16[256,512]{1,0:T(8,128)(2,1)S(1)}, bf16[256,512]{1,0:T(8,128)(2,1)}, u32[]{:S(2)}) copy-start(bf16[256,512]{1,0:T(8,128)(2,1)} %param.17) | copy-start | bytes 786436
  11.2 13.7 %copy-start.9 = (bf16[256,512]{1,0:T(8,128)(2,1)S(1)}, bf16[256,512]{1,0:T(8,128)(2,1)}, u32[]{:S(2)}) copy-start(bf16[256,512]{1,0:T(8,128)(2,1)} %param.18) | copy-start | bytes 786436
  12.3 58.5 %all-to-all-start = ((bf16[64,2,4,4,128]{4,2,3,1,0:T(4,128)(2,1)}), bf16[64,2,4,4,128]{4,2,3,1,0:T(4,128)(2,1)S(1)}, u32[]{:S(2)}, u32[]{:S(2)}) async-start(bf16[64,2,4,4,128]{4,2,3,1,0:T(4,128)(2,1)} %bitcast.3), calls=%async_computation | async-start | bytes 1048576 | tf_op jit(solution)/shard_map/all_to_all | solution.py:139
  22.4 6.5 %copy-start.6 = (bf16[2,4,256,128]{3,2,1,0:T(8,128)(2,1)S(1)}, bf16[2,4,256,128]{3,2,1,0:T(8,128)(2,1)}, u32[]{:S(2)}) copy-start(bf16[2,4,256,128]{3,2,1,0:T(8,128)(2,1)} %get-tuple-element.40) | copy-start | bytes 1572868
  24.9 26.8 %copy-start.10 = (bf16[256,512]{1,0:T(8,128)(2,1)S(1)}, bf16[256,512]{1,0:T(8,128)(2,1)}, u32[]{:S(2)}) copy-start(bf16[256,512]{1,0:T(8,128)(2,1)} %param.19) | copy-start | bytes 786436
  25.5 12.2 %collective-permute-start.2 = (bf16[2,4,32,128]{3,2,1,0:T(8,128)(2,1)}, bf16[2,4,32,128]{3,2,1,0:T(8,128)(2,1)S(1)}, u32[]{:S(2)}, u32[]{:S(2)}) collective-permute-start(bf16[2,4,32,128]{3,2,1,0:T(8,128)(2,1)} %collective-permute-done), channel_id=1, source_target_pairs={{0,32},{4,36},{8,40},{12,44},{16,48},{20,52},{24,56},{28,60},{32,6... | collective-permute-start | bytes 196616 | tf_op jit(solution)/shard_map/ppermute | solution.py:86
  27.0 10.7 %collective-permute-start.3 = (bf16[2,4,32,128]{3,2,1,0:T(8,128)(2,1)S(1)}, bf16[2,4,32,128]{3,2,1,0:T(8,128)(2,1)S(1)}, u32[]{:S(2)}, u32[]{:S(2)}) collective-permute-start(bf16[2,4,32,128]{3,2,1,0:T(8,128)(2,1)S(1)} %collective-permute-done.1), channel_id=1, source_target_pairs={{0,224},{4,228},{8,232},{12,236},{16,240},{20,244},{24,248},{28,25... | collective-permute-start | bytes 196616 | tf_op jit(solution)/shard_map/ppermute | solution.py:87
  37.7 5.5 %collective-permute-start.4 = (bf16[2,4,32,128]{3,2,1,0:T(8,128)(2,1)S(1)}, bf16[2,4,32,128]{3,2,1,0:T(8,128)(2,1)S(1)}, u32[]{:S(2)}, u32[]{:S(2)}) collective-permute-start(bf16[2,4,32,128]{3,2,1,0:T(8,128)(2,1)S(1)} %collective-permute-done.2), channel_id=1, source_target_pairs={{0,32},{4,36},{8,40},{12,44},{16,48},{20,52},{24,56},{28,60},{32,6... | collective-permute-start | bytes 196616 | tf_op jit(solution)/shard_map/ppermute | solution.py:86
  37.7 5.5 %collective-permute-start.5 = (bf16[2,4,32,128]{3,2,1,0:T(8,128)(2,1)S(1)}, bf16[2,4,32,128]{3,2,1,0:T(8,128)(2,1)S(1)}, u32[]{:S(2)}, u32[]{:S(2)}) collective-permute-start(bf16[2,4,32,128]{3,2,1,0:T(8,128)(2,1)S(1)} %collective-permute-done.3), channel_id=1, source_target_pairs={{0,224},{4,228},{8,232},{12,236},{16,240},{20,244},{24,248},{28,25... | collective-permute-start | bytes 196616 | tf_op jit(solution)/shard_map/ppermute | solution.py:87
  43.2 5.1 %collective-permute-start.6 = (bf16[2,4,16,128]{3,2,1,0:T(8,128)(2,1)S(1)}, bf16[2,4,16,128]{3,2,1,0:T(8,128)(2,1)S(1)}, u32[]{:S(2)}, u32[]{:S(2)}) collective-permute-start(bf16[2,4,16,128]{3,2,1,0:T(8,128)(2,1)S(1)} %slice.52), channel_id=1, source_target_pairs={{0,32},{4,36},{8,40},{12,44},{16,48},{20,52},{24,56},{28,60},{32,6... | collective-permute-start | bytes 98312 | tf_op jit(solution)/shard_map/ppermute | solution.py:91
  43.2 5.7 %collective-permute-start.7 = (bf16[2,4,16,128]{3,2,1,0:T(8,128)(2,1)S(1)}, bf16[2,4,16,128]{3,2,1,0:T(8,128)(2,1)S(1)}, u32[]{:S(2)}, u32[]{:S(2)}) collective-permute-start(bf16[2,4,16,128]{3,2,1,0:T(8,128)(2,1)S(1)} %slice.53), channel_id=1, source_target_pairs={{0,224},{4,228},{8,232},{12,236},{16,240},{20,244},{24,248},{28,25... | collective-permute-start | bytes 98312 | tf_op jit(solution)/shard_map/ppermute | solution.py:92
  49.6 11.8 %collective-permute-start.8 = (bf16[2,4,256,128]{3,2,1,0:T(8,128)(2,1)S(1)}, bf16[2,4,256,128]{3,2,1,0:T(8,128)(2,1)S(1)}, u32[]{:S(2)}, u32[]{:S(2)}) collective-permute-start(bf16[2,4,256,128]{3,2,1,0:T(8,128)(2,1)S(1)} %get-tuple-element.42), channel_id=1, source_target_pairs={{0,8},{4,12},{8,16},{12,20},{16,24},{20,28},{24,0},{28,4},{32,40},... | collective-permute-start | bytes 1572872 | tf_op jit(solution)/shard_map/ppermute | solution.py:86
  51.2 12.3 %collective-permute-start.9 = (bf16[2,4,256,128]{3,2,1,0:T(8,128)(2,1)S(1)}, bf16[2,4,256,128]{3,2,1,0:T(8,128)(2,1)S(1)}, u32[]{:S(2)}, u32[]{:S(2)}) collective-permute-start(bf16[2,4,256,128]{3,2,1,0:T(8,128)(2,1)S(1)} %get-tuple-element.42), channel_id=1, source_target_pairs={{0,24},{4,28},{8,0},{12,4},{16,8},{20,12},{24,16},{28,20},{32,56},... | collective-permute-start | bytes 1572872 | tf_op jit(solution)/shard_map/ppermute | solution.py:87
  61.4 6.6 %collective-permute-start.10 = (bf16[2,4,128,128]{3,2,1,0:T(8,128)(2,1)S(1)}, bf16[2,4,128,128]{3,2,1,0:T(8,128)(2,1)S(1)}, u32[]{:S(2)}, u32[]{:S(2)}) collective-permute-start(bf16[2,4,128,128]{3,2,1,0:T(8,128)(2,1)S(1)} %slice.54), channel_id=1, source_target_pairs={{0,8},{4,12},{8,16},{12,20},{16,24},{20,28},{24,0},{28,4},{32,40},... | collective-permute-start | bytes 786440 | tf_op jit(solution)/shard_map/ppermute | solution.py:91
  63.5 6.4 %collective-permute-start.11 = (bf16[2,4,128,128]{3,2,1,0:T(8,128)(2,1)S(1)}, bf16[2,4,128,128]{3,2,1,0:T(8,128)(2,1)S(1)}, u32[]{:S(2)}, u32[]{:S(2)}) collective-permute-start(bf16[2,4,128,128]{3,2,1,0:T(8,128)(2,1)S(1)} %slice.55), channel_id=1, source_target_pairs={{0,24},{4,28},{8,0},{12,4},{16,8},{20,12},{24,16},{28,20},{32,56},... | collective-permute-start | bytes 786440 | tf_op jit(solution)/shard_map/ppermute | solution.py:92
  70.8 4.4 %collective-permute-start.12 = (bf16[2,4,1024,128]{3,2,1,0:T(8,128)(2,1)}, bf16[2,4,1024,128]{3,2,1,0:T(8,128)(2,1)S(1)}, u32[]{:S(2)}, u32[]{:S(2)}) collective-permute-start(bf16[2,4,1024,128]{3,2,1,0:T(8,128)(2,1)} %constant_dynamic-update-slice_fusion.9), channel_id=1, source_target_pairs={{0,4},{4,0},{8,12},{12,8},{16,20},{20,16},{24,28},{28,24},{32,36},... | collective-permute-start | bytes 6291464 | tf_op jit(solution)/shard_map/ppermute | solution.py:104
  83.2 19.9 %copy-start.3 = (bf16[256,512]{1,0:T(8,128)(2,1)S(1)}, bf16[256,512]{1,0:T(8,128)(2,1)}, u32[]{:S(2)}) copy-start(bf16[256,512]{1,0:T(8,128)(2,1)} %param.16) | copy-start | bytes 786436
  103.3 17.4 %copy-start.4 = (f32[2048]{0:T(1024)S(1)}, f32[2048]{0:T(1024)}, u32[]{:S(2)}) copy-start(f32[2048]{0:T(1024)} %param.25) | copy-start | bytes 24580
  103.3 17.4 %copy-start.5 = (f32[2048]{0:T(1024)S(1)}, f32[2048]{0:T(1024)}, u32[]{:S(2)}) copy-start(f32[2048]{0:T(1024)} %param.24) | copy-start | bytes 24580
  103.4 18.0 %copy-start.7 = (bf16[2048,1024]{1,0:T(8,128)(2,1)S(1)}, bf16[2048,1024]{1,0:T(8,128)(2,1)}, u32[]{:S(2)}) copy-start(bf16[2048,1024]{1,0:T(8,128)(2,1)} %param.26) | copy-start | bytes 12582916
  120.4 1.1 copy-start.11
  121.5 3.7 %copy-start.8 = (bf16[1024,2048]{1,0:T(8,128)(2,1)S(1)}, bf16[1024,2048]{1,0:T(8,128)(2,1)}, u32[]{:S(2)}) copy-start(bf16[1024,2048]{1,0:T(8,128)(2,1)} %param.28) | copy-start | bytes 12582916
  127.5 16.9 %all-to-all-start.3 = ((bf16[4,256,512]{2,1,0:T(8,128)(2,1)}), bf16[4,256,512]{2,1,0:T(8,128)(2,1)S(1)}, u32[]{:S(2)}, u32[]{:S(2)}) async-start(bf16[4,256,512]{2,1,0:T(8,128)(2,1)} %bitcast.201), calls=%async_computation.3 | async-start | bytes 2097152 | tf_op jit(solution)/shard_map/all_to_all | solution.py:58

commit v10 on v8

--- a/solution.py
+++ b/solution.py
@@ -8,7 +8,7 @@
 
 NEGATIVE_FILL = -1e30
 NORM_EPSILON = 1e-05
-BLOCK_KEYS = 2048
+BLOCK_KEYS = 1024
 
 
 def attend(running, query_heads, key_heads, value_heads, allowed):

time: 145 us -> 146 us (level)
    dot_general x4 -> x5, matrix products: 3.62 us -> 3.88 us  [attend(): jnp.einsum('hqk,hkd->hqd', weights.astype(jnp.bfloat16), value_heads, pre...]
where the time goes in v10:
time: 146 us; the launch traced here: 145 us
  blocking collectives  36.7 us (25%)
  waiting for transfers between devices  35.2 us (24%)
  starting transfers between devices  33 us (23%)
  local copies, waits for them, and re-layouts  21.2 us (15%)
  matrix products  12 us (8%)
  other arithmetic  6.59 us (5%)
    all_to_all x1, blocking collectives, tensor_sum_scatter(): arrived = lax.all_to_all(pieces, 'tensor', 0, 0, tiled=True)  19.8 us
    all_to_all x1, blocking collectives, tensor_gather(): arrived = lax.all_to_all(copies, 'tensor', 0, 0, tiled=True)  16.9 us
    ppermute x4, waiting for transfers between devices, ring_along(): from_below = lax.ppermute(from_below, 'seq', up)  16.7 us
    all_to_all x1, waiting for transfers between devices, tensor_sum_scatter(): arrived = lax.all_to_all(pieces, 'tensor', 0, 0, tiled=True)  12.6 us
    unnamed x38, local copies, waits for them, and re-layouts  10.6 us
    ppermute x4, starting transfers between devices, ring_along(): from_above = lax.ppermute(from_above, 'seq', down)  9.51 us
    all_to_all x1, starting transfers between devices, per_device(): arrived = lax.all_to_all(picked, 'seq', 0, 0, tiled=True)  9.39 us
    ppermute x4, starting transfers between devices, ring_along(): from_below = lax.ppermute(from_below, 'seq', up)  5.01 us
  transfers between devices with their start and end apart: 15, of which 8 were waited for; matrix products, arithmetic and copies ran while one was open for 15% of the time, Pallas kernels for 0%

profile of v10, /device:TPU:2, one launch (start us, length us, event | category | flops | bytes accessed | tf_op | source)
XLA Modules:
  0.0 145.2 jit_solution(3269679416303417151)
XLA Ops:
  0.0 1.6 %bitcast_bitcast_fusion.13 = bf16[2,4,32,128]{3,2,1,0:T(8,128)(2,1)} fusion(bf16[2,32,512]{2,1,0:T(8,128)(2,1)} %param.22), kind=kLoop, calls=%fused_computation.104 | loop fusion | bytes 131072 | tf_op jit(solution)/shard_map/transpose | solution.py:50
  1.6 1.9 %collective-permute-start = (bf16[2,4,32,128]{3,2,1,0:T(8,128)(2,1)}, bf16[2,4,32,128]{3,2,1,0:T(8,128)(2,1)}, u32[]{:S(2)}, u32[]{:S(2)}) collective-permute-start(bf16[2,4,32,128]{3,2,1,0:T(8,128)(2,1)} %bitcast_bitcast_fusion.13), channel_id=1, source_target_pairs={{0,32},{4,36},{8,40},{12,44},{16,48},{20,52},{24,56},{28,60},{32,6... | collective-permute-start | bytes 196616 | tf_op jit(solution)/shard_map/ppermute | solution.py:86
  3.5 3.9 %collective-permute-start.1 = (bf16[2,4,32,128]{3,2,1,0:T(8,128)(2,1)}, bf16[2,4,32,128]{3,2,1,0:T(8,128)(2,1)S(1)}, u32[]{:S(2)}, u32[]{:S(2)}) collective-permute-start(bf16[2,4,32,128]{3,2,1,0:T(8,128)(2,1)} %bitcast_bitcast_fusion.13), channel_id=1, source_target_pairs={{0,224},{4,228},{8,232},{12,236},{16,240},{20,244},{24,248},{28,25... | collective-permute-start | bytes 196616 | tf_op jit(solution)/shard_map/ppermute | solution.py:87
  8.2 0.7 compare_and_fusion
  8.8 1.0 copy.72
  9.9 1.0 gather_fusion
  11.2 1.0 reshape.141
  12.2 9.4 %all-to-all-start = ((bf16[64,2,4,4,128]{4,2,3,1,0:T(4,128)(2,1)}), bf16[64,2,4,4,128]{4,2,3,1,0:T(4,128)(2,1)S(1)}, u32[]{:S(2)}, u32[]{:S(2)}) async-start(bf16[64,2,4,4,128]{4,2,3,1,0:T(4,128)(2,1)} %bitcast.3), calls=%async_computation | async-start | bytes 1048576 | tf_op jit(solution)/shard_map/all_to_all | solution.py:139
  21.6 0.7 constant_dynamic-update-slice_fusion.8
  23.6 0.9 bitcast_bitcast_fusion.12
  25.4 1.5 %collective-permute-start.2 = (bf16[2,4,32,128]{3,2,1,0:T(8,128)(2,1)}, bf16[2,4,32,128]{3,2,1,0:T(8,128)(2,1)S(1)}, u32[]{:S(2)}, u32[]{:S(2)}) collective-permute-start(bf16[2,4,32,128]{3,2,1,0:T(8,128)(2,1)} %collective-permute-done), channel_id=1, source_target_pairs={{0,32},{4,36},{8,40},{12,44},{16,48},{20,52},{24,56},{28,60},{32,6... | collective-permute-start | bytes 196616 | tf_op jit(solution)/shard_map/ppermute | solution.py:86
  26.9 1.8 %collective-permute-start.3 = (bf16[2,4,32,128]{3,2,1,0:T(8,128)(2,1)S(1)}, bf16[2,4,32,128]{3,2,1,0:T(8,128)(2,1)S(1)}, u32[]{:S(2)}, u32[]{:S(2)}) collective-permute-start(bf16[2,4,32,128]{3,2,1,0:T(8,128)(2,1)S(1)} %collective-permute-done.1), channel_id=1, source_target_pairs={{0,224},{4,228},{8,232},{12,236},{16,240},{20,244},{24,248},{28,25... | collective-permute-start | bytes 196616 | tf_op jit(solution)/shard_map/ppermute | solution.py:87
  28.7 1.5 %constant_dynamic-update-slice_fusion.7 = (bf16[2,4,256,128]{3,2,1,0:T(8,128)(2,1)S(1)}, bf16[2,4,1024,128]{3,2,1,0:T(8,128)(2,1)}) fusion(bf16[2,4,256,128]{3,2,1,0:T(8,128)(2,1)S(1)} %copy-done.6, bf16[2,4,32,128]{3,2,1,0:T(8,128)(2,1)} %collective-permute-done, bf16[2,4,1024,128]{3,2,1,0:T(8,128)(2,1)} %get-tuple-element.43), kind=kLoop, calls=%fused_computation.114 | loop fusion | bytes 196608
  30.9 6.8 %collective-permute-done.2 = bf16[2,4,32,128]{3,2,1,0:T(8,128)(2,1)S(1)} collective-permute-done((bf16[2,4,32,128]{3,2,1,0:T(8,128)(2,1)}, bf16[2,4,32,128]{3,2,1,0:T(8,128)(2,1)S(1)}, u32[]{:S(2)}, u32[]{:S(2)}) %collective-permute-start.2) | collective-permute-done | bytes 65568 | tf_op jit(solution)/shard_map/ppermute | solution.py:86
  37.7 3.2 %collective-permute-start.5 = (bf16[2,4,32,128]{3,2,1,0:T(8,128)(2,1)S(1)}, bf16[2,4,32,128]{3,2,1,0:T(8,128)(2,1)S(1)}, u32[]{:S(2)}, u32[]{:S(2)}) collective-permute-start(bf16[2,4,32,128]{3,2,1,0:T(8,128)(2,1)S(1)} %collective-permute-done.3), channel_id=1, source_target_pairs={{0,224},{4,228},{8,232},{12,236},{16,240},{20,244},{24,248},{28,25... | collective-permute-start | bytes 196616 | tf_op jit(solution)/shard_map/ppermute | solution.py:87
  41.0 0.7 constant_dynamic-update-slice_fusion.5
  41.7 0.7 constant_dynamic-update-slice_fusion.4
  42.3 0.9 collective-permute-done.4
  43.2 3.2 %collective-permute-start.7 = (bf16[2,4,16,128]{3,2,1,0:T(8,128)(2,1)S(1)}, bf16[2,4,16,128]{3,2,1,0:T(8,128)(2,1)S(1)}, u32[]{:S(2)}, u32[]{:S(2)}) collective-permute-start(bf16[2,4,16,128]{3,2,1,0:T(8,128)(2,1)S(1)} %slice.61), channel_id=1, source_target_pairs={{0,224},{4,228},{8,232},{12,236},{16,240},{20,244},{24,248},{28,25... | collective-permute-start | bytes 98312 | tf_op jit(solution)/shard_map/ppermute | solution.py:92
  46.4 0.7 constant_dynamic-update-slice_fusion.3
  47.1 0.7 constant_dynamic-update-slice_fusion.2
  49.6 1.5 %collective-permute-start.8 = (bf16[2,4,256,128]{3,2,1,0:T(8,128)(2,1)S(1)}, bf16[2,4,256,128]{3,2,1,0:T(8,128)(2,1)S(1)}, u32[]{:S(2)}, u32[]{:S(2)}) collective-permute-start(bf16[2,4,256,128]{3,2,1,0:T(8,128)(2,1)S(1)} %get-tuple-element.44), channel_id=1, source_target_pairs={{0,8},{4,12},{8,16},{12,20},{16,24},{20,28},{24,0},{28,4},{32,40},... | collective-permute-start | bytes 1572872 | tf_op jit(solution)/shard_map/ppermute | solution.py:86
  52.3 9.0 %collective-permute-done.8 = bf16[2,4,256,128]{3,2,1,0:T(8,128)(2,1)S(1)} collective-permute-done((bf16[2,4,256,128]{3,2,1,0:T(8,128)(2,1)S(1)}, bf16[2,4,256,128]{3,2,1,0:T(8,128)(2,1)S(1)}, u32[]{:S(2)}, u32[]{:S(2)}) %collective-permute-start.8) | collective-permute-done | bytes 524320 | tf_op jit(solution)/shard_map/ppermute | solution.py:86
  61.4 1.8 %collective-permute-start.10 = (bf16[2,4,128,128]{3,2,1,0:T(8,128)(2,1)S(1)}, bf16[2,4,128,128]{3,2,1,0:T(8,128)(2,1)S(1)}, u32[]{:S(2)}, u32[]{:S(2)}) collective-permute-start(bf16[2,4,128,128]{3,2,1,0:T(8,128)(2,1)S(1)} %slice.62), channel_id=1, source_target_pairs={{0,8},{4,12},{8,16},{12,20},{16,24},{20,28},{24,0},{28,4},{32,40},... | collective-permute-start | bytes 786440 | tf_op jit(solution)/shard_map/ppermute | solution.py:91
  64.1 0.9 constant_dynamic-update-slice_fusion.12
  65.0 0.9 constant_dynamic-update-slice_fusion.11
  65.9 2.1 %collective-permute-done.10 = bf16[2,4,128,128]{3,2,1,0:T(8,128)(2,1)S(1)} collective-permute-done((bf16[2,4,128,128]{3,2,1,0:T(8,128)(2,1)S(1)}, bf16[2,4,128,128]{3,2,1,0:T(8,128)(2,1)S(1)}, u32[]{:S(2)}, u32[]{:S(2)}) %collective-permute-start.10) | collective-permute-done | bytes 262176 | tf_op jit(solution)/shard_map/ppermute | solution.py:91
  68.0 0.7 constant_dynamic-update-slice_fusion.10
  68.7 1.2 collective-permute-done.11
  70.0 0.8 constant_dynamic-update-slice_fusion.9
  71.0 1.7 %constant_dynamic-update-slice_fusion.23 = bf16[2,4,2048,128]{3,2,1,0:T(8,128)(2,1)S(1)} fusion(bf16[2,4,1024,128]{3,2,1,0:T(8,128)(2,1)} %constant_dynamic-update-slice_fusion.9), kind=kLoop, calls=%fused_computation.130 | loop fusion | bytes 4194304
  73.2 1.9 %collective-permute-done.12 = bf16[2,4,1024,128]{3,2,1,0:T(8,128)(2,1)S(1)} collective-permute-done((bf16[2,4,1024,128]{3,2,1,0:T(8,128)(2,1)}, bf16[2,4,1024,128]{3,2,1,0:T(8,128)(2,1)S(1)}, u32[]{:S(2)}, u32[]{:S(2)}) %collective-permute-start.12) | collective-permute-done | bytes 2097184 | tf_op jit(solution)/shard_map/ppermute | solution.py:104
  75.7 0.7 bitcast_reduce_fusion
  76.4 0.7 bitcast_reduce_fusion.1
  77.9 1.1 fusion.6
  79.0 1.4 fusion.2
  80.4 1.6 %fusion.56 = bf16[256,4,128]{2,0,1:T(8,128)(2,1)S(1)} fusion(f32[4,256,128]{2,1,0:T(8,128)S(1)} %fusion.6, bf16[4,2048,128]{2,1,0:T(8,128)(2,1)S(1)} %get-tuple-element.26, f32[4,1024,256]{2,1,0:T(8,128)S(1)} %get-tuple-element.60, f32[4,256]{1,0:T(4,128)S(1)} %get-tuple-element.22, f32[4,256,128]{2,1,0:T(8,128)S(1)} %fusion.66, ...), kind=kOutput, calls=%fused_computation.73 | convolution fusion | flops 272629760 | bytes 7098368 | tf_op jit(solution)/shard_map/hqk,hkd->hqd/dot_general | solution.py:24
  82.1 0.7 convolution_convert_fusion
  83.0 19.8 %all_to_all.20 = bf16[4,256,512]{2,1,0:T(8,128)(2,1)S(1)} all-to-all(bf16[4,256,512]{2,1,0:T(8,128)(2,1)S(1)} %bitcast.189), channel_id=1, replica_groups=mesh['seq'=64,'tensor'=4] {'tensor'}, dimensions={0} | all-to-all | bytes 2097152 | tf_op jit(solution)/shard_map/all_to_all | solution.py:58
  103.3 16.9 %all_to_all.21 = bf16[4,256,512]{1,2,0:T(8,128)(2,1)S(1)} all-to-all(bf16[4,256,512]{1,2,0:T(8,128)(2,1)S(1)} %broadcast_in_dim.83), channel_id=1, replica_groups=mesh['seq'=64,'tensor'=4] {'tensor'}, dimensions={0} | all-to-all | bytes 2097152 | tf_op jit(solution)/shard_map/all_to_all | solution.py:65
  120.6 0.7 fusion.13
  121.3 3.7 %fusion.32 = bf16[256,1024]{1,0:T(8,128)(2,1)S(1)} fusion(bf16[256,2048]{0,1:T(8,128)(2,1)S(1)} %fusion.13, bf16[2048,1024]{1,0:T(8,128)(2,1)S(1)} %copy-done.7, f32[1024]{0:T(1024)S(1)} %copy-done.11), kind=kOutput, calls=%fused_computation.44 | convolution fusion | flops 1091043328 | bytes 5771264 | tf_op jit(solution)/shard_map/dot_general | solution.py:187
  125.0 1.3 convolution_convert_fusion.1
  126.3 1.1 copy.167
  127.4 3.5 %all-to-all-start.3 = ((bf16[4,256,512]{2,1,0:T(8,128)(2,1)}), bf16[4,256,512]{2,1,0:T(8,128)(2,1)S(1)}, u32[]{:S(2)}, u32[]{:S(2)}) async-start(bf16[4,256,512]{2,1,0:T(8,128)(2,1)} %bitcast.187), calls=%async_computation.3 | async-start | bytes 2097152 | tf_op jit(solution)/shard_map/all_to_all | solution.py:58
  130.9 0.8 dynamic_slice.7
  131.7 12.6 %all-to-all-done.3 = bf16[4,256,512]{2,1,0:T(8,128)(2,1)S(1)} async-done(((bf16[4,256,512]{2,1,0:T(8,128)(2,1)}), bf16[4,256,512]{2,1,0:T(8,128)(2,1)S(1)}, u32[]{:S(2)}, u32[]{:S(2)}) %all-to-all-start.3) | async-done | bytes 1048608 | tf_op jit(solution)/shard_map/all_to_all | solution.py:58
  144.4 0.8 add_convert_fusion
  (78 shorter events, 10.8 us)
Async XLA Ops:
  0.0 82.1 %copy-start = (bf16[512,2048]{1,0:T(8,128)(2,1)S(1)}, bf16[512,2048]{1,0:T(8,128)(2,1)}, u32[]{:S(2)}) copy-start(bf16[512,2048]{1,0:T(8,128)(2,1)} %param.23) | copy-start | bytes 6291460
  1.6 23.7 %collective-permute-start = (bf16[2,4,32,128]{3,2,1,0:T(8,128)(2,1)}, bf16[2,4,32,128]{3,2,1,0:T(8,128)(2,1)}, u32[]{:S(2)}, u32[]{:S(2)}) collective-permute-start(bf16[2,4,32,128]{3,2,1,0:T(8,128)(2,1)} %bitcast_bitcast_fusion.13), channel_id=1, source_target_pairs={{0,32},{4,36},{8,40},{12,44},{16,48},{20,52},{24,56},{28,60},{32,6... | collective-permute-start | bytes 196616 | tf_op jit(solution)/shard_map/ppermute | solution.py:86
  3.5 23.4 %collective-permute-start.1 = (bf16[2,4,32,128]{3,2,1,0:T(8,128)(2,1)}, bf16[2,4,32,128]{3,2,1,0:T(8,128)(2,1)S(1)}, u32[]{:S(2)}, u32[]{:S(2)}) collective-permute-start(bf16[2,4,32,128]{3,2,1,0:T(8,128)(2,1)} %bitcast_bitcast_fusion.13), channel_id=1, source_target_pairs={{0,224},{4,228},{8,232},{12,236},{16,240},{20,244},{24,248},{28,25... | collective-permute-start | bytes 196616 | tf_op jit(solution)/shard_map/ppermute | solution.py:87
  9.8 11.8 %copy-start.2 = (bf16[2,32,512]{2,1,0:T(8,128)(2,1)S(1)}, bf16[2,32,512]{2,1,0:T(8,128)(2,1)}, u32[]{:S(2)}) copy-start(bf16[2,32,512]{2,1,0:T(8,128)(2,1)} %param.22) | copy-start | bytes 196612
  9.8 12.5 %copy-start.12 = (s32[64]{0:T(128)S(1)}, s32[64]{0:T(128)}, u32[]{:S(2)}) copy-start(s32[64]{0:T(128)} %param.31) | copy-start | bytes 772
  10.9 13.7 %copy-start.1 = (bf16[256,512]{1,0:T(8,128)(2,1)S(1)}, bf16[256,512]{1,0:T(8,128)(2,1)}, u32[]{:S(2)}) copy-start(bf16[256,512]{1,0:T(8,128)(2,1)} %param.17) | copy-start | bytes 786436
  11.2 13.5 %copy-start.9 = (bf16[256,512]{1,0:T(8,128)(2,1)S(1)}, bf16[256,512]{1,0:T(8,128)(2,1)}, u32[]{:S(2)}) copy-start(bf16[256,512]{1,0:T(8,128)(2,1)} %param.18) | copy-start | bytes 786436
  12.2 58.5 %all-to-all-start = ((bf16[64,2,4,4,128]{4,2,3,1,0:T(4,128)(2,1)}), bf16[64,2,4,4,128]{4,2,3,1,0:T(4,128)(2,1)S(1)}, u32[]{:S(2)}, u32[]{:S(2)}) async-start(bf16[64,2,4,4,128]{4,2,3,1,0:T(4,128)(2,1)} %bitcast.3), calls=%async_computation | async-start | bytes 1048576 | tf_op jit(solution)/shard_map/all_to_all | solution.py:139
  22.3 6.3 %copy-start.6 = (bf16[2,4,256,128]{3,2,1,0:T(8,128)(2,1)S(1)}, bf16[2,4,256,128]{3,2,1,0:T(8,128)(2,1)}, u32[]{:S(2)}) copy-start(bf16[2,4,256,128]{3,2,1,0:T(8,128)(2,1)} %get-tuple-element.42) | copy-start | bytes 1572868
  24.8 27.0 %copy-start.10 = (bf16[256,512]{1,0:T(8,128)(2,1)S(1)}, bf16[256,512]{1,0:T(8,128)(2,1)}, u32[]{:S(2)}) copy-start(bf16[256,512]{1,0:T(8,128)(2,1)} %param.19) | copy-start | bytes 786436
  25.4 12.3 %collective-permute-start.2 = (bf16[2,4,32,128]{3,2,1,0:T(8,128)(2,1)}, bf16[2,4,32,128]{3,2,1,0:T(8,128)(2,1)S(1)}, u32[]{:S(2)}, u32[]{:S(2)}) collective-permute-start(bf16[2,4,32,128]{3,2,1,0:T(8,128)(2,1)} %collective-permute-done), channel_id=1, source_target_pairs={{0,32},{4,36},{8,40},{12,44},{16,48},{20,52},{24,56},{28,60},{32,6... | collective-permute-start | bytes 196616 | tf_op jit(solution)/shard_map/ppermute | solution.py:86
  26.9 10.8 %collective-permute-start.3 = (bf16[2,4,32,128]{3,2,1,0:T(8,128)(2,1)S(1)}, bf16[2,4,32,128]{3,2,1,0:T(8,128)(2,1)S(1)}, u32[]{:S(2)}, u32[]{:S(2)}) collective-permute-start(bf16[2,4,32,128]{3,2,1,0:T(8,128)(2,1)S(1)} %collective-permute-done.1), channel_id=1, source_target_pairs={{0,224},{4,228},{8,232},{12,236},{16,240},{20,244},{24,248},{28,25... | collective-permute-start | bytes 196616 | tf_op jit(solution)/shard_map/ppermute | solution.py:87
  37.7 5.5 %collective-permute-start.4 = (bf16[2,4,32,128]{3,2,1,0:T(8,128)(2,1)S(1)}, bf16[2,4,32,128]{3,2,1,0:T(8,128)(2,1)S(1)}, u32[]{:S(2)}, u32[]{:S(2)}) collective-permute-start(bf16[2,4,32,128]{3,2,1,0:T(8,128)(2,1)S(1)} %collective-permute-done.2), channel_id=1, source_target_pairs={{0,32},{4,36},{8,40},{12,44},{16,48},{20,52},{24,56},{28,60},{32,6... | collective-permute-start | bytes 196616 | tf_op jit(solution)/shard_map/ppermute | solution.py:86
  37.7 5.5 %collective-permute-start.5 = (bf16[2,4,32,128]{3,2,1,0:T(8,128)(2,1)S(1)}, bf16[2,4,32,128]{3,2,1,0:T(8,128)(2,1)S(1)}, u32[]{:S(2)}, u32[]{:S(2)}) collective-permute-start(bf16[2,4,32,128]{3,2,1,0:T(8,128)(2,1)S(1)} %collective-permute-done.3), channel_id=1, source_target_pairs={{0,224},{4,228},{8,232},{12,236},{16,240},{20,244},{24,248},{28,25... | collective-permute-start | bytes 196616 | tf_op jit(solution)/shard_map/ppermute | solution.py:87
  43.2 5.1 %collective-permute-start.6 = (bf16[2,4,16,128]{3,2,1,0:T(8,128)(2,1)S(1)}, bf16[2,4,16,128]{3,2,1,0:T(8,128)(2,1)S(1)}, u32[]{:S(2)}, u32[]{:S(2)}) collective-permute-start(bf16[2,4,16,128]{3,2,1,0:T(8,128)(2,1)S(1)} %slice.60), channel_id=1, source_target_pairs={{0,32},{4,36},{8,40},{12,44},{16,48},{20,52},{24,56},{28,60},{32,6... | collective-permute-start | bytes 98312 | tf_op jit(solution)/shard_map/ppermute | solution.py:91
  43.2 5.7 %collective-permute-start.7 = (bf16[2,4,16,128]{3,2,1,0:T(8,128)(2,1)S(1)}, bf16[2,4,16,128]{3,2,1,0:T(8,128)(2,1)S(1)}, u32[]{:S(2)}, u32[]{:S(2)}) collective-permute-start(bf16[2,4,16,128]{3,2,1,0:T(8,128)(2,1)S(1)} %slice.61), channel_id=1, source_target_pairs={{0,224},{4,228},{8,232},{12,236},{16,240},{20,244},{24,248},{28,25... | collective-permute-start | bytes 98312 | tf_op jit(solution)/shard_map/ppermute | solution.py:92
  49.6 11.8 %collective-permute-start.8 = (bf16[2,4,256,128]{3,2,1,0:T(8,128)(2,1)S(1)}, bf16[2,4,256,128]{3,2,1,0:T(8,128)(2,1)S(1)}, u32[]{:S(2)}, u32[]{:S(2)}) collective-permute-start(bf16[2,4,256,128]{3,2,1,0:T(8,128)(2,1)S(1)} %get-tuple-element.44), channel_id=1, source_target_pairs={{0,8},{4,12},{8,16},{12,20},{16,24},{20,28},{24,0},{28,4},{32,40},... | collective-permute-start | bytes 1572872 | tf_op jit(solution)/shard_map/ppermute | solution.py:86
  51.2 12.3 %collective-permute-start.9 = (bf16[2,4,256,128]{3,2,1,0:T(8,128)(2,1)S(1)}, bf16[2,4,256,128]{3,2,1,0:T(8,128)(2,1)S(1)}, u32[]{:S(2)}, u32[]{:S(2)}) collective-permute-start(bf16[2,4,256,128]{3,2,1,0:T(8,128)(2,1)S(1)} %get-tuple-element.44), channel_id=1, source_target_pairs={{0,24},{4,28},{8,0},{12,4},{16,8},{20,12},{24,16},{28,20},{32,56},... | collective-permute-start | bytes 1572872 | tf_op jit(solution)/shard_map/ppermute | solution.py:87
  61.4 6.6 %collective-permute-start.10 = (bf16[2,4,128,128]{3,2,1,0:T(8,128)(2,1)S(1)}, bf16[2,4,128,128]{3,2,1,0:T(8,128)(2,1)S(1)}, u32[]{:S(2)}, u32[]{:S(2)}) collective-permute-start(bf16[2,4,128,128]{3,2,1,0:T(8,128)(2,1)S(1)} %slice.62), channel_id=1, source_target_pairs={{0,8},{4,12},{8,16},{12,20},{16,24},{20,28},{24,0},{28,4},{32,40},... | collective-permute-start | bytes 786440 | tf_op jit(solution)/shard_map/ppermute | solution.py:91
  63.5 6.4 %collective-permute-start.11 = (bf16[2,4,128,128]{3,2,1,0:T(8,128)(2,1)S(1)}, bf16[2,4,128,128]{3,2,1,0:T(8,128)(2,1)S(1)}, u32[]{:S(2)}, u32[]{:S(2)}) collective-permute-start(bf16[2,4,128,128]{3,2,1,0:T(8,128)(2,1)S(1)} %slice.63), channel_id=1, source_target_pairs={{0,24},{4,28},{8,0},{12,4},{16,8},{20,12},{24,16},{28,20},{32,56},... | collective-permute-start | bytes 786440 | tf_op jit(solution)/shard_map/ppermute | solution.py:92
  70.7 4.4 %collective-permute-start.12 = (bf16[2,4,1024,128]{3,2,1,0:T(8,128)(2,1)}, bf16[2,4,1024,128]{3,2,1,0:T(8,128)(2,1)S(1)}, u32[]{:S(2)}, u32[]{:S(2)}) collective-permute-start(bf16[2,4,1024,128]{3,2,1,0:T(8,128)(2,1)} %constant_dynamic-update-slice_fusion.9), channel_id=1, source_target_pairs={{0,4},{4,0},{8,12},{12,8},{16,20},{20,16},{24,28},{28,24},{32,36},... | collective-permute-start | bytes 6291464 | tf_op jit(solution)/shard_map/ppermute | solution.py:104
  83.0 20.0 %copy-start.3 = (bf16[256,512]{1,0:T(8,128)(2,1)S(1)}, bf16[256,512]{1,0:T(8,128)(2,1)}, u32[]{:S(2)}) copy-start(bf16[256,512]{1,0:T(8,128)(2,1)} %param.16) | copy-start | bytes 786436
  103.2 17.4 %copy-start.4 = (f32[2048]{0:T(1024)S(1)}, f32[2048]{0:T(1024)}, u32[]{:S(2)}) copy-start(f32[2048]{0:T(1024)} %param.25) | copy-start | bytes 24580
  103.2 17.4 %copy-start.5 = (f32[2048]{0:T(1024)S(1)}, f32[2048]{0:T(1024)}, u32[]{:S(2)}) copy-start(f32[2048]{0:T(1024)} %param.24) | copy-start | bytes 24580
  103.3 18.0 %copy-start.7 = (bf16[2048,1024]{1,0:T(8,128)(2,1)S(1)}, bf16[2048,1024]{1,0:T(8,128)(2,1)}, u32[]{:S(2)}) copy-start(bf16[2048,1024]{1,0:T(8,128)(2,1)} %param.26) | copy-start | bytes 12582916
  120.2 1.1 copy-start.11
  121.3 3.7 %copy-start.8 = (bf16[1024,2048]{1,0:T(8,128)(2,1)S(1)}, bf16[1024,2048]{1,0:T(8,128)(2,1)}, u32[]{:S(2)}) copy-start(bf16[1024,2048]{1,0:T(8,128)(2,1)} %param.28) | copy-start | bytes 12582916
  127.4 16.9 %all-to-all-start.3 = ((bf16[4,256,512]{2,1,0:T(8,128)(2,1)}), bf16[4,256,512]{2,1,0:T(8,128)(2,1)S(1)}, u32[]{:S(2)}, u32[]{:S(2)}) async-start(bf16[4,256,512]{2,1,0:T(8,128)(2,1)} %bitcast.187), calls=%async_computation.3 | async-start | bytes 2097152 | tf_op jit(solution)/shard_map/all_to_all | solution.py:58

commit v11 on v8

--- a/solution.py
+++ b/solution.py
@@ -99,8 +99,8 @@
     lanes = 4
     shape = (seq_size // (lanes * cores), lanes, cores)
     gathered = ring_along(block, shape, 0)
+    gathered, companion = lax.optimization_barrier((gathered, companion))
     gathered = ring_along(gathered, shape, 1)
-    gathered, companion = lax.optimization_barrier((gathered, companion))
     partner = lax.ppermute(gathered, "seq", shift_pairs(shape, 2, 1))
     return jnp.concatenate([gathered, partner], axis=2), companion
 

time: 145 us -> 143 us (0.986)
  local copies, waits for them, and re-layouts: 21.1 us -> 11.1 us
  waiting for transfers between devices: 35 us -> 39.9 us
  matrix products: 11.6 us -> 14.2 us
    unnamed x38 -> x34, local copies, waits for them, and re-layouts: 10.6 us -> 1.86 us
    ppermute x2, waiting for transfers between devices: 2.66 us -> 5.54 us  [ring_along(): first = lax.ppermute(from_below[:, :, :half], 'seq', up)]
    dot_general x4, matrix products: 3.62 us -> 5.38 us  [attend(): jnp.einsum('hqk,hkd->hqd', weights.astype(jnp.bfloat16), value_heads, pre...]
    ppermute x1, waiting for transfers between devices: 1.91 us -> 3.43 us  [ring_gather_seq(): partner = lax.ppermute(gathered, 'seq', shift_pairs(shape, 2, 1))]
  transfers between devices with their start and end apart: 15 -> 15, of which waited for: 8 -> 8; matrix products, arithmetic and copies ran while one was open for 15% -> 10% of each run, Pallas kernels for 0% -> 0%
where the time goes in v11:
time: 143 us; the launch traced here: 142 us
  waiting for transfers between devices  39.9 us (28%)
  blocking collectives  36.6 us (26%)
  starting transfers between devices  33.2 us (23%)
  matrix products  14.2 us (10%)
  local copies, waits for them, and re-layouts  11.1 us (8%)
  other arithmetic  6.65 us (5%)
    all_to_all x1, blocking collectives, tensor_sum_scatter(): arrived = lax.all_to_all(pieces, 'tensor', 0, 0, tiled=True)  19.7 us
    all_to_all x1, blocking collectives, tensor_gather(): arrived = lax.all_to_all(copies, 'tensor', 0, 0, tiled=True)  16.9 us
    ppermute x4, waiting for transfers between devices, ring_along(): from_below = lax.ppermute(from_below, 'seq', up)  16.8 us
    all_to_all x1, waiting for transfers between devices, tensor_sum_scatter(): arrived = lax.all_to_all(pieces, 'tensor', 0, 0, tiled=True)  12.6 us
    all_to_all x1, starting transfers between devices, per_device(): arrived = lax.all_to_all(picked, 'seq', 0, 0, tiled=True)  9.53 us
    ppermute x4, starting transfers between devices, ring_along(): from_above = lax.ppermute(from_above, 'seq', down)  9.43 us
    ppermute x2, waiting for transfers between devices, ring_along(): first = lax.ppermute(from_below[:, :, :half], 'seq', up)  5.54 us
    dot_general x4, matrix products, attend(): jnp.einsum('hqk,hkd->hqd', weights.astype(jnp.bfloat16), value_heads, pre...  5.38 us
  transfers between devices with their start and end apart: 15, of which 8 were waited for; matrix products, arithmetic and copies ran while one was open for 10% of the time, Pallas kernels for 0%

profile of v11, /device:TPU:2, one launch (start us, length us, event | category | flops | bytes accessed | tf_op | source)
XLA Modules:
  0.0 142.2 jit_solution(14988694846399468473)
XLA Ops:
  0.0 1.6 %bitcast_bitcast_fusion.12 = bf16[2,4,32,128]{3,2,1,0:T(8,128)(2,1)} fusion(bf16[2,32,512]{2,1,0:T(8,128)(2,1)} %param.22), kind=kLoop, calls=%fused_computation.88 | loop fusion | bytes 131072 | tf_op jit(solution)/shard_map/transpose | solution.py:50
  1.6 1.9 %collective-permute-start = (bf16[2,4,32,128]{3,2,1,0:T(8,128)(2,1)}, bf16[2,4,32,128]{3,2,1,0:T(8,128)(2,1)}, u32[]{:S(2)}, u32[]{:S(2)}) collective-permute-start(bf16[2,4,32,128]{3,2,1,0:T(8,128)(2,1)} %bitcast_bitcast_fusion.12), channel_id=1, source_target_pairs={{0,32},{4,36},{8,40},{12,44},{16,48},{20,52},{24,56},{28,60},{32,6... | collective-permute-start | bytes 196616 | tf_op jit(solution)/shard_map/ppermute | solution.py:86
  3.6 3.9 %collective-permute-start.1 = (bf16[2,4,32,128]{3,2,1,0:T(8,128)(2,1)}, bf16[2,4,32,128]{3,2,1,0:T(8,128)(2,1)S(1)}, u32[]{:S(2)}, u32[]{:S(2)}) collective-permute-start(bf16[2,4,32,128]{3,2,1,0:T(8,128)(2,1)} %bitcast_bitcast_fusion.12), channel_id=1, source_target_pairs={{0,224},{4,228},{8,232},{12,236},{16,240},{20,244},{24,248},{28,25... | collective-permute-start | bytes 196616 | tf_op jit(solution)/shard_map/ppermute | solution.py:87
  7.5 0.7 compare_select_fusion
  8.2 0.7 compare_and_fusion
  8.8 1.0 copy.63
  9.8 1.0 gather_fusion
  11.2 1.0 reshape.139
  12.2 9.5 %all-to-all-start = ((bf16[64,2,4,4,128]{4,2,3,1,0:T(4,128)(2,1)}), bf16[64,2,4,4,128]{4,2,3,1,0:T(4,128)(2,1)S(1)}, u32[]{:S(2)}, u32[]{:S(2)}) async-start(bf16[64,2,4,4,128]{4,2,3,1,0:T(4,128)(2,1)} %bitcast.3), calls=%async_computation | async-start | bytes 1048576 | tf_op jit(solution)/shard_map/all_to_all | solution.py:139
  21.8 0.6 dynamic_slice.6
  22.4 0.6 iota_compare_fusion.1
  23.1 0.9 bitcast_bitcast_fusion.11
  24.3 1.3 fusion.65
  25.9 1.5 %fusion.14 = f32[4,256,128]{2,1,0:T(8,128)S(1)} fusion(f32[4,256,256]{1,2,0:T(8,128)S(1)} %get-tuple-element.42, f32[4,256]{1,0:T(4,128)S(1)} %get-tuple-element.38, pred[256,256]{0,1:T(8,128)(4,1)S(1)} %fusion.51, f32[4,256]{1,0:T(4,128)S(1)} %get-tuple-element.23, f32[4,256]{1,0:T(4,128)S(1)} %get-tuple-element.36, bf16[256,512]{1,0:T(8,128)(2,1)} %param.19), kind=kOutput, calls=%fused_computation.30 | convolution fusion | flops 68157440 | bytes 1912832 | tf_op jit(solution)/shard_map/hqk,hkd->hqd/dot_general | solution.py:24
  27.4 1.1 convolution_add_fusion.1
  28.6 1.5 %collective-permute-start.2 = (bf16[2,4,32,128]{3,2,1,0:T(8,128)(2,1)}, bf16[2,4,32,128]{3,2,1,0:T(8,128)(2,1)S(1)}, u32[]{:S(2)}, u32[]{:S(2)}) collective-permute-start(bf16[2,4,32,128]{3,2,1,0:T(8,128)(2,1)} %collective-permute-done), channel_id=1, source_target_pairs={{0,32},{4,36},{8,40},{12,44},{16,48},{20,52},{24,56},{28,60},{32,6... | collective-permute-start | bytes 196616 | tf_op jit(solution)/shard_map/ppermute | solution.py:86
  30.1 1.8 %collective-permute-start.3 = (bf16[2,4,32,128]{3,2,1,0:T(8,128)(2,1)S(1)}, bf16[2,4,32,128]{3,2,1,0:T(8,128)(2,1)S(1)}, u32[]{:S(2)}, u32[]{:S(2)}) collective-permute-start(bf16[2,4,32,128]{3,2,1,0:T(8,128)(2,1)S(1)} %collective-permute-done.1), channel_id=1, source_target_pairs={{0,224},{4,228},{8,232},{12,236},{16,240},{20,244},{24,248},{28,25... | collective-permute-start | bytes 196616 | tf_op jit(solution)/shard_map/ppermute | solution.py:87
  31.9 0.9 constant_dynamic-update-slice_fusion.7
  32.8 5.1 %collective-permute-done.2 = bf16[2,4,32,128]{3,2,1,0:T(8,128)(2,1)S(1)} collective-permute-done((bf16[2,4,32,128]{3,2,1,0:T(8,128)(2,1)}, bf16[2,4,32,128]{3,2,1,0:T(8,128)(2,1)S(1)}, u32[]{:S(2)}, u32[]{:S(2)}) %collective-permute-start.2) | collective-permute-done | bytes 65568 | tf_op jit(solution)/shard_map/ppermute | solution.py:86
  37.8 3.2 %collective-permute-start.5 = (bf16[2,4,32,128]{3,2,1,0:T(8,128)(2,1)S(1)}, bf16[2,4,32,128]{3,2,1,0:T(8,128)(2,1)S(1)}, u32[]{:S(2)}, u32[]{:S(2)}) collective-permute-start(bf16[2,4,32,128]{3,2,1,0:T(8,128)(2,1)S(1)} %collective-permute-done.3), channel_id=1, source_target_pairs={{0,224},{4,228},{8,232},{12,236},{16,240},{20,244},{24,248},{28,25... | collective-permute-start | bytes 196616 | tf_op jit(solution)/shard_map/ppermute | solution.py:87
  41.1 2.2 %collective-permute-done.4 = bf16[2,4,32,128]{3,2,1,0:T(8,128)(2,1)S(1)} collective-permute-done((bf16[2,4,32,128]{3,2,1,0:T(8,128)(2,1)S(1)}, bf16[2,4,32,128]{3,2,1,0:T(8,128)(2,1)S(1)}, u32[]{:S(2)}, u32[]{:S(2)}) %collective-permute-start.4) | collective-permute-done | bytes 65568 | tf_op jit(solution)/shard_map/ppermute | solution.py:86
  43.3 3.2 %collective-permute-start.7 = (bf16[2,4,16,128]{3,2,1,0:T(8,128)(2,1)S(1)}, bf16[2,4,16,128]{3,2,1,0:T(8,128)(2,1)S(1)}, u32[]{:S(2)}, u32[]{:S(2)}) collective-permute-start(bf16[2,4,16,128]{3,2,1,0:T(8,128)(2,1)S(1)} %slice.45), channel_id=1, source_target_pairs={{0,224},{4,228},{8,232},{12,236},{16,240},{20,244},{24,248},{28,25... | collective-permute-start | bytes 98312 | tf_op jit(solution)/shard_map/ppermute | solution.py:92
  46.6 1.8 %collective-permute-done.6 = bf16[2,4,16,128]{3,2,1,0:T(8,128)(2,1)S(1)} collective-permute-done((bf16[2,4,16,128]{3,2,1,0:T(8,128)(2,1)S(1)}, bf16[2,4,16,128]{3,2,1,0:T(8,128)(2,1)S(1)}, u32[]{:S(2)}, u32[]{:S(2)}) %collective-permute-start.6) | collective-permute-done | bytes 32800 | tf_op jit(solution)/shard_map/ppermute | solution.py:91
  48.5 1.6 %collective-permute-start.8 = (bf16[2,4,256,128]{3,2,1,0:T(8,128)(2,1)S(1)}, bf16[2,4,256,128]{3,2,1,0:T(8,128)(2,1)S(1)}, u32[]{:S(2)}, u32[]{:S(2)}) collective-permute-start(bf16[2,4,256,128]{3,2,1,0:T(8,128)(2,1)S(1)} %constant_dynamic-update-slice_fusion), channel_id=1, source_target_pairs={{0,8},{4,12},{8,16},{12,20},{16,24},{20,28},{24,0},{28,4},{32,40},... | collective-permute-start | bytes 1572872 | tf_op jit(solution)/shard_map/ppermute | solution.py:86
  50.1 0.5 collective-permute-start.9
  50.8 9.6 %collective-permute-done.8 = bf16[2,4,256,128]{3,2,1,0:T(8,128)(2,1)S(1)} collective-permute-done((bf16[2,4,256,128]{3,2,1,0:T(8,128)(2,1)S(1)}, bf16[2,4,256,128]{3,2,1,0:T(8,128)(2,1)S(1)}, u32[]{:S(2)}, u32[]{:S(2)}) %collective-permute-start.8) | collective-permute-done | bytes 524320 | tf_op jit(solution)/shard_map/ppermute | solution.py:86
  60.4 1.8 %collective-permute-start.10 = (bf16[2,4,128,128]{3,2,1,0:T(8,128)(2,1)S(1)}, bf16[2,4,128,128]{3,2,1,0:T(8,128)(2,1)S(1)}, u32[]{:S(2)}, u32[]{:S(2)}) collective-permute-start(bf16[2,4,128,128]{3,2,1,0:T(8,128)(2,1)S(1)} %slice.50), channel_id=1, source_target_pairs={{0,8},{4,12},{8,16},{12,20},{16,24},{20,28},{24,0},{28,4},{32,40},... | collective-permute-start | bytes 786440 | tf_op jit(solution)/shard_map/ppermute | solution.py:91
  62.2 0.5 collective-permute-start.11
  63.3 3.7 %collective-permute-done.10 = bf16[2,4,128,128]{3,2,1,0:T(8,128)(2,1)S(1)} collective-permute-done((bf16[2,4,128,128]{3,2,1,0:T(8,128)(2,1)S(1)}, bf16[2,4,128,128]{3,2,1,0:T(8,128)(2,1)S(1)}, u32[]{:S(2)}, u32[]{:S(2)}) %collective-permute-start.10) | collective-permute-done | bytes 262176 | tf_op jit(solution)/shard_map/ppermute | solution.py:91
  67.1 1.5 %collective-permute-done.11 = bf16[2,4,128,128]{3,2,1,0:T(8,128)(2,1)S(1)} collective-permute-done((bf16[2,4,128,128]{3,2,1,0:T(8,128)(2,1)S(1)}, bf16[2,4,128,128]{3,2,1,0:T(8,128)(2,1)S(1)}, u32[]{:S(2)}, u32[]{:S(2)}) %collective-permute-start.11) | collective-permute-done | bytes 262176 | tf_op jit(solution)/shard_map/ppermute | solution.py:92
  69.2 0.4 fusion.67
  69.6 3.4 %collective-permute-done.12 = bf16[2,4,1024,128]{3,2,1,0:T(8,128)(2,1)S(1)} collective-permute-done((bf16[2,4,1024,128]{3,2,1,0:T(8,128)(2,1)S(1)}, bf16[2,4,1024,128]{3,2,1,0:T(8,128)(2,1)S(1)}, u32[]{:S(2)}, u32[]{:S(2)}) %collective-permute-start.12) | collective-permute-done | bytes 2097184 | tf_op jit(solution)/shard_map/ppermute | solution.py:104
  73.3 1.3 bitcast_reduce_fusion
  74.6 0.4 fusion.37
  75.0 0.4 fusion.42
  75.4 1.4 fusion.1
  76.8 2.4 %fusion.34 = bf16[256,4,128]{2,0,1:T(8,128)(2,1)S(1)} fusion(bf16[2,4,2048,128]{3,2,1,0:T(8,128)(2,1)S(1)} %constant_dynamic-update-slice_fusion.14, f32[4,2048,256]{2,1,0:T(8,128)S(1)} %get-tuple-element.46, f32[4,256]{1,0:T(4,128)S(1)} %get-tuple-element.20, f32[4,256,128]{2,1,0:T(8,128)S(1)} %fusion.42, f32[4,256,128]{2,1,0:T(8,128)S(1)} %copy-done.2, ...), kind=kOutput, calls=%fused_computation.58 | convolution fusion | flops 543948800 | bytes 11812864 | tf_op jit(solution)/shard_map/hqk,hkd->hqd/dot_general | solution.py:24
  79.4 0.7 convolution_convert_fusion
  80.2 19.7 %all_to_all.20 = bf16[4,256,512]{2,1,0:T(8,128)(2,1)S(1)} all-to-all(bf16[4,256,512]{2,1,0:T(8,128)(2,1)S(1)} %bitcast.174), channel_id=1, replica_groups=mesh['seq'=64,'tensor'=4] {'tensor'}, dimensions={0} | all-to-all | bytes 2097152 | tf_op jit(solution)/shard_map/all_to_all | solution.py:58
  100.3 16.9 %all_to_all.21 = bf16[4,256,512]{1,2,0:T(8,128)(2,1)S(1)} all-to-all(bf16[4,256,512]{1,2,0:T(8,128)(2,1)S(1)} %broadcast_in_dim.79), channel_id=1, replica_groups=mesh['seq'=64,'tensor'=4] {'tensor'}, dimensions={0} | all-to-all | bytes 2097152 | tf_op jit(solution)/shard_map/all_to_all | solution.py:65
  117.6 0.7 fusion.11
  118.4 3.7 %fusion.20 = bf16[256,1024]{1,0:T(8,128)(2,1)S(1)} fusion(bf16[256,2048]{0,1:T(8,128)(2,1)S(1)} %fusion.11, bf16[2048,1024]{1,0:T(8,128)(2,1)S(1)} %copy-done.7, f32[1024]{0:T(1024)S(1)} %copy-done.9), kind=kOutput, calls=%fused_computation.35 | convolution fusion | flops 1091043328 | bytes 5771264 | tf_op jit(solution)/shard_map/dot_general | solution.py:187
  122.1 1.3 convolution_convert_fusion.1
  123.4 1.0 copy.144
  124.4 3.5 %all-to-all-start.3 = ((bf16[4,256,512]{2,1,0:T(8,128)(2,1)}), bf16[4,256,512]{2,1,0:T(8,128)(2,1)S(1)}, u32[]{:S(2)}, u32[]{:S(2)}) async-start(bf16[4,256,512]{2,1,0:T(8,128)(2,1)} %bitcast.172), calls=%async_computation.3 | async-start | bytes 2097152 | tf_op jit(solution)/shard_map/all_to_all | solution.py:58
  127.9 0.8 dynamic_slice.7
  128.7 12.6 %all-to-all-done.3 = bf16[4,256,512]{2,1,0:T(8,128)(2,1)S(1)} async-done(((bf16[4,256,512]{2,1,0:T(8,128)(2,1)}), bf16[4,256,512]{2,1,0:T(8,128)(2,1)S(1)}, u32[]{:S(2)}, u32[]{:S(2)}) %all-to-all-start.3) | async-done | bytes 1048608 | tf_op jit(solution)/shard_map/all_to_all | solution.py:58
  141.4 0.8 add_convert_fusion
  (71 shorter events, 4.0 us)
Async XLA Ops:
  0.0 79.3 %copy-start = (bf16[512,2048]{1,0:T(8,128)(2,1)S(1)}, bf16[512,2048]{1,0:T(8,128)(2,1)}, u32[]{:S(2)}) copy-start(bf16[512,2048]{1,0:T(8,128)(2,1)} %param.23) | copy-start | bytes 6291460
  0.0 21.8 %copy-start.10 = (s32[64]{0:T(128)S(1)}, s32[64]{0:T(128)}, u32[]{:S(2)}) copy-start(s32[64]{0:T(128)} %param.31) | copy-start | bytes 772
  0.0 24.1 %copy-start.1 = (bf16[256,512]{1,0:T(8,128)(2,1)S(1)}, bf16[256,512]{1,0:T(8,128)(2,1)}, u32[]{:S(2)}) copy-start(bf16[256,512]{1,0:T(8,128)(2,1)} %param.17) | copy-start | bytes 786436
  1.6 26.9 %collective-permute-start = (bf16[2,4,32,128]{3,2,1,0:T(8,128)(2,1)}, bf16[2,4,32,128]{3,2,1,0:T(8,128)(2,1)}, u32[]{:S(2)}, u32[]{:S(2)}) collective-permute-start(bf16[2,4,32,128]{3,2,1,0:T(8,128)(2,1)} %bitcast_bitcast_fusion.12), channel_id=1, source_target_pairs={{0,32},{4,36},{8,40},{12,44},{16,48},{20,52},{24,56},{28,60},{32,6... | collective-permute-start | bytes 196616 | tf_op jit(solution)/shard_map/ppermute | solution.py:86
  3.6 26.6 %collective-permute-start.1 = (bf16[2,4,32,128]{3,2,1,0:T(8,128)(2,1)}, bf16[2,4,32,128]{3,2,1,0:T(8,128)(2,1)S(1)}, u32[]{:S(2)}, u32[]{:S(2)}) collective-permute-start(bf16[2,4,32,128]{3,2,1,0:T(8,128)(2,1)} %bitcast_bitcast_fusion.12), channel_id=1, source_target_pairs={{0,224},{4,228},{8,232},{12,236},{16,240},{20,244},{24,248},{28,25... | collective-permute-start | bytes 196616 | tf_op jit(solution)/shard_map/ppermute | solution.py:87
  12.2 16.3 %copy-start.3 = (bf16[2,32,512]{2,1,0:T(8,128)(2,1)S(1)}, bf16[2,32,512]{2,1,0:T(8,128)(2,1)}, u32[]{:S(2)}) copy-start(bf16[2,32,512]{2,1,0:T(8,128)(2,1)} %param.22) | copy-start | bytes 196612
  12.2 36.2 %all-to-all-start = ((bf16[64,2,4,4,128]{4,2,3,1,0:T(4,128)(2,1)}), bf16[64,2,4,4,128]{4,2,3,1,0:T(4,128)(2,1)S(1)}, u32[]{:S(2)}, u32[]{:S(2)}) async-start(bf16[64,2,4,4,128]{4,2,3,1,0:T(4,128)(2,1)} %bitcast.3), calls=%async_computation | async-start | bytes 1048576 | tf_op jit(solution)/shard_map/all_to_all | solution.py:139
  28.6 9.3 %collective-permute-start.2 = (bf16[2,4,32,128]{3,2,1,0:T(8,128)(2,1)}, bf16[2,4,32,128]{3,2,1,0:T(8,128)(2,1)S(1)}, u32[]{:S(2)}, u32[]{:S(2)}) collective-permute-start(bf16[2,4,32,128]{3,2,1,0:T(8,128)(2,1)} %collective-permute-done), channel_id=1, source_target_pairs={{0,32},{4,36},{8,40},{12,44},{16,48},{20,52},{24,56},{28,60},{32,6... | collective-permute-start | bytes 196616 | tf_op jit(solution)/shard_map/ppermute | solution.py:86
  30.1 7.7 %collective-permute-start.3 = (bf16[2,4,32,128]{3,2,1,0:T(8,128)(2,1)S(1)}, bf16[2,4,32,128]{3,2,1,0:T(8,128)(2,1)S(1)}, u32[]{:S(2)}, u32[]{:S(2)}) collective-permute-start(bf16[2,4,32,128]{3,2,1,0:T(8,128)(2,1)S(1)} %collective-permute-done.1), channel_id=1, source_target_pairs={{0,224},{4,228},{8,232},{12,236},{16,240},{20,244},{24,248},{28,25... | collective-permute-start | bytes 196616 | tf_op jit(solution)/shard_map/ppermute | solution.py:87
  37.8 5.5 %collective-permute-start.4 = (bf16[2,4,32,128]{3,2,1,0:T(8,128)(2,1)S(1)}, bf16[2,4,32,128]{3,2,1,0:T(8,128)(2,1)S(1)}, u32[]{:S(2)}, u32[]{:S(2)}) collective-permute-start(bf16[2,4,32,128]{3,2,1,0:T(8,128)(2,1)S(1)} %collective-permute-done.2), channel_id=1, source_target_pairs={{0,32},{4,36},{8,40},{12,44},{16,48},{20,52},{24,56},{28,60},{32,6... | collective-permute-start | bytes 196616 | tf_op jit(solution)/shard_map/ppermute | solution.py:86
  37.8 5.5 %collective-permute-start.5 = (bf16[2,4,32,128]{3,2,1,0:T(8,128)(2,1)S(1)}, bf16[2,4,32,128]{3,2,1,0:T(8,128)(2,1)S(1)}, u32[]{:S(2)}, u32[]{:S(2)}) collective-permute-start(bf16[2,4,32,128]{3,2,1,0:T(8,128)(2,1)S(1)} %collective-permute-done.3), channel_id=1, source_target_pairs={{0,224},{4,228},{8,232},{12,236},{16,240},{20,244},{24,248},{28,25... | collective-permute-start | bytes 196616 | tf_op jit(solution)/shard_map/ppermute | solution.py:87
  43.3 5.1 %collective-permute-start.6 = (bf16[2,4,16,128]{3,2,1,0:T(8,128)(2,1)S(1)}, bf16[2,4,16,128]{3,2,1,0:T(8,128)(2,1)S(1)}, u32[]{:S(2)}, u32[]{:S(2)}) collective-permute-start(bf16[2,4,16,128]{3,2,1,0:T(8,128)(2,1)S(1)} %slice.44), channel_id=1, source_target_pairs={{0,32},{4,36},{8,40},{12,44},{16,48},{20,52},{24,56},{28,60},{32,6... | collective-permute-start | bytes 98312 | tf_op jit(solution)/shard_map/ppermute | solution.py:91
  43.3 5.1 %collective-permute-start.7 = (bf16[2,4,16,128]{3,2,1,0:T(8,128)(2,1)S(1)}, bf16[2,4,16,128]{3,2,1,0:T(8,128)(2,1)S(1)}, u32[]{:S(2)}, u32[]{:S(2)}) collective-permute-start(bf16[2,4,16,128]{3,2,1,0:T(8,128)(2,1)S(1)} %slice.45), channel_id=1, source_target_pairs={{0,224},{4,228},{8,232},{12,236},{16,240},{20,244},{24,248},{28,25... | collective-permute-start | bytes 98312 | tf_op jit(solution)/shard_map/ppermute | solution.py:92
  48.5 11.9 %collective-permute-start.8 = (bf16[2,4,256,128]{3,2,1,0:T(8,128)(2,1)S(1)}, bf16[2,4,256,128]{3,2,1,0:T(8,128)(2,1)S(1)}, u32[]{:S(2)}, u32[]{:S(2)}) collective-permute-start(bf16[2,4,256,128]{3,2,1,0:T(8,128)(2,1)S(1)} %constant_dynamic-update-slice_fusion), channel_id=1, source_target_pairs={{0,8},{4,12},{8,16},{12,20},{16,24},{20,28},{24,0},{28,4},{32,40},... | collective-permute-start | bytes 1572872 | tf_op jit(solution)/shard_map/ppermute | solution.py:86
  50.1 12.1 %collective-permute-start.9 = (bf16[2,4,256,128]{3,2,1,0:T(8,128)(2,1)S(1)}, bf16[2,4,256,128]{3,2,1,0:T(8,128)(2,1)S(1)}, u32[]{:S(2)}, u32[]{:S(2)}) collective-permute-start(bf16[2,4,256,128]{3,2,1,0:T(8,128)(2,1)S(1)} %constant_dynamic-update-slice_fusion), channel_id=1, source_target_pairs={{0,24},{4,28},{8,0},{12,4},{16,8},{20,12},{24,16},{28,20},{32,56},... | collective-permute-start | bytes 1572872 | tf_op jit(solution)/shard_map/ppermute | solution.py:87
  60.4 6.6 %collective-permute-start.10 = (bf16[2,4,128,128]{3,2,1,0:T(8,128)(2,1)S(1)}, bf16[2,4,128,128]{3,2,1,0:T(8,128)(2,1)S(1)}, u32[]{:S(2)}, u32[]{:S(2)}) collective-permute-start(bf16[2,4,128,128]{3,2,1,0:T(8,128)(2,1)S(1)} %slice.50), channel_id=1, source_target_pairs={{0,8},{4,12},{8,16},{12,20},{16,24},{20,28},{24,0},{28,4},{32,40},... | collective-permute-start | bytes 786440 | tf_op jit(solution)/shard_map/ppermute | solution.py:91
  62.2 6.4 %collective-permute-start.11 = (bf16[2,4,128,128]{3,2,1,0:T(8,128)(2,1)S(1)}, bf16[2,4,128,128]{3,2,1,0:T(8,128)(2,1)S(1)}, u32[]{:S(2)}, u32[]{:S(2)}) collective-permute-start(bf16[2,4,128,128]{3,2,1,0:T(8,128)(2,1)S(1)} %slice.51), channel_id=1, source_target_pairs={{0,24},{4,28},{8,0},{12,4},{16,8},{20,12},{24,16},{28,20},{32,56},... | collective-permute-start | bytes 786440 | tf_op jit(solution)/shard_map/ppermute | solution.py:92
  68.8 4.2 %collective-permute-start.12 = (bf16[2,4,1024,128]{3,2,1,0:T(8,128)(2,1)S(1)}, bf16[2,4,1024,128]{3,2,1,0:T(8,128)(2,1)S(1)}, u32[]{:S(2)}, u32[]{:S(2)}) collective-permute-start(bf16[2,4,1024,128]{3,2,1,0:T(8,128)(2,1)S(1)} %get-tuple-element.32), channel_id=1, source_target_pairs={{0,4},{4,0},{8,12},{12,8},{16,20},{20,16},{24,28},{28,24},{32,36},... | collective-permute-start | bytes 6291464 | tf_op jit(solution)/shard_map/ppermute | solution.py:104
  75.4 1.4 copy-start.2
  79.4 20.7 %copy-start.4 = (bf16[256,512]{1,0:T(8,128)(2,1)S(1)}, bf16[256,512]{1,0:T(8,128)(2,1)}, u32[]{:S(2)}) copy-start(bf16[256,512]{1,0:T(8,128)(2,1)} %param.16) | copy-start | bytes 786436
  99.8 17.7 %copy-start.5 = (f32[2048]{0:T(1024)S(1)}, f32[2048]{0:T(1024)}, u32[]{:S(2)}) copy-start(f32[2048]{0:T(1024)} %param.25) | copy-start | bytes 24580
  99.9 17.7 %copy-start.6 = (f32[2048]{0:T(1024)S(1)}, f32[2048]{0:T(1024)}, u32[]{:S(2)}) copy-start(f32[2048]{0:T(1024)} %param.24) | copy-start | bytes 24580
  100.0 18.3 %copy-start.9 = (f32[1024]{0:T(1024)S(1)}, f32[1024]{0:T(1024)}, u32[]{:S(2)}) copy-start(f32[1024]{0:T(1024)} %param.27) | copy-start | bytes 12292
  100.2 18.1 %copy-start.7 = (bf16[2048,1024]{1,0:T(8,128)(2,1)S(1)}, bf16[2048,1024]{1,0:T(8,128)(2,1)}, u32[]{:S(2)}) copy-start(bf16[2048,1024]{1,0:T(8,128)(2,1)} %param.26) | copy-start | bytes 12582916
  118.3 3.7 %copy-start.8 = (bf16[1024,2048]{1,0:T(8,128)(2,1)S(1)}, bf16[1024,2048]{1,0:T(8,128)(2,1)}, u32[]{:S(2)}) copy-start(bf16[1024,2048]{1,0:T(8,128)(2,1)} %param.28) | copy-start | bytes 12582916
  124.4 16.9 %all-to-all-start.3 = ((bf16[4,256,512]{2,1,0:T(8,128)(2,1)}), bf16[4,256,512]{2,1,0:T(8,128)(2,1)S(1)}, u32[]{:S(2)}, u32[]{:S(2)}) async-start(bf16[4,256,512]{2,1,0:T(8,128)(2,1)} %bitcast.172), calls=%async_computation.3 | async-start | bytes 2097152 | tf_op jit(solution)/shard_map/all_to_all | solution.py:58

commit v12 on v11

--- a/solution.py
+++ b/solution.py
@@ -98,9 +98,12 @@
     cores = 2
     lanes = 4
     shape = (seq_size // (lanes * cores), lanes, cores)
+    transfer, work = companion
     gathered = ring_along(block, shape, 0)
-    gathered, companion = lax.optimization_barrier((gathered, companion))
+    gathered, transfer = lax.optimization_barrier((gathered, transfer))
     gathered = ring_along(gathered, shape, 1)
+    gathered, work = lax.optimization_barrier((gathered, work))
+    companion = (transfer, work)
     partner = lax.ppermute(gathered, "seq", shift_pairs(shape, 2, 1))
     return jnp.concatenate([gathered, partner], axis=2), companion
 

time: 143 us -> 146 us (1.021)
  local copies, waits for them, and re-layouts: 11.1 us -> 17.2 us
  waiting for transfers between devices: 39.9 us -> 36.7 us
    unnamed x34 -> x35, local copies, waits for them, and re-layouts: 1.86 us -> 7.47 us
    ppermute x4, waiting for transfers between devices: 16.8 us -> 14.5 us  [ring_along(): from_below = lax.ppermute(from_below, 'seq', up)]
    ppermute x2, waiting for transfers between devices: 5.54 us -> 3.6 us  [ring_along(): first = lax.ppermute(from_below[:, :, :half], 'seq', up)]
  transfers between devices with their start and end apart: 15 -> 15, of which waited for: 8 -> 8; matrix products, arithmetic and copies ran while one was open for 10% -> 14% of each run, Pallas kernels for 0% -> 0%
where the time goes in v12:
time: 146 us; the launch traced here: 145 us
  waiting for transfers between devices  36.7 us (25%)
  blocking collectives  36.7 us (25%)
  starting transfers between devices  33 us (23%)
  local copies, waits for them, and re-layouts  17.2 us (12%)
  matrix products  13.8 us (9%)
  other arithmetic  6.63 us (5%)
    all_to_all x1, blocking collectives, tensor_sum_scatter(): arrived = lax.all_to_all(pieces, 'tensor', 0, 0, tiled=True)  19.8 us
    all_to_all x1, blocking collectives, tensor_gather(): arrived = lax.all_to_all(copies, 'tensor', 0, 0, tiled=True)  16.9 us
    ppermute x4, waiting for transfers between devices, ring_along(): from_below = lax.ppermute(from_below, 'seq', up)  14.5 us
    all_to_all x1, waiting for transfers between devices, tensor_sum_scatter(): arrived = lax.all_to_all(pieces, 'tensor', 0, 0, tiled=True)  12.6 us
    ppermute x4, starting transfers between devices, ring_along(): from_above = lax.ppermute(from_above, 'seq', down)  9.43 us
    all_to_all x1, starting transfers between devices, per_device(): arrived = lax.all_to_all(picked, 'seq', 0, 0, tiled=True)  9.39 us
    unnamed x35, local copies, waits for them, and re-layouts  7.47 us
    ppermute x4, starting transfers between devices, ring_along(): from_below = lax.ppermute(from_below, 'seq', up)  5.01 us
  transfers between devices with their start and end apart: 15, of which 8 were waited for; matrix products, arithmetic and copies ran while one was open for 14% of the time, Pallas kernels for 0%

profile of v12, /device:TPU:2, one launch (start us, length us, event | category | flops | bytes accessed | tf_op | source)
XLA Modules:
  0.0 144.6 jit_solution(14163891244683550803)
XLA Ops:
  0.0 1.6 %bitcast_bitcast_fusion.12 = bf16[2,4,32,128]{3,2,1,0:T(8,128)(2,1)} fusion(bf16[2,32,512]{2,1,0:T(8,128)(2,1)} %param.22), kind=kLoop, calls=%fused_computation.88 | loop fusion | bytes 131072 | tf_op jit(solution)/shard_map/transpose | solution.py:50
  1.6 1.9 %collective-permute-start = (bf16[2,4,32,128]{3,2,1,0:T(8,128)(2,1)}, bf16[2,4,32,128]{3,2,1,0:T(8,128)(2,1)}, u32[]{:S(2)}, u32[]{:S(2)}) collective-permute-start(bf16[2,4,32,128]{3,2,1,0:T(8,128)(2,1)} %bitcast_bitcast_fusion.12), channel_id=1, source_target_pairs={{0,32},{4,36},{8,40},{12,44},{16,48},{20,52},{24,56},{28,60},{32,6... | collective-permute-start | bytes 196616 | tf_op jit(solution)/shard_map/ppermute | solution.py:86
  3.5 3.9 %collective-permute-start.1 = (bf16[2,4,32,128]{3,2,1,0:T(8,128)(2,1)}, bf16[2,4,32,128]{3,2,1,0:T(8,128)(2,1)S(1)}, u32[]{:S(2)}, u32[]{:S(2)}) collective-permute-start(bf16[2,4,32,128]{3,2,1,0:T(8,128)(2,1)} %bitcast_bitcast_fusion.12), channel_id=1, source_target_pairs={{0,224},{4,228},{8,232},{12,236},{16,240},{20,244},{24,248},{28,25... | collective-permute-start | bytes 196616 | tf_op jit(solution)/shard_map/ppermute | solution.py:87
  7.5 0.7 compare_select_fusion
  8.2 0.7 compare_and_fusion
  8.8 1.0 copy.63
  9.9 1.0 gather_fusion
  11.2 1.0 reshape.139
  12.2 9.4 %all-to-all-start = ((bf16[64,2,4,4,128]{4,2,3,1,0:T(4,128)(2,1)}), bf16[64,2,4,4,128]{4,2,3,1,0:T(4,128)(2,1)S(1)}, u32[]{:S(2)}, u32[]{:S(2)}) async-start(bf16[64,2,4,4,128]{4,2,3,1,0:T(4,128)(2,1)} %bitcast.3), calls=%async_computation | async-start | bytes 1048576 | tf_op jit(solution)/shard_map/all_to_all | solution.py:142
  21.7 0.7 constant_dynamic-update-slice_fusion.8
  23.7 0.9 bitcast_bitcast_fusion.11
  24.8 1.3 fusion.65
  26.5 1.5 %collective-permute-start.2 = (bf16[2,4,32,128]{3,2,1,0:T(8,128)(2,1)}, bf16[2,4,32,128]{3,2,1,0:T(8,128)(2,1)S(1)}, u32[]{:S(2)}, u32[]{:S(2)}) collective-permute-start(bf16[2,4,32,128]{3,2,1,0:T(8,128)(2,1)} %collective-permute-done), channel_id=1, source_target_pairs={{0,32},{4,36},{8,40},{12,44},{16,48},{20,52},{24,56},{28,60},{32,6... | collective-permute-start | bytes 196616 | tf_op jit(solution)/shard_map/ppermute | solution.py:86
  28.0 1.8 %collective-permute-start.3 = (bf16[2,4,32,128]{3,2,1,0:T(8,128)(2,1)S(1)}, bf16[2,4,32,128]{3,2,1,0:T(8,128)(2,1)S(1)}, u32[]{:S(2)}, u32[]{:S(2)}) collective-permute-start(bf16[2,4,32,128]{3,2,1,0:T(8,128)(2,1)S(1)} %collective-permute-done.1), channel_id=1, source_target_pairs={{0,224},{4,228},{8,232},{12,236},{16,240},{20,244},{24,248},{28,25... | collective-permute-start | bytes 196616 | tf_op jit(solution)/shard_map/ppermute | solution.py:87
  29.8 1.5 %constant_dynamic-update-slice_fusion.7 = bf16[2,4,256,128]{3,2,1,0:T(8,128)(2,1)} fusion(bf16[2,4,256,128]{3,2,1,0:T(8,128)(2,1)} %constant_dynamic-update-slice_fusion.8, bf16[2,4,32,128]{3,2,1,0:T(8,128)(2,1)} %collective-permute-done), kind=kLoop, calls=%fused_computation.98 | loop fusion | bytes 131072
  31.3 0.7 constant_dynamic-update-slice_fusion.6
  31.9 5.8 %collective-permute-done.2 = bf16[2,4,32,128]{3,2,1,0:T(8,128)(2,1)S(1)} collective-permute-done((bf16[2,4,32,128]{3,2,1,0:T(8,128)(2,1)}, bf16[2,4,32,128]{3,2,1,0:T(8,128)(2,1)S(1)}, u32[]{:S(2)}, u32[]{:S(2)}) %collective-permute-start.2) | collective-permute-done | bytes 65568 | tf_op jit(solution)/shard_map/ppermute | solution.py:86
  37.7 3.2 %collective-permute-start.5 = (bf16[2,4,32,128]{3,2,1,0:T(8,128)(2,1)S(1)}, bf16[2,4,32,128]{3,2,1,0:T(8,128)(2,1)S(1)}, u32[]{:S(2)}, u32[]{:S(2)}) collective-permute-start(bf16[2,4,32,128]{3,2,1,0:T(8,128)(2,1)S(1)} %collective-permute-done.3), channel_id=1, source_target_pairs={{0,224},{4,228},{8,232},{12,236},{16,240},{20,244},{24,248},{28,25... | collective-permute-start | bytes 196616 | tf_op jit(solution)/shard_map/ppermute | solution.py:87
  41.0 0.7 constant_dynamic-update-slice_fusion.5
  41.6 0.6 constant_dynamic-update-slice_fusion.4
  42.3 0.9 collective-permute-done.4
  43.2 3.2 %collective-permute-start.7 = (bf16[2,4,16,128]{3,2,1,0:T(8,128)(2,1)S(1)}, bf16[2,4,16,128]{3,2,1,0:T(8,128)(2,1)S(1)}, u32[]{:S(2)}, u32[]{:S(2)}) collective-permute-start(bf16[2,4,16,128]{3,2,1,0:T(8,128)(2,1)S(1)} %slice.45), channel_id=1, source_target_pairs={{0,224},{4,228},{8,232},{12,236},{16,240},{20,244},{24,248},{28,25... | collective-permute-start | bytes 98312 | tf_op jit(solution)/shard_map/ppermute | solution.py:92
  46.4 0.6 constant_dynamic-update-slice_fusion.3
  47.1 0.6 constant_dynamic-update-slice_fusion.2
  48.3 0.6 constant_dynamic-update-slice_fusion.1
  49.0 0.6 constant_dynamic-update-slice_fusion
  49.6 1.5 %collective-permute-start.8 = (bf16[2,4,256,128]{3,2,1,0:T(8,128)(2,1)}, bf16[2,4,256,128]{3,2,1,0:T(8,128)(2,1)S(1)}, u32[]{:S(2)}, u32[]{:S(2)}) collective-permute-start(bf16[2,4,256,128]{3,2,1,0:T(8,128)(2,1)} %constant_dynamic-update-slice_fusion), channel_id=1, source_target_pairs={{0,8},{4,12},{8,16},{12,20},{16,24},{20,28},{24,0},{28,4},{32,40},... | collective-permute-start | bytes 1572872 | tf_op jit(solution)/shard_map/ppermute | solution.py:86
  51.6 1.8 %fusion.14 = f32[4,256,128]{2,1,0:T(8,128)S(1)} fusion(f32[4,256,256]{1,2,0:T(8,128)} %copy-done.2, f32[4,256]{1,0:T(4,128)S(1)} %get-tuple-element.30, pred[256,256]{0,1:T(8,128)(4,1)S(1)} %fusion.51, f32[4,256]{1,0:T(4,128)S(1)} %get-tuple-element.25, f32[4,256]{1,0:T(4,128)S(1)} %get-tuple-element.28, bf16[256,512]{1,0:T(8,128)(2,1)} %param.19), kind=kOutput, calls=%fused_computation.30 | convolution fusion | flops 68157440 | bytes 1912832 | tf_op jit(solution)/shard_map/hqk,hkd->hqd/dot_general | solution.py:24
  53.8 7.8 %collective-permute-done.8 = bf16[2,4,256,128]{3,2,1,0:T(8,128)(2,1)S(1)} collective-permute-done((bf16[2,4,256,128]{3,2,1,0:T(8,128)(2,1)}, bf16[2,4,256,128]{3,2,1,0:T(8,128)(2,1)S(1)}, u32[]{:S(2)}, u32[]{:S(2)}) %collective-permute-start.8) | collective-permute-done | bytes 524320 | tf_op jit(solution)/shard_map/ppermute | solution.py:86
  61.6 1.8 %collective-permute-start.10 = (bf16[2,4,128,128]{3,2,1,0:T(8,128)(2,1)S(1)}, bf16[2,4,128,128]{3,2,1,0:T(8,128)(2,1)S(1)}, u32[]{:S(2)}, u32[]{:S(2)}) collective-permute-start(bf16[2,4,128,128]{3,2,1,0:T(8,128)(2,1)S(1)} %slice.46), channel_id=1, source_target_pairs={{0,8},{4,12},{8,16},{12,20},{16,24},{20,28},{24,0},{28,4},{32,40},... | collective-permute-start | bytes 786440 | tf_op jit(solution)/shard_map/ppermute | solution.py:91
  63.4 1.1 constant_dynamic-update-slice_fusion.13
  65.2 3.0 %collective-permute-done.10 = bf16[2,4,128,128]{3,2,1,0:T(8,128)(2,1)S(1)} collective-permute-done((bf16[2,4,128,128]{3,2,1,0:T(8,128)(2,1)S(1)}, bf16[2,4,128,128]{3,2,1,0:T(8,128)(2,1)S(1)}, u32[]{:S(2)}, u32[]{:S(2)}) %collective-permute-start.10) | collective-permute-done | bytes 262176 | tf_op jit(solution)/shard_map/ppermute | solution.py:91
  68.3 2.7 %collective-permute-done.11 = bf16[2,4,128,128]{3,2,1,0:T(8,128)(2,1)S(1)} collective-permute-done((bf16[2,4,128,128]{3,2,1,0:T(8,128)(2,1)S(1)}, bf16[2,4,128,128]{3,2,1,0:T(8,128)(2,1)S(1)}, u32[]{:S(2)}, u32[]{:S(2)}) %collective-permute-start.11) | collective-permute-done | bytes 262176 | tf_op jit(solution)/shard_map/ppermute | solution.py:92
  72.0 3.3 %collective-permute-done.12 = bf16[2,4,1024,128]{3,2,1,0:T(8,128)(2,1)S(1)} collective-permute-done((bf16[2,4,1024,128]{3,2,1,0:T(8,128)(2,1)S(1)}, bf16[2,4,1024,128]{3,2,1,0:T(8,128)(2,1)S(1)}, u32[]{:S(2)}, u32[]{:S(2)}) %collective-permute-start.12) | collective-permute-done | bytes 2097184 | tf_op jit(solution)/shard_map/ppermute | solution.py:107
  75.6 1.3 bitcast_reduce_fusion
  77.6 1.4 fusion.1
  79.0 2.4 %fusion.34 = bf16[256,4,128]{2,0,1:T(8,128)(2,1)S(1)} fusion(bf16[2,4,2048,128]{3,2,1,0:T(8,128)(2,1)S(1)} %constant_dynamic-update-slice_fusion.14, f32[4,2048,256]{2,1,0:T(8,128)S(1)} %get-tuple-element.38, f32[4,256]{1,0:T(4,128)S(1)} %get-tuple-element.22, f32[4,256,128]{2,1,0:T(8,128)S(1)} %fusion.42, f32[4,256,128]{2,1,0:T(8,128)S(1)} %convolution_add_fusion.1, ...), kind=kOutput, calls=%fused_computation.58 | convolution fusion | flops 543948800 | bytes 11812864 | tf_op jit(solution)/shard_map/hqk,hkd->hqd/dot_general | solution.py:24
  81.6 0.7 convolution_convert_fusion
  82.4 19.8 %all_to_all.20 = bf16[4,256,512]{2,1,0:T(8,128)(2,1)S(1)} all-to-all(bf16[4,256,512]{2,1,0:T(8,128)(2,1)S(1)} %bitcast.174), channel_id=1, replica_groups=mesh['seq'=64,'tensor'=4] {'tensor'}, dimensions={0} | all-to-all | bytes 2097152 | tf_op jit(solution)/shard_map/all_to_all | solution.py:58
  102.7 16.9 %all_to_all.21 = bf16[4,256,512]{1,2,0:T(8,128)(2,1)S(1)} all-to-all(bf16[4,256,512]{1,2,0:T(8,128)(2,1)S(1)} %broadcast_in_dim.79), channel_id=1, replica_groups=mesh['seq'=64,'tensor'=4] {'tensor'}, dimensions={0} | all-to-all | bytes 2097152 | tf_op jit(solution)/shard_map/all_to_all | solution.py:65
  120.0 0.7 fusion.11
  120.7 3.7 %fusion.20 = bf16[256,1024]{1,0:T(8,128)(2,1)S(1)} fusion(bf16[256,2048]{0,1:T(8,128)(2,1)S(1)} %fusion.11, bf16[2048,1024]{1,0:T(8,128)(2,1)S(1)} %copy-done.7, f32[1024]{0:T(1024)S(1)} %copy-done.9), kind=kOutput, calls=%fused_computation.35 | convolution fusion | flops 1091043328 | bytes 5771264 | tf_op jit(solution)/shard_map/dot_general | solution.py:190
  124.5 1.3 convolution_convert_fusion.1
  125.7 1.0 copy.144
  126.8 3.5 %all-to-all-start.3 = ((bf16[4,256,512]{2,1,0:T(8,128)(2,1)}), bf16[4,256,512]{2,1,0:T(8,128)(2,1)S(1)}, u32[]{:S(2)}, u32[]{:S(2)}) async-start(bf16[4,256,512]{2,1,0:T(8,128)(2,1)} %bitcast.172), calls=%async_computation.3 | async-start | bytes 2097152 | tf_op jit(solution)/shard_map/all_to_all | solution.py:58
  130.3 0.8 dynamic_slice.7
  131.1 12.6 %all-to-all-done.3 = bf16[4,256,512]{2,1,0:T(8,128)(2,1)S(1)} async-done(((bf16[4,256,512]{2,1,0:T(8,128)(2,1)}), bf16[4,256,512]{2,1,0:T(8,128)(2,1)S(1)}, u32[]{:S(2)}, u32[]{:S(2)}) %all-to-all-start.3) | async-done | bytes 1048608 | tf_op jit(solution)/shard_map/all_to_all | solution.py:58
  143.8 0.8 add_convert_fusion
  (72 shorter events, 7.5 us)
Async XLA Ops:
  0.0 81.6 %copy-start = (bf16[512,2048]{1,0:T(8,128)(2,1)S(1)}, bf16[512,2048]{1,0:T(8,128)(2,1)}, u32[]{:S(2)}) copy-start(bf16[512,2048]{1,0:T(8,128)(2,1)} %param.23) | copy-start | bytes 6291460
  1.6 24.8 %collective-permute-start = (bf16[2,4,32,128]{3,2,1,0:T(8,128)(2,1)}, bf16[2,4,32,128]{3,2,1,0:T(8,128)(2,1)}, u32[]{:S(2)}, u32[]{:S(2)}) collective-permute-start(bf16[2,4,32,128]{3,2,1,0:T(8,128)(2,1)} %bitcast_bitcast_fusion.12), channel_id=1, source_target_pairs={{0,32},{4,36},{8,40},{12,44},{16,48},{20,52},{24,56},{28,60},{32,6... | collective-permute-start | bytes 196616 | tf_op jit(solution)/shard_map/ppermute | solution.py:86
  3.5 24.5 %collective-permute-start.1 = (bf16[2,4,32,128]{3,2,1,0:T(8,128)(2,1)}, bf16[2,4,32,128]{3,2,1,0:T(8,128)(2,1)S(1)}, u32[]{:S(2)}, u32[]{:S(2)}) collective-permute-start(bf16[2,4,32,128]{3,2,1,0:T(8,128)(2,1)} %bitcast_bitcast_fusion.12), channel_id=1, source_target_pairs={{0,224},{4,228},{8,232},{12,236},{16,240},{20,244},{24,248},{28,25... | collective-permute-start | bytes 196616 | tf_op jit(solution)/shard_map/ppermute | solution.py:87
  9.8 11.8 %copy-start.3 = (bf16[2,32,512]{2,1,0:T(8,128)(2,1)S(1)}, bf16[2,32,512]{2,1,0:T(8,128)(2,1)}, u32[]{:S(2)}) copy-start(bf16[2,32,512]{2,1,0:T(8,128)(2,1)} %param.22) | copy-start | bytes 196612
  9.8 12.5 %copy-start.10 = (s32[64]{0:T(128)S(1)}, s32[64]{0:T(128)}, u32[]{:S(2)}) copy-start(s32[64]{0:T(128)} %param.31) | copy-start | bytes 772
  9.9 14.7 %copy-start.1 = (bf16[256,512]{1,0:T(8,128)(2,1)S(1)}, bf16[256,512]{1,0:T(8,128)(2,1)}, u32[]{:S(2)}) copy-start(bf16[256,512]{1,0:T(8,128)(2,1)} %param.17) | copy-start | bytes 786436
  12.2 37.4 %all-to-all-start = ((bf16[64,2,4,4,128]{4,2,3,1,0:T(4,128)(2,1)}), bf16[64,2,4,4,128]{4,2,3,1,0:T(4,128)(2,1)S(1)}, u32[]{:S(2)}, u32[]{:S(2)}) async-start(bf16[64,2,4,4,128]{4,2,3,1,0:T(4,128)(2,1)} %bitcast.3), calls=%async_computation | async-start | bytes 1048576 | tf_op jit(solution)/shard_map/all_to_all | solution.py:142
  26.1 22.8 %copy-start.2 = (f32[4,256,256]{1,2,0:T(8,128)}, f32[4,256,256]{1,2,0:T(8,128)S(1)}, u32[]{:S(2)}) copy-start(f32[4,256,256]{1,2,0:T(8,128)S(1)} %get-tuple-element.34) | copy-start | bytes 3145732
  26.5 11.3 %collective-permute-start.2 = (bf16[2,4,32,128]{3,2,1,0:T(8,128)(2,1)}, bf16[2,4,32,128]{3,2,1,0:T(8,128)(2,1)S(1)}, u32[]{:S(2)}, u32[]{:S(2)}) collective-permute-start(bf16[2,4,32,128]{3,2,1,0:T(8,128)(2,1)} %collective-permute-done), channel_id=1, source_target_pairs={{0,32},{4,36},{8,40},{12,44},{16,48},{20,52},{24,56},{28,60},{32,6... | collective-permute-start | bytes 196616 | tf_op jit(solution)/shard_map/ppermute | solution.py:86
  28.0 9.7 %collective-permute-start.3 = (bf16[2,4,32,128]{3,2,1,0:T(8,128)(2,1)S(1)}, bf16[2,4,32,128]{3,2,1,0:T(8,128)(2,1)S(1)}, u32[]{:S(2)}, u32[]{:S(2)}) collective-permute-start(bf16[2,4,32,128]{3,2,1,0:T(8,128)(2,1)S(1)} %collective-permute-done.1), channel_id=1, source_target_pairs={{0,224},{4,228},{8,232},{12,236},{16,240},{20,244},{24,248},{28,25... | collective-permute-start | bytes 196616 | tf_op jit(solution)/shard_map/ppermute | solution.py:87
  37.7 5.5 %collective-permute-start.4 = (bf16[2,4,32,128]{3,2,1,0:T(8,128)(2,1)S(1)}, bf16[2,4,32,128]{3,2,1,0:T(8,128)(2,1)S(1)}, u32[]{:S(2)}, u32[]{:S(2)}) collective-permute-start(bf16[2,4,32,128]{3,2,1,0:T(8,128)(2,1)S(1)} %collective-permute-done.2), channel_id=1, source_target_pairs={{0,32},{4,36},{8,40},{12,44},{16,48},{20,52},{24,56},{28,60},{32,6... | collective-permute-start | bytes 196616 | tf_op jit(solution)/shard_map/ppermute | solution.py:86
  37.7 5.5 %collective-permute-start.5 = (bf16[2,4,32,128]{3,2,1,0:T(8,128)(2,1)S(1)}, bf16[2,4,32,128]{3,2,1,0:T(8,128)(2,1)S(1)}, u32[]{:S(2)}, u32[]{:S(2)}) collective-permute-start(bf16[2,4,32,128]{3,2,1,0:T(8,128)(2,1)S(1)} %collective-permute-done.3), channel_id=1, source_target_pairs={{0,224},{4,228},{8,232},{12,236},{16,240},{20,244},{24,248},{28,25... | collective-permute-start | bytes 196616 | tf_op jit(solution)/shard_map/ppermute | solution.py:87
  43.2 5.1 %collective-permute-start.6 = (bf16[2,4,16,128]{3,2,1,0:T(8,128)(2,1)S(1)}, bf16[2,4,16,128]{3,2,1,0:T(8,128)(2,1)S(1)}, u32[]{:S(2)}, u32[]{:S(2)}) collective-permute-start(bf16[2,4,16,128]{3,2,1,0:T(8,128)(2,1)S(1)} %slice.44), channel_id=1, source_target_pairs={{0,32},{4,36},{8,40},{12,44},{16,48},{20,52},{24,56},{28,60},{32,6... | collective-permute-start | bytes 98312 | tf_op jit(solution)/shard_map/ppermute | solution.py:91
  43.2 5.7 %collective-permute-start.7 = (bf16[2,4,16,128]{3,2,1,0:T(8,128)(2,1)S(1)}, bf16[2,4,16,128]{3,2,1,0:T(8,128)(2,1)S(1)}, u32[]{:S(2)}, u32[]{:S(2)}) collective-permute-start(bf16[2,4,16,128]{3,2,1,0:T(8,128)(2,1)S(1)} %slice.45), channel_id=1, source_target_pairs={{0,224},{4,228},{8,232},{12,236},{16,240},{20,244},{24,248},{28,25... | collective-permute-start | bytes 98312 | tf_op jit(solution)/shard_map/ppermute | solution.py:92
  49.6 12.0 %collective-permute-start.8 = (bf16[2,4,256,128]{3,2,1,0:T(8,128)(2,1)}, bf16[2,4,256,128]{3,2,1,0:T(8,128)(2,1)S(1)}, u32[]{:S(2)}, u32[]{:S(2)}) collective-permute-start(bf16[2,4,256,128]{3,2,1,0:T(8,128)(2,1)} %constant_dynamic-update-slice_fusion), channel_id=1, source_target_pairs={{0,8},{4,12},{8,16},{12,20},{16,24},{20,28},{24,0},{28,4},{32,40},... | collective-permute-start | bytes 1572872 | tf_op jit(solution)/shard_map/ppermute | solution.py:86
  51.1 13.4 %collective-permute-start.9 = (bf16[2,4,256,128]{3,2,1,0:T(8,128)(2,1)}, bf16[2,4,256,128]{3,2,1,0:T(8,128)(2,1)S(1)}, u32[]{:S(2)}, u32[]{:S(2)}) collective-permute-start(bf16[2,4,256,128]{3,2,1,0:T(8,128)(2,1)} %constant_dynamic-update-slice_fusion), channel_id=1, source_target_pairs={{0,24},{4,28},{8,0},{12,4},{16,8},{20,12},{24,16},{28,20},{32,56},... | collective-permute-start | bytes 1572872 | tf_op jit(solution)/shard_map/ppermute | solution.py:87
  61.6 6.6 %collective-permute-start.10 = (bf16[2,4,128,128]{3,2,1,0:T(8,128)(2,1)S(1)}, bf16[2,4,128,128]{3,2,1,0:T(8,128)(2,1)S(1)}, u32[]{:S(2)}, u32[]{:S(2)}) collective-permute-start(bf16[2,4,128,128]{3,2,1,0:T(8,128)(2,1)S(1)} %slice.46), channel_id=1, source_target_pairs={{0,8},{4,12},{8,16},{12,20},{16,24},{20,28},{24,0},{28,4},{32,40},... | collective-permute-start | bytes 786440 | tf_op jit(solution)/shard_map/ppermute | solution.py:91
  64.6 6.4 %collective-permute-start.11 = (bf16[2,4,128,128]{3,2,1,0:T(8,128)(2,1)S(1)}, bf16[2,4,128,128]{3,2,1,0:T(8,128)(2,1)S(1)}, u32[]{:S(2)}, u32[]{:S(2)}) collective-permute-start(bf16[2,4,128,128]{3,2,1,0:T(8,128)(2,1)S(1)} %slice.47), channel_id=1, source_target_pairs={{0,24},{4,28},{8,0},{12,4},{16,8},{20,12},{24,16},{28,20},{32,56},... | collective-permute-start | bytes 786440 | tf_op jit(solution)/shard_map/ppermute | solution.py:92
  71.0 4.2 %collective-permute-start.12 = (bf16[2,4,1024,128]{3,2,1,0:T(8,128)(2,1)S(1)}, bf16[2,4,1024,128]{3,2,1,0:T(8,128)(2,1)S(1)}, u32[]{:S(2)}, u32[]{:S(2)}) collective-permute-start(bf16[2,4,1024,128]{3,2,1,0:T(8,128)(2,1)S(1)} %constant_dynamic-update-slice_fusion.9), channel_id=1, source_target_pairs={{0,4},{4,0},{8,12},{12,8},{16,20},{20,16},{24,28},{28,24},{32,36},... | collective-permute-start | bytes 6291464 | tf_op jit(solution)/shard_map/ppermute | solution.py:107
  82.4 20.0 %copy-start.4 = (bf16[256,512]{1,0:T(8,128)(2,1)S(1)}, bf16[256,512]{1,0:T(8,128)(2,1)}, u32[]{:S(2)}) copy-start(bf16[256,512]{1,0:T(8,128)(2,1)} %param.16) | copy-start | bytes 786436
  102.6 17.4 %copy-start.5 = (f32[2048]{0:T(1024)S(1)}, f32[2048]{0:T(1024)}, u32[]{:S(2)}) copy-start(f32[2048]{0:T(1024)} %param.25) | copy-start | bytes 24580
  102.6 17.4 %copy-start.6 = (f32[2048]{0:T(1024)S(1)}, f32[2048]{0:T(1024)}, u32[]{:S(2)}) copy-start(f32[2048]{0:T(1024)} %param.24) | copy-start | bytes 24580
  102.7 18.0 %copy-start.7 = (bf16[2048,1024]{1,0:T(8,128)(2,1)S(1)}, bf16[2048,1024]{1,0:T(8,128)(2,1)}, u32[]{:S(2)}) copy-start(bf16[2048,1024]{1,0:T(8,128)(2,1)} %param.26) | copy-start | bytes 12582916
  119.6 1.1 copy-start.9
  120.7 3.7 %copy-start.8 = (bf16[1024,2048]{1,0:T(8,128)(2,1)S(1)}, bf16[1024,2048]{1,0:T(8,128)(2,1)}, u32[]{:S(2)}) copy-start(bf16[1024,2048]{1,0:T(8,128)(2,1)} %param.28) | copy-start | bytes 12582916
  126.8 16.9 %all-to-all-start.3 = ((bf16[4,256,512]{2,1,0:T(8,128)(2,1)}), bf16[4,256,512]{2,1,0:T(8,128)(2,1)S(1)}, u32[]{:S(2)}, u32[]{:S(2)}) async-start(bf16[4,256,512]{2,1,0:T(8,128)(2,1)} %bitcast.172), calls=%async_computation.3 | async-start | bytes 2097152 | tf_op jit(solution)/shard_map/all_to_all | solution.py:58

commit v13 on v11

--- a/solution.py
+++ b/solution.py
@@ -94,13 +94,15 @@
     return jnp.concatenate(pieces, axis=2)
 
 
-def ring_gather_seq(block, seq_size, companion):
+def ring_gather_seq(block, seq_size, companion, between):
     cores = 2
     lanes = 4
     shape = (seq_size // (lanes * cores), lanes, cores)
     gathered = ring_along(block, shape, 0)
     gathered, companion = lax.optimization_barrier((gathered, companion))
+    companion = between(companion)
     gathered = ring_along(gathered, shape, 1)
+    gathered, companion = lax.optimization_barrier((gathered, companion))
     partner = lax.ppermute(gathered, "seq", shift_pairs(shape, 2, 1))
     return jnp.concatenate([gathered, partner], axis=2), companion
 
@@ -156,14 +158,17 @@
     )
     leaf_heads = head_major(leaf_kv, head_count)
     running = attend(running, query_heads, leaf_heads[0], leaf_heads[1], True)
-    root_full, (arrived, running) = ring_gather_seq(
-        head_major(root_kv, head_count), seq_size, (arrived, running)
-    )
-    branch_mine = jnp.transpose(arrived, (1, 2, 0, 3, 4)).reshape(
-        2, head_count, seq_size * local_rows, HD
-    )
-
-    running = attend_blocks(running, query_heads, branch_mine[0], branch_mine[1])
+    def attend_branch(companion):
+        arrived, running = companion
+        branch_mine = jnp.transpose(arrived, (1, 2, 0, 3, 4)).reshape(
+            2, head_count, seq_size * local_rows, HD
+        )
+        return attend_blocks(running, query_heads, branch_mine[0], branch_mine[1])
+
+    root_full, running = ring_gather_seq(
+        head_major(root_kv, head_count), seq_size, (arrived, running), attend_branch
+    )
+
     running = attend_blocks(running, query_heads, root_full[0], root_full[1])
     largest, totals, accumulated = running
     attention = (

time: 143 us -> 145 us (1.014)
  local copies, waits for them, and re-layouts: 11.1 us -> 17.2 us
  waiting for transfers between devices: 39.9 us -> 37.1 us
  matrix products: 14.2 us -> 12.4 us
    unnamed x34 -> x37, local copies, waits for them, and re-layouts: 1.86 us -> 8.3 us
    ppermute x4, waiting for transfers between devices: 16.8 us -> 14.2 us  [ring_along(): from_below = lax.ppermute(from_below, 'seq', up)]
    ppermute x2, waiting for transfers between devices: 5.54 us -> 3.58 us  [ring_along(): first = lax.ppermute(from_below[:, :, :half], 'seq', up)]
    dot_general x4, matrix products: 5.38 us -> 3.49 us  [attend(): jnp.einsum('hqk,hkd->hqd', weights.astype(jnp.bfloat16), value_heads, pre...]
  transfers between devices with their start and end apart: 15 -> 15, of which waited for: 8 -> 8; matrix products, arithmetic and copies ran while one was open for 10% -> 14% of each run, Pallas kernels for 0% -> 0%
where the time goes in v13:
time: 145 us; the launch traced here: 144 us
  waiting for transfers between devices  37.1 us (26%)
  blocking collectives  36.7 us (25%)
  starting transfers between devices  32.8 us (23%)
  local copies, waits for them, and re-layouts  17.2 us (12%)
  matrix products  12.4 us (9%)
  other arithmetic  6.92 us (5%)
    all_to_all x1, blocking collectives, tensor_sum_scatter(): arrived = lax.all_to_all(pieces, 'tensor', 0, 0, tiled=True)  19.8 us
    all_to_all x1, blocking collectives, tensor_gather(): arrived = lax.all_to_all(copies, 'tensor', 0, 0, tiled=True)  16.9 us
    ppermute x4, waiting for transfers between devices, ring_along(): from_below = lax.ppermute(from_below, 'seq', up)  14.2 us
    all_to_all x1, waiting for transfers between devices, tensor_sum_scatter(): arrived = lax.all_to_all(pieces, 'tensor', 0, 0, tiled=True)  12.6 us
    ppermute x4, starting transfers between devices, ring_along(): from_above = lax.ppermute(from_above, 'seq', down)  9.44 us
    all_to_all x1, starting transfers between devices, per_device(): arrived = lax.all_to_all(picked, 'seq', 0, 0, tiled=True)  9.39 us
    unnamed x37, local copies, waits for them, and re-layouts  8.3 us
    ppermute x4, starting transfers between devices, ring_along(): from_below = lax.ppermute(from_below, 'seq', up)  4.92 us
  transfers between devices with their start and end apart: 15, of which 8 were waited for; matrix products, arithmetic and copies ran while one was open for 14% of the time, Pallas kernels for 0%

profile of v13, /device:TPU:2, one launch (start us, length us, event | category | flops | bytes accessed | tf_op | source)
XLA Modules:
  0.0 143.7 jit_solution(10958210527421574715)
XLA Ops:
  0.0 1.6 %bitcast_bitcast_fusion.12 = bf16[2,4,32,128]{3,2,1,0:T(8,128)(2,1)} fusion(bf16[2,32,512]{2,1,0:T(8,128)(2,1)} %param.22), kind=kLoop, calls=%fused_computation.86 | loop fusion | bytes 131072 | tf_op jit(solution)/shard_map/transpose | solution.py:50
  1.6 1.9 %collective-permute-start = (bf16[2,4,32,128]{3,2,1,0:T(8,128)(2,1)}, bf16[2,4,32,128]{3,2,1,0:T(8,128)(2,1)}, u32[]{:S(2)}, u32[]{:S(2)}) collective-permute-start(bf16[2,4,32,128]{3,2,1,0:T(8,128)(2,1)} %bitcast_bitcast_fusion.12), channel_id=1, source_target_pairs={{0,32},{4,36},{8,40},{12,44},{16,48},{20,52},{24,56},{28,60},{32,6... | collective-permute-start | bytes 196616 | tf_op jit(solution)/shard_map/ppermute | solution.py:86
  3.5 3.9 %collective-permute-start.1 = (bf16[2,4,32,128]{3,2,1,0:T(8,128)(2,1)}, bf16[2,4,32,128]{3,2,1,0:T(8,128)(2,1)}, u32[]{:S(2)}, u32[]{:S(2)}) collective-permute-start(bf16[2,4,32,128]{3,2,1,0:T(8,128)(2,1)} %bitcast_bitcast_fusion.12), channel_id=1, source_target_pairs={{0,224},{4,228},{8,232},{12,236},{16,240},{20,244},{24,248},{28,25... | collective-permute-start | bytes 196616 | tf_op jit(solution)/shard_map/ppermute | solution.py:87
  7.5 0.7 compare_select_fusion
  8.2 0.7 compare_and_fusion
  8.8 1.0 copy.57
  9.9 1.0 gather_fusion
  11.2 1.0 reshape.139
  12.2 9.4 %all-to-all-start = ((bf16[64,2,4,4,128]{4,2,3,1,0:T(4,128)(2,1)}), bf16[64,2,4,4,128]{4,2,3,1,0:T(4,128)(2,1)S(1)}, u32[]{:S(2)}, u32[]{:S(2)}) async-start(bf16[64,2,4,4,128]{4,2,3,1,0:T(4,128)(2,1)} %bitcast.3), calls=%async_computation | async-start | bytes 1048576 | tf_op jit(solution)/shard_map/all_to_all | solution.py:141
  21.7 0.7 dynamic_slice.6
  22.3 0.7 iota_compare_fusion.1
  23.4 1.3 fusion.54
  25.9 0.6 constant_dynamic-update-slice_fusion.8
  26.6 1.5 %collective-permute-start.2 = (bf16[2,4,32,128]{3,2,1,0:T(8,128)(2,1)}, bf16[2,4,32,128]{3,2,1,0:T(8,128)(2,1)S(1)}, u32[]{:S(2)}, u32[]{:S(2)}) collective-permute-start(bf16[2,4,32,128]{3,2,1,0:T(8,128)(2,1)} %collective-permute-done), channel_id=1, source_target_pairs={{0,32},{4,36},{8,40},{12,44},{16,48},{20,52},{24,56},{28,60},{32,6... | collective-permute-start | bytes 196616 | tf_op jit(solution)/shard_map/ppermute | solution.py:86
  28.0 1.8 %collective-permute-start.3 = (bf16[2,4,32,128]{3,2,1,0:T(8,128)(2,1)}, bf16[2,4,32,128]{3,2,1,0:T(8,128)(2,1)S(1)}, u32[]{:S(2)}, u32[]{:S(2)}) collective-permute-start(bf16[2,4,32,128]{3,2,1,0:T(8,128)(2,1)} %collective-permute-done.1), channel_id=1, source_target_pairs={{0,224},{4,228},{8,232},{12,236},{16,240},{20,244},{24,248},{28,25... | collective-permute-start | bytes 196616 | tf_op jit(solution)/shard_map/ppermute | solution.py:87
  29.8 1.5 %constant_dynamic-update-slice_fusion.7 = bf16[2,4,256,128]{3,2,1,0:T(8,128)(2,1)} fusion(bf16[2,4,256,128]{3,2,1,0:T(8,128)(2,1)} %constant_dynamic-update-slice_fusion.8, bf16[2,4,32,128]{3,2,1,0:T(8,128)(2,1)} %collective-permute-done), kind=kLoop, calls=%fused_computation.96 | loop fusion | bytes 131072
  31.3 1.5 %constant_dynamic-update-slice_fusion.6 = bf16[2,4,256,128]{3,2,1,0:T(8,128)(2,1)} fusion(bf16[2,4,256,128]{3,2,1,0:T(8,128)(2,1)} %constant_dynamic-update-slice_fusion.7, bf16[2,4,32,128]{3,2,1,0:T(8,128)(2,1)} %collective-permute-done.1), kind=kLoop, calls=%fused_computation.95 | loop fusion | bytes 131072
  32.8 4.9 %collective-permute-done.2 = bf16[2,4,32,128]{3,2,1,0:T(8,128)(2,1)S(1)} collective-permute-done((bf16[2,4,32,128]{3,2,1,0:T(8,128)(2,1)}, bf16[2,4,32,128]{3,2,1,0:T(8,128)(2,1)S(1)}, u32[]{:S(2)}, u32[]{:S(2)}) %collective-permute-start.2) | collective-permute-done | bytes 65568 | tf_op jit(solution)/shard_map/ppermute | solution.py:86
  37.7 3.2 %collective-permute-start.5 = (bf16[2,4,32,128]{3,2,1,0:T(8,128)(2,1)S(1)}, bf16[2,4,32,128]{3,2,1,0:T(8,128)(2,1)S(1)}, u32[]{:S(2)}, u32[]{:S(2)}) collective-permute-start(bf16[2,4,32,128]{3,2,1,0:T(8,128)(2,1)S(1)} %collective-permute-done.3), channel_id=1, source_target_pairs={{0,224},{4,228},{8,232},{12,236},{16,240},{20,244},{24,248},{28,25... | collective-permute-start | bytes 196616 | tf_op jit(solution)/shard_map/ppermute | solution.py:87
  41.0 0.7 constant_dynamic-update-slice_fusion.5
  41.6 0.6 constant_dynamic-update-slice_fusion.4
  42.3 0.9 collective-permute-done.4
  43.2 3.2 %collective-permute-start.7 = (bf16[2,4,16,128]{3,2,1,0:T(8,128)(2,1)S(1)}, bf16[2,4,16,128]{3,2,1,0:T(8,128)(2,1)S(1)}, u32[]{:S(2)}, u32[]{:S(2)}) collective-permute-start(bf16[2,4,16,128]{3,2,1,0:T(8,128)(2,1)S(1)} %slice.45), channel_id=1, source_target_pairs={{0,224},{4,228},{8,232},{12,236},{16,240},{20,244},{24,248},{28,25... | collective-permute-start | bytes 98312 | tf_op jit(solution)/shard_map/ppermute | solution.py:92
  46.4 0.6 constant_dynamic-update-slice_fusion.3
  47.1 0.7 constant_dynamic-update-slice_fusion.2
  48.3 0.6 constant_dynamic-update-slice_fusion.1
  49.0 0.6 constant_dynamic-update-slice_fusion
  49.6 1.5 %collective-permute-start.8 = (bf16[2,4,256,128]{3,2,1,0:T(8,128)(2,1)}, bf16[2,4,256,128]{3,2,1,0:T(8,128)(2,1)S(1)}, u32[]{:S(2)}, u32[]{:S(2)}) collective-permute-start(bf16[2,4,256,128]{3,2,1,0:T(8,128)(2,1)} %constant_dynamic-update-slice_fusion), channel_id=1, source_target_pairs={{0,8},{4,12},{8,16},{12,20},{16,24},{20,28},{24,0},{28,4},{32,40},... | collective-permute-start | bytes 1572872 | tf_op jit(solution)/shard_map/ppermute | solution.py:86
  53.4 8.3 %collective-permute-done.8 = bf16[2,4,256,128]{3,2,1,0:T(8,128)(2,1)S(1)} collective-permute-done((bf16[2,4,256,128]{3,2,1,0:T(8,128)(2,1)}, bf16[2,4,256,128]{3,2,1,0:T(8,128)(2,1)S(1)}, u32[]{:S(2)}, u32[]{:S(2)}) %collective-permute-start.8) | collective-permute-done | bytes 524320 | tf_op jit(solution)/shard_map/ppermute | solution.py:86
  61.7 1.7 %collective-permute-start.10 = (bf16[2,4,128,128]{3,2,1,0:T(8,128)(2,1)S(1)}, bf16[2,4,128,128]{3,2,1,0:T(8,128)(2,1)S(1)}, u32[]{:S(2)}, u32[]{:S(2)}) collective-permute-start(bf16[2,4,128,128]{3,2,1,0:T(8,128)(2,1)S(1)} %slice.48), channel_id=1, source_target_pairs={{0,8},{4,12},{8,16},{12,20},{16,24},{20,28},{24,0},{28,4},{32,40},... | collective-permute-start | bytes 786440 | tf_op jit(solution)/shard_map/ppermute | solution.py:91
  63.4 1.1 constant_dynamic-update-slice_fusion.13
  65.2 3.0 %collective-permute-done.10 = bf16[2,4,128,128]{3,2,1,0:T(8,128)(2,1)S(1)} collective-permute-done((bf16[2,4,128,128]{3,2,1,0:T(8,128)(2,1)S(1)}, bf16[2,4,128,128]{3,2,1,0:T(8,128)(2,1)S(1)}, u32[]{:S(2)}, u32[]{:S(2)}) %collective-permute-start.10) | collective-permute-done | bytes 262176 | tf_op jit(solution)/shard_map/ppermute | solution.py:91
  68.2 2.7 %collective-permute-done.11 = bf16[2,4,128,128]{3,2,1,0:T(8,128)(2,1)S(1)} collective-permute-done((bf16[2,4,128,128]{3,2,1,0:T(8,128)(2,1)S(1)}, bf16[2,4,128,128]{3,2,1,0:T(8,128)(2,1)S(1)}, u32[]{:S(2)}, u32[]{:S(2)}) %collective-permute-start.11) | collective-permute-done | bytes 262176 | tf_op jit(solution)/shard_map/ppermute | solution.py:92
  71.3 4.0 %collective-permute-done.12 = bf16[2,4,1024,128]{3,2,1,0:T(8,128)(2,1)S(1)} collective-permute-done((bf16[2,4,1024,128]{3,2,1,0:T(8,128)(2,1)S(1)}, bf16[2,4,1024,128]{3,2,1,0:T(8,128)(2,1)S(1)}, u32[]{:S(2)}, u32[]{:S(2)}) %collective-permute-start.12) | collective-permute-done | bytes 2097184 | tf_op jit(solution)/shard_map/ppermute | solution.py:106
  75.6 1.3 bitcast_reduce_fusion
  76.8 1.4 fusion.1
  78.2 2.3 %fusion.38 = bf16[256,4,128]{2,0,1:T(8,128)(2,1)S(1)} fusion(f32[4,256]{1,0:T(4,128)S(1)} %get-tuple-element.25, f32[4,256,128]{2,1,0:T(8,128)S(1)} %multiply_add_fusion, f32[4,256]{1,0:T(4,128)S(1)} %get-tuple-element.26, bf16[2,4,2048,128]{3,2,1,0:T(8,128)(2,1)S(1)} %constant_dynamic-update-slice_fusion.14, f32[4,2048,256]{2,1,0:T(8,128)S(1)} %get-tuple-element.45, ...), kind=kOutput, calls=%fused_computation.76 | convolution fusion | flops 543686656 | bytes 11284480 | tf_op jit(solution)/shard_map/hqk,hkd->hqd/dot_general | solution.py:24
  80.7 0.7 convolution_convert_fusion
  81.5 19.8 %all_to_all.20 = bf16[4,256,512]{2,1,0:T(8,128)(2,1)S(1)} all-to-all(bf16[4,256,512]{2,1,0:T(8,128)(2,1)S(1)} %bitcast.163), channel_id=1, replica_groups=mesh['seq'=64,'tensor'=4] {'tensor'}, dimensions={0} | all-to-all | bytes 2097152 | tf_op jit(solution)/shard_map/all_to_all | solution.py:58
  101.8 16.9 %all_to_all.21 = bf16[4,256,512]{1,2,0:T(8,128)(2,1)S(1)} all-to-all(bf16[4,256,512]{1,2,0:T(8,128)(2,1)S(1)} %broadcast_in_dim.79), channel_id=1, replica_groups=mesh['seq'=64,'tensor'=4] {'tensor'}, dimensions={0} | all-to-all | bytes 2097152 | tf_op jit(solution)/shard_map/all_to_all | solution.py:65
  119.1 0.7 fusion.11
  119.8 3.7 %fusion.17 = bf16[256,1024]{1,0:T(8,128)(2,1)S(1)} fusion(bf16[256,2048]{0,1:T(8,128)(2,1)S(1)} %fusion.11, bf16[2048,1024]{1,0:T(8,128)(2,1)S(1)} %copy-done.7, f32[1024]{0:T(1024)S(1)} %copy-done.10), kind=kOutput, calls=%fused_computation.34 | convolution fusion | flops 1091043328 | bytes 5771264 | tf_op jit(solution)/shard_map/dot_general | solution.py:192
  123.6 1.3 convolution_convert_fusion.1
  124.8 1.0 copy.129
  125.9 3.5 %all-to-all-start.3 = ((bf16[4,256,512]{2,1,0:T(8,128)(2,1)}), bf16[4,256,512]{2,1,0:T(8,128)(2,1)S(1)}, u32[]{:S(2)}, u32[]{:S(2)}) async-start(bf16[4,256,512]{2,1,0:T(8,128)(2,1)} %bitcast.161), calls=%async_computation.3 | async-start | bytes 2097152 | tf_op jit(solution)/shard_map/all_to_all | solution.py:58
  129.4 0.8 dynamic_slice.7
  130.2 12.6 %all-to-all-done.3 = bf16[4,256,512]{2,1,0:T(8,128)(2,1)S(1)} async-done(((bf16[4,256,512]{2,1,0:T(8,128)(2,1)}), bf16[4,256,512]{2,1,0:T(8,128)(2,1)S(1)}, u32[]{:S(2)}, u32[]{:S(2)}) %all-to-all-start.3) | async-done | bytes 1048608 | tf_op jit(solution)/shard_map/all_to_all | solution.py:58
  142.9 0.8 add_convert_fusion
  (78 shorter events, 7.2 us)
Async XLA Ops:
  0.0 80.6 %copy-start = (bf16[512,2048]{1,0:T(8,128)(2,1)S(1)}, bf16[512,2048]{1,0:T(8,128)(2,1)}, u32[]{:S(2)}) copy-start(bf16[512,2048]{1,0:T(8,128)(2,1)} %param.23) | copy-start | bytes 6291460
  1.6 24.9 %collective-permute-start = (bf16[2,4,32,128]{3,2,1,0:T(8,128)(2,1)}, bf16[2,4,32,128]{3,2,1,0:T(8,128)(2,1)}, u32[]{:S(2)}, u32[]{:S(2)}) collective-permute-start(bf16[2,4,32,128]{3,2,1,0:T(8,128)(2,1)} %bitcast_bitcast_fusion.12), channel_id=1, source_target_pairs={{0,32},{4,36},{8,40},{12,44},{16,48},{20,52},{24,56},{28,60},{32,6... | collective-permute-start | bytes 196616 | tf_op jit(solution)/shard_map/ppermute | solution.py:86
  3.5 24.5 %collective-permute-start.1 = (bf16[2,4,32,128]{3,2,1,0:T(8,128)(2,1)}, bf16[2,4,32,128]{3,2,1,0:T(8,128)(2,1)}, u32[]{:S(2)}, u32[]{:S(2)}) collective-permute-start(bf16[2,4,32,128]{3,2,1,0:T(8,128)(2,1)} %bitcast_bitcast_fusion.12), channel_id=1, source_target_pairs={{0,224},{4,228},{8,232},{12,236},{16,240},{20,244},{24,248},{28,25... | collective-permute-start | bytes 196616 | tf_op jit(solution)/shard_map/ppermute | solution.py:87
  9.8 11.8 %copy-start.11 = (s32[64]{0:T(128)S(1)}, s32[64]{0:T(128)}, u32[]{:S(2)}) copy-start(s32[64]{0:T(128)} %param.31) | copy-start | bytes 772
  9.8 13.3 %copy-start.1 = (bf16[256,512]{1,0:T(8,128)(2,1)S(1)}, bf16[256,512]{1,0:T(8,128)(2,1)}, u32[]{:S(2)}) copy-start(bf16[256,512]{1,0:T(8,128)(2,1)} %param.17) | copy-start | bytes 786436
  10.9 12.2 %copy-start.4 = (bf16[2,64,512]{2,1,0:T(8,128)(2,1)S(1)}, bf16[2,64,512]{2,1,0:T(8,128)(2,1)}, u32[]{:S(2)}) copy-start(bf16[2,64,512]{2,1,0:T(8,128)(2,1)} %param.20) | copy-start | bytes 393220
  12.2 37.3 %all-to-all-start = ((bf16[64,2,4,4,128]{4,2,3,1,0:T(4,128)(2,1)}), bf16[64,2,4,4,128]{4,2,3,1,0:T(4,128)(2,1)S(1)}, u32[]{:S(2)}, u32[]{:S(2)}) async-start(bf16[64,2,4,4,128]{4,2,3,1,0:T(4,128)(2,1)} %bitcast.3), calls=%async_computation | async-start | bytes 1048576 | tf_op jit(solution)/shard_map/all_to_all | solution.py:141
  21.6 3.4 %copy-start.9 = (bf16[256,512]{1,0:T(8,128)(2,1)S(1)}, bf16[256,512]{1,0:T(8,128)(2,1)}, u32[]{:S(2)}) copy-start(bf16[256,512]{1,0:T(8,128)(2,1)} %param.19) | copy-start | bytes 786436
  24.9 1.0 copy-start.2
  26.6 11.2 %collective-permute-start.2 = (bf16[2,4,32,128]{3,2,1,0:T(8,128)(2,1)}, bf16[2,4,32,128]{3,2,1,0:T(8,128)(2,1)S(1)}, u32[]{:S(2)}, u32[]{:S(2)}) collective-permute-start(bf16[2,4,32,128]{3,2,1,0:T(8,128)(2,1)} %collective-permute-done), channel_id=1, source_target_pairs={{0,32},{4,36},{8,40},{12,44},{16,48},{20,52},{24,56},{28,60},{32,6... | collective-permute-start | bytes 196616 | tf_op jit(solution)/shard_map/ppermute | solution.py:86
  28.0 9.7 %collective-permute-start.3 = (bf16[2,4,32,128]{3,2,1,0:T(8,128)(2,1)}, bf16[2,4,32,128]{3,2,1,0:T(8,128)(2,1)S(1)}, u32[]{:S(2)}, u32[]{:S(2)}) collective-permute-start(bf16[2,4,32,128]{3,2,1,0:T(8,128)(2,1)} %collective-permute-done.1), channel_id=1, source_target_pairs={{0,224},{4,228},{8,232},{12,236},{16,240},{20,244},{24,248},{28,25... | collective-permute-start | bytes 196616 | tf_op jit(solution)/shard_map/ppermute | solution.py:87
  37.7 5.5 %collective-permute-start.4 = (bf16[2,4,32,128]{3,2,1,0:T(8,128)(2,1)S(1)}, bf16[2,4,32,128]{3,2,1,0:T(8,128)(2,1)S(1)}, u32[]{:S(2)}, u32[]{:S(2)}) collective-permute-start(bf16[2,4,32,128]{3,2,1,0:T(8,128)(2,1)S(1)} %collective-permute-done.2), channel_id=1, source_target_pairs={{0,32},{4,36},{8,40},{12,44},{16,48},{20,52},{24,56},{28,60},{32,6... | collective-permute-start | bytes 196616 | tf_op jit(solution)/shard_map/ppermute | solution.py:86
  37.7 5.5 %collective-permute-start.5 = (bf16[2,4,32,128]{3,2,1,0:T(8,128)(2,1)S(1)}, bf16[2,4,32,128]{3,2,1,0:T(8,128)(2,1)S(1)}, u32[]{:S(2)}, u32[]{:S(2)}) collective-permute-start(bf16[2,4,32,128]{3,2,1,0:T(8,128)(2,1)S(1)} %collective-permute-done.3), channel_id=1, source_target_pairs={{0,224},{4,228},{8,232},{12,236},{16,240},{20,244},{24,248},{28,25... | collective-permute-start | bytes 196616 | tf_op jit(solution)/shard_map/ppermute | solution.py:87
  43.2 5.1 %collective-permute-start.6 = (bf16[2,4,16,128]{3,2,1,0:T(8,128)(2,1)S(1)}, bf16[2,4,16,128]{3,2,1,0:T(8,128)(2,1)S(1)}, u32[]{:S(2)}, u32[]{:S(2)}) collective-permute-start(bf16[2,4,16,128]{3,2,1,0:T(8,128)(2,1)S(1)} %slice.44), channel_id=1, source_target_pairs={{0,32},{4,36},{8,40},{12,44},{16,48},{20,52},{24,56},{28,60},{32,6... | collective-permute-start | bytes 98312 | tf_op jit(solution)/shard_map/ppermute | solution.py:91
  43.2 5.7 %collective-permute-start.7 = (bf16[2,4,16,128]{3,2,1,0:T(8,128)(2,1)S(1)}, bf16[2,4,16,128]{3,2,1,0:T(8,128)(2,1)S(1)}, u32[]{:S(2)}, u32[]{:S(2)}) collective-permute-start(bf16[2,4,16,128]{3,2,1,0:T(8,128)(2,1)S(1)} %slice.45), channel_id=1, source_target_pairs={{0,224},{4,228},{8,232},{12,236},{16,240},{20,244},{24,248},{28,25... | collective-permute-start | bytes 98312 | tf_op jit(solution)/shard_map/ppermute | solution.py:92
  49.6 12.2 %collective-permute-start.8 = (bf16[2,4,256,128]{3,2,1,0:T(8,128)(2,1)}, bf16[2,4,256,128]{3,2,1,0:T(8,128)(2,1)S(1)}, u32[]{:S(2)}, u32[]{:S(2)}) collective-permute-start(bf16[2,4,256,128]{3,2,1,0:T(8,128)(2,1)} %constant_dynamic-update-slice_fusion), channel_id=1, source_target_pairs={{0,8},{4,12},{8,16},{12,20},{16,24},{20,28},{24,0},{28,4},{32,40},... | collective-permute-start | bytes 1572872 | tf_op jit(solution)/shard_map/ppermute | solution.py:86
  51.1 13.4 %collective-permute-start.9 = (bf16[2,4,256,128]{3,2,1,0:T(8,128)(2,1)}, bf16[2,4,256,128]{3,2,1,0:T(8,128)(2,1)S(1)}, u32[]{:S(2)}, u32[]{:S(2)}) collective-permute-start(bf16[2,4,256,128]{3,2,1,0:T(8,128)(2,1)} %constant_dynamic-update-slice_fusion), channel_id=1, source_target_pairs={{0,24},{4,28},{8,0},{12,4},{16,8},{20,12},{24,16},{28,20},{32,56},... | collective-permute-start | bytes 1572872 | tf_op jit(solution)/shard_map/ppermute | solution.py:87
  61.7 6.4 %collective-permute-start.10 = (bf16[2,4,128,128]{3,2,1,0:T(8,128)(2,1)S(1)}, bf16[2,4,128,128]{3,2,1,0:T(8,128)(2,1)S(1)}, u32[]{:S(2)}, u32[]{:S(2)}) collective-permute-start(bf16[2,4,128,128]{3,2,1,0:T(8,128)(2,1)S(1)} %slice.48), channel_id=1, source_target_pairs={{0,8},{4,12},{8,16},{12,20},{16,24},{20,28},{24,0},{28,4},{32,40},... | collective-permute-start | bytes 786440 | tf_op jit(solution)/shard_map/ppermute | solution.py:91
  64.5 6.4 %collective-permute-start.11 = (bf16[2,4,128,128]{3,2,1,0:T(8,128)(2,1)S(1)}, bf16[2,4,128,128]{3,2,1,0:T(8,128)(2,1)S(1)}, u32[]{:S(2)}, u32[]{:S(2)}) collective-permute-start(bf16[2,4,128,128]{3,2,1,0:T(8,128)(2,1)S(1)} %slice.49), channel_id=1, source_target_pairs={{0,24},{4,28},{8,0},{12,4},{16,8},{20,12},{24,16},{28,20},{32,56},... | collective-permute-start | bytes 786440 | tf_op jit(solution)/shard_map/ppermute | solution.py:92
  71.0 4.2 %collective-permute-start.12 = (bf16[2,4,1024,128]{3,2,1,0:T(8,128)(2,1)S(1)}, bf16[2,4,1024,128]{3,2,1,0:T(8,128)(2,1)S(1)}, u32[]{:S(2)}, u32[]{:S(2)}) collective-permute-start(bf16[2,4,1024,128]{3,2,1,0:T(8,128)(2,1)S(1)} %constant_dynamic-update-slice_fusion.9), channel_id=1, source_target_pairs={{0,4},{4,0},{8,12},{12,8},{16,20},{20,16},{24,28},{28,24},{32,36},... | collective-permute-start | bytes 6291464 | tf_op jit(solution)/shard_map/ppermute | solution.py:106
  81.5 20.0 %copy-start.3 = (bf16[256,512]{1,0:T(8,128)(2,1)S(1)}, bf16[256,512]{1,0:T(8,128)(2,1)}, u32[]{:S(2)}) copy-start(bf16[256,512]{1,0:T(8,128)(2,1)} %param.16) | copy-start | bytes 786436
  101.7 17.4 %copy-start.5 = (f32[2048]{0:T(1024)S(1)}, f32[2048]{0:T(1024)}, u32[]{:S(2)}) copy-start(f32[2048]{0:T(1024)} %param.25) | copy-start | bytes 24580
  101.7 17.4 %copy-start.6 = (f32[2048]{0:T(1024)S(1)}, f32[2048]{0:T(1024)}, u32[]{:S(2)}) copy-start(f32[2048]{0:T(1024)} %param.24) | copy-start | bytes 24580
  101.8 18.0 %copy-start.7 = (bf16[2048,1024]{1,0:T(8,128)(2,1)S(1)}, bf16[2048,1024]{1,0:T(8,128)(2,1)}, u32[]{:S(2)}) copy-start(bf16[2048,1024]{1,0:T(8,128)(2,1)} %param.26) | copy-start | bytes 12582916
  118.7 1.1 copy-start.10
  119.8 3.7 %copy-start.8 = (bf16[1024,2048]{1,0:T(8,128)(2,1)S(1)}, bf16[1024,2048]{1,0:T(8,128)(2,1)}, u32[]{:S(2)}) copy-start(bf16[1024,2048]{1,0:T(8,128)(2,1)} %param.28) | copy-start | bytes 12582916
  125.9 16.9 %all-to-all-start.3 = ((bf16[4,256,512]{2,1,0:T(8,128)(2,1)}), bf16[4,256,512]{2,1,0:T(8,128)(2,1)S(1)}, u32[]{:S(2)}, u32[]{:S(2)}) async-start(bf16[4,256,512]{2,1,0:T(8,128)(2,1)} %bitcast.161), calls=%async_computation.3 | async-start | bytes 2097152 | tf_op jit(solution)/shard_map/all_to_all | solution.py:58
